TPU v7x, 256 devices: a whole 4x4x8 slice. The times are simulated.
256 devices in a mesh: dp: 32 (over x_lo, z, core), tensor: 8 (over x_hi, y).
Axes of the slice: x: 4 (x_hi: 2, x_lo: 2; x = x_hi * 2 + x_lo), y: 4, z: 8, core: 2. Of those that a mesh axis runs over, the one named last changes fastest.
Arguments:
- hidden_input_state: bfloat16 [12288, 4608], P('dp', 'tensor'), may hold values from -80 to 80
- norm_gain: float32 [4608], replicated, may hold values from 0.5 to 1.5
- head_weight: bfloat16 [4608, 8192], P(None, 'tensor'), may hold values from -2 to 2
- target_ids: int32 [12288], P('dp'), may hold values from 0 to 8191
Outputs:
- hidden_state_gradient: float32 [12288, 4608], P('dp', 'tensor')
- grad_head: float32 [4608, 8192], P('dp', 'tensor')
- norm_gain_gradient: float32 [4608], P('tensor')
All inputs are finite; a program needn't handle non-finite values.
Results may differ from a plain program's by a relative error of at most 0.0039.
Values may be sent and summed in bfloat16 or wider, within the bound.
No kernel may reach another device: no remote copies, remote signals or barrier semaphores. Data moves between devices by JAX's collectives and lax.ppermute only.
A program may use at most 192 MiB of HBM per device.

v0:
```python
import jax
import jax.numpy as jnp
from jax import lax
from jax.sharding import Mesh, PartitionSpec as P

epsilon = 1e-06


def shift_gather(x, axis, n):
    me = lax.axis_index(axis)
    got = [x]
    for k in range(1, n):
        got.append(lax.ppermute(x, axis, [(c, (c + k) % n) for c in range(n)]))
    rev = jnp.stack(got[::-1])
    doubled = jnp.concatenate([rev, rev], axis=0)
    return lax.dynamic_slice_in_dim(doubled, (n - 1) - me, n, axis=0)


def butterfly_sum(x, axis, n):
    b = 1
    while b < n:
        x = x + lax.ppermute(x, axis, [(c, c ^ b) for c in range(n)])
        b *= 2
    return x


def two_stage_reduce_scatter(parts, axis, n_hi, n_lo):
    me = lax.axis_index(axis)
    h = me // n_lo
    lo = me % n_lo
    rows = parts.shape[2]
    half = (rows // 2) // 8 * 8
    fwd = parts[:, :, :half, :]
    bwd = parts[:, :, half:, :]
    perm_f = [(a * n_lo + l, a * n_lo + (l + 1) % n_lo) for a in range(n_hi) for l in range(n_lo)]
    perm_b = [(a * n_lo + l, a * n_lo + (l - 1) % n_lo) for a in range(n_hi) for l in range(n_lo)]
    recv_f = recv_b = None
    for s in range(n_lo - 1):
        send_f = lax.dynamic_index_in_dim(fwd, (lo - 1 - s) % n_lo, 1, keepdims=False)
        send_b = lax.dynamic_index_in_dim(bwd, (lo + 1 + s) % n_lo, 1, keepdims=False)
        if recv_f is not None:
            send_f = send_f + recv_f
            send_b = send_b + recv_b
        recv_f = lax.ppermute(send_f, axis, perm_f)
        recv_b = lax.ppermute(send_b, axis, perm_b)
    sum_f = lax.dynamic_index_in_dim(fwd, lo, 1, keepdims=False) + recv_f
    sum_b = lax.dynamic_index_in_dim(bwd, lo, 1, keepdims=False) + recv_b
    perm_h = [(a * n_lo + l, (n_hi - 1 - a) * n_lo + l) for a in range(n_hi) for l in range(n_lo)]
    out_f = lax.dynamic_index_in_dim(sum_f, h, 0, keepdims=False) + lax.ppermute(
        lax.dynamic_index_in_dim(sum_f, n_hi - 1 - h, 0, keepdims=False), axis, perm_h
    )
    out_b = lax.dynamic_index_in_dim(sum_b, h, 0, keepdims=False) + lax.ppermute(
        lax.dynamic_index_in_dim(sum_b, n_hi - 1 - h, 0, keepdims=False), axis, perm_h
    )
    return jnp.concatenate([out_f, out_b], axis=0)


def shards(hidden_input_state, norm_gain, head_weight, target_ids):
    tokens, local_cols = hidden_input_state.shape
    width, vocab_rows = head_weight.shape
    n_tensor = width // local_cols
    n_outer = lax.psum(1, "outer")
    blocks = shift_gather(hidden_input_state, "tensor", n_tensor)
    gathered = jnp.transpose(blocks, (1, 0, 2)).reshape(tokens, width)
    values = gathered.astype(jnp.float32)
    scaled_rows = lax.rsqrt(jnp.mean(values * values, axis=1, keepdims=True) + epsilon)
    normalized = values * scaled_rows
    normed = (normalized * norm_gain[None, :]).astype(jnp.bfloat16)
    logits = jnp.dot(normed, head_weight, preferred_element_type=jnp.float32)
    local_top = jnp.max(logits, axis=1)
    local_total = jnp.sum(jnp.exp(logits - local_top[:, None]), axis=1)
    stats = shift_gather(jnp.stack([local_top, local_total]), "tensor", n_tensor)
    row_top = jnp.max(stats[:, 0, :], axis=0)
    row_total = jnp.sum(stats[:, 1, :] * jnp.exp(stats[:, 0, :] - row_top[None, :]), axis=0)
    log_total = row_top + jnp.log(row_total)
    offset = lax.axis_index("tensor") * vocab_rows
    column_ids = offset + lax.broadcasted_iota(jnp.int32, (1, vocab_rows), 1)
    onehot = (column_ids == target_ids[:, None]).astype(jnp.float32)
    dlogits = (jnp.exp(logits - log_total[:, None]) - onehot).astype(jnp.bfloat16)

    head_partial = lax.dot_general(
        normed, dlogits, (((0,), (0,)), ((), ())), preferred_element_type=jnp.float32
    )
    grad_head = lax.psum_scatter(head_partial, ("outer", "core"), scatter_dimension=0, tiled=True)

    partial = lax.dot_general(
        head_weight, dlogits, (((1,), (1,)), ((), ())), preferred_element_type=jnp.float32
    )
    normalized_t = normalized.T
    inner_part = jnp.sum(partial * (norm_gain[:, None] * normalized_t), axis=0)
    gain_part = jnp.sum(partial * normalized_t, axis=1)

    n_lo = 4 if n_tensor % 4 == 0 else n_tensor
    n_hi = n_tensor // n_lo
    gain_rows = -(-local_cols // tokens)
    gain_chunks = jnp.pad(
        gain_part.reshape(n_tensor, local_cols), ((0, 0), (0, gain_rows * tokens - local_cols))
    ).reshape(n_tensor, gain_rows, tokens)
    extra = jnp.concatenate(
        [
            jnp.broadcast_to(inner_part[None, None, :], (n_tensor, 1, tokens)),
            gain_chunks,
            jnp.zeros((n_tensor, 7 - gain_rows, tokens), jnp.float32),
        ],
        axis=1,
    )
    chunks = jnp.concatenate([partial.reshape(n_tensor, local_cols, tokens), extra], axis=1)
    summed = two_stage_reduce_scatter(
        chunks.reshape(n_hi, n_lo, local_cols + 8, tokens), "tensor", n_hi, n_lo
    )
    grad_cols = summed[:local_cols]
    row_inner_sum = summed[local_cols] / width
    gain_local = summed[local_cols + 1 : local_cols + 1 + gain_rows].reshape(-1)[:local_cols]

    normed_gradient = grad_cols.T
    start_col = lax.axis_index("tensor") * local_cols
    normalized_slice = hidden_input_state.astype(jnp.float32) * scaled_rows
    gain_slice = lax.dynamic_slice_in_dim(norm_gain, start_col, local_cols)
    weighted_rows = normed_gradient * gain_slice[None, :]
    hidden_state_gradient = scaled_rows * (
        weighted_rows - normalized_slice * row_inner_sum[:, None]
    )
    norm_gain_gradient = butterfly_sum(butterfly_sum(gain_local, "outer", n_outer), "core", 2)
    return (hidden_state_gradient, grad_head, norm_gain_gradient)


def solution(mesh):
    n_dp, n_tensor = mesh.devices.shape
    split = Mesh(mesh.devices.reshape(n_dp // 2, 2, n_tensor), ("outer", "core", "tensor"))
    dp = ("outer", "core")
    return jax.shard_map(
        shards,
        mesh=split,
        in_specs=(P(dp, "tensor"), P(), P(None, "tensor"), P(dp)),
        out_specs=(P(dp, "tensor"), P(dp, "tensor"), P("tensor")),
        check_vma=False,
    )
```

profile of v0, /device:TPU:1, one launch (start us, length us, event | category | flops | bytes accessed | tf_op | source)
XLA Modules:
  0.0 289.8 jit_solution(8469898625485168333)
XLA Ops:
  7.2 6.1 %collective-permute-start = (bf16[384,576]{0,1:T(8,128)(2,1)}, bf16[384,576]{0,1:T(8,128)(2,1)S(1)}, u32[]{:S(2)}, u32[]{:S(2)}) collective-permute-start(bf16[384,576]{0,1:T(8,128)(2,1)} %param.4), channel_id=1, source_target_pairs={{0,7},{1,0},{2,1},{3,2},{4,3},{5,4},{6,5},{7,6},{8,15},{9,8},{10,9... | collective-permute-start | bytes 1327112 | tf_op jit(solution)/shard_map/ppermute | solution.py:13
  18.3 10.5 %collective-permute-done = bf16[384,576]{0,1:T(8,128)(2,1)S(1)} collective-permute-done((bf16[384,576]{0,1:T(8,128)(2,1)}, bf16[384,576]{0,1:T(8,128)(2,1)S(1)}, u32[]{:S(2)}, u32[]{:S(2)}) %collective-permute-start) | collective-permute-done | bytes 442400 | tf_op jit(solution)/shard_map/ppermute | solution.py:13
  28.8 15.9 %collective-permute-done.1 = bf16[384,576]{0,1:T(8,128)(2,1)S(1)} collective-permute-done((bf16[384,576]{0,1:T(8,128)(2,1)}, bf16[384,576]{0,1:T(8,128)(2,1)S(1)}, u32[]{:S(2)}, u32[]{:S(2)}) %collective-permute-start.1) | collective-permute-done | bytes 442400 | tf_op jit(solution)/shard_map/ppermute | solution.py:13
  45.1 5.6 %collective-permute-done.2 = bf16[384,576]{0,1:T(8,128)(2,1)S(1)} collective-permute-done((bf16[384,576]{0,1:T(8,128)(2,1)}, bf16[384,576]{0,1:T(8,128)(2,1)S(1)}, u32[]{:S(2)}, u32[]{:S(2)}) %collective-permute-start.2) | collective-permute-done | bytes 442400 | tf_op jit(solution)/shard_map/ppermute | solution.py:13
  50.7 3.9 %collective-permute-done.3 = bf16[384,576]{0,1:T(8,128)(2,1)S(1)} collective-permute-done((bf16[384,576]{0,1:T(8,128)(2,1)}, bf16[384,576]{0,1:T(8,128)(2,1)S(1)}, u32[]{:S(2)}, u32[]{:S(2)}) %collective-permute-start.3) | collective-permute-done | bytes 442400 | tf_op jit(solution)/shard_map/ppermute | solution.py:13
  57.5 3.4 %dynamic-slice_convert_fusion = f32[8,384,576]{1,2,0:T(8,128)} fusion(bf16[16,384,576]{1,2,0:T(8,128)(2,1)S(1)} %bitcast_dynamic-update-slice_fusion.1, s32[]{:T(128)S(6)} %select_n.76), kind=kLoop, calls=%fused_computation.11 | loop fusion | flops 1769472 | bytes 10616836 | tf_op jit(solution)/shard_map/convert_element_type | solution.py:65
  60.9 8.0 %copy.12 = f32[384,4608]{1,0:T(8,128)} copy(f32[384,4608]{0,1:T(8,128)} %bitcast.93) | data formatting | bytes 14155776 | tf_op jit(solution)/shard_map/convert_element_type | solution.py:65
  68.9 8.7 %fusion.14 = (f32[384]{0:T(512)S(1)}, f32[384,1024]{1,0:T(8,128)S(1)}) fusion(bf16[4608,1024]{1,0:T(8,128)(2,1)} %param.6, f32[384,4608]{1,0:T(8,128)} %copy.12, f32[4608]{0:T(1024)S(1)} %copy-done.4, f32[384]{0:T(512)S(1)} %add_rsqrt_fusion), kind=kOutput, calls=%fused_computation.63 | convolution fusion | flops 3629579776 | bytes 18109440 | tf_op jit(solution)/shard_map/dot_general | solution.py:69
  80.0 11.5 %collective-permute-start.12 = (f32[2,384]{1,0:T(2,128)S(1)}, f32[2,384]{1,0:T(2,128)S(1)}, u32[]{:S(2)}, u32[]{:S(2)}) collective-permute-start(f32[2,384]{1,0:T(2,128)S(1)} %pad_maximum_fusion.3), channel_id=1, source_target_pairs={{0,2},{1,3},{2,4},{3,5},{4,6},{5,7},{6,0},{7,1},{8,10},{9,11},{10,... | collective-permute-start | bytes 9224 | tf_op jit(solution)/shard_map/ppermute | solution.py:13
  94.9 3.2 %collective-permute-start.9 = (f32[2,384]{1,0:T(2,128)S(1)}, f32[2,384]{1,0:T(2,128)S(1)}, u32[]{:S(2)}, u32[]{:S(2)}) collective-permute-start(f32[2,384]{1,0:T(2,128)S(1)} %pad_maximum_fusion.3), channel_id=1, source_target_pairs={{0,5},{1,6},{2,7},{3,0},{4,1},{5,2},{6,3},{7,4},{8,13},{9,14},{10,... | collective-permute-start | bytes 9224 | tf_op jit(solution)/shard_map/ppermute | solution.py:13
  102.2 12.3 %fusion.12 = f32[4608,1024]{1,0:T(8,128)} fusion(f32[384,1024]{1,0:T(8,128)S(1)} %get-tuple-element.6, s32[1024]{0:T(1024)S(1)} %iota_add_fusion, f32[384]{0:T(512)S(1)} %log_add_fusion, s32[384]{0:T(512)S(1)} %copy-done.5, f32[384,4608]{1,0:T(8,128)} %copy.12, f32[4608]{0:T(1024)S(1)} %copy-done.4, f32[384]{0:T(512)S(1)} %add_rsqrt_fusion), kind=kOutput, calls=%fused_computation.61 | convolution fusion | flops 3631153152 | bytes 27552256 | tf_op jit(solution)/shard_map/dot_general | solution.py:81
  114.7 16.7 %fusion.1 = (f32[384]{0:T(512)S(1)}, f32[4608]{0:T(1024)S(1)}, f32[4608,384]{0,1:T(8,128)}) fusion(f32[384,4608]{1,0:T(8,128)} %copy.12, f32[4608]{0:T(1024)S(1)} %copy-done.4, f32[384]{0:T(512)S(1)} %add_rsqrt_fusion, bf16[4608,1024]{1,0:T(8,128)(2,1)} %param.6, f32[384,1024]{1,0:T(8,128)S(1)} %get-tuple-element.6, s32[1024]{0:T(1024)S(1)} %iota_add_fusion, ...), kind=kOutput, calls=%fused_computation.4 | convolution fusion | flops 3636456448 | bytes 25212928 | tf_op jit(solution)/shard_map/dot_general | solution.py:86
  131.4 8.1 %copy.27 = f32[4608,384]{1,0:T(8,128)} copy(f32[4608,384]{0,1:T(8,128)} %get-tuple-element.7) | data formatting | bytes 14155776 | tf_op jit(solution)/shard_map/dot_general | solution.py:86
  144.8 4.1 %collective-permute-start.18 = (f32[2,296,384]{2,1,0:T(8,128)}, f32[2,296,384]{2,1,0:T(8,128)}, u32[]{:S(2)}, u32[]{:S(2)}) collective-permute-start(f32[2,296,384]{2,1,0:T(8,128)} %dynamic-slice_bitcast_fusion), channel_id=1, source_target_pairs={{0,3},{1,0},{2,1},{3,2},{4,7},{5,4},{6,5},{7,6},{8,11},{9,8},{10,9... | collective-permute-start | bytes 2727944 | tf_op jit(solution)/shard_map/ppermute | solution.py:45
  152.1 11.9 %collective-permute-done.18 = f32[2,296,384]{2,1,0:T(8,128)} collective-permute-done((f32[2,296,384]{2,1,0:T(8,128)}, f32[2,296,384]{2,1,0:T(8,128)}, u32[]{:S(2)}, u32[]{:S(2)}) %collective-permute-start.18) | collective-permute-done | bytes 909344 | tf_op jit(solution)/shard_map/ppermute | solution.py:45
  166.5 3.4 %collective-permute-start.19 = (f32[2,296,384]{2,1,0:T(8,128)}, f32[2,296,384]{2,1,0:T(8,128)}, u32[]{:S(2)}, u32[]{:S(2)}) collective-permute-start(f32[2,296,384]{2,1,0:T(8,128)} %bitcast_add_fusion), channel_id=1, source_target_pairs={{0,3},{1,0},{2,1},{3,2},{4,7},{5,4},{6,5},{7,6},{8,11},{9,8},{10,9... | collective-permute-start | bytes 2727944 | tf_op jit(solution)/shard_map/ppermute | solution.py:45
  172.1 12.0 %collective-permute-done.19 = f32[2,296,384]{2,1,0:T(8,128)} collective-permute-done((f32[2,296,384]{2,1,0:T(8,128)}, f32[2,296,384]{2,1,0:T(8,128)}, u32[]{:S(2)}, u32[]{:S(2)}) %collective-permute-start.19) | collective-permute-done | bytes 909344 | tf_op jit(solution)/shard_map/ppermute | solution.py:45
  186.6 3.5 %collective-permute-start.20 = (f32[2,296,384]{2,1,0:T(8,128)}, f32[2,296,384]{2,1,0:T(8,128)}, u32[]{:S(2)}, u32[]{:S(2)}) collective-permute-start(f32[2,296,384]{2,1,0:T(8,128)} %bitcast_add_fusion.1), channel_id=1, source_target_pairs={{0,3},{1,0},{2,1},{3,2},{4,7},{5,4},{6,5},{7,6},{8,11},{9,8},{10,9... | collective-permute-start | bytes 2727944 | tf_op jit(solution)/shard_map/ppermute | solution.py:45
  192.2 11.1 %collective-permute-done.20 = f32[2,296,384]{2,1,0:T(8,128)} collective-permute-done((f32[2,296,384]{2,1,0:T(8,128)}, f32[2,296,384]{2,1,0:T(8,128)}, u32[]{:S(2)}, u32[]{:S(2)}) %collective-permute-start.20) | collective-permute-done | bytes 909344 | tf_op jit(solution)/shard_map/ppermute | solution.py:45
  211.9 29.5 %collective-permute-done.21 = f32[296,384]{1,0:T(8,128)} collective-permute-done((f32[296,384]{1,0:T(8,128)}, f32[296,384]{1,0:T(8,128)}, u32[]{:S(2)}, u32[]{:S(2)}) %collective-permute-start.21) | collective-permute-done | bytes 454688 | tf_op jit(solution)/shard_map/ppermute | solution.py:52
  246.4 3.0 %collective-permute-done.23 = f32[576]{0:T(1024)S(1)} collective-permute-done((f32[576]{0:T(1024)S(1)}, f32[576]{0:T(1024)S(1)}, u32[]{:S(2)}, u32[]{:S(2)}) %collective-permute-start.23) | collective-permute-done | bytes 2336 | tf_op jit(solution)/shard_map/ppermute | solution.py:22
  249.4 2.9 %collective-permute-start.24 = (f32[576]{0:T(1024)S(1)}, f32[576]{0:T(1024)S(1)}, u32[]{:S(2)}, u32[]{:S(2)}) collective-permute-start(f32[576]{0:T(1024)S(1)} %add.195), channel_id=1, source_target_pairs={{0,64},{16,80},{32,96},{48,112},{64,0},{80,16},{96,32},{112,48},{1... | collective-permute-start | bytes 6920 | tf_op jit(solution)/shard_map/ppermute | solution.py:22
  252.3 20.6 %collective-permute-done.17 = f32[288,384]{1,0:T(8,128)S(1)} collective-permute-done((f32[288,384]{1,0:T(8,128)S(1)}, f32[288,384]{1,0:T(8,128)S(1)}, u32[]{:S(2)}, u32[]{:S(2)}) %collective-permute-start.17) | collective-permute-done | bytes 442400 | tf_op jit(solution)/shard_map/ppermute | solution.py:49
  276.6 3.6 %collective-permute-start.26 = (f32[576]{0:T(1024)S(1)}, f32[576]{0:T(1024)S(1)}, u32[]{:S(2)}, u32[]{:S(2)}) collective-permute-start(f32[576]{0:T(1024)S(1)} %add.197), channel_id=1, source_target_pairs={{0,8},{8,0},{1,9},{9,1},{2,10},{10,2},{3,11},{11,3},{4,12},{12,4},... | collective-permute-start | bytes 6920 | tf_op jit(solution)/shard_map/ppermute | solution.py:22
  (116 shorter events, 56.0 us)
Async XLA Ops:
  7.2 275.7 %reduce-scatter.2.cloned.1.call-start = ((), (), s32[]{:S(2)}) async-start(), calls=%async_computation.1 | async-start | bytes 19464192 | tf_op jit(solution)/shard_map/reduce_scatter | solution.py:84
  7.2 21.6 %collective-permute-start = (bf16[384,576]{0,1:T(8,128)(2,1)}, bf16[384,576]{0,1:T(8,128)(2,1)S(1)}, u32[]{:S(2)}, u32[]{:S(2)}) collective-permute-start(bf16[384,576]{0,1:T(8,128)(2,1)} %param.4), channel_id=1, source_target_pairs={{0,7},{1,0},{2,1},{3,2},{4,3},{5,4},{6,5},{7,6},{8,15},{9,8},{10,9... | collective-permute-start | bytes 1327112 | tf_op jit(solution)/shard_map/ppermute | solution.py:13
  13.3 31.4 %collective-permute-start.1 = (bf16[384,576]{0,1:T(8,128)(2,1)}, bf16[384,576]{0,1:T(8,128)(2,1)S(1)}, u32[]{:S(2)}, u32[]{:S(2)}) collective-permute-start(bf16[384,576]{0,1:T(8,128)(2,1)} %param.4), channel_id=1, source_target_pairs={{0,6},{1,7},{2,0},{3,1},{4,2},{5,3},{6,4},{7,5},{8,14},{9,15},{10,... | collective-permute-start | bytes 1327112 | tf_op jit(solution)/shard_map/ppermute | solution.py:13
  13.7 41.2 %collective-permute-start.6 = (bf16[384,576]{0,1:T(8,128)(2,1)}, bf16[384,576]{0,1:T(8,128)(2,1)S(1)}, u32[]{:S(2)}, u32[]{:S(2)}) collective-permute-start(bf16[384,576]{0,1:T(8,128)(2,1)} %param.4), channel_id=1, source_target_pairs={{0,1},{1,2},{2,3},{3,4},{4,5},{5,6},{6,7},{7,0},{8,9},{9,10},{10,1... | collective-permute-start | bytes 1327112 | tf_op jit(solution)/shard_map/ppermute | solution.py:13
  14.4 40.4 %collective-permute-start.5 = (bf16[384,576]{0,1:T(8,128)(2,1)}, bf16[384,576]{0,1:T(8,128)(2,1)S(1)}, u32[]{:S(2)}, u32[]{:S(2)}) collective-permute-start(bf16[384,576]{0,1:T(8,128)(2,1)} %param.4), channel_id=1, source_target_pairs={{0,2},{1,3},{2,4},{3,5},{4,6},{5,7},{6,0},{7,1},{8,10},{9,11},{10,... | collective-permute-start | bytes 1327112 | tf_op jit(solution)/shard_map/ppermute | solution.py:13
  16.3 38.4 %collective-permute-start.4 = (bf16[384,576]{0,1:T(8,128)(2,1)}, bf16[384,576]{0,1:T(8,128)(2,1)S(1)}, u32[]{:S(2)}, u32[]{:S(2)}) collective-permute-start(bf16[384,576]{0,1:T(8,128)(2,1)} %param.4), channel_id=1, source_target_pairs={{0,3},{1,4},{2,5},{3,6},{4,7},{5,0},{6,1},{7,2},{8,11},{9,12},{10,... | collective-permute-start | bytes 1327112 | tf_op jit(solution)/shard_map/ppermute | solution.py:13
  28.8 21.9 %collective-permute-start.2 = (bf16[384,576]{0,1:T(8,128)(2,1)}, bf16[384,576]{0,1:T(8,128)(2,1)S(1)}, u32[]{:S(2)}, u32[]{:S(2)}) collective-permute-start(bf16[384,576]{0,1:T(8,128)(2,1)} %param.4), channel_id=1, source_target_pairs={{0,5},{1,6},{2,7},{3,0},{4,1},{5,2},{6,3},{7,4},{8,13},{9,14},{10,... | collective-permute-start | bytes 1327112 | tf_op jit(solution)/shard_map/ppermute | solution.py:13
  44.8 9.8 %collective-permute-start.3 = (bf16[384,576]{0,1:T(8,128)(2,1)}, bf16[384,576]{0,1:T(8,128)(2,1)S(1)}, u32[]{:S(2)}, u32[]{:S(2)}) collective-permute-start(bf16[384,576]{0,1:T(8,128)(2,1)} %param.4), channel_id=1, source_target_pairs={{0,4},{1,5},{2,6},{3,7},{4,0},{5,1},{6,2},{7,3},{8,12},{9,13},{10,... | collective-permute-start | bytes 1327112 | tf_op jit(solution)/shard_map/ppermute | solution.py:13
  78.1 20.0 %collective-permute-start.13 = (f32[2,384]{1,0:T(2,128)S(1)}, f32[2,384]{1,0:T(2,128)S(1)}, u32[]{:S(2)}, u32[]{:S(2)}) collective-permute-start(f32[2,384]{1,0:T(2,128)S(1)} %pad_maximum_fusion.3), channel_id=1, source_target_pairs={{0,1},{1,2},{2,3},{3,4},{4,5},{5,6},{6,7},{7,0},{8,9},{9,10},{10,1... | collective-permute-start | bytes 9224 | tf_op jit(solution)/shard_map/ppermute | solution.py:13
  80.0 18.5 %collective-permute-start.12 = (f32[2,384]{1,0:T(2,128)S(1)}, f32[2,384]{1,0:T(2,128)S(1)}, u32[]{:S(2)}, u32[]{:S(2)}) collective-permute-start(f32[2,384]{1,0:T(2,128)S(1)} %pad_maximum_fusion.3), channel_id=1, source_target_pairs={{0,2},{1,3},{2,4},{3,5},{4,6},{5,7},{6,0},{7,1},{8,10},{9,11},{10,... | collective-permute-start | bytes 9224 | tf_op jit(solution)/shard_map/ppermute | solution.py:13
  91.5 9.0 %collective-permute-start.11 = (f32[2,384]{1,0:T(2,128)S(1)}, f32[2,384]{1,0:T(2,128)S(1)}, u32[]{:S(2)}, u32[]{:S(2)}) collective-permute-start(f32[2,384]{1,0:T(2,128)S(1)} %pad_maximum_fusion.3), channel_id=1, source_target_pairs={{0,3},{1,4},{2,5},{3,6},{4,7},{5,0},{6,1},{7,2},{8,11},{9,12},{10,... | collective-permute-start | bytes 9224 | tf_op jit(solution)/shard_map/ppermute | solution.py:13
  93.6 6.9 %collective-permute-start.10 = (f32[2,384]{1,0:T(2,128)S(1)}, f32[2,384]{1,0:T(2,128)S(1)}, u32[]{:S(2)}, u32[]{:S(2)}) collective-permute-start(f32[2,384]{1,0:T(2,128)S(1)} %pad_maximum_fusion.3), channel_id=1, source_target_pairs={{0,4},{1,5},{2,6},{3,7},{4,0},{5,1},{6,2},{7,3},{8,12},{9,13},{10,... | collective-permute-start | bytes 9224 | tf_op jit(solution)/shard_map/ppermute | solution.py:13
  94.9 5.7 %collective-permute-start.9 = (f32[2,384]{1,0:T(2,128)S(1)}, f32[2,384]{1,0:T(2,128)S(1)}, u32[]{:S(2)}, u32[]{:S(2)}) collective-permute-start(f32[2,384]{1,0:T(2,128)S(1)} %pad_maximum_fusion.3), channel_id=1, source_target_pairs={{0,5},{1,6},{2,7},{3,0},{4,1},{5,2},{6,3},{7,4},{8,13},{9,14},{10,... | collective-permute-start | bytes 9224 | tf_op jit(solution)/shard_map/ppermute | solution.py:13
  98.1 4.0 %collective-permute-start.8 = (f32[2,384]{1,0:T(2,128)S(1)}, f32[2,384]{1,0:T(2,128)S(1)}, u32[]{:S(2)}, u32[]{:S(2)}) collective-permute-start(f32[2,384]{1,0:T(2,128)S(1)} %pad_maximum_fusion.3), channel_id=1, source_target_pairs={{0,6},{1,7},{2,0},{3,1},{4,2},{5,3},{6,4},{7,5},{8,14},{9,15},{10,... | collective-permute-start | bytes 9224 | tf_op jit(solution)/shard_map/ppermute | solution.py:13
  144.8 19.2 %collective-permute-start.18 = (f32[2,296,384]{2,1,0:T(8,128)}, f32[2,296,384]{2,1,0:T(8,128)}, u32[]{:S(2)}, u32[]{:S(2)}) collective-permute-start(f32[2,296,384]{2,1,0:T(8,128)} %dynamic-slice_bitcast_fusion), channel_id=1, source_target_pairs={{0,3},{1,0},{2,1},{3,2},{4,7},{5,4},{6,5},{7,6},{8,11},{9,8},{10,9... | collective-permute-start | bytes 2727944 | tf_op jit(solution)/shard_map/ppermute | solution.py:45
  152.1 17.8 %collective-permute-start.14 = (f32[2,288,384]{2,1,0:T(8,128)}, f32[2,288,384]{2,1,0:T(8,128)}, u32[]{:S(2)}, u32[]{:S(2)}) collective-permute-start(f32[2,288,384]{2,1,0:T(8,128)} %dynamic-slice_bitcast_fusion.1), channel_id=1, source_target_pairs={{0,1},{1,2},{2,3},{3,0},{4,5},{5,6},{6,7},{7,4},{8,9},{9,10},{10,1... | collective-permute-start | bytes 2654216 | tf_op jit(solution)/shard_map/ppermute | solution.py:44
  166.5 17.5 %collective-permute-start.19 = (f32[2,296,384]{2,1,0:T(8,128)}, f32[2,296,384]{2,1,0:T(8,128)}, u32[]{:S(2)}, u32[]{:S(2)}) collective-permute-start(f32[2,296,384]{2,1,0:T(8,128)} %bitcast_add_fusion), channel_id=1, source_target_pairs={{0,3},{1,0},{2,1},{3,2},{4,7},{5,4},{6,5},{7,6},{8,11},{9,8},{10,9... | collective-permute-start | bytes 2727944 | tf_op jit(solution)/shard_map/ppermute | solution.py:45
  172.1 17.9 %collective-permute-start.15 = (f32[2,288,384]{2,1,0:T(8,128)}, f32[2,288,384]{2,1,0:T(8,128)}, u32[]{:S(2)}, u32[]{:S(2)}) collective-permute-start(f32[2,288,384]{2,1,0:T(8,128)} %bitcast_add_fusion.3), channel_id=1, source_target_pairs={{0,1},{1,2},{2,3},{3,0},{4,5},{5,6},{6,7},{7,4},{8,9},{9,10},{10,1... | collective-permute-start | bytes 2654216 | tf_op jit(solution)/shard_map/ppermute | solution.py:44
  186.6 16.7 %collective-permute-start.20 = (f32[2,296,384]{2,1,0:T(8,128)}, f32[2,296,384]{2,1,0:T(8,128)}, u32[]{:S(2)}, u32[]{:S(2)}) collective-permute-start(f32[2,296,384]{2,1,0:T(8,128)} %bitcast_add_fusion.1), channel_id=1, source_target_pairs={{0,3},{1,0},{2,1},{3,2},{4,7},{5,4},{6,5},{7,6},{8,11},{9,8},{10,9... | collective-permute-start | bytes 2727944 | tf_op jit(solution)/shard_map/ppermute | solution.py:45
  192.2 15.9 %collective-permute-start.16 = (f32[2,288,384]{2,1,0:T(8,128)}, f32[2,288,384]{2,1,0:T(8,128)}, u32[]{:S(2)}, u32[]{:S(2)}) collective-permute-start(f32[2,288,384]{2,1,0:T(8,128)} %bitcast_add_fusion.4), channel_id=1, source_target_pairs={{0,1},{1,2},{2,3},{3,0},{4,5},{5,6},{6,7},{7,4},{8,9},{9,10},{10,1... | collective-permute-start | bytes 2654216 | tf_op jit(solution)/shard_map/ppermute | solution.py:44
  206.6 34.8 %collective-permute-start.21 = (f32[296,384]{1,0:T(8,128)}, f32[296,384]{1,0:T(8,128)}, u32[]{:S(2)}, u32[]{:S(2)}) collective-permute-start(f32[296,384]{1,0:T(8,128)} %dynamic-slice_bitcast_fusion.2), channel_id=1, source_target_pairs={{0,4},{1,5},{2,6},{3,7},{4,0},{5,1},{6,2},{7,3},{8,12},{9,13},{10,... | collective-permute-start | bytes 1363976 | tf_op jit(solution)/shard_map/ppermute | solution.py:52
  210.3 62.6 %collective-permute-start.17 = (f32[288,384]{1,0:T(8,128)S(1)}, f32[288,384]{1,0:T(8,128)S(1)}, u32[]{:S(2)}, u32[]{:S(2)}) collective-permute-start(f32[288,384]{1,0:T(8,128)S(1)} %dynamic-slice_bitcast_fusion.3), channel_id=1, source_target_pairs={{0,4},{1,5},{2,6},{3,7},{4,0},{5,1},{6,2},{7,3},{8,12},{9,13},{10,... | collective-permute-start | bytes 1327112 | tf_op jit(solution)/shard_map/ppermute | solution.py:49
  249.4 24.6 %collective-permute-start.24 = (f32[576]{0:T(1024)S(1)}, f32[576]{0:T(1024)S(1)}, u32[]{:S(2)}, u32[]{:S(2)}) collective-permute-start(f32[576]{0:T(1024)S(1)} %add.195), channel_id=1, source_target_pairs={{0,64},{16,80},{32,96},{48,112},{64,0},{80,16},{96,32},{112,48},{1... | collective-permute-start | bytes 6920 | tf_op jit(solution)/shard_map/ppermute | solution.py:22
  276.6 5.8 %collective-permute-start.26 = (f32[576]{0:T(1024)S(1)}, f32[576]{0:T(1024)S(1)}, u32[]{:S(2)}, u32[]{:S(2)}) collective-permute-start(f32[576]{0:T(1024)S(1)} %add.197), channel_id=1, source_target_pairs={{0,8},{8,0},{1,9},{9,1},{2,10},{10,2},{3,11},{11,3},{4,12},{12,4},... | collective-permute-start | bytes 6920 | tf_op jit(solution)/shard_map/ppermute | solution.py:22
  (10 other events, 107.2 us)
Sparse Core Ops, SparseCore 0:
  114.7 152.8 reduce-scatter.1
where the time goes:
time: 291 us; the launch traced here: 290 us
  waiting for transfers between devices  132 us (45%)
  starting transfers between devices  53.6 us (18%)
  matrix products  37.7 us (13%)
  local copies, waits for them, and re-layouts  28.1 us (10%)
  other arithmetic  24.4 us (8%)
  between operations  14.5 us (5%)
    ppermute x14, waiting for transfers between devices, shift_gather(): got.append(lax.ppermute(x, axis, [(c, (c + k) % n) for c in range(n)]))  37.3 us
    ppermute x3, waiting for transfers between devices, two_stage_reduce_scatter(): recv_b = lax.ppermute(send_b, axis, perm_b)  34.9 us
    ppermute x14, starting transfers between devices, shift_gather(): got.append(lax.ppermute(x, axis, [(c, (c + k) % n) for c in range(n)]))  33.7 us
    ppermute x1, waiting for transfers between devices, two_stage_reduce_scatter(): lax.ppermute(lax.dynamic_index_in_dim(sum_b, n_hi - 1 - h, 0, keepdims=Fa...  29.5 us
    ppermute x1, waiting for transfers between devices, two_stage_reduce_scatter(): lax.ppermute(lax.dynamic_index_in_dim(sum_f, n_hi - 1 - h, 0, keepdims=Fa...  20.6 us
    dot_general x1, matrix products, shards(): lax.dot_general(head_weight, dlogits, (((1,), (1,)), ((), ())), preferred...  16.7 us
    dot_general x1, matrix products, shards(): lax.dot_general(normed, dlogits, (((0,), (0,)), ((), ())), preferred_elem...  12.3 us
    ppermute x3, starting transfers between devices, two_stage_reduce_scatter(): recv_b = lax.ppermute(send_b, axis, perm_b)  10.9 us
  transfers between devices with their start and end apart: 28, of which 14 were waited for; matrix products, arithmetic and copies ran while one was open for 18% of the time, Pallas kernels for 0%

commit v1 on v0

--- a/solution.py
+++ b/solution.py
@@ -22,6 +22,20 @@
         x = x + lax.ppermute(x, axis, [(c, c ^ b) for c in range(n)])
         b *= 2
     return x
+
+
+def butterfly_softmax_stats(top, logits, axis, n):
+    total = jnp.sum(jnp.exp(logits - top[:, None]), axis=1)
+    b = 1
+    while b < n:
+        perm = [(c, c ^ b) for c in range(n)]
+        other_top = lax.ppermute(top, axis, perm)
+        other_total = lax.ppermute(total, axis, perm)
+        new_top = jnp.maximum(top, other_top)
+        total = total * jnp.exp(top - new_top) + other_total * jnp.exp(other_top - new_top)
+        top = new_top
+        b *= 2
+    return top, total
 
 
 def two_stage_reduce_scatter(parts, axis, n_hi, n_lo):
@@ -60,18 +74,18 @@
     width, vocab_rows = head_weight.shape
     n_tensor = width // local_cols
     n_outer = lax.psum(1, "outer")
-    blocks = shift_gather(hidden_input_state, "tensor", n_tensor)
-    gathered = jnp.transpose(blocks, (1, 0, 2)).reshape(tokens, width)
-    values = gathered.astype(jnp.float32)
-    scaled_rows = lax.rsqrt(jnp.mean(values * values, axis=1, keepdims=True) + epsilon)
-    normalized = values * scaled_rows
-    normed = (normalized * norm_gain[None, :]).astype(jnp.bfloat16)
-    logits = jnp.dot(normed, head_weight, preferred_element_type=jnp.float32)
-    local_top = jnp.max(logits, axis=1)
-    local_total = jnp.sum(jnp.exp(logits - local_top[:, None]), axis=1)
-    stats = shift_gather(jnp.stack([local_top, local_total]), "tensor", n_tensor)
-    row_top = jnp.max(stats[:, 0, :], axis=0)
-    row_total = jnp.sum(stats[:, 1, :] * jnp.exp(stats[:, 0, :] - row_top[None, :]), axis=0)
+    blocks = shift_gather(hidden_input_state.T, "tensor", n_tensor)
+    values_t = blocks.reshape(width, tokens).astype(jnp.float32)
+    scaled = lax.rsqrt(jnp.mean(values_t * values_t, axis=0) + epsilon)
+    scaled_rows = scaled[:, None]
+    normalized_t = values_t * scaled[None, :]
+    normed_t = (normalized_t * norm_gain[:, None]).astype(jnp.bfloat16)
+    logits = lax.dot_general(
+        normed_t, head_weight, (((0,), (0,)), ((), ())), preferred_element_type=jnp.float32
+    )
+    row_top, row_total = butterfly_softmax_stats(
+        jnp.max(logits, axis=1), logits, "tensor", n_tensor
+    )
     log_total = row_top + jnp.log(row_total)
     offset = lax.axis_index("tensor") * vocab_rows
     column_ids = offset + lax.broadcasted_iota(jnp.int32, (1, vocab_rows), 1)
@@ -79,14 +93,13 @@
     dlogits = (jnp.exp(logits - log_total[:, None]) - onehot).astype(jnp.bfloat16)
 
     head_partial = lax.dot_general(
-        normed, dlogits, (((0,), (0,)), ((), ())), preferred_element_type=jnp.float32
+        normed_t, dlogits, (((1,), (0,)), ((), ())), preferred_element_type=jnp.float32
     )
     grad_head = lax.psum_scatter(head_partial, ("outer", "core"), scatter_dimension=0, tiled=True)
 
     partial = lax.dot_general(
         head_weight, dlogits, (((1,), (1,)), ((), ())), preferred_element_type=jnp.float32
     )
-    normalized_t = normalized.T
     inner_part = jnp.sum(partial * (norm_gain[:, None] * normalized_t), axis=0)
     gain_part = jnp.sum(partial * normalized_t, axis=1)
 

time: 291 us -> 290 us (level)
  starting transfers between devices: 53.6 us -> 43.2 us
  waiting for transfers between devices: 132 us -> 142 us
    ppermute x14 -> x7, starting transfers between devices: 33.7 us -> 11.3 us  [shift_gather(): got.append(lax.ppermute(x, axis, [(c, (c + k) % n) for c in range(n)]))]
    ppermute x0 -> x6, starting transfers between devices: none -> 16.9 us  [the longest x3 16.3 us: butterfly_softmax_stats(): other_total = lax.ppermute(total, axis, perm)]
    ppermute x0 -> x6, waiting for transfers between devices: none -> 9.69 us  [the longest x3 7.15 us: butterfly_softmax_stats(): other_top = lax.ppermute(top, axis, perm)]
    ppermute x3, starting transfers between devices: 10.9 us -> 3.15 us  [two_stage_reduce_scatter(): recv_b = lax.ppermute(send_b, axis, perm_b)]
    ppermute x1, waiting for transfers between devices: 20.6 us -> 25.9 us  [two_stage_reduce_scatter(): lax.ppermute(lax.dynamic_index_in_dim(sum_f, n_hi - 1 - h, 0, keepdims=Fa...]
    ppermute x1, waiting for transfers between devices: 29.5 us -> 26.2 us  [two_stage_reduce_scatter(): lax.ppermute(lax.dynamic_index_in_dim(sum_b, n_hi - 1 - h, 0, keepdims=Fa...]
    ppermute x14 -> x7, waiting for transfers between devices: 37.3 us -> 35.9 us  [shift_gather(): got.append(lax.ppermute(x, axis, [(c, (c + k) % n) for c in range(n)]))]
  transfers between devices with their start and end apart: 28 -> 27, of which waited for: 14 -> 18; matrix products, arithmetic and copies ran while one was open for 18% -> 18% of each run, Pallas kernels for 0% -> 0%
where the time goes in v1:
time: 290 us; the launch traced here: 289 us
  waiting for transfers between devices  142 us (49%)
  starting transfers between devices  43.2 us (15%)
  matrix products  37.7 us (13%)
  local copies, waits for them, and re-layouts  28.2 us (10%)
  other arithmetic  24.3 us (8%)
  between operations  14.4 us (5%)
    ppermute x7, waiting for transfers between devices, shift_gather(): got.append(lax.ppermute(x, axis, [(c, (c + k) % n) for c in range(n)]))  35.9 us
    ppermute x3, waiting for transfers between devices, two_stage_reduce_scatter(): recv_b = lax.ppermute(send_b, axis, perm_b)  35.7 us
    ppermute x1, waiting for transfers between devices, two_stage_reduce_scatter(): lax.ppermute(lax.dynamic_index_in_dim(sum_b, n_hi - 1 - h, 0, keepdims=Fa...  26.2 us
    ppermute x1, waiting for transfers between devices, two_stage_reduce_scatter(): lax.ppermute(lax.dynamic_index_in_dim(sum_f, n_hi - 1 - h, 0, keepdims=Fa...  25.9 us
    dot_general x1, matrix products, shards(): lax.dot_general(head_weight, dlogits, (((1,), (1,)), ((), ())), preferred...  16.7 us
    ppermute x3, starting transfers between devices, butterfly_softmax_stats(): other_total = lax.ppermute(total, axis, perm)  16.3 us
    dot_general x1, matrix products, shards(): lax.dot_general(normed_t, dlogits, (((1,), (0,)), ((), ())), preferred_el...  12.3 us
    ppermute x7, starting transfers between devices, shift_gather(): got.append(lax.ppermute(x, axis, [(c, (c + k) % n) for c in range(n)]))  11.3 us
  transfers between devices with their start and end apart: 27, of which 18 were waited for; matrix products, arithmetic and copies ran while one was open for 18% of the time, Pallas kernels for 0%

profile of v1, /device:TPU:1, one launch (start us, length us, event | category | flops | bytes accessed | tf_op | source)
XLA Modules:
  0.0 289.5 jit_solution(13256933402483627060)
XLA Ops:
  7.2 6.1 %collective-permute-start = (bf16[576,384]{1,0:T(8,128)(2,1)}, bf16[576,384]{1,0:T(8,128)(2,1)S(1)}, u32[]{:S(2)}, u32[]{:S(2)}) collective-permute-start(bf16[576,384]{1,0:T(8,128)(2,1)} %bitcast.66), channel_id=1, source_target_pairs={{0,7},{1,0},{2,1},{3,2},{4,3},{5,4},{6,5},{7,6},{8,15},{9,8},{10,9... | collective-permute-start | bytes 1327112 | tf_op jit(solution)/shard_map/ppermute | solution.py:13
  18.3 10.5 %collective-permute-done = bf16[576,384]{1,0:T(8,128)(2,1)S(1)} collective-permute-done((bf16[576,384]{1,0:T(8,128)(2,1)}, bf16[576,384]{1,0:T(8,128)(2,1)S(1)}, u32[]{:S(2)}, u32[]{:S(2)}) %collective-permute-start) | collective-permute-done | bytes 442400 | tf_op jit(solution)/shard_map/ppermute | solution.py:13
  28.8 15.9 %collective-permute-done.1 = bf16[576,384]{1,0:T(8,128)(2,1)S(1)} collective-permute-done((bf16[576,384]{1,0:T(8,128)(2,1)}, bf16[576,384]{1,0:T(8,128)(2,1)S(1)}, u32[]{:S(2)}, u32[]{:S(2)}) %collective-permute-start.1) | collective-permute-done | bytes 442400 | tf_op jit(solution)/shard_map/ppermute | solution.py:13
  45.1 5.6 %collective-permute-done.2 = bf16[576,384]{1,0:T(8,128)(2,1)S(1)} collective-permute-done((bf16[576,384]{1,0:T(8,128)(2,1)}, bf16[576,384]{1,0:T(8,128)(2,1)S(1)}, u32[]{:S(2)}, u32[]{:S(2)}) %collective-permute-start.2) | collective-permute-done | bytes 442400 | tf_op jit(solution)/shard_map/ppermute | solution.py:13
  50.7 3.9 %collective-permute-done.3 = bf16[576,384]{1,0:T(8,128)(2,1)S(1)} collective-permute-done((bf16[576,384]{1,0:T(8,128)(2,1)}, bf16[576,384]{1,0:T(8,128)(2,1)S(1)}, u32[]{:S(2)}, u32[]{:S(2)}) %collective-permute-start.3) | collective-permute-done | bytes 442400 | tf_op jit(solution)/shard_map/ppermute | solution.py:13
  57.5 3.3 %dynamic-slice_convert_fusion = f32[8,576,384]{2,1,0:T(8,128)} fusion(bf16[16,576,384]{2,1,0:T(8,128)(2,1)S(1)} %bitcast_dynamic-update-slice_fusion.1, s32[]{:T(128)S(6)} %select_n.75), kind=kLoop, calls=%fused_computation.8 | loop fusion | flops 1769472 | bytes 10616836 | tf_op jit(solution)/shard_map/convert_element_type | solution.py:78
  60.9 8.0 %copy.8 = f32[4608,384]{0,1:T(8,128)} copy(f32[4608,384]{1,0:T(8,128)} %bitcast.65) | data formatting | bytes 14155776 | tf_op jit(solution)/shard_map/convert_element_type | solution.py:78
  68.9 8.7 %fusion.10 = (f32[384]{0:T(512)S(1)}, f32[384,1024]{1,0:T(8,128)S(1)}) fusion(bf16[4608,1024]{1,0:T(8,128)(2,1)} %param.6, f32[4608,384]{0,1:T(8,128)} %copy.8, f32[4608]{0:T(1024)S(1)} %copy-done.4, f32[384]{0:T(512)S(1)} %add_rsqrt_fusion), kind=kOutput, calls=%fused_computation.58 | convolution fusion | flops 3629579776 | bytes 18109440 | tf_op jit(solution)/shard_map/dot_general | solution.py:83
  82.3 11.6 %collective-permute-start.11 = (f32[384]{0:T(512)S(1)}, f32[384]{0:T(512)S(1)}, u32[]{:S(2)}, u32[]{:S(2)}) collective-permute-start(f32[384]{0:T(512)S(1)} %get-tuple-element.7), channel_id=1, source_target_pairs={{0,2},{1,3},{2,0},{3,1},{4,6},{5,7},{6,4},{7,5},{8,10},{9,11},{10,... | collective-permute-start | bytes 4616 | tf_op jit(solution)/shard_map/ppermute | solution.py:33
  94.9 3.0 %collective-permute-done.8 = f32[384]{0:T(512)S(1)} collective-permute-done((f32[384]{0:T(512)S(1)}, f32[384]{0:T(512)S(1)}, u32[]{:S(2)}, u32[]{:S(2)}) %collective-permute-start.8) | collective-permute-done | bytes 1568 | tf_op jit(solution)/shard_map/ppermute | solution.py:32
  97.9 2.8 collective-permute-start.12
  101.9 2.7 collective-permute-done.9
  104.7 12.3 %fusion.8 = f32[4608,1024]{1,0:T(8,128)} fusion(f32[384,1024]{1,0:T(8,128)S(1)} %get-tuple-element.10, s32[1024]{0:T(1024)S(1)} %iota_add_fusion, f32[384]{0:T(512)S(1)} %log_add_fusion, s32[384]{0:T(512)S(1)} %copy-done.5, f32[4608,384]{0,1:T(8,128)} %copy.8, f32[4608]{0:T(1024)S(1)} %copy-done.4, f32[384]{0:T(512)S(1)} %add_rsqrt_fusion), kind=kOutput, calls=%fused_computation.56 | convolution fusion | flops 3631153152 | bytes 27552256 | tf_op jit(solution)/shard_map/dot_general | solution.py:95
  117.1 16.7 %multiply_reduce_fusion.1 = (f32[384]{0:T(512)S(1)}, f32[4608]{0:T(1024)S(1)}, f32[4608,384]{0,1:T(8,128)}) fusion(f32[4608,384]{0,1:T(8,128)} %copy.8, f32[4608]{0:T(1024)S(1)} %copy-done.4, f32[384]{0:T(512)S(1)} %add_rsqrt_fusion, bf16[4608,1024]{1,0:T(8,128)(2,1)} %param.6, f32[384,1024]{1,0:T(8,128)S(1)} %get-tuple-element.10, ...), kind=kOutput, calls=%fused_computation.2 | convolution fusion | flops 3636456448 | bytes 25212928 | tf_op jit(solution)/shard_map/dot_general | solution.py:100
  133.9 8.3 %copy.9 = f32[4608,384]{1,0:T(8,128)} copy(f32[4608,384]{0,1:T(8,128)} %get-tuple-element.11) | data formatting | bytes 14155776 | tf_op jit(solution)/shard_map/dot_general | solution.py:100
  152.2 11.0 %collective-permute-done.17 = f32[2,296,384]{2,1,0:T(8,128)} collective-permute-done((f32[2,296,384]{2,1,0:T(8,128)}, f32[2,296,384]{2,1,0:T(8,128)}, u32[]{:S(2)}, u32[]{:S(2)}) %collective-permute-start.17) | collective-permute-done | bytes 909344 | tf_op jit(solution)/shard_map/ppermute | solution.py:59
  169.4 12.4 %collective-permute-done.18 = f32[2,296,384]{2,1,0:T(8,128)} collective-permute-done((f32[2,296,384]{2,1,0:T(8,128)}, f32[2,296,384]{2,1,0:T(8,128)}, u32[]{:S(2)}, u32[]{:S(2)}) %collective-permute-start.18) | collective-permute-done | bytes 909344 | tf_op jit(solution)/shard_map/ppermute | solution.py:59
  188.2 12.3 %collective-permute-done.19 = f32[2,296,384]{2,1,0:T(8,128)} collective-permute-done((f32[2,296,384]{2,1,0:T(8,128)}, f32[2,296,384]{2,1,0:T(8,128)}, u32[]{:S(2)}, u32[]{:S(2)}) %collective-permute-start.19) | collective-permute-done | bytes 909344 | tf_op jit(solution)/shard_map/ppermute | solution.py:59
  206.5 2.6 collective-permute-start.16
  209.1 26.2 %collective-permute-done.20 = f32[296,384]{1,0:T(8,128)} collective-permute-done((f32[296,384]{1,0:T(8,128)}, f32[296,384]{1,0:T(8,128)}, u32[]{:S(2)}, u32[]{:S(2)}) %collective-permute-start.20) | collective-permute-done | bytes 454688 | tf_op jit(solution)/shard_map/ppermute | solution.py:66
  236.6 2.8 collective-permute-done.21
  240.2 3.1 %collective-permute-done.22 = f32[576]{0:T(1024)S(1)} collective-permute-done((f32[576]{0:T(1024)S(1)}, f32[576]{0:T(1024)S(1)}, u32[]{:S(2)}, u32[]{:S(2)}) %collective-permute-start.22) | collective-permute-done | bytes 2336 | tf_op jit(solution)/shard_map/ppermute | solution.py:22
  244.0 25.9 %collective-permute-done.16 = f32[288,384]{1,0:T(8,128)S(1)} collective-permute-done((f32[288,384]{1,0:T(8,128)S(1)}, f32[288,384]{1,0:T(8,128)S(1)}, u32[]{:S(2)}, u32[]{:S(2)}) %collective-permute-start.16) | collective-permute-done | bytes 442400 | tf_op jit(solution)/shard_map/ppermute | solution.py:63
  273.9 6.0 %collective-permute-start.25 = (f32[576]{0:T(1024)S(1)}, f32[576]{0:T(1024)S(1)}, u32[]{:S(2)}, u32[]{:S(2)}) collective-permute-start(f32[576]{0:T(1024)S(1)} %add.207), channel_id=1, source_target_pairs={{0,8},{8,0},{1,9},{9,1},{2,10},{10,2},{3,11},{11,3},{4,12},{12,4},... | collective-permute-start | bytes 6920 | tf_op jit(solution)/shard_map/ppermute | solution.py:22
  (102 shorter events, 53.3 us)
Async XLA Ops:
  7.2 275.4 %reduce-scatter.2.cloned.1.call-start = ((), (), s32[]{:S(2)}) async-start(), calls=%async_computation.1 | async-start | bytes 19464192 | tf_op jit(solution)/shard_map/reduce_scatter | solution.py:98
  7.2 21.6 %collective-permute-start = (bf16[576,384]{1,0:T(8,128)(2,1)}, bf16[576,384]{1,0:T(8,128)(2,1)S(1)}, u32[]{:S(2)}, u32[]{:S(2)}) collective-permute-start(bf16[576,384]{1,0:T(8,128)(2,1)} %bitcast.66), channel_id=1, source_target_pairs={{0,7},{1,0},{2,1},{3,2},{4,3},{5,4},{6,5},{7,6},{8,15},{9,8},{10,9... | collective-permute-start | bytes 1327112 | tf_op jit(solution)/shard_map/ppermute | solution.py:13
  13.3 31.4 %collective-permute-start.1 = (bf16[576,384]{1,0:T(8,128)(2,1)}, bf16[576,384]{1,0:T(8,128)(2,1)S(1)}, u32[]{:S(2)}, u32[]{:S(2)}) collective-permute-start(bf16[576,384]{1,0:T(8,128)(2,1)} %bitcast.67), channel_id=1, source_target_pairs={{0,6},{1,7},{2,0},{3,1},{4,2},{5,3},{6,4},{7,5},{8,14},{9,15},{10,... | collective-permute-start | bytes 1327112 | tf_op jit(solution)/shard_map/ppermute | solution.py:13
  13.7 41.2 %collective-permute-start.6 = (bf16[576,384]{1,0:T(8,128)(2,1)}, bf16[576,384]{1,0:T(8,128)(2,1)S(1)}, u32[]{:S(2)}, u32[]{:S(2)}) collective-permute-start(bf16[576,384]{1,0:T(8,128)(2,1)} %bitcast.68), channel_id=1, source_target_pairs={{0,1},{1,2},{2,3},{3,4},{4,5},{5,6},{6,7},{7,0},{8,9},{9,10},{10,1... | collective-permute-start | bytes 1327112 | tf_op jit(solution)/shard_map/ppermute | solution.py:13
  14.4 40.4 %collective-permute-start.5 = (bf16[576,384]{1,0:T(8,128)(2,1)}, bf16[576,384]{1,0:T(8,128)(2,1)S(1)}, u32[]{:S(2)}, u32[]{:S(2)}) collective-permute-start(bf16[576,384]{1,0:T(8,128)(2,1)} %bitcast.69), channel_id=1, source_target_pairs={{0,2},{1,3},{2,4},{3,5},{4,6},{5,7},{6,0},{7,1},{8,10},{9,11},{10,... | collective-permute-start | bytes 1327112 | tf_op jit(solution)/shard_map/ppermute | solution.py:13
  16.3 38.4 %collective-permute-start.4 = (bf16[576,384]{1,0:T(8,128)(2,1)}, bf16[576,384]{1,0:T(8,128)(2,1)S(1)}, u32[]{:S(2)}, u32[]{:S(2)}) collective-permute-start(bf16[576,384]{1,0:T(8,128)(2,1)} %bitcast.70), channel_id=1, source_target_pairs={{0,3},{1,4},{2,5},{3,6},{4,7},{5,0},{6,1},{7,2},{8,11},{9,12},{10,... | collective-permute-start | bytes 1327112 | tf_op jit(solution)/shard_map/ppermute | solution.py:13
  28.8 21.9 %collective-permute-start.2 = (bf16[576,384]{1,0:T(8,128)(2,1)}, bf16[576,384]{1,0:T(8,128)(2,1)S(1)}, u32[]{:S(2)}, u32[]{:S(2)}) collective-permute-start(bf16[576,384]{1,0:T(8,128)(2,1)} %bitcast.71), channel_id=1, source_target_pairs={{0,5},{1,6},{2,7},{3,0},{4,1},{5,2},{6,3},{7,4},{8,13},{9,14},{10,... | collective-permute-start | bytes 1327112 | tf_op jit(solution)/shard_map/ppermute | solution.py:13
  44.8 9.8 %collective-permute-start.3 = (bf16[576,384]{1,0:T(8,128)(2,1)}, bf16[576,384]{1,0:T(8,128)(2,1)S(1)}, u32[]{:S(2)}, u32[]{:S(2)}) collective-permute-start(bf16[576,384]{1,0:T(8,128)(2,1)} %bitcast.72), channel_id=1, source_target_pairs={{0,4},{1,5},{2,6},{3,7},{4,0},{5,1},{6,2},{7,3},{8,12},{9,13},{10,... | collective-permute-start | bytes 1327112 | tf_op jit(solution)/shard_map/ppermute | solution.py:13
  82.3 12.6 %collective-permute-start.11 = (f32[384]{0:T(512)S(1)}, f32[384]{0:T(512)S(1)}, u32[]{:S(2)}, u32[]{:S(2)}) collective-permute-start(f32[384]{0:T(512)S(1)} %get-tuple-element.7), channel_id=1, source_target_pairs={{0,2},{1,3},{2,0},{3,1},{4,6},{5,7},{6,4},{7,5},{8,10},{9,11},{10,... | collective-permute-start | bytes 4616 | tf_op jit(solution)/shard_map/ppermute | solution.py:33
  94.0 3.9 %collective-permute-start.8 = (f32[384]{0:T(512)S(1)}, f32[384]{0:T(512)S(1)}, u32[]{:S(2)}, u32[]{:S(2)}) collective-permute-start(f32[384]{0:T(512)S(1)} %get-tuple-element.8), channel_id=1, source_target_pairs={{0,2},{1,3},{2,0},{3,1},{4,6},{5,7},{6,4},{7,5},{8,10},{9,11},{10,... | collective-permute-start | bytes 4616 | tf_op jit(solution)/shard_map/ppermute | solution.py:32
  97.9 4.0 %collective-permute-start.12 = (f32[384]{0:T(512)S(1)}, f32[384]{0:T(512)S(1)}, u32[]{:S(2)}, u32[]{:S(2)}) collective-permute-start(f32[384]{0:T(512)S(1)} %get-tuple-element.5), channel_id=1, source_target_pairs={{0,4},{1,5},{2,6},{3,7},{4,0},{5,1},{6,2},{7,3},{8,12},{9,13},{10,... | collective-permute-start | bytes 4616 | tf_op jit(solution)/shard_map/ppermute | solution.py:33
  100.7 3.9 %collective-permute-start.9 = (f32[384]{0:T(512)S(1)}, f32[384]{0:T(512)S(1)}, u32[]{:S(2)}, u32[]{:S(2)}) collective-permute-start(f32[384]{0:T(512)S(1)} %get-tuple-element.6), channel_id=1, source_target_pairs={{0,4},{1,5},{2,6},{3,7},{4,0},{5,1},{6,2},{7,3},{8,12},{9,13},{10,... | collective-permute-start | bytes 4616 | tf_op jit(solution)/shard_map/ppermute | solution.py:32
  147.5 15.7 %collective-permute-start.17 = (f32[2,296,384]{2,1,0:T(8,128)}, f32[2,296,384]{2,1,0:T(8,128)}, u32[]{:S(2)}, u32[]{:S(2)}) collective-permute-start(f32[2,296,384]{2,1,0:T(8,128)} %dynamic-slice_bitcast_fusion), channel_id=1, source_target_pairs={{0,3},{1,0},{2,1},{3,2},{4,7},{5,4},{6,5},{7,6},{8,11},{9,8},{10,9... | collective-permute-start | bytes 2727944 | tf_op jit(solution)/shard_map/ppermute | solution.py:59
  150.8 16.4 %collective-permute-start.13 = (f32[2,288,384]{2,1,0:T(8,128)}, f32[2,288,384]{2,1,0:T(8,128)}, u32[]{:S(2)}, u32[]{:S(2)}) collective-permute-start(f32[2,288,384]{2,1,0:T(8,128)} %dynamic-slice_bitcast_fusion.1), channel_id=1, source_target_pairs={{0,1},{1,2},{2,3},{3,0},{4,5},{5,6},{6,7},{7,4},{8,9},{9,10},{10,1... | collective-permute-start | bytes 2654216 | tf_op jit(solution)/shard_map/ppermute | solution.py:58
  165.7 16.1 %collective-permute-start.18 = (f32[2,296,384]{2,1,0:T(8,128)}, f32[2,296,384]{2,1,0:T(8,128)}, u32[]{:S(2)}, u32[]{:S(2)}) collective-permute-start(f32[2,296,384]{2,1,0:T(8,128)} %bitcast_add_fusion), channel_id=1, source_target_pairs={{0,3},{1,0},{2,1},{3,2},{4,7},{5,4},{6,5},{7,6},{8,11},{9,8},{10,9... | collective-permute-start | bytes 2727944 | tf_op jit(solution)/shard_map/ppermute | solution.py:59
  169.4 16.6 %collective-permute-start.14 = (f32[2,288,384]{2,1,0:T(8,128)}, f32[2,288,384]{2,1,0:T(8,128)}, u32[]{:S(2)}, u32[]{:S(2)}) collective-permute-start(f32[2,288,384]{2,1,0:T(8,128)} %bitcast_add_fusion.3), channel_id=1, source_target_pairs={{0,1},{1,2},{2,3},{3,0},{4,5},{5,6},{6,7},{7,4},{8,9},{9,10},{10,1... | collective-permute-start | bytes 2654216 | tf_op jit(solution)/shard_map/ppermute | solution.py:58
  184.3 16.2 %collective-permute-start.19 = (f32[2,296,384]{2,1,0:T(8,128)}, f32[2,296,384]{2,1,0:T(8,128)}, u32[]{:S(2)}, u32[]{:S(2)}) collective-permute-start(f32[2,296,384]{2,1,0:T(8,128)} %bitcast_add_fusion.1), channel_id=1, source_target_pairs={{0,3},{1,0},{2,1},{3,2},{4,7},{5,4},{6,5},{7,6},{8,11},{9,8},{10,9... | collective-permute-start | bytes 2727944 | tf_op jit(solution)/shard_map/ppermute | solution.py:59
  188.2 16.1 %collective-permute-start.15 = (f32[2,288,384]{2,1,0:T(8,128)}, f32[2,288,384]{2,1,0:T(8,128)}, u32[]{:S(2)}, u32[]{:S(2)}) collective-permute-start(f32[2,288,384]{2,1,0:T(8,128)} %bitcast_add_fusion.4), channel_id=1, source_target_pairs={{0,1},{1,2},{2,3},{3,0},{4,5},{5,6},{6,7},{7,4},{8,9},{9,10},{10,1... | collective-permute-start | bytes 2654216 | tf_op jit(solution)/shard_map/ppermute | solution.py:58
  203.8 31.5 %collective-permute-start.20 = (f32[296,384]{1,0:T(8,128)}, f32[296,384]{1,0:T(8,128)}, u32[]{:S(2)}, u32[]{:S(2)}) collective-permute-start(f32[296,384]{1,0:T(8,128)} %dynamic-slice_bitcast_fusion.2), channel_id=1, source_target_pairs={{0,4},{1,5},{2,6},{3,7},{4,0},{5,1},{6,2},{7,3},{8,12},{9,13},{10,... | collective-permute-start | bytes 1363976 | tf_op jit(solution)/shard_map/ppermute | solution.py:66
  206.5 63.5 %collective-permute-start.16 = (f32[288,384]{1,0:T(8,128)S(1)}, f32[288,384]{1,0:T(8,128)S(1)}, u32[]{:S(2)}, u32[]{:S(2)}) collective-permute-start(f32[288,384]{1,0:T(8,128)S(1)} %dynamic-slice_bitcast_fusion.3), channel_id=1, source_target_pairs={{0,4},{1,5},{2,6},{3,7},{4,0},{5,1},{6,2},{7,3},{8,12},{9,13},{10,... | collective-permute-start | bytes 1327112 | tf_op jit(solution)/shard_map/ppermute | solution.py:63
  236.5 2.9 %collective-permute-start.21 = (f32[576]{0:T(1024)S(1)}, f32[576]{0:T(1024)S(1)}, u32[]{:S(2)}, u32[]{:S(2)}) collective-permute-start(f32[576]{0:T(1024)S(1)} %bitcast.73), channel_id=1, source_target_pairs={{0,16},{16,0},{32,48},{48,32},{64,80},{80,64},{96,112},{112,96},{1... | collective-permute-start | bytes 6920 | tf_op jit(solution)/shard_map/ppermute | solution.py:22
  239.4 3.8 %collective-permute-start.22 = (f32[576]{0:T(1024)S(1)}, f32[576]{0:T(1024)S(1)}, u32[]{:S(2)}, u32[]{:S(2)}) collective-permute-start(f32[576]{0:T(1024)S(1)} %slice_add_fusion), channel_id=1, source_target_pairs={{0,32},{16,48},{32,0},{48,16},{64,96},{80,112},{96,64},{112,80},{1... | collective-permute-start | bytes 6920 | tf_op jit(solution)/shard_map/ppermute | solution.py:22
  243.3 27.8 %collective-permute-start.23 = (f32[576]{0:T(1024)S(1)}, f32[576]{0:T(1024)S(1)}, u32[]{:S(2)}, u32[]{:S(2)}) collective-permute-start(f32[576]{0:T(1024)S(1)} %add.205), channel_id=1, source_target_pairs={{0,64},{16,80},{32,96},{48,112},{64,0},{80,16},{96,32},{112,48},{1... | collective-permute-start | bytes 6920 | tf_op jit(solution)/shard_map/ppermute | solution.py:22
  273.9 8.1 %collective-permute-start.25 = (f32[576]{0:T(1024)S(1)}, f32[576]{0:T(1024)S(1)}, u32[]{:S(2)}, u32[]{:S(2)}) collective-permute-start(f32[576]{0:T(1024)S(1)} %add.207), channel_id=1, source_target_pairs={{0,8},{8,0},{1,9},{9,1},{2,10},{10,2},{3,11},{11,3},{4,12},{12,4},... | collective-permute-start | bytes 6920 | tf_op jit(solution)/shard_map/ppermute | solution.py:22
  (9 other events, 105.0 us)
Sparse Core Ops, SparseCore 0:
  117.1 151.0 reduce-scatter.1

commit v2 on v1

--- a/solution.py
+++ b/solution.py
@@ -98,8 +98,11 @@
     grad_head = lax.psum_scatter(head_partial, ("outer", "core"), scatter_dimension=0, tiled=True)
 
     partial = lax.dot_general(
-        head_weight, dlogits, (((1,), (1,)), ((), ())), preferred_element_type=jnp.float32
-    )
+        head_weight.reshape(n_tensor, local_cols, vocab_rows),
+        jnp.broadcast_to(dlogits[None], (n_tensor, tokens, vocab_rows)),
+        (((2,), (2,)), ((0,), (0,))),
+        preferred_element_type=jnp.float32,
+    ).reshape(width, tokens)
     inner_part = jnp.sum(partial * (norm_gain[:, None] * normalized_t), axis=0)
     gain_part = jnp.sum(partial * normalized_t, axis=1)
 

time: 290 us -> 273 us (0.941)
  matrix products: 37.7 us -> 23.1 us
  local copies, waits for them, and re-layouts: 28.2 us -> 18 us
  starting transfers between devices: 43.2 us -> 46.4 us
  waiting for transfers between devices: 142 us -> 145 us
    dot_general x1 -> x0, local copies, waits for them, and re-layouts: 8.35 us -> none  [shards(): lax.dot_general(head_weight, dlogits, (((1,), (1,)), ((), ())), preferred...]
    convert_element_type x1 -> x0, local copies, waits for them, and re-layouts: 8.02 us -> none  [shards(): values_t = blocks.reshape(width, tokens).astype(jnp.float32)]
    dot_general x1, matrix products: 16.7 us -> 10.2 us  [shards(): lax.dot_general(head_weight.reshape(n_tensor, local_cols, vocab_rows), jn...]
    unnamed x27 -> x43, local copies, waits for them, and re-layouts: 5.73 us -> 11.5 us
    dot_general x1, matrix products: 8.72 us -> 3.91 us  [shards(): lax.dot_general(normed_t, head_weight, (((0,), (0,)), ((), ())), preferre...]
    ppermute x5, starting transfers between devices: 7.3 us -> 10.7 us  [butterfly_sum(): x = x + lax.ppermute(x, axis, [(c, c ^ b) for c in range(n)])]
    dot_general x1, matrix products: 12.3 us -> 9.05 us  [shards(): lax.dot_general(normed_t, dlogits, (((1,), (0,)), ((), ())), preferred_el...]
  transfers between devices with their start and end apart: 27 -> 27, of which waited for: 18 -> 20; matrix products, arithmetic and copies ran while one was open for 18% -> 13% of each run, Pallas kernels for 0% -> 0%
where the time goes in v2:
time: 273 us
  waiting for transfers between devices  145 us (53%)
  starting transfers between devices  46.4 us (17%)
  other arithmetic  25.4 us (9%)
  matrix products  23.1 us (8%)
  local copies, waits for them, and re-layouts  18 us (7%)
  between operations  14.5 us (5%)
    ppermute x7, waiting for transfers between devices, shift_gather(): got.append(lax.ppermute(x, axis, [(c, (c + k) % n) for c in range(n)]))  35.9 us
    ppermute x3, waiting for transfers between devices, two_stage_reduce_scatter(): recv_b = lax.ppermute(send_b, axis, perm_b)  34 us
    ppermute x1, waiting for transfers between devices, two_stage_reduce_scatter(): lax.ppermute(lax.dynamic_index_in_dim(sum_b, n_hi - 1 - h, 0, keepdims=Fa...  29 us
    ppermute x1, waiting for transfers between devices, two_stage_reduce_scatter(): lax.ppermute(lax.dynamic_index_in_dim(sum_f, n_hi - 1 - h, 0, keepdims=Fa...  26.2 us
    ppermute x3, starting transfers between devices, butterfly_softmax_stats(): other_total = lax.ppermute(total, axis, perm)  16.2 us
    unnamed x43, local copies, waits for them, and re-layouts  11.5 us
    ppermute x7, starting transfers between devices, shift_gather(): got.append(lax.ppermute(x, axis, [(c, (c + k) % n) for c in range(n)]))  11.3 us
    ppermute x5, starting transfers between devices, butterfly_sum(): x = x + lax.ppermute(x, axis, [(c, c ^ b) for c in range(n)])  10.7 us
  transfers between devices with their start and end apart: 27, of which 20 were waited for; matrix products, arithmetic and copies ran while one was open for 13% of the time, Pallas kernels for 0%

profile of v2, /device:TPU:1, one launch (start us, length us, event | category | flops | bytes accessed | tf_op | source)
XLA Modules:
  0.0 272.6 jit_solution(1885363370340024698)
XLA Ops:
  7.2 6.1 %collective-permute-start = (bf16[576,384]{1,0:T(8,128)(2,1)}, bf16[576,384]{1,0:T(8,128)(2,1)S(1)}, u32[]{:S(2)}, u32[]{:S(2)}) collective-permute-start(bf16[576,384]{1,0:T(8,128)(2,1)} %bitcast.83), channel_id=1, source_target_pairs={{0,7},{1,0},{2,1},{3,2},{4,3},{5,4},{6,5},{7,6},{8,15},{9,8},{10,9... | collective-permute-start | bytes 1327112 | tf_op jit(solution)/shard_map/ppermute | solution.py:13
  18.3 10.5 %collective-permute-done = bf16[576,384]{1,0:T(8,128)(2,1)S(1)} collective-permute-done((bf16[576,384]{1,0:T(8,128)(2,1)}, bf16[576,384]{1,0:T(8,128)(2,1)S(1)}, u32[]{:S(2)}, u32[]{:S(2)}) %collective-permute-start) | collective-permute-done | bytes 442400 | tf_op jit(solution)/shard_map/ppermute | solution.py:13
  28.8 15.9 %collective-permute-done.1 = bf16[576,384]{1,0:T(8,128)(2,1)S(1)} collective-permute-done((bf16[576,384]{1,0:T(8,128)(2,1)}, bf16[576,384]{1,0:T(8,128)(2,1)S(1)}, u32[]{:S(2)}, u32[]{:S(2)}) %collective-permute-start.1) | collective-permute-done | bytes 442400 | tf_op jit(solution)/shard_map/ppermute | solution.py:13
  45.1 5.6 %collective-permute-done.2 = bf16[576,384]{1,0:T(8,128)(2,1)S(1)} collective-permute-done((bf16[576,384]{1,0:T(8,128)(2,1)}, bf16[576,384]{1,0:T(8,128)(2,1)S(1)}, u32[]{:S(2)}, u32[]{:S(2)}) %collective-permute-start.2) | collective-permute-done | bytes 442400 | tf_op jit(solution)/shard_map/ppermute | solution.py:13
  50.7 3.9 %collective-permute-done.3 = bf16[576,384]{1,0:T(8,128)(2,1)S(1)} collective-permute-done((bf16[576,384]{1,0:T(8,128)(2,1)}, bf16[576,384]{1,0:T(8,128)(2,1)S(1)}, u32[]{:S(2)}, u32[]{:S(2)}) %collective-permute-start.3) | collective-permute-done | bytes 442400 | tf_op jit(solution)/shard_map/ppermute | solution.py:13
  57.6 2.7 copy-done.2
  62.3 3.9 %fusion.14 = (f32[384]{0:T(512)S(1)}, f32[384,1024]{1,0:T(8,128)S(1)}) fusion(bf16[4608,384]{1,0:T(8,128)(2,1)S(1)} %fusion.3, bf16[4608,1024]{1,0:T(8,128)(2,1)S(1)} %bitcast.80), kind=kOutput, calls=%fused_computation.60 | convolution fusion | flops 3624271360 | bytes 14550528 | tf_op jit(solution)/shard_map/dot_general | solution.py:83
  72.2 11.6 %collective-permute-start.11 = (f32[384]{0:T(512)S(1)}, f32[384]{0:T(512)}, u32[]{:S(2)}, u32[]{:S(2)}) collective-permute-start(f32[384]{0:T(512)S(1)} %get-tuple-element.7), channel_id=1, source_target_pairs={{0,2},{1,3},{2,0},{3,1},{4,6},{5,7},{6,4},{7,5},{8,10},{9,11},{10,... | collective-permute-start | bytes 4616 | tf_op jit(solution)/shard_map/ppermute | solution.py:33
  84.8 3.0 %collective-permute-done.8 = f32[384]{0:T(512)} collective-permute-done((f32[384]{0:T(512)S(1)}, f32[384]{0:T(512)}, u32[]{:S(2)}, u32[]{:S(2)}) %collective-permute-start.8) | collective-permute-done | bytes 1568 | tf_op jit(solution)/shard_map/ppermute | solution.py:32
  88.5 2.7 collective-permute-start.12
  92.5 2.7 collective-permute-done.9
  97.9 9.1 %fusion.15 = f32[4608,1024]{1,0:T(8,128)} fusion(bf16[4608,384]{1,0:T(8,128)(2,1)S(1)} %fusion.3, bf16[384,1024]{1,0:T(8,128)(2,1)S(1)} %subtract_convert_fusion), kind=kOutput, calls=%fused_computation.61 | convolution fusion | flops 3623878656 | bytes 23199744 | tf_op jit(solution)/shard_map/dot_general | solution.py:95
  108.1 10.2 %fusion.1 = (f32[384]{0:T(512)S(1)}, f32[8,576]{1,0:T(8,128)S(1)}, f32[8,384,576]{1,2,0:T(8,128)}) fusion(f32[8,576]{1,0:T(8,128)S(1)} %mul.117, f32[384]{0:T(512)S(1)} %add_rsqrt_fusion, bf16[16,576,384]{2,1,0:T(8,128)(2,1)} %copy-done.2, s32[]{:T(128)S(6)} %select_n.75, bf16[8,576,1024]{2,1,0:T(8,128)(2,1)} %bitcast.78, bf16[384,1024]{1,0:T(8,128)(2,1)S(1)} %copy-done.7), kind=kOutput, calls=%fused_computation.3 | convolution fusion | flops 3636259840 | bytes 20880388 | tf_op jit(solution)/shard_map/dot_general | solution.py:100
  123.5 2.7 slice.25
  128.6 10.1 %collective-permute-done.17 = f32[2,296,384]{2,1,0:T(8,128)} collective-permute-done((f32[2,296,384]{2,1,0:T(8,128)}, f32[2,296,384]{2,1,0:T(8,128)}, u32[]{:S(2)}, u32[]{:S(2)}) %collective-permute-start.17) | collective-permute-done | bytes 909344 | tf_op jit(solution)/shard_map/ppermute | solution.py:59
  145.7 11.7 %collective-permute-done.18 = f32[2,296,384]{2,1,0:T(8,128)} collective-permute-done((f32[2,296,384]{2,1,0:T(8,128)}, f32[2,296,384]{2,1,0:T(8,128)}, u32[]{:S(2)}, u32[]{:S(2)}) %collective-permute-start.18) | collective-permute-done | bytes 909344 | tf_op jit(solution)/shard_map/ppermute | solution.py:59
  163.8 12.2 %collective-permute-done.19 = f32[2,296,384]{2,1,0:T(8,128)} collective-permute-done((f32[2,296,384]{2,1,0:T(8,128)}, f32[2,296,384]{2,1,0:T(8,128)}, u32[]{:S(2)}, u32[]{:S(2)}) %collective-permute-start.19) | collective-permute-done | bytes 909344 | tf_op jit(solution)/shard_map/ppermute | solution.py:59
  182.0 2.6 collective-permute-start.16
  184.6 29.0 %collective-permute-done.20 = f32[296,384]{1,0:T(8,128)} collective-permute-done((f32[296,384]{1,0:T(8,128)}, f32[296,384]{1,0:T(8,128)}, u32[]{:S(2)}, u32[]{:S(2)}) %collective-permute-start.20) | collective-permute-done | bytes 454688 | tf_op jit(solution)/shard_map/ppermute | solution.py:66
  214.9 2.8 %collective-permute-done.21 = f32[576]{0:T(1024)S(1)} collective-permute-done((f32[576]{0:T(1024)S(1)}, f32[576]{0:T(1024)S(1)}, u32[]{:S(2)}, u32[]{:S(2)}) %collective-permute-start.21) | collective-permute-done | bytes 2336 | tf_op jit(solution)/shard_map/ppermute | solution.py:22
  218.6 3.0 %collective-permute-done.22 = f32[576]{0:T(1024)S(1)} collective-permute-done((f32[576]{0:T(1024)S(1)}, f32[576]{0:T(1024)S(1)}, u32[]{:S(2)}, u32[]{:S(2)}) %collective-permute-start.22) | collective-permute-done | bytes 2336 | tf_op jit(solution)/shard_map/ppermute | solution.py:22
  222.9 26.2 %collective-permute-done.16 = f32[288,384]{1,0:T(8,128)S(1)} collective-permute-done((f32[288,384]{1,0:T(8,128)S(1)}, f32[288,384]{1,0:T(8,128)S(1)}, u32[]{:S(2)}, u32[]{:S(2)}) %collective-permute-start.16) | collective-permute-done | bytes 442400 | tf_op jit(solution)/shard_map/ppermute | solution.py:63
  250.4 3.6 %collective-permute-done.24 = f32[576]{0:T(1024)S(1)} collective-permute-done((f32[576]{0:T(1024)S(1)}, f32[576]{0:T(1024)S(1)}, u32[]{:S(2)}, u32[]{:S(2)}) %collective-permute-start.24) | collective-permute-done | bytes 2336 | tf_op jit(solution)/shard_map/ppermute | solution.py:22
  253.9 9.1 %collective-permute-start.25 = (f32[576]{0:T(1024)S(1)}, f32[576]{0:T(1024)S(1)}, u32[]{:S(2)}, u32[]{:S(2)}) collective-permute-start(f32[576]{0:T(1024)S(1)} %add.207), channel_id=1, source_target_pairs={{0,8},{8,0},{1,9},{9,1},{2,10},{10,2},{3,11},{11,3},{4,12},{12,4},... | collective-permute-start | bytes 6920 | tf_op jit(solution)/shard_map/ppermute | solution.py:22
  (118 shorter events, 57.4 us)
Async XLA Ops:
  7.2 258.6 %reduce-scatter.2.cloned.1.call-start = ((), (), s32[]{:S(2)}) async-start(), calls=%async_computation.1 | async-start | bytes 19464192 | tf_op jit(solution)/shard_map/reduce_scatter | solution.py:98
  7.2 21.6 %collective-permute-start = (bf16[576,384]{1,0:T(8,128)(2,1)}, bf16[576,384]{1,0:T(8,128)(2,1)S(1)}, u32[]{:S(2)}, u32[]{:S(2)}) collective-permute-start(bf16[576,384]{1,0:T(8,128)(2,1)} %bitcast.83), channel_id=1, source_target_pairs={{0,7},{1,0},{2,1},{3,2},{4,3},{5,4},{6,5},{7,6},{8,15},{9,8},{10,9... | collective-permute-start | bytes 1327112 | tf_op jit(solution)/shard_map/ppermute | solution.py:13
  13.3 31.4 %collective-permute-start.1 = (bf16[576,384]{1,0:T(8,128)(2,1)}, bf16[576,384]{1,0:T(8,128)(2,1)S(1)}, u32[]{:S(2)}, u32[]{:S(2)}) collective-permute-start(bf16[576,384]{1,0:T(8,128)(2,1)} %bitcast.84), channel_id=1, source_target_pairs={{0,6},{1,7},{2,0},{3,1},{4,2},{5,3},{6,4},{7,5},{8,14},{9,15},{10,... | collective-permute-start | bytes 1327112 | tf_op jit(solution)/shard_map/ppermute | solution.py:13
  13.7 41.2 %collective-permute-start.6 = (bf16[576,384]{1,0:T(8,128)(2,1)}, bf16[576,384]{1,0:T(8,128)(2,1)S(1)}, u32[]{:S(2)}, u32[]{:S(2)}) collective-permute-start(bf16[576,384]{1,0:T(8,128)(2,1)} %bitcast.85), channel_id=1, source_target_pairs={{0,1},{1,2},{2,3},{3,4},{4,5},{5,6},{6,7},{7,0},{8,9},{9,10},{10,1... | collective-permute-start | bytes 1327112 | tf_op jit(solution)/shard_map/ppermute | solution.py:13
  14.4 40.4 %collective-permute-start.5 = (bf16[576,384]{1,0:T(8,128)(2,1)}, bf16[576,384]{1,0:T(8,128)(2,1)S(1)}, u32[]{:S(2)}, u32[]{:S(2)}) collective-permute-start(bf16[576,384]{1,0:T(8,128)(2,1)} %bitcast.86), channel_id=1, source_target_pairs={{0,2},{1,3},{2,4},{3,5},{4,6},{5,7},{6,0},{7,1},{8,10},{9,11},{10,... | collective-permute-start | bytes 1327112 | tf_op jit(solution)/shard_map/ppermute | solution.py:13
  16.3 38.4 %collective-permute-start.4 = (bf16[576,384]{1,0:T(8,128)(2,1)}, bf16[576,384]{1,0:T(8,128)(2,1)S(1)}, u32[]{:S(2)}, u32[]{:S(2)}) collective-permute-start(bf16[576,384]{1,0:T(8,128)(2,1)} %bitcast.87), channel_id=1, source_target_pairs={{0,3},{1,4},{2,5},{3,6},{4,7},{5,0},{6,1},{7,2},{8,11},{9,12},{10,... | collective-permute-start | bytes 1327112 | tf_op jit(solution)/shard_map/ppermute | solution.py:13
  28.8 21.9 %collective-permute-start.2 = (bf16[576,384]{1,0:T(8,128)(2,1)}, bf16[576,384]{1,0:T(8,128)(2,1)S(1)}, u32[]{:S(2)}, u32[]{:S(2)}) collective-permute-start(bf16[576,384]{1,0:T(8,128)(2,1)} %bitcast.88), channel_id=1, source_target_pairs={{0,5},{1,6},{2,7},{3,0},{4,1},{5,2},{6,3},{7,4},{8,13},{9,14},{10,... | collective-permute-start | bytes 1327112 | tf_op jit(solution)/shard_map/ppermute | solution.py:13
  44.8 9.8 %collective-permute-start.3 = (bf16[576,384]{1,0:T(8,128)(2,1)}, bf16[576,384]{1,0:T(8,128)(2,1)S(1)}, u32[]{:S(2)}, u32[]{:S(2)}) collective-permute-start(bf16[576,384]{1,0:T(8,128)(2,1)} %bitcast.89), channel_id=1, source_target_pairs={{0,4},{1,5},{2,6},{3,7},{4,0},{5,1},{6,2},{7,3},{8,12},{9,13},{10,... | collective-permute-start | bytes 1327112 | tf_op jit(solution)/shard_map/ppermute | solution.py:13
  72.2 12.7 %collective-permute-start.11 = (f32[384]{0:T(512)S(1)}, f32[384]{0:T(512)}, u32[]{:S(2)}, u32[]{:S(2)}) collective-permute-start(f32[384]{0:T(512)S(1)} %get-tuple-element.7), channel_id=1, source_target_pairs={{0,2},{1,3},{2,0},{3,1},{4,6},{5,7},{6,4},{7,5},{8,10},{9,11},{10,... | collective-permute-start | bytes 4616 | tf_op jit(solution)/shard_map/ppermute | solution.py:33
  83.8 4.0 %collective-permute-start.8 = (f32[384]{0:T(512)S(1)}, f32[384]{0:T(512)}, u32[]{:S(2)}, u32[]{:S(2)}) collective-permute-start(f32[384]{0:T(512)S(1)} %get-tuple-element.8), channel_id=1, source_target_pairs={{0,2},{1,3},{2,0},{3,1},{4,6},{5,7},{6,4},{7,5},{8,10},{9,11},{10,... | collective-permute-start | bytes 4616 | tf_op jit(solution)/shard_map/ppermute | solution.py:32
  88.5 4.0 %collective-permute-start.12 = (f32[384]{0:T(512)S(1)}, f32[384]{0:T(512)S(1)}, u32[]{:S(2)}, u32[]{:S(2)}) collective-permute-start(f32[384]{0:T(512)S(1)} %get-tuple-element.5), channel_id=1, source_target_pairs={{0,4},{1,5},{2,6},{3,7},{4,0},{5,1},{6,2},{7,3},{8,12},{9,13},{10,... | collective-permute-start | bytes 4616 | tf_op jit(solution)/shard_map/ppermute | solution.py:33
  91.2 3.9 %collective-permute-start.9 = (f32[384]{0:T(512)S(1)}, f32[384]{0:T(512)S(1)}, u32[]{:S(2)}, u32[]{:S(2)}) collective-permute-start(f32[384]{0:T(512)S(1)} %get-tuple-element.6), channel_id=1, source_target_pairs={{0,4},{1,5},{2,6},{3,7},{4,0},{5,1},{6,2},{7,3},{8,12},{9,13},{10,... | collective-permute-start | bytes 4616 | tf_op jit(solution)/shard_map/ppermute | solution.py:32
  123.5 15.3 %collective-permute-start.17 = (f32[2,296,384]{2,1,0:T(8,128)}, f32[2,296,384]{2,1,0:T(8,128)}, u32[]{:S(2)}, u32[]{:S(2)}) collective-permute-start(f32[2,296,384]{2,1,0:T(8,128)} %dynamic-slice_bitcast_fusion), channel_id=1, source_target_pairs={{0,3},{1,0},{2,1},{3,2},{4,7},{5,4},{6,5},{7,6},{8,11},{9,8},{10,9... | collective-permute-start | bytes 2727944 | tf_op jit(solution)/shard_map/ppermute | solution.py:59
  127.2 16.3 %collective-permute-start.13 = (f32[2,288,384]{2,1,0:T(8,128)}, f32[2,288,384]{2,1,0:T(8,128)}, u32[]{:S(2)}, u32[]{:S(2)}) collective-permute-start(f32[2,288,384]{2,1,0:T(8,128)} %dynamic-slice_bitcast_fusion.1), channel_id=1, source_target_pairs={{0,1},{1,2},{2,3},{3,0},{4,5},{5,6},{6,7},{7,4},{8,9},{9,10},{10,1... | collective-permute-start | bytes 2654216 | tf_op jit(solution)/shard_map/ppermute | solution.py:58
  141.2 16.1 %collective-permute-start.18 = (f32[2,296,384]{2,1,0:T(8,128)}, f32[2,296,384]{2,1,0:T(8,128)}, u32[]{:S(2)}, u32[]{:S(2)}) collective-permute-start(f32[2,296,384]{2,1,0:T(8,128)} %bitcast_add_fusion), channel_id=1, source_target_pairs={{0,3},{1,0},{2,1},{3,2},{4,7},{5,4},{6,5},{7,6},{8,11},{9,8},{10,9... | collective-permute-start | bytes 2727944 | tf_op jit(solution)/shard_map/ppermute | solution.py:59
  145.7 15.9 %collective-permute-start.14 = (f32[2,288,384]{2,1,0:T(8,128)}, f32[2,288,384]{2,1,0:T(8,128)}, u32[]{:S(2)}, u32[]{:S(2)}) collective-permute-start(f32[2,288,384]{2,1,0:T(8,128)} %bitcast_add_fusion.3), channel_id=1, source_target_pairs={{0,1},{1,2},{2,3},{3,0},{4,5},{5,6},{6,7},{7,4},{8,9},{9,10},{10,1... | collective-permute-start | bytes 2654216 | tf_op jit(solution)/shard_map/ppermute | solution.py:58
  159.9 16.1 %collective-permute-start.19 = (f32[2,296,384]{2,1,0:T(8,128)}, f32[2,296,384]{2,1,0:T(8,128)}, u32[]{:S(2)}, u32[]{:S(2)}) collective-permute-start(f32[2,296,384]{2,1,0:T(8,128)} %bitcast_add_fusion.1), channel_id=1, source_target_pairs={{0,3},{1,0},{2,1},{3,2},{4,7},{5,4},{6,5},{7,6},{8,11},{9,8},{10,9... | collective-permute-start | bytes 2727944 | tf_op jit(solution)/shard_map/ppermute | solution.py:59
  163.8 16.0 %collective-permute-start.15 = (f32[2,288,384]{2,1,0:T(8,128)}, f32[2,288,384]{2,1,0:T(8,128)}, u32[]{:S(2)}, u32[]{:S(2)}) collective-permute-start(f32[2,288,384]{2,1,0:T(8,128)} %bitcast_add_fusion.4), channel_id=1, source_target_pairs={{0,1},{1,2},{2,3},{3,0},{4,5},{5,6},{6,7},{7,4},{8,9},{9,10},{10,1... | collective-permute-start | bytes 2654216 | tf_op jit(solution)/shard_map/ppermute | solution.py:58
  179.3 34.3 %collective-permute-start.20 = (f32[296,384]{1,0:T(8,128)}, f32[296,384]{1,0:T(8,128)}, u32[]{:S(2)}, u32[]{:S(2)}) collective-permute-start(f32[296,384]{1,0:T(8,128)} %dynamic-slice_bitcast_fusion.2), channel_id=1, source_target_pairs={{0,4},{1,5},{2,6},{3,7},{4,0},{5,1},{6,2},{7,3},{8,12},{9,13},{10,... | collective-permute-start | bytes 1363976 | tf_op jit(solution)/shard_map/ppermute | solution.py:66
  182.0 67.1 %collective-permute-start.16 = (f32[288,384]{1,0:T(8,128)S(1)}, f32[288,384]{1,0:T(8,128)S(1)}, u32[]{:S(2)}, u32[]{:S(2)}) collective-permute-start(f32[288,384]{1,0:T(8,128)S(1)} %dynamic-slice_bitcast_fusion.3), channel_id=1, source_target_pairs={{0,4},{1,5},{2,6},{3,7},{4,0},{5,1},{6,2},{7,3},{8,12},{9,13},{10,... | collective-permute-start | bytes 1327112 | tf_op jit(solution)/shard_map/ppermute | solution.py:63
  217.8 3.8 %collective-permute-start.22 = (f32[576]{0:T(1024)S(1)}, f32[576]{0:T(1024)S(1)}, u32[]{:S(2)}, u32[]{:S(2)}) collective-permute-start(f32[576]{0:T(1024)S(1)} %slice_add_fusion), channel_id=1, source_target_pairs={{0,32},{16,48},{32,0},{48,16},{64,96},{80,112},{96,64},{112,80},{1... | collective-permute-start | bytes 6920 | tf_op jit(solution)/shard_map/ppermute | solution.py:22
  221.6 28.7 %collective-permute-start.23 = (f32[576]{0:T(1024)S(1)}, f32[576]{0:T(1024)S(1)}, u32[]{:S(2)}, u32[]{:S(2)}) collective-permute-start(f32[576]{0:T(1024)S(1)} %add.205), channel_id=1, source_target_pairs={{0,64},{16,80},{32,96},{48,112},{64,0},{80,16},{96,32},{112,48},{1... | collective-permute-start | bytes 6920 | tf_op jit(solution)/shard_map/ppermute | solution.py:22
  250.2 3.7 %collective-permute-start.24 = (f32[576]{0:T(1024)S(1)}, f32[576]{0:T(1024)S(1)}, u32[]{:S(2)}, u32[]{:S(2)}) collective-permute-start(f32[576]{0:T(1024)S(1)} %add.206), channel_id=1, source_target_pairs={{0,128},{16,144},{32,160},{48,176},{64,192},{80,208},{96,224},{112... | collective-permute-start | bytes 6920 | tf_op jit(solution)/shard_map/ppermute | solution.py:22
  253.9 11.2 %collective-permute-start.25 = (f32[576]{0:T(1024)S(1)}, f32[576]{0:T(1024)S(1)}, u32[]{:S(2)}, u32[]{:S(2)}) collective-permute-start(f32[576]{0:T(1024)S(1)} %add.207), channel_id=1, source_target_pairs={{0,8},{8,0},{1,9},{9,1},{2,10},{10,2},{3,11},{11,3},{4,12},{12,4},... | collective-permute-start | bytes 6920 | tf_op jit(solution)/shard_map/ppermute | solution.py:22
  (17 other events, 130.8 us)
Sparse Core Ops, SparseCore 0:
  107.1 150.9 reduce-scatter.1

commit v3 on v2

--- a/solution.py
+++ b/solution.py
@@ -74,27 +74,43 @@
     width, vocab_rows = head_weight.shape
     n_tensor = width // local_cols
     n_outer = lax.psum(1, "outer")
-    blocks = shift_gather(hidden_input_state.T, "tensor", n_tensor)
-    values_t = blocks.reshape(width, tokens).astype(jnp.float32)
-    scaled = lax.rsqrt(jnp.mean(values_t * values_t, axis=0) + epsilon)
-    scaled_rows = scaled[:, None]
-    normalized_t = values_t * scaled[None, :]
-    normed_t = (normalized_t * norm_gain[:, None]).astype(jnp.bfloat16)
-    logits = lax.dot_general(
-        normed_t, head_weight, (((0,), (0,)), ((), ())), preferred_element_type=jnp.float32
-    )
-    row_top, row_total = butterfly_softmax_stats(
-        jnp.max(logits, axis=1), logits, "tensor", n_tensor
-    )
-    log_total = row_top + jnp.log(row_total)
     offset = lax.axis_index("tensor") * vocab_rows
     column_ids = offset + lax.broadcasted_iota(jnp.int32, (1, vocab_rows), 1)
-    onehot = (column_ids == target_ids[:, None]).astype(jnp.float32)
-    dlogits = (jnp.exp(logits - log_total[:, None]) - onehot).astype(jnp.bfloat16)
 
-    head_partial = lax.dot_general(
-        normed_t, dlogits, (((1,), (0,)), ((), ())), preferred_element_type=jnp.float32
-    )
+    def front(hidden_t, targets):
+        blocks = shift_gather(hidden_t, "tensor", n_tensor)
+        values_t = blocks.reshape(width, hidden_t.shape[1]).astype(jnp.float32)
+        scaled = lax.rsqrt(jnp.mean(values_t * values_t, axis=0) + epsilon)
+        normalized_t = values_t * scaled[None, :]
+        normed_t = (normalized_t * norm_gain[:, None]).astype(jnp.bfloat16)
+        logits = lax.dot_general(
+            normed_t, head_weight, (((0,), (0,)), ((), ())), preferred_element_type=jnp.float32
+        )
+        local_top = jnp.max(logits, axis=1)
+        local_total = jnp.sum(jnp.exp(logits - local_top[:, None]), axis=1)
+        stats = shift_gather(jnp.stack([local_top, local_total]), "tensor", n_tensor)
+        row_top = jnp.max(stats[:, 0, :], axis=0)
+        row_total = jnp.sum(stats[:, 1, :] * jnp.exp(stats[:, 0, :] - row_top[None, :]), axis=0)
+        log_total = row_top + jnp.log(row_total)
+        onehot = (column_ids == targets[:, None]).astype(jnp.float32)
+        dlogits = (jnp.exp(logits - log_total[:, None]) - onehot).astype(jnp.bfloat16)
+        head_part = lax.dot_general(
+            normed_t, dlogits, (((1,), (0,)), ((), ())), preferred_element_type=jnp.float32
+        )
+        return scaled, normalized_t, dlogits, head_part
+
+    first = 256 if tokens > 256 and tokens % 128 == 0 else tokens
+    hidden_t = hidden_input_state.T
+    parts = [front(hidden_t[:, :first], target_ids[:first])]
+    if first < tokens:
+        parts.append(front(hidden_t[:, first:], target_ids[first:]))
+    scaled = jnp.concatenate([p[0] for p in parts])
+    scaled_rows = scaled[:, None]
+    normalized_t = jnp.concatenate([p[1] for p in parts], axis=1)
+    dlogits = jnp.concatenate([p[2] for p in parts], axis=0)
+    head_partial = parts[0][3]
+    for p in parts[1:]:
+        head_partial = head_partial + p[3]
     grad_head = lax.psum_scatter(head_partial, ("outer", "core"), scatter_dimension=0, tiled=True)
 
     partial = lax.dot_general(

time: 273 us -> 356 us (1.30); the launches traced: 273 us -> 351 us
  starting transfers between devices: 46.4 us -> 111 us
  matrix products: 23.1 us -> 40.3 us
  waiting for transfers between devices: 145 us -> 128 us
  local copies, waits for them, and re-layouts: 18 us -> 25.7 us
  other arithmetic: 25.4 us -> 30.7 us
    ppermute x7 -> x28, starting transfers between devices: 11.3 us -> 74.1 us  [shift_gather(): got.append(lax.ppermute(x, axis, [(c, (c + k) % n) for c in range(n)]))]
    dot_general x2 -> x4, matrix products: 13 us -> 30.5 us  [the longest x2 19.9 us: front(): lax.dot_general(normed_t, dlogits, (((1,), (0,)), ((), ())), preferred_el...]
    ppermute x6 -> x0, starting transfers between devices: 16.8 us -> none  [the longest x3 16.2 us: butterfly_softmax_stats(): other_total = lax.ppermute(total, axis, perm)]
    ppermute x1, waiting for transfers between devices: 29 us -> 17.1 us  [two_stage_reduce_scatter(): lax.ppermute(lax.dynamic_index_in_dim(sum_b, n_hi - 1 - h, 0, keepdims=Fa...]
    ppermute x5, starting transfers between devices: 10.7 us -> 21 us  [butterfly_sum(): x = x + lax.ppermute(x, axis, [(c, c ^ b) for c in range(n)])]
    ppermute x6 -> x0, waiting for transfers between devices: 9.78 us -> none  [the longest x3 7.1 us: butterfly_softmax_stats(): other_top = lax.ppermute(top, axis, perm)]
    ppermute x3, starting transfers between devices: 3 us -> 9.98 us  [two_stage_reduce_scatter(): recv_b = lax.ppermute(send_b, axis, perm_b)]
    ppermute x7 -> x28, waiting for transfers between devices: 35.9 us -> 39.8 us  [shift_gather(): got.append(lax.ppermute(x, axis, [(c, (c + k) % n) for c in range(n)]))]
  transfers between devices with their start and end apart: 27 -> 42, of which waited for: 20 -> 21; matrix products, arithmetic and copies ran while one was open for 13% -> 15% of each run, Pallas kernels for 0% -> 0%
where the time goes in v3:
time: 356 us; the launch traced here: 351 us
  waiting for transfers between devices  128 us (36%)
  starting transfers between devices  111 us (31%)
  matrix products  40.3 us (11%)
  other arithmetic  30.7 us (9%)
  local copies, waits for them, and re-layouts  25.7 us (7%)
  between operations  15.1 us (4%)
    ppermute x28, starting transfers between devices, shift_gather(): got.append(lax.ppermute(x, axis, [(c, (c + k) % n) for c in range(n)]))  74.1 us
    ppermute x28, waiting for transfers between devices, shift_gather(): got.append(lax.ppermute(x, axis, [(c, (c + k) % n) for c in range(n)]))  39.8 us
    ppermute x3, waiting for transfers between devices, two_stage_reduce_scatter(): recv_b = lax.ppermute(send_b, axis, perm_b)  37.6 us
    ppermute x1, waiting for transfers between devices, two_stage_reduce_scatter(): lax.ppermute(lax.dynamic_index_in_dim(sum_f, n_hi - 1 - h, 0, keepdims=Fa...  23.4 us
    ppermute x5, starting transfers between devices, butterfly_sum(): x = x + lax.ppermute(x, axis, [(c, c ^ b) for c in range(n)])  21 us
    dot_general x2, matrix products, front(): lax.dot_general(normed_t, dlogits, (((1,), (0,)), ((), ())), preferred_el...  19.9 us
    ppermute x1, waiting for transfers between devices, two_stage_reduce_scatter(): lax.ppermute(lax.dynamic_index_in_dim(sum_b, n_hi - 1 - h, 0, keepdims=Fa...  17.1 us
    unnamed x92, local copies, waits for them, and re-layouts  11.4 us
  transfers between devices with their start and end apart: 42, of which 21 were waited for; matrix products, arithmetic and copies ran while one was open for 15% of the time, Pallas kernels for 0%

profile of v3, /device:TPU:1, one launch (start us, length us, event | category | flops | bytes accessed | tf_op | source)
XLA Modules:
  0.0 351.1 jit_solution(876877628993385876)
XLA Ops:
  8.2 6.1 %collective-permute-start.7 = (bf16[576,128]{1,0:T(8,128)(2,1)S(1)}, bf16[576,128]{1,0:T(8,128)(2,1)S(1)}, u32[]{:S(2)}, u32[]{:S(2)}) collective-permute-start(bf16[576,128]{1,0:T(8,128)(2,1)S(1)} %slice.60), channel_id=1, source_target_pairs={{0,7},{1,0},{2,1},{3,2},{4,3},{5,4},{6,5},{7,6},{8,15},{9,8},{10,9... | collective-permute-start | bytes 442376 | tf_op jit(solution)/shard_map/ppermute | solution.py:13
  20.7 4.8 %collective-permute-start.8 = (bf16[576,128]{1,0:T(8,128)(2,1)S(1)}, bf16[576,128]{1,0:T(8,128)(2,1)S(1)}, u32[]{:S(2)}, u32[]{:S(2)}) collective-permute-start(bf16[576,128]{1,0:T(8,128)(2,1)S(1)} %slice.60), channel_id=1, source_target_pairs={{0,6},{1,7},{2,0},{3,1},{4,2},{5,3},{6,4},{7,5},{8,14},{9,15},{10,... | collective-permute-start | bytes 442376 | tf_op jit(solution)/shard_map/ppermute | solution.py:13
  25.5 4.1 %collective-permute-done.8 = bf16[576,128]{1,0:T(8,128)(2,1)S(1)} collective-permute-done((bf16[576,128]{1,0:T(8,128)(2,1)S(1)}, bf16[576,128]{1,0:T(8,128)(2,1)S(1)}, u32[]{:S(2)}, u32[]{:S(2)}) %collective-permute-start.8) | collective-permute-done | bytes 147488 | tf_op jit(solution)/shard_map/ppermute | solution.py:13
  29.6 4.1 %collective-permute-start.9 = (bf16[576,128]{1,0:T(8,128)(2,1)S(1)}, bf16[576,128]{1,0:T(8,128)(2,1)S(1)}, u32[]{:S(2)}, u32[]{:S(2)}) collective-permute-start(bf16[576,128]{1,0:T(8,128)(2,1)S(1)} %slice.60), channel_id=1, source_target_pairs={{0,5},{1,6},{2,7},{3,0},{4,1},{5,2},{6,3},{7,4},{8,13},{9,14},{10,... | collective-permute-start | bytes 442376 | tf_op jit(solution)/shard_map/ppermute | solution.py:13
  35.7 4.9 %collective-permute-start.6 = (bf16[576,256]{1,0:T(8,128)(2,1)S(1)}, bf16[576,256]{1,0:T(8,128)(2,1)S(1)}, u32[]{:S(2)}, u32[]{:S(2)}) collective-permute-start(bf16[576,256]{1,0:T(8,128)(2,1)S(1)} %slice.59), channel_id=1, source_target_pairs={{0,1},{1,2},{2,3},{3,4},{4,5},{5,6},{6,7},{7,0},{8,9},{9,10},{10,1... | collective-permute-start | bytes 884744 | tf_op jit(solution)/shard_map/ppermute | solution.py:13
  51.0 5.2 %fusion.17 = (f32[128]{0:T(128)S(1)}, f32[128,1024]{1,0:T(8,128)S(1)}) fusion(bf16[4608,128]{1,0:T(8,128)(2,1)S(1)} %fusion.8, bf16[4608,1024]{1,0:T(8,128)(2,1)} %param.6), kind=kOutput, calls=%fused_computation.112 | convolution fusion | flops 1208090496 | bytes 11141632 | tf_op jit(solution)/shard_map/dot_general | solution.py:86
  60.4 8.9 %collective-permute-start.22 = (f32[2,128]{1,0:T(2,128)S(1)}, f32[2,128]{1,0:T(2,128)S(1)}, u32[]{:S(2)}, u32[]{:S(2)}) collective-permute-start(f32[2,128]{1,0:T(2,128)S(1)} %pad_maximum_fusion.7), channel_id=1, source_target_pairs={{0,6},{1,7},{2,0},{3,1},{4,2},{5,3},{6,4},{7,5},{8,14},{9,15},{10,... | collective-permute-start | bytes 3080 | tf_op jit(solution)/shard_map/ppermute | solution.py:13
  82.4 4.2 %collective-permute-start.26 = (f32[2,128]{1,0:T(2,128)S(1)}, f32[2,128]{1,0:T(2,128)S(1)}, u32[]{:S(2)}, u32[]{:S(2)}) collective-permute-start(f32[2,128]{1,0:T(2,128)S(1)} %pad_maximum_fusion.7), channel_id=1, source_target_pairs={{0,2},{1,3},{2,4},{3,5},{4,6},{5,7},{6,0},{7,1},{8,10},{9,11},{10,... | collective-permute-start | bytes 3080 | tf_op jit(solution)/shard_map/ppermute | solution.py:13
  91.3 4.8 %collective-permute-done.27 = f32[2,128]{1,0:T(2,128)S(1)} collective-permute-done((f32[2,128]{1,0:T(2,128)S(1)}, f32[2,128]{1,0:T(2,128)S(1)}, u32[]{:S(2)}, u32[]{:S(2)}) %collective-permute-start.27) | collective-permute-done | bytes 1056 | tf_op jit(solution)/shard_map/ppermute | solution.py:13
  96.3 5.4 %collective-permute-done = bf16[576,256]{1,0:T(8,128)(2,1)S(1)} collective-permute-done((bf16[576,256]{1,0:T(8,128)(2,1)S(1)}, bf16[576,256]{1,0:T(8,128)(2,1)S(1)}, u32[]{:S(2)}, u32[]{:S(2)}) %collective-permute-start) | collective-permute-done | bytes 294944 | tf_op jit(solution)/shard_map/ppermute | solution.py:13
  104.1 4.4 %collective-permute-done.2 = bf16[576,256]{1,0:T(8,128)(2,1)S(1)} collective-permute-done((bf16[576,256]{1,0:T(8,128)(2,1)S(1)}, bf16[576,256]{1,0:T(8,128)(2,1)S(1)}, u32[]{:S(2)}, u32[]{:S(2)}) %collective-permute-start.2) | collective-permute-done | bytes 294944 | tf_op jit(solution)/shard_map/ppermute | solution.py:13
  108.5 5.9 %collective-permute-done.3 = bf16[576,256]{1,0:T(8,128)(2,1)S(1)} collective-permute-done((bf16[576,256]{1,0:T(8,128)(2,1)S(1)}, bf16[576,256]{1,0:T(8,128)(2,1)S(1)}, u32[]{:S(2)}, u32[]{:S(2)}) %collective-permute-start.3) | collective-permute-done | bytes 294944 | tf_op jit(solution)/shard_map/ppermute | solution.py:13
  119.6 5.4 %fusion.18 = (f32[256]{0:T(256)S(1)}, f32[256,1024]{1,0:T(8,128)S(1)}) fusion(bf16[4608,256]{1,0:T(8,128)(2,1)S(1)} %fusion.3, bf16[4608,1024]{1,0:T(8,128)(2,1)} %param.6), kind=kOutput, calls=%fused_computation.113 | convolution fusion | flops 2416180992 | bytes 12846080 | tf_op jit(solution)/shard_map/dot_general | solution.py:86
  126.5 12.7 %collective-permute-start.18 = (f32[2,256]{1,0:T(2,128)S(1)}, f32[2,256]{1,0:T(2,128)S(1)}, u32[]{:S(2)}, u32[]{:S(2)}) collective-permute-start(f32[2,256]{1,0:T(2,128)S(1)} %pad_maximum_fusion.6), channel_id=1, source_target_pairs={{0,3},{1,4},{2,5},{3,6},{4,7},{5,0},{6,1},{7,2},{8,11},{9,12},{10,... | collective-permute-start | bytes 6152 | tf_op jit(solution)/shard_map/ppermute | solution.py:13
  157.3 7.8 %fusion.19 = f32[4608,1024]{1,0:T(8,128)} fusion(bf16[4608,256]{1,0:T(8,128)(2,1)S(1)} %fusion.3, bf16[256,1024]{1,0:T(8,128)(2,1)S(1)} %subtract_convert_fusion), kind=kOutput, calls=%fused_computation.114 | convolution fusion | flops 2415919104 | bytes 21757952 | tf_op jit(solution)/shard_map/dot_general | solution.py:97
  165.2 12.1 %convolution_add_fusion = f32[4608,1024]{1,0:T(8,128)} fusion(f32[4608,1024]{1,0:T(8,128)} %fusion.19, bf16[4608,128]{1,0:T(8,128)(2,1)S(1)} %fusion.8, bf16[128,1024]{1,0:T(8,128)(2,1)S(1)} %copy-done.14), kind=kOutput, calls=%fused_computation | convolution fusion | flops 1212678144 | bytes 39190528 | tf_op jit(solution)/shard_map/dot_general | solution.py:97
  181.4 9.8 %fusion.1 = (f32[384]{0:T(512)S(1)}, f32[8,576]{1,0:T(8,128)S(1)}, f32[8,384,576]{1,2,0:T(8,128)}) fusion(f32[8,576,128]{2,1,0:T(8,128)S(1)} %broadcast_multiply_fusion.1, f32[8,576,256]{2,1,0:T(8,128)S(1)} %broadcast_multiply_fusion, f32[8,576]{1,0:T(8,128)S(1)} %mul.128, bf16[8,576,1024]{2,1,0:T(8,128)(2,1)} %bitcast.162, ...), kind=kOutput, calls=%fused_computation.5 | convolution fusion | flops 3634490368 | bytes 24417792 | tf_op jit(solution)/shard_map/dot_general | solution.py:116
  202.7 7.3 %collective-permute-done.32 = f32[2,296,384]{2,1,0:T(8,128)} collective-permute-done((f32[2,296,384]{2,1,0:T(8,128)}, f32[2,296,384]{2,1,0:T(8,128)}, u32[]{:S(2)}, u32[]{:S(2)}) %collective-permute-start.32) | collective-permute-done | bytes 909344 | tf_op jit(solution)/shard_map/ppermute | solution.py:59
  218.3 14.9 %collective-permute-done.33 = f32[2,296,384]{2,1,0:T(8,128)} collective-permute-done((f32[2,296,384]{2,1,0:T(8,128)}, f32[2,296,384]{2,1,0:T(8,128)}, u32[]{:S(2)}, u32[]{:S(2)}) %collective-permute-start.33) | collective-permute-done | bytes 909344 | tf_op jit(solution)/shard_map/ppermute | solution.py:59
  241.9 15.4 %collective-permute-done.34 = f32[2,296,384]{2,1,0:T(8,128)} collective-permute-done((f32[2,296,384]{2,1,0:T(8,128)}, f32[2,296,384]{2,1,0:T(8,128)}, u32[]{:S(2)}, u32[]{:S(2)}) %collective-permute-start.34) | collective-permute-done | bytes 909344 | tf_op jit(solution)/shard_map/ppermute | solution.py:59
  267.8 17.1 %collective-permute-done.35 = f32[296,384]{1,0:T(8,128)} collective-permute-done((f32[296,384]{1,0:T(8,128)}, f32[296,384]{1,0:T(8,128)}, u32[]{:S(2)}, u32[]{:S(2)}) %collective-permute-start.35) | collective-permute-done | bytes 454688 | tf_op jit(solution)/shard_map/ppermute | solution.py:66
  296.3 23.4 %collective-permute-done.31 = f32[288,384]{1,0:T(8,128)S(1)} collective-permute-done((f32[288,384]{1,0:T(8,128)S(1)}, f32[288,384]{1,0:T(8,128)S(1)}, u32[]{:S(2)}, u32[]{:S(2)}) %collective-permute-start.31) | collective-permute-done | bytes 442400 | tf_op jit(solution)/shard_map/ppermute | solution.py:63
  320.9 4.0 %collective-permute-done.39 = f32[576]{0:T(1024)S(1)} collective-permute-done((f32[576]{0:T(1024)S(1)}, f32[576]{0:T(1024)S(1)}, u32[]{:S(2)}, u32[]{:S(2)}) %collective-permute-start.39) | collective-permute-done | bytes 2336 | tf_op jit(solution)/shard_map/ppermute | solution.py:22
  325.0 17.3 %collective-permute-start.40 = (f32[576]{0:T(1024)S(1)}, f32[576]{0:T(1024)S(1)}, u32[]{:S(2)}, u32[]{:S(2)}) collective-permute-start(f32[576]{0:T(1024)S(1)} %add.222), channel_id=1, source_target_pairs={{0,8},{8,0},{1,9},{9,1},{2,10},{10,2},{3,11},{11,3},{4,12},{12,4},... | collective-permute-start | bytes 6920 | tf_op jit(solution)/shard_map/ppermute | solution.py:22
  (229 shorter events, 126.1 us)
Async XLA Ops:
  7.2 336.8 %reduce-scatter.2.cloned.1.call-start = ((), (), s32[]{:S(2)}) async-start(), calls=%async_computation.1 | async-start | bytes 19464192 | tf_op jit(solution)/shard_map/reduce_scatter | solution.py:114
  8.2 12.5 %collective-permute-start.7 = (bf16[576,128]{1,0:T(8,128)(2,1)S(1)}, bf16[576,128]{1,0:T(8,128)(2,1)S(1)}, u32[]{:S(2)}, u32[]{:S(2)}) collective-permute-start(bf16[576,128]{1,0:T(8,128)(2,1)S(1)} %slice.60), channel_id=1, source_target_pairs={{0,7},{1,0},{2,1},{3,2},{4,3},{5,4},{6,5},{7,6},{8,15},{9,8},{10,9... | collective-permute-start | bytes 442376 | tf_op jit(solution)/shard_map/ppermute | solution.py:13
  14.3 32.1 %collective-permute-start.13 = (bf16[576,128]{1,0:T(8,128)(2,1)S(1)}, bf16[576,128]{1,0:T(8,128)(2,1)S(1)}, u32[]{:S(2)}, u32[]{:S(2)}) collective-permute-start(bf16[576,128]{1,0:T(8,128)(2,1)S(1)} %slice.60), channel_id=1, source_target_pairs={{0,1},{1,2},{2,3},{3,4},{4,5},{5,6},{6,7},{7,0},{8,9},{9,10},{10,1... | collective-permute-start | bytes 442376 | tf_op jit(solution)/shard_map/ppermute | solution.py:13
  14.3 28.4 %collective-permute-start.12 = (bf16[576,128]{1,0:T(8,128)(2,1)S(1)}, bf16[576,128]{1,0:T(8,128)(2,1)S(1)}, u32[]{:S(2)}, u32[]{:S(2)}) collective-permute-start(bf16[576,128]{1,0:T(8,128)(2,1)S(1)} %slice.60), channel_id=1, source_target_pairs={{0,2},{1,3},{2,4},{3,5},{4,6},{5,7},{6,0},{7,1},{8,10},{9,11},{10,... | collective-permute-start | bytes 442376 | tf_op jit(solution)/shard_map/ppermute | solution.py:13
  14.3 26.5 %collective-permute-start.11 = (bf16[576,128]{1,0:T(8,128)(2,1)S(1)}, bf16[576,128]{1,0:T(8,128)(2,1)S(1)}, u32[]{:S(2)}, u32[]{:S(2)}) collective-permute-start(bf16[576,128]{1,0:T(8,128)(2,1)S(1)} %slice.60), channel_id=1, source_target_pairs={{0,3},{1,4},{2,5},{3,6},{4,7},{5,0},{6,1},{7,2},{8,11},{9,12},{10,... | collective-permute-start | bytes 442376 | tf_op jit(solution)/shard_map/ppermute | solution.py:13
  16.9 23.7 %collective-permute-start.10 = (bf16[576,128]{1,0:T(8,128)(2,1)S(1)}, bf16[576,128]{1,0:T(8,128)(2,1)S(1)}, u32[]{:S(2)}, u32[]{:S(2)}) collective-permute-start(bf16[576,128]{1,0:T(8,128)(2,1)S(1)} %slice.60), channel_id=1, source_target_pairs={{0,4},{1,5},{2,6},{3,7},{4,0},{5,1},{6,2},{7,3},{8,12},{9,13},{10,... | collective-permute-start | bytes 442376 | tf_op jit(solution)/shard_map/ppermute | solution.py:13
  35.7 78.8 %collective-permute-start.6 = (bf16[576,256]{1,0:T(8,128)(2,1)S(1)}, bf16[576,256]{1,0:T(8,128)(2,1)S(1)}, u32[]{:S(2)}, u32[]{:S(2)}) collective-permute-start(bf16[576,256]{1,0:T(8,128)(2,1)S(1)} %slice.59), channel_id=1, source_target_pairs={{0,1},{1,2},{2,3},{3,4},{4,5},{5,6},{6,7},{7,0},{8,9},{9,10},{10,1... | collective-permute-start | bytes 884744 | tf_op jit(solution)/shard_map/ppermute | solution.py:13
  40.6 73.8 %collective-permute-start.5 = (bf16[576,256]{1,0:T(8,128)(2,1)S(1)}, bf16[576,256]{1,0:T(8,128)(2,1)S(1)}, u32[]{:S(2)}, u32[]{:S(2)}) collective-permute-start(bf16[576,256]{1,0:T(8,128)(2,1)S(1)} %slice.59), channel_id=1, source_target_pairs={{0,2},{1,3},{2,4},{3,5},{4,6},{5,7},{6,0},{7,1},{8,10},{9,11},{10,... | collective-permute-start | bytes 884744 | tf_op jit(solution)/shard_map/ppermute | solution.py:13
  40.8 73.7 %collective-permute-start.4 = (bf16[576,256]{1,0:T(8,128)(2,1)S(1)}, bf16[576,256]{1,0:T(8,128)(2,1)S(1)}, u32[]{:S(2)}, u32[]{:S(2)}) collective-permute-start(bf16[576,256]{1,0:T(8,128)(2,1)S(1)} %slice.59), channel_id=1, source_target_pairs={{0,3},{1,4},{2,5},{3,6},{4,7},{5,0},{6,1},{7,2},{8,11},{9,12},{10,... | collective-permute-start | bytes 884744 | tf_op jit(solution)/shard_map/ppermute | solution.py:13
  42.7 59.1 %collective-permute-start.1 = (bf16[576,256]{1,0:T(8,128)(2,1)S(1)}, bf16[576,256]{1,0:T(8,128)(2,1)S(1)}, u32[]{:S(2)}, u32[]{:S(2)}) collective-permute-start(bf16[576,256]{1,0:T(8,128)(2,1)S(1)} %slice.59), channel_id=1, source_target_pairs={{0,6},{1,7},{2,0},{3,1},{4,2},{5,3},{6,4},{7,5},{8,14},{9,15},{10,... | collective-permute-start | bytes 884744 | tf_op jit(solution)/shard_map/ppermute | solution.py:13
  101.8 12.6 %collective-permute-start.3 = (bf16[576,256]{1,0:T(8,128)(2,1)S(1)}, bf16[576,256]{1,0:T(8,128)(2,1)S(1)}, u32[]{:S(2)}, u32[]{:S(2)}) collective-permute-start(bf16[576,256]{1,0:T(8,128)(2,1)S(1)} %slice.59), channel_id=1, source_target_pairs={{0,4},{1,5},{2,6},{3,7},{4,0},{5,1},{6,2},{7,3},{8,12},{9,13},{10,... | collective-permute-start | bytes 884744 | tf_op jit(solution)/shard_map/ppermute | solution.py:13
  126.3 15.0 %collective-permute-start.20 = (f32[2,256]{1,0:T(2,128)S(1)}, f32[2,256]{1,0:T(2,128)S(1)}, u32[]{:S(2)}, u32[]{:S(2)}) collective-permute-start(f32[2,256]{1,0:T(2,128)S(1)} %pad_maximum_fusion.6), channel_id=1, source_target_pairs={{0,1},{1,2},{2,3},{3,4},{4,5},{5,6},{6,7},{7,0},{8,9},{9,10},{10,1... | collective-permute-start | bytes 6152 | tf_op jit(solution)/shard_map/ppermute | solution.py:13
  126.4 18.8 %collective-permute-start.19 = (f32[2,256]{1,0:T(2,128)S(1)}, f32[2,256]{1,0:T(2,128)S(1)}, u32[]{:S(2)}, u32[]{:S(2)}) collective-permute-start(f32[2,256]{1,0:T(2,128)S(1)} %pad_maximum_fusion.6), channel_id=1, source_target_pairs={{0,2},{1,3},{2,4},{3,5},{4,6},{5,7},{6,0},{7,1},{8,10},{9,11},{10,... | collective-permute-start | bytes 6152 | tf_op jit(solution)/shard_map/ppermute | solution.py:13
  126.5 21.4 %collective-permute-start.18 = (f32[2,256]{1,0:T(2,128)S(1)}, f32[2,256]{1,0:T(2,128)S(1)}, u32[]{:S(2)}, u32[]{:S(2)}) collective-permute-start(f32[2,256]{1,0:T(2,128)S(1)} %pad_maximum_fusion.6), channel_id=1, source_target_pairs={{0,3},{1,4},{2,5},{3,6},{4,7},{5,0},{6,1},{7,2},{8,11},{9,12},{10,... | collective-permute-start | bytes 6152 | tf_op jit(solution)/shard_map/ppermute | solution.py:13
  196.4 13.6 %collective-permute-start.32 = (f32[2,296,384]{2,1,0:T(8,128)}, f32[2,296,384]{2,1,0:T(8,128)}, u32[]{:S(2)}, u32[]{:S(2)}) collective-permute-start(f32[2,296,384]{2,1,0:T(8,128)} %dynamic-slice_bitcast_fusion), channel_id=1, source_target_pairs={{0,3},{1,0},{2,1},{3,2},{4,7},{5,4},{6,5},{7,6},{8,11},{9,8},{10,9... | collective-permute-start | bytes 2727944 | tf_op jit(solution)/shard_map/ppermute | solution.py:59
  202.7 13.5 %collective-permute-start.28 = (f32[2,288,384]{2,1,0:T(8,128)}, f32[2,288,384]{2,1,0:T(8,128)}, u32[]{:S(2)}, u32[]{:S(2)}) collective-permute-start(f32[2,288,384]{2,1,0:T(8,128)} %dynamic-slice_bitcast_fusion.1), channel_id=1, source_target_pairs={{0,1},{1,2},{2,3},{3,0},{4,5},{5,6},{6,7},{7,4},{8,9},{9,10},{10,1... | collective-permute-start | bytes 2654216 | tf_op jit(solution)/shard_map/ppermute | solution.py:58
  212.5 20.7 %collective-permute-start.33 = (f32[2,296,384]{2,1,0:T(8,128)}, f32[2,296,384]{2,1,0:T(8,128)}, u32[]{:S(2)}, u32[]{:S(2)}) collective-permute-start(f32[2,296,384]{2,1,0:T(8,128)} %bitcast_add_fusion), channel_id=1, source_target_pairs={{0,3},{1,0},{2,1},{3,2},{4,7},{5,4},{6,5},{7,6},{8,11},{9,8},{10,9... | collective-permute-start | bytes 2727944 | tf_op jit(solution)/shard_map/ppermute | solution.py:59
  218.3 21.4 %collective-permute-start.29 = (f32[2,288,384]{2,1,0:T(8,128)}, f32[2,288,384]{2,1,0:T(8,128)}, u32[]{:S(2)}, u32[]{:S(2)}) collective-permute-start(f32[2,288,384]{2,1,0:T(8,128)} %bitcast_add_fusion.3), channel_id=1, source_target_pairs={{0,1},{1,2},{2,3},{3,0},{4,5},{5,6},{6,7},{7,4},{8,9},{9,10},{10,1... | collective-permute-start | bytes 2654216 | tf_op jit(solution)/shard_map/ppermute | solution.py:58
  235.8 21.5 %collective-permute-start.34 = (f32[2,296,384]{2,1,0:T(8,128)}, f32[2,296,384]{2,1,0:T(8,128)}, u32[]{:S(2)}, u32[]{:S(2)}) collective-permute-start(f32[2,296,384]{2,1,0:T(8,128)} %bitcast_add_fusion.1), channel_id=1, source_target_pairs={{0,3},{1,0},{2,1},{3,2},{4,7},{5,4},{6,5},{7,6},{8,11},{9,8},{10,9... | collective-permute-start | bytes 2727944 | tf_op jit(solution)/shard_map/ppermute | solution.py:59
  241.9 22.3 %collective-permute-start.30 = (f32[2,288,384]{2,1,0:T(8,128)}, f32[2,288,384]{2,1,0:T(8,128)}, u32[]{:S(2)}, u32[]{:S(2)}) collective-permute-start(f32[2,288,384]{2,1,0:T(8,128)} %bitcast_add_fusion.4), channel_id=1, source_target_pairs={{0,1},{1,2},{2,3},{3,0},{4,5},{5,6},{6,7},{7,4},{8,9},{9,10},{10,1... | collective-permute-start | bytes 2654216 | tf_op jit(solution)/shard_map/ppermute | solution.py:58
  260.6 24.3 %collective-permute-start.35 = (f32[296,384]{1,0:T(8,128)}, f32[296,384]{1,0:T(8,128)}, u32[]{:S(2)}, u32[]{:S(2)}) collective-permute-start(f32[296,384]{1,0:T(8,128)} %dynamic-slice_bitcast_fusion.2), channel_id=1, source_target_pairs={{0,4},{1,5},{2,6},{3,7},{4,0},{5,1},{6,2},{7,3},{8,12},{9,13},{10,... | collective-permute-start | bytes 1363976 | tf_op jit(solution)/shard_map/ppermute | solution.py:66
  265.6 54.0 %collective-permute-start.31 = (f32[288,384]{1,0:T(8,128)S(1)}, f32[288,384]{1,0:T(8,128)S(1)}, u32[]{:S(2)}, u32[]{:S(2)}) collective-permute-start(f32[288,384]{1,0:T(8,128)S(1)} %dynamic-slice_bitcast_fusion.3), channel_id=1, source_target_pairs={{0,4},{1,5},{2,6},{3,7},{4,0},{5,1},{6,2},{7,3},{8,12},{9,13},{10,... | collective-permute-start | bytes 1327112 | tf_op jit(solution)/shard_map/ppermute | solution.py:63
  292.8 28.0 %collective-permute-start.38 = (f32[576]{0:T(1024)S(1)}, f32[576]{0:T(1024)S(1)}, u32[]{:S(2)}, u32[]{:S(2)}) collective-permute-start(f32[576]{0:T(1024)S(1)} %add.220), channel_id=1, source_target_pairs={{0,64},{16,80},{32,96},{48,112},{64,0},{80,16},{96,32},{112,48},{1... | collective-permute-start | bytes 6920 | tf_op jit(solution)/shard_map/ppermute | solution.py:22
  325.0 18.4 %collective-permute-start.40 = (f32[576]{0:T(1024)S(1)}, f32[576]{0:T(1024)S(1)}, u32[]{:S(2)}, u32[]{:S(2)}) collective-permute-start(f32[576]{0:T(1024)S(1)} %add.222), channel_id=1, source_target_pairs={{0,8},{8,0},{1,9},{9,1},{2,10},{10,2},{3,11},{11,3},{4,12},{12,4},... | collective-permute-start | bytes 6920 | tf_op jit(solution)/shard_map/ppermute | solution.py:22
  (42 other events, 381.3 us)
Sparse Core Ops, SparseCore 0:
  177.4 159.3 reduce-scatter.1

commit v4 on v2

--- a/solution.py
+++ b/solution.py
@@ -28,9 +28,8 @@
     total = jnp.sum(jnp.exp(logits - top[:, None]), axis=1)
     b = 1
     while b < n:
-        perm = [(c, c ^ b) for c in range(n)]
-        other_top = lax.ppermute(top, axis, perm)
-        other_total = lax.ppermute(total, axis, perm)
+        other = lax.ppermute(jnp.stack([top, total]), axis, [(c, c ^ b) for c in range(n)])
+        other_top, other_total = other[0], other[1]
         new_top = jnp.maximum(top, other_top)
         total = total * jnp.exp(top - new_top) + other_total * jnp.exp(other_top - new_top)
         top = new_top
@@ -59,14 +58,13 @@
         recv_b = lax.ppermute(send_b, axis, perm_b)
     sum_f = lax.dynamic_index_in_dim(fwd, lo, 1, keepdims=False) + recv_f
     sum_b = lax.dynamic_index_in_dim(bwd, lo, 1, keepdims=False) + recv_b
+    both = jnp.concatenate([sum_f, sum_b], axis=1)
+    if n_hi == 1:
+        return both[0]
     perm_h = [(a * n_lo + l, (n_hi - 1 - a) * n_lo + l) for a in range(n_hi) for l in range(n_lo)]
-    out_f = lax.dynamic_index_in_dim(sum_f, h, 0, keepdims=False) + lax.ppermute(
-        lax.dynamic_index_in_dim(sum_f, n_hi - 1 - h, 0, keepdims=False), axis, perm_h
+    return lax.dynamic_index_in_dim(both, h, 0, keepdims=False) + lax.ppermute(
+        lax.dynamic_index_in_dim(both, n_hi - 1 - h, 0, keepdims=False), axis, perm_h
     )
-    out_b = lax.dynamic_index_in_dim(sum_b, h, 0, keepdims=False) + lax.ppermute(
-        lax.dynamic_index_in_dim(sum_b, n_hi - 1 - h, 0, keepdims=False), axis, perm_h
-    )
-    return jnp.concatenate([out_f, out_b], axis=0)
 
 
 def shards(hidden_input_state, norm_gain, head_weight, target_ids):

time: 273 us -> 286 us (1.048)
  starting transfers between devices: 46.4 us -> 58.3 us
  waiting for transfers between devices: 145 us -> 150 us
    ppermute x3, waiting for transfers between devices: 34 us -> 4.91 us  [two_stage_reduce_scatter(): recv_b = lax.ppermute(send_b, axis, perm_b)]
    ppermute x3, waiting for transfers between devices: 0.99 us -> 28.6 us  [two_stage_reduce_scatter(): recv_f = lax.ppermute(send_f, axis, perm_f)]
    ppermute x3, starting transfers between devices: 3 us -> 9.92 us  [two_stage_reduce_scatter(): recv_b = lax.ppermute(send_b, axis, perm_b)]
    ppermute x5, starting transfers between devices: 10.7 us -> 17.3 us  [butterfly_sum(): x = x + lax.ppermute(x, axis, [(c, c ^ b) for c in range(n)])]
    ppermute x8 -> x4, waiting for transfers between devices: 65 us -> 70.2 us  [the longest x1 66.5 us: two_stage_reduce_scatter(): lax.ppermute(lax.dynamic_index_in_dim(both, n_hi - 1 - h, 0, keepdims=Fal...]
    unnamed x43 -> x47, local copies, waits for them, and re-layouts: 11.5 us -> 10.4 us
    ppermute x8 -> x4, starting transfers between devices: 19.9 us -> 19 us  [the longest x3 16.2 us: butterfly_softmax_stats(): lax.ppermute(jnp.stack([top, total]), axis, [(c, c ^ b) for c in range(n)])]
  transfers between devices with their start and end apart: 27 -> 23, of which waited for: 20 -> 18; matrix products, arithmetic and copies ran while one was open for 13% -> 11% of each run, Pallas kernels for 0% -> 0%
where the time goes in v4:
time: 286 us; the launch traced here: 285 us
  waiting for transfers between devices  150 us (52%)
  starting transfers between devices  58.3 us (20%)
  other arithmetic  23.2 us (8%)
  matrix products  23.2 us (8%)
  local copies, waits for them, and re-layouts  16.5 us (6%)
  between operations  14.5 us (5%)
    ppermute x1, waiting for transfers between devices, two_stage_reduce_scatter(): lax.ppermute(lax.dynamic_index_in_dim(both, n_hi - 1 - h, 0, keepdims=Fal...  66.5 us
    ppermute x7, waiting for transfers between devices, shift_gather(): got.append(lax.ppermute(x, axis, [(c, (c + k) % n) for c in range(n)]))  35.9 us
    ppermute x3, waiting for transfers between devices, two_stage_reduce_scatter(): recv_f = lax.ppermute(send_f, axis, perm_f)  28.6 us
    ppermute x5, starting transfers between devices, butterfly_sum(): x = x + lax.ppermute(x, axis, [(c, c ^ b) for c in range(n)])  17.3 us
    ppermute x3, starting transfers between devices, butterfly_softmax_stats(): lax.ppermute(jnp.stack([top, total]), axis, [(c, c ^ b) for c in range(n)])  16.2 us
    ppermute x7, starting transfers between devices, shift_gather(): got.append(lax.ppermute(x, axis, [(c, (c + k) % n) for c in range(n)]))  11.3 us
    unnamed x47, local copies, waits for them, and re-layouts  10.4 us
    ppermute x5, waiting for transfers between devices, butterfly_sum(): x = x + lax.ppermute(x, axis, [(c, c ^ b) for c in range(n)])  10.3 us
  transfers between devices with their start and end apart: 23, of which 18 were waited for; matrix products, arithmetic and copies ran while one was open for 11% of the time, Pallas kernels for 0%

profile of v4, /device:TPU:1, one launch (start us, length us, event | category | flops | bytes accessed | tf_op | source)
XLA Modules:
  0.0 285.5 jit_solution(5689229608543928118)
XLA Ops:
  7.2 6.1 %collective-permute-start = (bf16[576,384]{1,0:T(8,128)(2,1)}, bf16[576,384]{1,0:T(8,128)(2,1)S(1)}, u32[]{:S(2)}, u32[]{:S(2)}) collective-permute-start(bf16[576,384]{1,0:T(8,128)(2,1)} %bitcast.81), channel_id=1, source_target_pairs={{0,7},{1,0},{2,1},{3,2},{4,3},{5,4},{6,5},{7,6},{8,15},{9,8},{10,9... | collective-permute-start | bytes 1327112 | tf_op jit(solution)/shard_map/ppermute | solution.py:13
  18.3 10.5 %collective-permute-done = bf16[576,384]{1,0:T(8,128)(2,1)S(1)} collective-permute-done((bf16[576,384]{1,0:T(8,128)(2,1)}, bf16[576,384]{1,0:T(8,128)(2,1)S(1)}, u32[]{:S(2)}, u32[]{:S(2)}) %collective-permute-start) | collective-permute-done | bytes 442400 | tf_op jit(solution)/shard_map/ppermute | solution.py:13
  28.8 15.9 %collective-permute-done.1 = bf16[576,384]{1,0:T(8,128)(2,1)S(1)} collective-permute-done((bf16[576,384]{1,0:T(8,128)(2,1)}, bf16[576,384]{1,0:T(8,128)(2,1)S(1)}, u32[]{:S(2)}, u32[]{:S(2)}) %collective-permute-start.1) | collective-permute-done | bytes 442400 | tf_op jit(solution)/shard_map/ppermute | solution.py:13
  45.1 5.6 %collective-permute-done.2 = bf16[576,384]{1,0:T(8,128)(2,1)S(1)} collective-permute-done((bf16[576,384]{1,0:T(8,128)(2,1)}, bf16[576,384]{1,0:T(8,128)(2,1)S(1)}, u32[]{:S(2)}, u32[]{:S(2)}) %collective-permute-start.2) | collective-permute-done | bytes 442400 | tf_op jit(solution)/shard_map/ppermute | solution.py:13
  50.7 3.9 %collective-permute-done.3 = bf16[576,384]{1,0:T(8,128)(2,1)S(1)} collective-permute-done((bf16[576,384]{1,0:T(8,128)(2,1)}, bf16[576,384]{1,0:T(8,128)(2,1)S(1)}, u32[]{:S(2)}, u32[]{:S(2)}) %collective-permute-start.3) | collective-permute-done | bytes 442400 | tf_op jit(solution)/shard_map/ppermute | solution.py:13
  57.6 2.7 copy-done.3
  62.3 3.9 %fusion.22 = (f32[384]{0:T(512)S(1)}, f32[384,1024]{1,0:T(8,128)S(1)}) fusion(bf16[4608,384]{1,0:T(8,128)(2,1)S(1)} %fusion.3, bf16[4608,1024]{1,0:T(8,128)(2,1)S(1)} %bitcast.78), kind=kOutput, calls=%fused_computation.81 | convolution fusion | flops 3624271360 | bytes 14550528 | tf_op jit(solution)/shard_map/dot_general | solution.py:81
  72.4 11.7 %collective-permute-start.8 = (f32[2,384]{1,0:T(2,128)}, f32[2,384]{1,0:T(2,128)}, u32[]{:S(2)}, u32[]{:S(2)}) collective-permute-start(f32[2,384]{1,0:T(2,128)} %pad_maximum_fusion.3), channel_id=1, source_target_pairs={{0,2},{1,3},{2,0},{3,1},{4,6},{5,7},{6,4},{7,5},{8,10},{9,11},{10,... | collective-permute-start | bytes 9224 | tf_op jit(solution)/shard_map/ppermute | solution.py:31
  86.2 2.7 collective-permute-start.9
  93.7 9.1 %fusion.23 = f32[4608,1024]{1,0:T(8,128)} fusion(bf16[4608,384]{1,0:T(8,128)(2,1)S(1)} %fusion.3, bf16[384,1024]{1,0:T(8,128)(2,1)S(1)} %subtract_convert_fusion), kind=kOutput, calls=%fused_computation.82 | convolution fusion | flops 3623878656 | bytes 23199744 | tf_op jit(solution)/shard_map/dot_general | solution.py:93
  103.9 10.2 %fusion.1 = (f32[384]{0:T(512)S(1)}, f32[8,576]{1,0:T(8,128)S(1)}, f32[8,384,576]{1,2,0:T(8,128)}) fusion(f32[8,576]{1,0:T(8,128)S(1)} %mul.159, f32[384]{0:T(512)S(1)} %add_rsqrt_fusion, bf16[16,576,384]{2,1,0:T(8,128)(2,1)} %copy-done.3, s32[]{:T(128)S(6)} %select_n.72, bf16[8,576,1024]{2,1,0:T(8,128)(2,1)} %bitcast.76, bf16[384,1024]{1,0:T(8,128)(2,1)S(1)} %copy-done.8), kind=kOutput, calls=%fused_computation.3 | convolution fusion | flops 3636259840 | bytes 20880388 | tf_op jit(solution)/shard_map/dot_general | solution.py:98
  122.3 3.1 %collective-permute-start.13 = (f32[2,296,384]{2,1,0:T(8,128)}, f32[2,296,384]{2,1,0:T(8,128)}, u32[]{:S(2)}, u32[]{:S(2)}) collective-permute-start(f32[2,296,384]{2,1,0:T(8,128)} %dynamic-slice_bitcast_fusion), channel_id=1, source_target_pairs={{0,3},{1,0},{2,1},{3,2},{4,7},{5,4},{6,5},{7,6},{8,11},{9,8},{10,9... | collective-permute-start | bytes 2727944 | tf_op jit(solution)/shard_map/ppermute | solution.py:58
  125.4 10.4 %collective-permute-done.10 = f32[2,288,384]{2,1,0:T(8,128)} collective-permute-done((f32[2,288,384]{2,1,0:T(8,128)}, f32[2,288,384]{2,1,0:T(8,128)}, u32[]{:S(2)}, u32[]{:S(2)}) %collective-permute-start.10) | collective-permute-done | bytes 884768 | tf_op jit(solution)/shard_map/ppermute | solution.py:57
  141.6 3.4 %collective-permute-start.14 = (f32[2,296,384]{2,1,0:T(8,128)}, f32[2,296,384]{2,1,0:T(8,128)}, u32[]{:S(2)}, u32[]{:S(2)}) collective-permute-start(f32[2,296,384]{2,1,0:T(8,128)} %bitcast_add_fusion), channel_id=1, source_target_pairs={{0,3},{1,0},{2,1},{3,2},{4,7},{5,4},{6,5},{7,6},{8,11},{9,8},{10,9... | collective-permute-start | bytes 2727944 | tf_op jit(solution)/shard_map/ppermute | solution.py:58
  145.0 9.4 %collective-permute-done.11 = f32[2,288,384]{2,1,0:T(8,128)} collective-permute-done((f32[2,288,384]{2,1,0:T(8,128)}, f32[2,288,384]{2,1,0:T(8,128)}, u32[]{:S(2)}, u32[]{:S(2)}) %collective-permute-start.11) | collective-permute-done | bytes 884768 | tf_op jit(solution)/shard_map/ppermute | solution.py:57
  160.3 3.4 %collective-permute-start.15 = (f32[2,296,384]{2,1,0:T(8,128)}, f32[2,296,384]{2,1,0:T(8,128)}, u32[]{:S(2)}, u32[]{:S(2)}) collective-permute-start(f32[2,296,384]{2,1,0:T(8,128)} %bitcast_add_fusion.1), channel_id=1, source_target_pairs={{0,3},{1,0},{2,1},{3,2},{4,7},{5,4},{6,5},{7,6},{8,11},{9,8},{10,9... | collective-permute-start | bytes 2727944 | tf_op jit(solution)/shard_map/ppermute | solution.py:58
  163.7 8.8 %collective-permute-done.12 = f32[2,288,384]{2,1,0:T(8,128)} collective-permute-done((f32[2,288,384]{2,1,0:T(8,128)}, f32[2,288,384]{2,1,0:T(8,128)}, u32[]{:S(2)}, u32[]{:S(2)}) %collective-permute-start.12) | collective-permute-done | bytes 884768 | tf_op jit(solution)/shard_map/ppermute | solution.py:57
  173.7 2.6 collective-permute-done.15
  178.0 2.8 collective-permute-start.16
  180.9 66.5 %collective-permute-done.16 = f32[584,384]{1,0:T(8,128)S(1)} collective-permute-done((f32[584,384]{1,0:T(8,128)S(1)}, f32[584,384]{1,0:T(8,128)S(1)}, u32[]{:S(2)}, u32[]{:S(2)}) %collective-permute-start.16) | collective-permute-done | bytes 897056 | tf_op jit(solution)/shard_map/ppermute | solution.py:65
  248.6 2.9 %collective-permute-done.17 = f32[576]{0:T(1024)S(1)} collective-permute-done((f32[576]{0:T(1024)S(1)}, f32[576]{0:T(1024)S(1)}, u32[]{:S(2)}, u32[]{:S(2)}) %collective-permute-start.17) | collective-permute-done | bytes 2336 | tf_op jit(solution)/shard_map/ppermute | solution.py:22
  251.5 3.6 %collective-permute-done.18 = f32[576]{0:T(1024)S(1)} collective-permute-done((f32[576]{0:T(1024)S(1)}, f32[576]{0:T(1024)S(1)}, u32[]{:S(2)}, u32[]{:S(2)}) %collective-permute-start.18) | collective-permute-done | bytes 2336 | tf_op jit(solution)/shard_map/ppermute | solution.py:22
  255.1 4.2 %collective-permute-start.19 = (f32[576]{0:T(1024)S(1)}, f32[576]{0:T(1024)S(1)}, u32[]{:S(2)}, u32[]{:S(2)}) collective-permute-start(f32[576]{0:T(1024)S(1)} %add.223), channel_id=1, source_target_pairs={{0,64},{16,80},{32,96},{48,112},{64,0},{80,16},{96,32},{112,48},{1... | collective-permute-start | bytes 6920 | tf_op jit(solution)/shard_map/ppermute | solution.py:22
  264.0 12.9 %collective-permute-start.21 = (f32[576]{0:T(1024)S(1)}, f32[576]{0:T(1024)S(1)}, u32[]{:S(2)}, u32[]{:S(2)}) collective-permute-start(f32[576]{0:T(1024)S(1)} %add.225), channel_id=1, source_target_pairs={{0,8},{8,0},{1,9},{9,1},{2,10},{10,2},{3,11},{11,3},{4,12},{12,4},... | collective-permute-start | bytes 6920 | tf_op jit(solution)/shard_map/ppermute | solution.py:22
  (118 shorter events, 54.7 us)
Async XLA Ops:
  7.2 271.5 %reduce-scatter.2.cloned.1.call-start = ((), (), s32[]{:S(2)}) async-start(), calls=%async_computation.1 | async-start | bytes 19464192 | tf_op jit(solution)/shard_map/reduce_scatter | solution.py:96
  7.2 21.6 %collective-permute-start = (bf16[576,384]{1,0:T(8,128)(2,1)}, bf16[576,384]{1,0:T(8,128)(2,1)S(1)}, u32[]{:S(2)}, u32[]{:S(2)}) collective-permute-start(bf16[576,384]{1,0:T(8,128)(2,1)} %bitcast.81), channel_id=1, source_target_pairs={{0,7},{1,0},{2,1},{3,2},{4,3},{5,4},{6,5},{7,6},{8,15},{9,8},{10,9... | collective-permute-start | bytes 1327112 | tf_op jit(solution)/shard_map/ppermute | solution.py:13
  13.3 31.4 %collective-permute-start.1 = (bf16[576,384]{1,0:T(8,128)(2,1)}, bf16[576,384]{1,0:T(8,128)(2,1)S(1)}, u32[]{:S(2)}, u32[]{:S(2)}) collective-permute-start(bf16[576,384]{1,0:T(8,128)(2,1)} %bitcast.82), channel_id=1, source_target_pairs={{0,6},{1,7},{2,0},{3,1},{4,2},{5,3},{6,4},{7,5},{8,14},{9,15},{10,... | collective-permute-start | bytes 1327112 | tf_op jit(solution)/shard_map/ppermute | solution.py:13
  13.7 41.2 %collective-permute-start.6 = (bf16[576,384]{1,0:T(8,128)(2,1)}, bf16[576,384]{1,0:T(8,128)(2,1)S(1)}, u32[]{:S(2)}, u32[]{:S(2)}) collective-permute-start(bf16[576,384]{1,0:T(8,128)(2,1)} %bitcast.83), channel_id=1, source_target_pairs={{0,1},{1,2},{2,3},{3,4},{4,5},{5,6},{6,7},{7,0},{8,9},{9,10},{10,1... | collective-permute-start | bytes 1327112 | tf_op jit(solution)/shard_map/ppermute | solution.py:13
  14.4 40.4 %collective-permute-start.5 = (bf16[576,384]{1,0:T(8,128)(2,1)}, bf16[576,384]{1,0:T(8,128)(2,1)S(1)}, u32[]{:S(2)}, u32[]{:S(2)}) collective-permute-start(bf16[576,384]{1,0:T(8,128)(2,1)} %bitcast.84), channel_id=1, source_target_pairs={{0,2},{1,3},{2,4},{3,5},{4,6},{5,7},{6,0},{7,1},{8,10},{9,11},{10,... | collective-permute-start | bytes 1327112 | tf_op jit(solution)/shard_map/ppermute | solution.py:13
  16.3 38.4 %collective-permute-start.4 = (bf16[576,384]{1,0:T(8,128)(2,1)}, bf16[576,384]{1,0:T(8,128)(2,1)S(1)}, u32[]{:S(2)}, u32[]{:S(2)}) collective-permute-start(bf16[576,384]{1,0:T(8,128)(2,1)} %bitcast.85), channel_id=1, source_target_pairs={{0,3},{1,4},{2,5},{3,6},{4,7},{5,0},{6,1},{7,2},{8,11},{9,12},{10,... | collective-permute-start | bytes 1327112 | tf_op jit(solution)/shard_map/ppermute | solution.py:13
  28.8 21.9 %collective-permute-start.2 = (bf16[576,384]{1,0:T(8,128)(2,1)}, bf16[576,384]{1,0:T(8,128)(2,1)S(1)}, u32[]{:S(2)}, u32[]{:S(2)}) collective-permute-start(bf16[576,384]{1,0:T(8,128)(2,1)} %bitcast.86), channel_id=1, source_target_pairs={{0,5},{1,6},{2,7},{3,0},{4,1},{5,2},{6,3},{7,4},{8,13},{9,14},{10,... | collective-permute-start | bytes 1327112 | tf_op jit(solution)/shard_map/ppermute | solution.py:13
  44.8 9.8 %collective-permute-start.3 = (bf16[576,384]{1,0:T(8,128)(2,1)}, bf16[576,384]{1,0:T(8,128)(2,1)S(1)}, u32[]{:S(2)}, u32[]{:S(2)}) collective-permute-start(bf16[576,384]{1,0:T(8,128)(2,1)} %bitcast.87), channel_id=1, source_target_pairs={{0,4},{1,5},{2,6},{3,7},{4,0},{5,1},{6,2},{7,3},{8,12},{9,13},{10,... | collective-permute-start | bytes 1327112 | tf_op jit(solution)/shard_map/ppermute | solution.py:13
  67.8 2.9 %collective-permute-start.7 = (f32[2,384]{1,0:T(2,128)S(1)}, f32[2,384]{1,0:T(2,128)S(1)}, u32[]{:S(2)}, u32[]{:S(2)}) collective-permute-start(f32[2,384]{1,0:T(2,128)S(1)} %pad_maximum_fusion.2), channel_id=1, source_target_pairs={{0,1},{1,0},{2,3},{3,2},{4,5},{5,4},{6,7},{7,6},{8,9},{9,8},{10,11... | collective-permute-start | bytes 9224 | tf_op jit(solution)/shard_map/ppermute | solution.py:31
  72.4 13.0 %collective-permute-start.8 = (f32[2,384]{1,0:T(2,128)}, f32[2,384]{1,0:T(2,128)}, u32[]{:S(2)}, u32[]{:S(2)}) collective-permute-start(f32[2,384]{1,0:T(2,128)} %pad_maximum_fusion.3), channel_id=1, source_target_pairs={{0,2},{1,3},{2,0},{3,1},{4,6},{5,7},{6,4},{7,5},{8,10},{9,11},{10,... | collective-permute-start | bytes 9224 | tf_op jit(solution)/shard_map/ppermute | solution.py:31
  86.2 4.0 %collective-permute-start.9 = (f32[2,384]{1,0:T(2,128)S(1)}, f32[2,384]{1,0:T(2,128)S(1)}, u32[]{:S(2)}, u32[]{:S(2)}) collective-permute-start(f32[2,384]{1,0:T(2,128)S(1)} %pad_maximum_fusion.4), channel_id=1, source_target_pairs={{0,4},{1,5},{2,6},{3,7},{4,0},{5,1},{6,2},{7,3},{8,12},{9,13},{10,... | collective-permute-start | bytes 9224 | tf_op jit(solution)/shard_map/ppermute | solution.py:31
  118.1 17.7 %collective-permute-start.10 = (f32[2,288,384]{2,1,0:T(8,128)}, f32[2,288,384]{2,1,0:T(8,128)}, u32[]{:S(2)}, u32[]{:S(2)}) collective-permute-start(f32[2,288,384]{2,1,0:T(8,128)} %dynamic-slice_bitcast_fusion.1), channel_id=1, source_target_pairs={{0,1},{1,2},{2,3},{3,0},{4,5},{5,6},{6,7},{7,4},{8,9},{9,10},{10,1... | collective-permute-start | bytes 2654216 | tf_op jit(solution)/shard_map/ppermute | solution.py:57
  122.3 16.8 %collective-permute-start.13 = (f32[2,296,384]{2,1,0:T(8,128)}, f32[2,296,384]{2,1,0:T(8,128)}, u32[]{:S(2)}, u32[]{:S(2)}) collective-permute-start(f32[2,296,384]{2,1,0:T(8,128)} %dynamic-slice_bitcast_fusion), channel_id=1, source_target_pairs={{0,3},{1,0},{2,1},{3,2},{4,7},{5,4},{6,5},{7,6},{8,11},{9,8},{10,9... | collective-permute-start | bytes 2727944 | tf_op jit(solution)/shard_map/ppermute | solution.py:58
  138.0 16.3 %collective-permute-start.11 = (f32[2,288,384]{2,1,0:T(8,128)}, f32[2,288,384]{2,1,0:T(8,128)}, u32[]{:S(2)}, u32[]{:S(2)}) collective-permute-start(f32[2,288,384]{2,1,0:T(8,128)} %bitcast_add_fusion.3), channel_id=1, source_target_pairs={{0,1},{1,2},{2,3},{3,0},{4,5},{5,6},{6,7},{7,4},{8,9},{9,10},{10,1... | collective-permute-start | bytes 2654216 | tf_op jit(solution)/shard_map/ppermute | solution.py:57
  141.6 16.2 %collective-permute-start.14 = (f32[2,296,384]{2,1,0:T(8,128)}, f32[2,296,384]{2,1,0:T(8,128)}, u32[]{:S(2)}, u32[]{:S(2)}) collective-permute-start(f32[2,296,384]{2,1,0:T(8,128)} %bitcast_add_fusion), channel_id=1, source_target_pairs={{0,3},{1,0},{2,1},{3,2},{4,7},{5,4},{6,5},{7,6},{8,11},{9,8},{10,9... | collective-permute-start | bytes 2727944 | tf_op jit(solution)/shard_map/ppermute | solution.py:58
  156.5 15.9 %collective-permute-start.12 = (f32[2,288,384]{2,1,0:T(8,128)}, f32[2,288,384]{2,1,0:T(8,128)}, u32[]{:S(2)}, u32[]{:S(2)}) collective-permute-start(f32[2,288,384]{2,1,0:T(8,128)} %bitcast_add_fusion.4), channel_id=1, source_target_pairs={{0,1},{1,2},{2,3},{3,0},{4,5},{5,6},{6,7},{7,4},{8,9},{9,10},{10,1... | collective-permute-start | bytes 2654216 | tf_op jit(solution)/shard_map/ppermute | solution.py:57
  160.3 16.1 %collective-permute-start.15 = (f32[2,296,384]{2,1,0:T(8,128)}, f32[2,296,384]{2,1,0:T(8,128)}, u32[]{:S(2)}, u32[]{:S(2)}) collective-permute-start(f32[2,296,384]{2,1,0:T(8,128)} %bitcast_add_fusion.1), channel_id=1, source_target_pairs={{0,3},{1,0},{2,1},{3,2},{4,7},{5,4},{6,5},{7,6},{8,11},{9,8},{10,9... | collective-permute-start | bytes 2727944 | tf_op jit(solution)/shard_map/ppermute | solution.py:58
  173.7 103.2 %copy-start.6 = (bf16[384,576]{0,1:T(8,128)(2,1)S(1)}, bf16[384,576]{0,1:T(8,128)(2,1)}, u32[]{:S(2)}) copy-start(bf16[384,576]{0,1:T(8,128)(2,1)} %param.4) | copy-start | bytes 1327108
  178.0 69.3 %collective-permute-start.16 = (f32[584,384]{1,0:T(8,128)S(1)}, f32[584,384]{1,0:T(8,128)S(1)}, u32[]{:S(2)}, u32[]{:S(2)}) collective-permute-start(f32[584,384]{1,0:T(8,128)S(1)} %fusion.8), channel_id=1, source_target_pairs={{0,4},{1,5},{2,6},{3,7},{4,0},{5,1},{6,2},{7,3},{8,12},{9,13},{10,... | collective-permute-start | bytes 2691080 | tf_op jit(solution)/shard_map/ppermute | solution.py:65
  248.5 3.0 %collective-permute-start.17 = (f32[576]{0:T(1024)S(1)}, f32[576]{0:T(1024)S(1)}, u32[]{:S(2)}, u32[]{:S(2)}) collective-permute-start(f32[576]{0:T(1024)S(1)} %bitcast.88), channel_id=1, source_target_pairs={{0,16},{16,0},{32,48},{48,32},{64,80},{80,64},{96,112},{112,96},{1... | collective-permute-start | bytes 6920 | tf_op jit(solution)/shard_map/ppermute | solution.py:22
  251.5 3.7 %collective-permute-start.18 = (f32[576]{0:T(1024)S(1)}, f32[576]{0:T(1024)S(1)}, u32[]{:S(2)}, u32[]{:S(2)}) collective-permute-start(f32[576]{0:T(1024)S(1)} %slice_add_fusion), channel_id=1, source_target_pairs={{0,32},{16,48},{32,0},{48,16},{64,96},{80,112},{96,64},{112,80},{1... | collective-permute-start | bytes 6920 | tf_op jit(solution)/shard_map/ppermute | solution.py:22
  255.1 6.4 %collective-permute-start.19 = (f32[576]{0:T(1024)S(1)}, f32[576]{0:T(1024)S(1)}, u32[]{:S(2)}, u32[]{:S(2)}) collective-permute-start(f32[576]{0:T(1024)S(1)} %add.223), channel_id=1, source_target_pairs={{0,64},{16,80},{32,96},{48,112},{64,0},{80,16},{96,32},{112,48},{1... | collective-permute-start | bytes 6920 | tf_op jit(solution)/shard_map/ppermute | solution.py:22
  261.5 2.5 collective-permute-start.20
  264.0 14.1 %collective-permute-start.21 = (f32[576]{0:T(1024)S(1)}, f32[576]{0:T(1024)S(1)}, u32[]{:S(2)}, u32[]{:S(2)}) collective-permute-start(f32[576]{0:T(1024)S(1)} %add.225), channel_id=1, source_target_pairs={{0,8},{8,0},{1,9},{9,1},{2,10},{10,2},{3,11},{11,3},{4,12},{12,4},... | collective-permute-start | bytes 6920 | tf_op jit(solution)/shard_map/ppermute | solution.py:22
  (15 other events, 101.4 us)
Sparse Core Ops, SparseCore 0:
  102.9 153.9 reduce-scatter.1

commit v5 on v4

--- a/solution.py
+++ b/solution.py
@@ -58,13 +58,17 @@
         recv_b = lax.ppermute(send_b, axis, perm_b)
     sum_f = lax.dynamic_index_in_dim(fwd, lo, 1, keepdims=False) + recv_f
     sum_b = lax.dynamic_index_in_dim(bwd, lo, 1, keepdims=False) + recv_b
-    both = jnp.concatenate([sum_f, sum_b], axis=1)
-    if n_hi == 1:
-        return both[0]
     perm_h = [(a * n_lo + l, (n_hi - 1 - a) * n_lo + l) for a in range(n_hi) for l in range(n_lo)]
-    return lax.dynamic_index_in_dim(both, h, 0, keepdims=False) + lax.ppermute(
-        lax.dynamic_index_in_dim(both, n_hi - 1 - h, 0, keepdims=False), axis, perm_h
-    )
+    out = []
+    for part in (sum_f, sum_b):
+        cut = (part.shape[1] // 2) // 8 * 8
+        for piece in (part[:, :cut], part[:, cut:]):
+            mine = lax.dynamic_index_in_dim(piece, h, 0, keepdims=False)
+            if n_hi > 1:
+                other = lax.dynamic_index_in_dim(piece, n_hi - 1 - h, 0, keepdims=False)
+                mine = mine + lax.ppermute(other, axis, perm_h)
+            out.append(mine)
+    return jnp.concatenate(out, axis=0)
 
 
 def shards(hidden_input_state, norm_gain, head_weight, target_ids):

time: 286 us -> 267 us (0.934)
  waiting for transfers between devices: 150 us -> 123 us
  local copies, waits for them, and re-layouts: 16.5 us -> 19.4 us
    ppermute x1 -> x4, waiting for transfers between devices: 66.5 us -> 47.7 us  [two_stage_reduce_scatter(): mine = mine + lax.ppermute(other, axis, perm_h)]
    ppermute x3, waiting for transfers between devices: 28.6 us -> 15.2 us  [two_stage_reduce_scatter(): recv_f = lax.ppermute(send_f, axis, perm_f)]
    ppermute x3, waiting for transfers between devices: 4.91 us -> 16.7 us  [two_stage_reduce_scatter(): recv_b = lax.ppermute(send_b, axis, perm_b)]
    ppermute x1 -> x4, starting transfers between devices: 2.82 us -> 9.28 us  [two_stage_reduce_scatter(): mine = mine + lax.ppermute(other, axis, perm_h)]
    ppermute x5, waiting for transfers between devices: 10.3 us -> 4.4 us  [butterfly_sum(): x = x + lax.ppermute(x, axis, [(c, c ^ b) for c in range(n)])]
    unnamed x47 -> x43, local copies, waits for them, and re-layouts: 10.4 us -> 13.2 us
  transfers between devices with their start and end apart: 23 -> 26, of which waited for: 18 -> 18; matrix products, arithmetic and copies ran while one was open for 11% -> 12% of each run, Pallas kernels for 0% -> 0%
where the time goes in v5:
time: 267 us; the launch traced here: 264 us
  waiting for transfers between devices  123 us (46%)
  starting transfers between devices  60.6 us (23%)
  other arithmetic  24.2 us (9%)
  matrix products  22.2 us (8%)
  local copies, waits for them, and re-layouts  19.4 us (7%)
  between operations  14.5 us (5%)
    ppermute x4, waiting for transfers between devices, two_stage_reduce_scatter(): mine = mine + lax.ppermute(other, axis, perm_h)  47.7 us
    ppermute x7, waiting for transfers between devices, shift_gather(): got.append(lax.ppermute(x, axis, [(c, (c + k) % n) for c in range(n)]))  35.9 us
    ppermute x3, waiting for transfers between devices, two_stage_reduce_scatter(): recv_b = lax.ppermute(send_b, axis, perm_b)  16.7 us
    ppermute x3, starting transfers between devices, butterfly_softmax_stats(): lax.ppermute(jnp.stack([top, total]), axis, [(c, c ^ b) for c in range(n)])  16.2 us
    ppermute x3, waiting for transfers between devices, two_stage_reduce_scatter(): recv_f = lax.ppermute(send_f, axis, perm_f)  15.2 us
    ppermute x5, starting transfers between devices, butterfly_sum(): x = x + lax.ppermute(x, axis, [(c, c ^ b) for c in range(n)])  14.9 us
    unnamed x43, local copies, waits for them, and re-layouts  13.2 us
    ppermute x7, starting transfers between devices, shift_gather(): got.append(lax.ppermute(x, axis, [(c, (c + k) % n) for c in range(n)]))  11.3 us
  transfers between devices with their start and end apart: 26, of which 18 were waited for; matrix products, arithmetic and copies ran while one was open for 12% of the time, Pallas kernels for 0%

profile of v5, /device:TPU:1, one launch (start us, length us, event | category | flops | bytes accessed | tf_op | source)
XLA Modules:
  0.0 264.3 jit_solution(16364785528478832404)
XLA Ops:
  7.2 6.1 %collective-permute-start = (bf16[576,384]{1,0:T(8,128)(2,1)}, bf16[576,384]{1,0:T(8,128)(2,1)S(1)}, u32[]{:S(2)}, u32[]{:S(2)}) collective-permute-start(bf16[576,384]{1,0:T(8,128)(2,1)} %bitcast.91), channel_id=1, source_target_pairs={{0,7},{1,0},{2,1},{3,2},{4,3},{5,4},{6,5},{7,6},{8,15},{9,8},{10,9... | collective-permute-start | bytes 1327112 | tf_op jit(solution)/shard_map/ppermute | solution.py:13
  18.3 10.5 %collective-permute-done = bf16[576,384]{1,0:T(8,128)(2,1)S(1)} collective-permute-done((bf16[576,384]{1,0:T(8,128)(2,1)}, bf16[576,384]{1,0:T(8,128)(2,1)S(1)}, u32[]{:S(2)}, u32[]{:S(2)}) %collective-permute-start) | collective-permute-done | bytes 442400 | tf_op jit(solution)/shard_map/ppermute | solution.py:13
  28.8 15.9 %collective-permute-done.1 = bf16[576,384]{1,0:T(8,128)(2,1)S(1)} collective-permute-done((bf16[576,384]{1,0:T(8,128)(2,1)}, bf16[576,384]{1,0:T(8,128)(2,1)S(1)}, u32[]{:S(2)}, u32[]{:S(2)}) %collective-permute-start.1) | collective-permute-done | bytes 442400 | tf_op jit(solution)/shard_map/ppermute | solution.py:13
  45.1 5.6 %collective-permute-done.2 = bf16[576,384]{1,0:T(8,128)(2,1)S(1)} collective-permute-done((bf16[576,384]{1,0:T(8,128)(2,1)}, bf16[576,384]{1,0:T(8,128)(2,1)S(1)}, u32[]{:S(2)}, u32[]{:S(2)}) %collective-permute-start.2) | collective-permute-done | bytes 442400 | tf_op jit(solution)/shard_map/ppermute | solution.py:13
  50.7 3.9 %collective-permute-done.3 = bf16[576,384]{1,0:T(8,128)(2,1)S(1)} collective-permute-done((bf16[576,384]{1,0:T(8,128)(2,1)}, bf16[576,384]{1,0:T(8,128)(2,1)S(1)}, u32[]{:S(2)}, u32[]{:S(2)}) %collective-permute-start.3) | collective-permute-done | bytes 442400 | tf_op jit(solution)/shard_map/ppermute | solution.py:13
  62.3 3.9 %fusion.19 = (f32[384]{0:T(512)S(1)}, f32[384,1024]{1,0:T(8,128)S(1)}) fusion(bf16[4608,384]{1,0:T(8,128)(2,1)S(1)} %fusion.3, bf16[4608,1024]{1,0:T(8,128)(2,1)S(1)} %bitcast.88), kind=kOutput, calls=%fused_computation.84 | convolution fusion | flops 3624271360 | bytes 14550528 | tf_op jit(solution)/shard_map/dot_general | solution.py:85
  72.5 11.7 %collective-permute-start.8 = (f32[2,384]{1,0:T(2,128)}, f32[2,384]{1,0:T(2,128)}, u32[]{:S(2)}, u32[]{:S(2)}) collective-permute-start(f32[2,384]{1,0:T(2,128)} %pad_maximum_fusion.6), channel_id=1, source_target_pairs={{0,2},{1,3},{2,0},{3,1},{4,6},{5,7},{6,4},{7,5},{8,10},{9,11},{10,... | collective-permute-start | bytes 9224 | tf_op jit(solution)/shard_map/ppermute | solution.py:31
  93.7 9.1 %fusion.20 = f32[4608,1024]{1,0:T(8,128)} fusion(bf16[4608,384]{1,0:T(8,128)(2,1)S(1)} %fusion.3, bf16[384,1024]{1,0:T(8,128)(2,1)S(1)} %subtract_convert_fusion), kind=kOutput, calls=%fused_computation.85 | convolution fusion | flops 3623878656 | bytes 23199744 | tf_op jit(solution)/shard_map/dot_general | solution.py:97
  103.9 9.2 %fusion.1 = (f32[384]{0:T(512)S(1)}, f32[8,576]{1,0:T(8,128)}, f32[8,384,576]{1,2,0:T(8,128)S(1)}) fusion(f32[8,576]{1,0:T(8,128)S(1)} %mul.159, f32[384]{0:T(512)S(1)} %add_rsqrt_fusion, bf16[16,576,384]{2,1,0:T(8,128)(2,1)} %copy-done.3, s32[]{:T(128)S(6)} %select_n.79, bf16[8,576,1024]{2,1,0:T(8,128)(2,1)} %bitcast.86, bf16[384,1024]{1,0:T(8,128)(2,1)S(1)} %copy-done.7), kind=kOutput, calls=%fused_computation.3 | convolution fusion | flops 3636259840 | bytes 20880388 | tf_op jit(solution)/shard_map/dot_general | solution.py:102
  128.3 6.6 %collective-permute-done.10 = f32[2,288,384]{2,1,0:T(8,128)} collective-permute-done((f32[2,288,384]{2,1,0:T(8,128)}, f32[2,288,384]{2,1,0:T(8,128)}, u32[]{:S(2)}, u32[]{:S(2)}) %collective-permute-start.10) | collective-permute-done | bytes 884768 | tf_op jit(solution)/shard_map/ppermute | solution.py:57
  137.2 6.0 %collective-permute-done.15 = f32[2,296,384]{2,1,0:T(8,128)} collective-permute-done((f32[2,296,384]{2,1,0:T(8,128)}, f32[2,296,384]{2,1,0:T(8,128)}, u32[]{:S(2)}, u32[]{:S(2)}) %collective-permute-start.15) | collective-permute-done | bytes 909344 | tf_op jit(solution)/shard_map/ppermute | solution.py:58
  148.4 5.2 %collective-permute-done.11 = f32[2,288,384]{2,1,0:T(8,128)} collective-permute-done((f32[2,288,384]{2,1,0:T(8,128)}, f32[2,288,384]{2,1,0:T(8,128)}, u32[]{:S(2)}, u32[]{:S(2)}) %collective-permute-start.11) | collective-permute-done | bytes 884768 | tf_op jit(solution)/shard_map/ppermute | solution.py:57
  155.7 6.1 %collective-permute-done.16 = f32[2,296,384]{2,1,0:T(8,128)} collective-permute-done((f32[2,296,384]{2,1,0:T(8,128)}, f32[2,296,384]{2,1,0:T(8,128)}, u32[]{:S(2)}, u32[]{:S(2)}) %collective-permute-start.16) | collective-permute-done | bytes 909344 | tf_op jit(solution)/shard_map/ppermute | solution.py:58
  164.3 3.1 %collective-permute-start.17 = (f32[2,296,384]{2,1,0:T(8,128)}, f32[2,296,384]{2,1,0:T(8,128)}, u32[]{:S(2)}, u32[]{:S(2)}) collective-permute-start(f32[2,296,384]{2,1,0:T(8,128)} %bitcast_add_fusion.1), channel_id=1, source_target_pairs={{0,3},{1,0},{2,1},{3,2},{4,7},{5,4},{6,5},{7,6},{8,11},{9,8},{10,9... | collective-permute-start | bytes 2727944 | tf_op jit(solution)/shard_map/ppermute | solution.py:58
  168.2 3.4 %collective-permute-done.12 = f32[2,288,384]{2,1,0:T(8,128)} collective-permute-done((f32[2,288,384]{2,1,0:T(8,128)}, f32[2,288,384]{2,1,0:T(8,128)}, u32[]{:S(2)}, u32[]{:S(2)}) %collective-permute-start.12) | collective-permute-done | bytes 884768 | tf_op jit(solution)/shard_map/ppermute | solution.py:57
  173.0 3.0 %collective-permute-start.14 = (f32[144,384]{1,0:T(8,128)S(1)}, f32[144,384]{1,0:T(8,128)S(1)}, u32[]{:S(2)}, u32[]{:S(2)}) collective-permute-start(f32[144,384]{1,0:T(8,128)S(1)} %dynamic-slice_bitcast_fusion.4), channel_id=1, source_target_pairs={{0,4},{1,5},{2,6},{3,7},{4,0},{5,1},{6,2},{7,3},{8,12},{9,13},{10,... | collective-permute-start | bytes 663560 | tf_op jit(solution)/shard_map/ppermute | solution.py:69
  176.0 4.5 %collective-permute-done.17 = f32[2,296,384]{2,1,0:T(8,128)} collective-permute-done((f32[2,296,384]{2,1,0:T(8,128)}, f32[2,296,384]{2,1,0:T(8,128)}, u32[]{:S(2)}, u32[]{:S(2)}) %collective-permute-start.17) | collective-permute-done | bytes 909344 | tf_op jit(solution)/shard_map/ppermute | solution.py:58
  182.1 3.1 %collective-permute-start.19 = (f32[152,384]{1,0:T(8,128)S(1)}, f32[152,384]{1,0:T(8,128)S(1)}, u32[]{:S(2)}, u32[]{:S(2)}) collective-permute-start(f32[152,384]{1,0:T(8,128)S(1)} %dynamic-slice_bitcast_fusion.2), channel_id=1, source_target_pairs={{0,4},{1,5},{2,6},{3,7},{4,0},{5,1},{6,2},{7,3},{8,12},{9,13},{10,... | collective-permute-start | bytes 700424 | tf_op jit(solution)/shard_map/ppermute | solution.py:69
  185.4 3.0 %collective-permute-start.18 = (f32[144,384]{1,0:T(8,128)S(1)}, f32[144,384]{1,0:T(8,128)S(1)}, u32[]{:S(2)}, u32[]{:S(2)}) collective-permute-start(f32[144,384]{1,0:T(8,128)S(1)} %dynamic-slice_bitcast_fusion.3), channel_id=1, source_target_pairs={{0,4},{1,5},{2,6},{3,7},{4,0},{5,1},{6,2},{7,3},{8,12},{9,13},{10,... | collective-permute-start | bytes 663560 | tf_op jit(solution)/shard_map/ppermute | solution.py:69
  188.5 16.1 %collective-permute-done.19 = f32[152,384]{1,0:T(8,128)S(1)} collective-permute-done((f32[152,384]{1,0:T(8,128)S(1)}, f32[152,384]{1,0:T(8,128)S(1)}, u32[]{:S(2)}, u32[]{:S(2)}) %collective-permute-start.19) | collective-permute-done | bytes 233504 | tf_op jit(solution)/shard_map/ppermute | solution.py:69
  207.6 14.4 %collective-permute-done.13 = f32[144,384]{1,0:T(8,128)S(1)} collective-permute-done((f32[144,384]{1,0:T(8,128)S(1)}, f32[144,384]{1,0:T(8,128)S(1)}, u32[]{:S(2)}, u32[]{:S(2)}) %collective-permute-start.13) | collective-permute-done | bytes 221216 | tf_op jit(solution)/shard_map/ppermute | solution.py:69
  222.1 17.2 %collective-permute-done.18 = f32[144,384]{1,0:T(8,128)S(1)} collective-permute-done((f32[144,384]{1,0:T(8,128)S(1)}, f32[144,384]{1,0:T(8,128)S(1)}, u32[]{:S(2)}, u32[]{:S(2)}) %collective-permute-start.18) | collective-permute-done | bytes 221216 | tf_op jit(solution)/shard_map/ppermute | solution.py:69
  239.4 4.6 %collective-permute-start.23 = (f32[576]{0:T(1024)S(1)}, f32[576]{0:T(1024)S(1)}, u32[]{:S(2)}, u32[]{:S(2)}) collective-permute-start(f32[576]{0:T(1024)S(1)} %add.243), channel_id=1, source_target_pairs={{0,128},{16,144},{32,160},{48,176},{64,192},{80,208},{96,224},{112... | collective-permute-start | bytes 6920 | tf_op jit(solution)/shard_map/ppermute | solution.py:22
  245.6 10.1 %collective-permute-start.24 = (f32[576]{0:T(1024)S(1)}, f32[576]{0:T(1024)S(1)}, u32[]{:S(2)}, u32[]{:S(2)}) collective-permute-start(f32[576]{0:T(1024)S(1)} %add.244), channel_id=1, source_target_pairs={{0,8},{8,0},{1,9},{9,1},{2,10},{10,2},{3,11},{11,3},{4,12},{12,4},... | collective-permute-start | bytes 6920 | tf_op jit(solution)/shard_map/ppermute | solution.py:22
  (129 shorter events, 67.5 us)
Async XLA Ops:
  7.2 250.3 %reduce-scatter.2.cloned.1.call-start = ((), (), s32[]{:S(2)}) async-start(), calls=%async_computation.1 | async-start | bytes 19464192 | tf_op jit(solution)/shard_map/reduce_scatter | solution.py:100
  7.2 21.6 %collective-permute-start = (bf16[576,384]{1,0:T(8,128)(2,1)}, bf16[576,384]{1,0:T(8,128)(2,1)S(1)}, u32[]{:S(2)}, u32[]{:S(2)}) collective-permute-start(bf16[576,384]{1,0:T(8,128)(2,1)} %bitcast.91), channel_id=1, source_target_pairs={{0,7},{1,0},{2,1},{3,2},{4,3},{5,4},{6,5},{7,6},{8,15},{9,8},{10,9... | collective-permute-start | bytes 1327112 | tf_op jit(solution)/shard_map/ppermute | solution.py:13
  13.3 31.4 %collective-permute-start.1 = (bf16[576,384]{1,0:T(8,128)(2,1)}, bf16[576,384]{1,0:T(8,128)(2,1)S(1)}, u32[]{:S(2)}, u32[]{:S(2)}) collective-permute-start(bf16[576,384]{1,0:T(8,128)(2,1)} %bitcast.92), channel_id=1, source_target_pairs={{0,6},{1,7},{2,0},{3,1},{4,2},{5,3},{6,4},{7,5},{8,14},{9,15},{10,... | collective-permute-start | bytes 1327112 | tf_op jit(solution)/shard_map/ppermute | solution.py:13
  13.7 41.2 %collective-permute-start.6 = (bf16[576,384]{1,0:T(8,128)(2,1)}, bf16[576,384]{1,0:T(8,128)(2,1)S(1)}, u32[]{:S(2)}, u32[]{:S(2)}) collective-permute-start(bf16[576,384]{1,0:T(8,128)(2,1)} %bitcast.93), channel_id=1, source_target_pairs={{0,1},{1,2},{2,3},{3,4},{4,5},{5,6},{6,7},{7,0},{8,9},{9,10},{10,1... | collective-permute-start | bytes 1327112 | tf_op jit(solution)/shard_map/ppermute | solution.py:13
  14.4 40.4 %collective-permute-start.5 = (bf16[576,384]{1,0:T(8,128)(2,1)}, bf16[576,384]{1,0:T(8,128)(2,1)S(1)}, u32[]{:S(2)}, u32[]{:S(2)}) collective-permute-start(bf16[576,384]{1,0:T(8,128)(2,1)} %bitcast.94), channel_id=1, source_target_pairs={{0,2},{1,3},{2,4},{3,5},{4,6},{5,7},{6,0},{7,1},{8,10},{9,11},{10,... | collective-permute-start | bytes 1327112 | tf_op jit(solution)/shard_map/ppermute | solution.py:13
  16.3 38.4 %collective-permute-start.4 = (bf16[576,384]{1,0:T(8,128)(2,1)}, bf16[576,384]{1,0:T(8,128)(2,1)S(1)}, u32[]{:S(2)}, u32[]{:S(2)}) collective-permute-start(bf16[576,384]{1,0:T(8,128)(2,1)} %bitcast.95), channel_id=1, source_target_pairs={{0,3},{1,4},{2,5},{3,6},{4,7},{5,0},{6,1},{7,2},{8,11},{9,12},{10,... | collective-permute-start | bytes 1327112 | tf_op jit(solution)/shard_map/ppermute | solution.py:13
  28.8 21.9 %collective-permute-start.2 = (bf16[576,384]{1,0:T(8,128)(2,1)}, bf16[576,384]{1,0:T(8,128)(2,1)S(1)}, u32[]{:S(2)}, u32[]{:S(2)}) collective-permute-start(bf16[576,384]{1,0:T(8,128)(2,1)} %bitcast.96), channel_id=1, source_target_pairs={{0,5},{1,6},{2,7},{3,0},{4,1},{5,2},{6,3},{7,4},{8,13},{9,14},{10,... | collective-permute-start | bytes 1327112 | tf_op jit(solution)/shard_map/ppermute | solution.py:13
  44.8 9.8 %collective-permute-start.3 = (bf16[576,384]{1,0:T(8,128)(2,1)}, bf16[576,384]{1,0:T(8,128)(2,1)S(1)}, u32[]{:S(2)}, u32[]{:S(2)}) collective-permute-start(bf16[576,384]{1,0:T(8,128)(2,1)} %bitcast.97), channel_id=1, source_target_pairs={{0,4},{1,5},{2,6},{3,7},{4,0},{5,1},{6,2},{7,3},{8,12},{9,13},{10,... | collective-permute-start | bytes 1327112 | tf_op jit(solution)/shard_map/ppermute | solution.py:13
  72.5 13.0 %collective-permute-start.8 = (f32[2,384]{1,0:T(2,128)}, f32[2,384]{1,0:T(2,128)}, u32[]{:S(2)}, u32[]{:S(2)}) collective-permute-start(f32[2,384]{1,0:T(2,128)} %pad_maximum_fusion.6), channel_id=1, source_target_pairs={{0,2},{1,3},{2,0},{3,1},{4,6},{5,7},{6,4},{7,5},{8,10},{9,11},{10,... | collective-permute-start | bytes 9224 | tf_op jit(solution)/shard_map/ppermute | solution.py:31
  86.2 4.0 %collective-permute-start.9 = (f32[2,384]{1,0:T(2,128)S(1)}, f32[2,384]{1,0:T(2,128)S(1)}, u32[]{:S(2)}, u32[]{:S(2)}) collective-permute-start(f32[2,384]{1,0:T(2,128)S(1)} %pad_maximum_fusion.7), channel_id=1, source_target_pairs={{0,4},{1,5},{2,6},{3,7},{4,0},{5,1},{6,2},{7,3},{8,12},{9,13},{10,... | collective-permute-start | bytes 9224 | tf_op jit(solution)/shard_map/ppermute | solution.py:31
  117.2 17.7 %collective-permute-start.10 = (f32[2,288,384]{2,1,0:T(8,128)}, f32[2,288,384]{2,1,0:T(8,128)}, u32[]{:S(2)}, u32[]{:S(2)}) collective-permute-start(f32[2,288,384]{2,1,0:T(8,128)} %dynamic-slice_bitcast_fusion.1), channel_id=1, source_target_pairs={{0,1},{1,2},{2,3},{3,0},{4,5},{5,6},{6,7},{7,4},{8,9},{9,10},{10,1... | collective-permute-start | bytes 2654216 | tf_op jit(solution)/shard_map/ppermute | solution.py:57
  126.0 17.2 %collective-permute-start.15 = (f32[2,296,384]{2,1,0:T(8,128)}, f32[2,296,384]{2,1,0:T(8,128)}, u32[]{:S(2)}, u32[]{:S(2)}) collective-permute-start(f32[2,296,384]{2,1,0:T(8,128)} %dynamic-slice_bitcast_fusion), channel_id=1, source_target_pairs={{0,3},{1,0},{2,1},{3,2},{4,7},{5,4},{6,5},{7,6},{8,11},{9,8},{10,9... | collective-permute-start | bytes 2727944 | tf_op jit(solution)/shard_map/ppermute | solution.py:58
  137.2 16.4 %collective-permute-start.11 = (f32[2,288,384]{2,1,0:T(8,128)}, f32[2,288,384]{2,1,0:T(8,128)}, u32[]{:S(2)}, u32[]{:S(2)}) collective-permute-start(f32[2,288,384]{2,1,0:T(8,128)} %bitcast_add_fusion.3), channel_id=1, source_target_pairs={{0,1},{1,2},{2,3},{3,0},{4,5},{5,6},{6,7},{7,4},{8,9},{9,10},{10,1... | collective-permute-start | bytes 2654216 | tf_op jit(solution)/shard_map/ppermute | solution.py:57
  145.7 16.1 %collective-permute-start.16 = (f32[2,296,384]{2,1,0:T(8,128)}, f32[2,296,384]{2,1,0:T(8,128)}, u32[]{:S(2)}, u32[]{:S(2)}) collective-permute-start(f32[2,296,384]{2,1,0:T(8,128)} %bitcast_add_fusion), channel_id=1, source_target_pairs={{0,3},{1,0},{2,1},{3,2},{4,7},{5,4},{6,5},{7,6},{8,11},{9,8},{10,9... | collective-permute-start | bytes 2727944 | tf_op jit(solution)/shard_map/ppermute | solution.py:58
  155.7 15.9 %collective-permute-start.12 = (f32[2,288,384]{2,1,0:T(8,128)}, f32[2,288,384]{2,1,0:T(8,128)}, u32[]{:S(2)}, u32[]{:S(2)}) collective-permute-start(f32[2,288,384]{2,1,0:T(8,128)} %bitcast_add_fusion.4), channel_id=1, source_target_pairs={{0,1},{1,2},{2,3},{3,0},{4,5},{5,6},{6,7},{7,4},{8,9},{9,10},{10,1... | collective-permute-start | bytes 2654216 | tf_op jit(solution)/shard_map/ppermute | solution.py:57
  164.3 16.2 %collective-permute-start.17 = (f32[2,296,384]{2,1,0:T(8,128)}, f32[2,296,384]{2,1,0:T(8,128)}, u32[]{:S(2)}, u32[]{:S(2)}) collective-permute-start(f32[2,296,384]{2,1,0:T(8,128)} %bitcast_add_fusion.1), channel_id=1, source_target_pairs={{0,3},{1,0},{2,1},{3,2},{4,7},{5,4},{6,5},{7,6},{8,11},{9,8},{10,9... | collective-permute-start | bytes 2727944 | tf_op jit(solution)/shard_map/ppermute | solution.py:58
  173.0 31.8 %collective-permute-start.14 = (f32[144,384]{1,0:T(8,128)S(1)}, f32[144,384]{1,0:T(8,128)S(1)}, u32[]{:S(2)}, u32[]{:S(2)}) collective-permute-start(f32[144,384]{1,0:T(8,128)S(1)} %dynamic-slice_bitcast_fusion.4), channel_id=1, source_target_pairs={{0,4},{1,5},{2,6},{3,7},{4,0},{5,1},{6,2},{7,3},{8,12},{9,13},{10,... | collective-permute-start | bytes 663560 | tf_op jit(solution)/shard_map/ppermute | solution.py:69
  182.1 22.4 %collective-permute-start.19 = (f32[152,384]{1,0:T(8,128)S(1)}, f32[152,384]{1,0:T(8,128)S(1)}, u32[]{:S(2)}, u32[]{:S(2)}) collective-permute-start(f32[152,384]{1,0:T(8,128)S(1)} %dynamic-slice_bitcast_fusion.2), channel_id=1, source_target_pairs={{0,4},{1,5},{2,6},{3,7},{4,0},{5,1},{6,2},{7,3},{8,12},{9,13},{10,... | collective-permute-start | bytes 700424 | tf_op jit(solution)/shard_map/ppermute | solution.py:69
  185.3 36.7 %collective-permute-start.13 = (f32[144,384]{1,0:T(8,128)S(1)}, f32[144,384]{1,0:T(8,128)S(1)}, u32[]{:S(2)}, u32[]{:S(2)}) collective-permute-start(f32[144,384]{1,0:T(8,128)S(1)} %dynamic-slice_bitcast_fusion.5), channel_id=1, source_target_pairs={{0,4},{1,5},{2,6},{3,7},{4,0},{5,1},{6,2},{7,3},{8,12},{9,13},{10,... | collective-permute-start | bytes 663560 | tf_op jit(solution)/shard_map/ppermute | solution.py:69
  185.4 53.9 %collective-permute-start.18 = (f32[144,384]{1,0:T(8,128)S(1)}, f32[144,384]{1,0:T(8,128)S(1)}, u32[]{:S(2)}, u32[]{:S(2)}) collective-permute-start(f32[144,384]{1,0:T(8,128)S(1)} %dynamic-slice_bitcast_fusion.3), channel_id=1, source_target_pairs={{0,4},{1,5},{2,6},{3,7},{4,0},{5,1},{6,2},{7,3},{8,12},{9,13},{10,... | collective-permute-start | bytes 663560 | tf_op jit(solution)/shard_map/ppermute | solution.py:69
  207.6 14.4 %collective-permute-start.21 = (f32[576]{0:T(1024)S(1)}, f32[576]{0:T(1024)S(1)}, u32[]{:S(2)}, u32[]{:S(2)}) collective-permute-start(f32[576]{0:T(1024)S(1)} %slice_add_fusion), channel_id=1, source_target_pairs={{0,32},{16,48},{32,0},{48,16},{64,96},{80,112},{96,64},{112,80},{1... | collective-permute-start | bytes 6920 | tf_op jit(solution)/shard_map/ppermute | solution.py:22
  222.0 17.4 %collective-permute-start.22 = (f32[576]{0:T(1024)S(1)}, f32[576]{0:T(1024)S(1)}, u32[]{:S(2)}, u32[]{:S(2)}) collective-permute-start(f32[576]{0:T(1024)S(1)} %add.242), channel_id=1, source_target_pairs={{0,64},{16,80},{32,96},{48,112},{64,0},{80,16},{96,32},{112,48},{1... | collective-permute-start | bytes 6920 | tf_op jit(solution)/shard_map/ppermute | solution.py:22
  239.4 6.2 %collective-permute-start.23 = (f32[576]{0:T(1024)S(1)}, f32[576]{0:T(1024)S(1)}, u32[]{:S(2)}, u32[]{:S(2)}) collective-permute-start(f32[576]{0:T(1024)S(1)} %add.243), channel_id=1, source_target_pairs={{0,128},{16,144},{32,160},{48,176},{64,192},{80,208},{96,224},{112... | collective-permute-start | bytes 6920 | tf_op jit(solution)/shard_map/ppermute | solution.py:22
  245.6 11.3 %collective-permute-start.24 = (f32[576]{0:T(1024)S(1)}, f32[576]{0:T(1024)S(1)}, u32[]{:S(2)}, u32[]{:S(2)}) collective-permute-start(f32[576]{0:T(1024)S(1)} %add.244), channel_id=1, source_target_pairs={{0,8},{8,0},{1,9},{9,1},{2,10},{10,2},{3,11},{11,3},{4,12},{12,4},... | collective-permute-start | bytes 6920 | tf_op jit(solution)/shard_map/ppermute | solution.py:22
  (16 other events, 180.0 us)
Sparse Core Ops, SparseCore 0:
  102.9 153.3 reduce-scatter.1

commit v6 on v5

--- a/solution.py
+++ b/solution.py
@@ -94,10 +94,18 @@
     onehot = (column_ids == target_ids[:, None]).astype(jnp.float32)
     dlogits = (jnp.exp(logits - log_total[:, None]) - onehot).astype(jnp.bfloat16)
 
-    head_partial = lax.dot_general(
-        normed_t, dlogits, (((1,), (0,)), ((), ())), preferred_element_type=jnp.float32
-    )
-    grad_head = lax.psum_scatter(head_partial, ("outer", "core"), scatter_dimension=0, tiled=True)
+    split_at = vocab_rows // 2 if vocab_rows % 256 == 0 else vocab_rows
+    halves = []
+    for lo, hi in ((0, split_at), (split_at, vocab_rows)):
+        if hi > lo:
+            head_partial = lax.dot_general(
+                normed_t, dlogits[:, lo:hi], (((1,), (0,)), ((), ())),
+                preferred_element_type=jnp.float32,
+            )
+            halves.append(
+                lax.psum_scatter(head_partial, ("outer", "core"), scatter_dimension=0, tiled=True)
+            )
+    grad_head = jnp.concatenate(halves, axis=1)
 
     partial = lax.dot_general(
         head_weight.reshape(n_tensor, local_cols, vocab_rows),

time: 267 us -> 384 us (1.44)
  waiting for transfers between devices: 123 us -> 244 us
  starting transfers between devices: 60.6 us -> 52.2 us
    reduce_scatter x1 -> x2, waiting for transfers between devices: 0.01 us -> 132 us  [shards(): lax.psum_scatter(head_partial, ('outer', 'core'), scatter_dimension=0, ti...]
    ppermute x4, waiting for transfers between devices: 47.7 us -> 17.3 us  [two_stage_reduce_scatter(): mine = mine + lax.ppermute(other, axis, perm_h)]
    ppermute x3, starting transfers between devices: 16.2 us -> 5.12 us  [butterfly_softmax_stats(): lax.ppermute(jnp.stack([top, total]), axis, [(c, c ^ b) for c in range(n)])]
    ppermute x7, starting transfers between devices: 11.3 us -> 20.9 us  [shift_gather(): got.append(lax.ppermute(x, axis, [(c, (c + k) % n) for c in range(n)]))]
    ppermute x7, waiting for transfers between devices: 35.9 us -> 44.2 us  [shift_gather(): got.append(lax.ppermute(x, axis, [(c, (c + k) % n) for c in range(n)]))]
    ppermute x4, starting transfers between devices: 9.28 us -> 3.33 us  [two_stage_reduce_scatter(): mine = mine + lax.ppermute(other, axis, perm_h)]
    ppermute x3, waiting for transfers between devices: 15.2 us -> 19.6 us  [two_stage_reduce_scatter(): recv_f = lax.ppermute(send_f, axis, perm_f)]
    dot_general x1 -> x2, matrix products: 9.08 us -> 11.1 us  [shards(): lax.dot_general(normed_t, dlogits[:, lo:hi], (((1,), (0,)), ((), ())), pr...]
  transfers between devices with their start and end apart: 26 -> 27, of which waited for: 18 -> 20; matrix products, arithmetic and copies ran while one was open for 12% -> 10% of each run, Pallas kernels for 0% -> 0%
where the time goes in v6:
time: 384 us; the launch traced here: 380 us
  waiting for transfers between devices  244 us (64%)
  starting transfers between devices  52.2 us (14%)
  other arithmetic  26.1 us (7%)
  matrix products  24.2 us (6%)
  local copies, waits for them, and re-layouts  19.4 us (5%)
  between operations  14.5 us (4%)
    reduce_scatter x2, waiting for transfers between devices, shards(): lax.psum_scatter(head_partial, ('outer', 'core'), scatter_dimension=0, ti...  132 us
    ppermute x7, waiting for transfers between devices, shift_gather(): got.append(lax.ppermute(x, axis, [(c, (c + k) % n) for c in range(n)]))  44.2 us
    ppermute x7, starting transfers between devices, shift_gather(): got.append(lax.ppermute(x, axis, [(c, (c + k) % n) for c in range(n)]))  20.9 us
    ppermute x3, waiting for transfers between devices, two_stage_reduce_scatter(): recv_f = lax.ppermute(send_f, axis, perm_f)  19.6 us
    ppermute x3, waiting for transfers between devices, two_stage_reduce_scatter(): recv_b = lax.ppermute(send_b, axis, perm_b)  19.2 us
    ppermute x4, waiting for transfers between devices, two_stage_reduce_scatter(): mine = mine + lax.ppermute(other, axis, perm_h)  17.3 us
    ppermute x5, starting transfers between devices, butterfly_sum(): x = x + lax.ppermute(x, axis, [(c, c ^ b) for c in range(n)])  14.1 us
    unnamed x43, local copies, waits for them, and re-layouts  13.2 us
  transfers between devices with their start and end apart: 27, of which 20 were waited for; matrix products, arithmetic and copies ran while one was open for 10% of the time, Pallas kernels for 0%

profile of v6, /device:TPU:1, one launch (start us, length us, event | category | flops | bytes accessed | tf_op | source)
XLA Modules:
  0.0 380.3 jit_solution(8677548987385373936)
XLA Ops:
  7.2 6.1 %collective-permute-start = (bf16[576,384]{1,0:T(8,128)(2,1)}, bf16[576,384]{1,0:T(8,128)(2,1)S(1)}, u32[]{:S(2)}, u32[]{:S(2)}) collective-permute-start(bf16[576,384]{1,0:T(8,128)(2,1)} %bitcast.91), channel_id=1, source_target_pairs={{0,7},{1,0},{2,1},{3,2},{4,3},{5,4},{6,5},{7,6},{8,15},{9,8},{10,9... | collective-permute-start | bytes 1327112 | tf_op jit(solution)/shard_map/ppermute | solution.py:13
  17.1 11.7 %collective-permute-done = bf16[576,384]{1,0:T(8,128)(2,1)S(1)} collective-permute-done((bf16[576,384]{1,0:T(8,128)(2,1)}, bf16[576,384]{1,0:T(8,128)(2,1)S(1)}, u32[]{:S(2)}, u32[]{:S(2)}) %collective-permute-start) | collective-permute-done | bytes 442400 | tf_op jit(solution)/shard_map/ppermute | solution.py:13
  28.8 15.6 %collective-permute-done.1 = bf16[576,384]{1,0:T(8,128)(2,1)S(1)} collective-permute-done((bf16[576,384]{1,0:T(8,128)(2,1)}, bf16[576,384]{1,0:T(8,128)(2,1)S(1)}, u32[]{:S(2)}, u32[]{:S(2)}) %collective-permute-start.1) | collective-permute-done | bytes 442400 | tf_op jit(solution)/shard_map/ppermute | solution.py:13
  44.4 11.1 %collective-permute-start.6 = (bf16[576,384]{1,0:T(8,128)(2,1)}, bf16[576,384]{1,0:T(8,128)(2,1)S(1)}, u32[]{:S(2)}, u32[]{:S(2)}) collective-permute-start(bf16[576,384]{1,0:T(8,128)(2,1)} %bitcast.97), channel_id=1, source_target_pairs={{0,1},{1,2},{2,3},{3,4},{4,5},{5,6},{6,7},{7,0},{8,9},{9,10},{10,1... | collective-permute-start | bytes 1327112 | tf_op jit(solution)/shard_map/ppermute | solution.py:13
  55.7 9.3 %collective-permute-done.3 = bf16[576,384]{1,0:T(8,128)(2,1)S(1)} collective-permute-done((bf16[576,384]{1,0:T(8,128)(2,1)}, bf16[576,384]{1,0:T(8,128)(2,1)S(1)}, u32[]{:S(2)}, u32[]{:S(2)}) %collective-permute-start.3) | collective-permute-done | bytes 442400 | tf_op jit(solution)/shard_map/ppermute | solution.py:13
  65.2 7.6 %collective-permute-done.6 = bf16[576,384]{1,0:T(8,128)(2,1)S(1)} collective-permute-done((bf16[576,384]{1,0:T(8,128)(2,1)}, bf16[576,384]{1,0:T(8,128)(2,1)S(1)}, u32[]{:S(2)}, u32[]{:S(2)}) %collective-permute-start.6) | collective-permute-done | bytes 442400 | tf_op jit(solution)/shard_map/ppermute | solution.py:13
  80.3 3.9 %fusion.23 = (f32[384]{0:T(512)S(1)}, f32[384,1024]{1,0:T(8,128)S(1)}) fusion(bf16[4608,384]{1,0:T(8,128)(2,1)S(1)} %fusion.3, bf16[4608,1024]{1,0:T(8,128)(2,1)S(1)} %bitcast.88), kind=kOutput, calls=%fused_computation.89 | convolution fusion | flops 3624271360 | bytes 14550528 | tf_op jit(solution)/shard_map/dot_general | solution.py:85
  95.9 3.9 %collective-permute-done.9 = f32[2,384]{1,0:T(2,128)S(1)} collective-permute-done((f32[2,384]{1,0:T(2,128)S(1)}, f32[2,384]{1,0:T(2,128)S(1)}, u32[]{:S(2)}, u32[]{:S(2)}) %collective-permute-start.9) | collective-permute-done | bytes 3104 | tf_op jit(solution)/shard_map/ppermute | solution.py:31
  103.3 5.0 %fusion.11 = f32[4608,512]{1,0:T(8,128)} fusion(bf16[4608,384]{1,0:T(8,128)(2,1)S(1)} %fusion.3, bf16[384,1024]{1,0:T(8,128)(2,1)S(1)} %subtract_convert_fusion), kind=kOutput, calls=%fused_computation.47 | convolution fusion | flops 1811939328 | bytes 13369344 | tf_op jit(solution)/shard_map/dot_general | solution.py:101
  108.4 6.1 %fusion.13 = f32[4608,512]{1,0:T(8,128)} fusion(bf16[4608,384]{1,0:T(8,128)(2,1)S(1)} %fusion.3, bf16[384,1024]{1,0:T(8,128)(2,1)} %copy-done.6), kind=kOutput, calls=%fused_computation.49 | convolution fusion | flops 1811939328 | bytes 13369344 | tf_op jit(solution)/shard_map/dot_general | solution.py:101
  115.6 9.2 %fusion.1 = (f32[384]{0:T(512)S(1)}, f32[8,576]{1,0:T(8,128)}, f32[8,384,576]{1,2,0:T(8,128)S(1)}) fusion(f32[8,576]{1,0:T(8,128)S(1)} %mul.159, f32[384]{0:T(512)S(1)} %add_rsqrt_fusion, bf16[16,576,384]{2,1,0:T(8,128)(2,1)} %copy-done.3, s32[]{:T(128)S(6)} %select_n.79, bf16[8,576,1024]{2,1,0:T(8,128)(2,1)} %bitcast.86, bf16[384,1024]{1,0:T(8,128)(2,1)S(1)} %copy-done.7), kind=kOutput, calls=%fused_computation.3 | convolution fusion | flops 3636259840 | bytes 20880388 | tf_op jit(solution)/shard_map/dot_general | solution.py:110
  139.5 8.3 %collective-permute-done.10 = f32[2,288,384]{2,1,0:T(8,128)} collective-permute-done((f32[2,288,384]{2,1,0:T(8,128)}, f32[2,288,384]{2,1,0:T(8,128)}, u32[]{:S(2)}, u32[]{:S(2)}) %collective-permute-start.10) | collective-permute-done | bytes 884768 | tf_op jit(solution)/shard_map/ppermute | solution.py:57
  150.0 6.1 %collective-permute-done.15 = f32[2,296,384]{2,1,0:T(8,128)} collective-permute-done((f32[2,296,384]{2,1,0:T(8,128)}, f32[2,296,384]{2,1,0:T(8,128)}, u32[]{:S(2)}, u32[]{:S(2)}) %collective-permute-start.15) | collective-permute-done | bytes 909344 | tf_op jit(solution)/shard_map/ppermute | solution.py:58
  161.2 6.8 %collective-permute-done.11 = f32[2,288,384]{2,1,0:T(8,128)} collective-permute-done((f32[2,288,384]{2,1,0:T(8,128)}, f32[2,288,384]{2,1,0:T(8,128)}, u32[]{:S(2)}, u32[]{:S(2)}) %collective-permute-start.11) | collective-permute-done | bytes 884768 | tf_op jit(solution)/shard_map/ppermute | solution.py:57
  170.2 5.9 %collective-permute-done.16 = f32[2,296,384]{2,1,0:T(8,128)} collective-permute-done((f32[2,296,384]{2,1,0:T(8,128)}, f32[2,296,384]{2,1,0:T(8,128)}, u32[]{:S(2)}, u32[]{:S(2)}) %collective-permute-start.16) | collective-permute-done | bytes 909344 | tf_op jit(solution)/shard_map/ppermute | solution.py:58
  178.6 3.4 collective-permute-start.17
  182.8 4.5 %collective-permute-done.12 = f32[2,288,384]{2,1,0:T(8,128)} collective-permute-done((f32[2,288,384]{2,1,0:T(8,128)}, f32[2,288,384]{2,1,0:T(8,128)}, u32[]{:S(2)}, u32[]{:S(2)}) %collective-permute-start.12) | collective-permute-done | bytes 884768 | tf_op jit(solution)/shard_map/ppermute | solution.py:57
  188.8 7.2 %collective-permute-done.17 = f32[2,296,384]{2,1,0:T(8,128)} collective-permute-done((f32[2,296,384]{2,1,0:T(8,128)}, f32[2,296,384]{2,1,0:T(8,128)}, u32[]{:S(2)}, u32[]{:S(2)}) %collective-permute-start.17) | collective-permute-done | bytes 909344 | tf_op jit(solution)/shard_map/ppermute | solution.py:58
  200.9 7.0 %collective-permute-done.19 = f32[152,384]{1,0:T(8,128)S(1)} collective-permute-done((f32[152,384]{1,0:T(8,128)S(1)}, f32[152,384]{1,0:T(8,128)S(1)}, u32[]{:S(2)}, u32[]{:S(2)}) %collective-permute-start.19) | collective-permute-done | bytes 233504 | tf_op jit(solution)/shard_map/ppermute | solution.py:69
  210.9 4.9 %collective-permute-done.13 = f32[144,384]{1,0:T(8,128)S(1)} collective-permute-done((f32[144,384]{1,0:T(8,128)S(1)}, f32[144,384]{1,0:T(8,128)S(1)}, u32[]{:S(2)}, u32[]{:S(2)}) %collective-permute-start.13) | collective-permute-done | bytes 221216 | tf_op jit(solution)/shard_map/ppermute | solution.py:69
  215.9 3.6 collective-permute-start.22
  219.4 5.3 %collective-permute-done.18 = f32[144,384]{1,0:T(8,128)S(1)} collective-permute-done((f32[144,384]{1,0:T(8,128)S(1)}, f32[144,384]{1,0:T(8,128)S(1)}, u32[]{:S(2)}, u32[]{:S(2)}) %collective-permute-start.18) | collective-permute-done | bytes 221216 | tf_op jit(solution)/shard_map/ppermute | solution.py:69
  227.9 10.3 %collective-permute-start.24 = (f32[576]{0:T(1024)S(1)}, f32[576]{0:T(1024)S(1)}, u32[]{:S(2)}, u32[]{:S(2)}) collective-permute-start(f32[576]{0:T(1024)S(1)} %add.246), channel_id=1, source_target_pairs={{0,8},{8,0},{1,9},{9,1},{2,10},{10,2},{3,11},{11,3},{4,12},{12,4},... | collective-permute-start | bytes 6920 | tf_op jit(solution)/shard_map/ppermute | solution.py:22
  241.8 129.7 %reduce-scatter.3.cloned.1.call-done = f32[144,512]{1,0:T(8,128)} async-done(((f32[4608,512]{1,0:T(8,128)}), f32[144,512]{1,0:T(8,128)}) %reduce-scatter.3.cloned.1.call-update) | async-done | bytes 294928 | tf_op jit(solution)/shard_map/reduce_scatter | solution.py:106
  (134 shorter events, 73.1 us)
Async XLA Ops:
  7.2 234.6 %reduce-scatter.5.cloned.1.call-start = ((), (), s32[]{:S(2)}) async-start(), calls=%async_computation.3 | async-start | bytes 9732096 | tf_op jit(solution)/shard_map/reduce_scatter | solution.py:106
  7.2 21.6 %collective-permute-start = (bf16[576,384]{1,0:T(8,128)(2,1)}, bf16[576,384]{1,0:T(8,128)(2,1)S(1)}, u32[]{:S(2)}, u32[]{:S(2)}) collective-permute-start(bf16[576,384]{1,0:T(8,128)(2,1)} %bitcast.91), channel_id=1, source_target_pairs={{0,7},{1,0},{2,1},{3,2},{4,3},{5,4},{6,5},{7,6},{8,15},{9,8},{10,9... | collective-permute-start | bytes 1327112 | tf_op jit(solution)/shard_map/ppermute | solution.py:13
  13.3 31.1 %collective-permute-start.1 = (bf16[576,384]{1,0:T(8,128)(2,1)}, bf16[576,384]{1,0:T(8,128)(2,1)S(1)}, u32[]{:S(2)}, u32[]{:S(2)}) collective-permute-start(bf16[576,384]{1,0:T(8,128)(2,1)} %bitcast.92), channel_id=1, source_target_pairs={{0,6},{1,7},{2,0},{3,1},{4,2},{5,3},{6,4},{7,5},{8,14},{9,15},{10,... | collective-permute-start | bytes 1327112 | tf_op jit(solution)/shard_map/ppermute | solution.py:13
  13.7 41.9 %collective-permute-start.2 = (bf16[576,384]{1,0:T(8,128)(2,1)}, bf16[576,384]{1,0:T(8,128)(2,1)S(1)}, u32[]{:S(2)}, u32[]{:S(2)}) collective-permute-start(bf16[576,384]{1,0:T(8,128)(2,1)} %bitcast.93), channel_id=1, source_target_pairs={{0,5},{1,6},{2,7},{3,0},{4,1},{5,2},{6,3},{7,4},{8,13},{9,14},{10,... | collective-permute-start | bytes 1327112 | tf_op jit(solution)/shard_map/ppermute | solution.py:13
  14.3 50.7 %collective-permute-start.3 = (bf16[576,384]{1,0:T(8,128)(2,1)}, bf16[576,384]{1,0:T(8,128)(2,1)S(1)}, u32[]{:S(2)}, u32[]{:S(2)}) collective-permute-start(bf16[576,384]{1,0:T(8,128)(2,1)} %bitcast.94), channel_id=1, source_target_pairs={{0,4},{1,5},{2,6},{3,7},{4,0},{5,1},{6,2},{7,3},{8,12},{9,13},{10,... | collective-permute-start | bytes 1327112 | tf_op jit(solution)/shard_map/ppermute | solution.py:13
  17.1 48.0 %collective-permute-start.4 = (bf16[576,384]{1,0:T(8,128)(2,1)}, bf16[576,384]{1,0:T(8,128)(2,1)S(1)}, u32[]{:S(2)}, u32[]{:S(2)}) collective-permute-start(bf16[576,384]{1,0:T(8,128)(2,1)} %bitcast.95), channel_id=1, source_target_pairs={{0,3},{1,4},{2,5},{3,6},{4,7},{5,0},{6,1},{7,2},{8,11},{9,12},{10,... | collective-permute-start | bytes 1327112 | tf_op jit(solution)/shard_map/ppermute | solution.py:13
  28.8 36.4 %collective-permute-start.5 = (bf16[576,384]{1,0:T(8,128)(2,1)}, bf16[576,384]{1,0:T(8,128)(2,1)S(1)}, u32[]{:S(2)}, u32[]{:S(2)}) collective-permute-start(bf16[576,384]{1,0:T(8,128)(2,1)} %bitcast.96), channel_id=1, source_target_pairs={{0,2},{1,3},{2,4},{3,5},{4,6},{5,7},{6,0},{7,1},{8,10},{9,11},{10,... | collective-permute-start | bytes 1327112 | tf_op jit(solution)/shard_map/ppermute | solution.py:13
  44.4 28.4 %collective-permute-start.6 = (bf16[576,384]{1,0:T(8,128)(2,1)}, bf16[576,384]{1,0:T(8,128)(2,1)S(1)}, u32[]{:S(2)}, u32[]{:S(2)}) collective-permute-start(bf16[576,384]{1,0:T(8,128)(2,1)} %bitcast.97), channel_id=1, source_target_pairs={{0,1},{1,2},{2,3},{3,4},{4,5},{5,6},{6,7},{7,0},{8,9},{9,10},{10,1... | collective-permute-start | bytes 1327112 | tf_op jit(solution)/shard_map/ppermute | solution.py:13
  90.7 4.3 %collective-permute-start.8 = (f32[2,384]{1,0:T(2,128)}, f32[2,384]{1,0:T(2,128)}, u32[]{:S(2)}, u32[]{:S(2)}) collective-permute-start(f32[2,384]{1,0:T(2,128)} %pad_maximum_fusion.7), channel_id=1, source_target_pairs={{0,2},{1,3},{2,0},{3,1},{4,6},{5,7},{6,4},{7,5},{8,10},{9,11},{10,... | collective-permute-start | bytes 9224 | tf_op jit(solution)/shard_map/ppermute | solution.py:31
  95.8 4.0 %collective-permute-start.9 = (f32[2,384]{1,0:T(2,128)S(1)}, f32[2,384]{1,0:T(2,128)S(1)}, u32[]{:S(2)}, u32[]{:S(2)}) collective-permute-start(f32[2,384]{1,0:T(2,128)S(1)} %pad_maximum_fusion.8), channel_id=1, source_target_pairs={{0,4},{1,5},{2,6},{3,7},{4,0},{5,1},{6,2},{7,3},{8,12},{9,13},{10,... | collective-permute-start | bytes 9224 | tf_op jit(solution)/shard_map/ppermute | solution.py:31
  108.4 263.2 %reduce-scatter.3.cloned.1.call-start = ((), (), s32[]{:S(2)}) async-start(), calls=%async_computation.2 | async-start | bytes 9732096 | tf_op jit(solution)/shard_map/reduce_scatter | solution.py:106
  128.9 18.9 %collective-permute-start.10 = (f32[2,288,384]{2,1,0:T(8,128)}, f32[2,288,384]{2,1,0:T(8,128)}, u32[]{:S(2)}, u32[]{:S(2)}) collective-permute-start(f32[2,288,384]{2,1,0:T(8,128)} %dynamic-slice_bitcast_fusion.1), channel_id=1, source_target_pairs={{0,1},{1,2},{2,3},{3,0},{4,5},{5,6},{6,7},{7,4},{8,9},{9,10},{10,1... | collective-permute-start | bytes 2654216 | tf_op jit(solution)/shard_map/ppermute | solution.py:57
  138.4 17.7 %collective-permute-start.15 = (f32[2,296,384]{2,1,0:T(8,128)}, f32[2,296,384]{2,1,0:T(8,128)}, u32[]{:S(2)}, u32[]{:S(2)}) collective-permute-start(f32[2,296,384]{2,1,0:T(8,128)} %dynamic-slice_bitcast_fusion), channel_id=1, source_target_pairs={{0,3},{1,0},{2,1},{3,2},{4,7},{5,4},{6,5},{7,6},{8,11},{9,8},{10,9... | collective-permute-start | bytes 2727944 | tf_op jit(solution)/shard_map/ppermute | solution.py:58
  150.0 18.0 %collective-permute-start.11 = (f32[2,288,384]{2,1,0:T(8,128)}, f32[2,288,384]{2,1,0:T(8,128)}, u32[]{:S(2)}, u32[]{:S(2)}) collective-permute-start(f32[2,288,384]{2,1,0:T(8,128)} %bitcast_add_fusion.3), channel_id=1, source_target_pairs={{0,1},{1,2},{2,3},{3,0},{4,5},{5,6},{6,7},{7,4},{8,9},{9,10},{10,1... | collective-permute-start | bytes 2654216 | tf_op jit(solution)/shard_map/ppermute | solution.py:57
  158.6 17.5 %collective-permute-start.16 = (f32[2,296,384]{2,1,0:T(8,128)}, f32[2,296,384]{2,1,0:T(8,128)}, u32[]{:S(2)}, u32[]{:S(2)}) collective-permute-start(f32[2,296,384]{2,1,0:T(8,128)} %bitcast_add_fusion), channel_id=1, source_target_pairs={{0,3},{1,0},{2,1},{3,2},{4,7},{5,4},{6,5},{7,6},{8,11},{9,8},{10,9... | collective-permute-start | bytes 2727944 | tf_op jit(solution)/shard_map/ppermute | solution.py:58
  170.2 17.1 %collective-permute-start.12 = (f32[2,288,384]{2,1,0:T(8,128)}, f32[2,288,384]{2,1,0:T(8,128)}, u32[]{:S(2)}, u32[]{:S(2)}) collective-permute-start(f32[2,288,384]{2,1,0:T(8,128)} %bitcast_add_fusion.4), channel_id=1, source_target_pairs={{0,1},{1,2},{2,3},{3,0},{4,5},{5,6},{6,7},{7,4},{8,9},{9,10},{10,1... | collective-permute-start | bytes 2654216 | tf_op jit(solution)/shard_map/ppermute | solution.py:57
  178.6 17.4 %collective-permute-start.17 = (f32[2,296,384]{2,1,0:T(8,128)}, f32[2,296,384]{2,1,0:T(8,128)}, u32[]{:S(2)}, u32[]{:S(2)}) collective-permute-start(f32[2,296,384]{2,1,0:T(8,128)} %bitcast_add_fusion.1), channel_id=1, source_target_pairs={{0,3},{1,0},{2,1},{3,2},{4,7},{5,4},{6,5},{7,6},{8,11},{9,8},{10,9... | collective-permute-start | bytes 2727944 | tf_op jit(solution)/shard_map/ppermute | solution.py:58
  188.7 19.5 %collective-permute-start.14 = (f32[144,384]{1,0:T(8,128)S(1)}, f32[144,384]{1,0:T(8,128)S(1)}, u32[]{:S(2)}, u32[]{:S(2)}) collective-permute-start(f32[144,384]{1,0:T(8,128)S(1)} %dynamic-slice_bitcast_fusion.4), channel_id=1, source_target_pairs={{0,4},{1,5},{2,6},{3,7},{4,0},{5,1},{6,2},{7,3},{8,12},{9,13},{10,... | collective-permute-start | bytes 663560 | tf_op jit(solution)/shard_map/ppermute | solution.py:69
  197.6 10.4 %collective-permute-start.19 = (f32[152,384]{1,0:T(8,128)S(1)}, f32[152,384]{1,0:T(8,128)S(1)}, u32[]{:S(2)}, u32[]{:S(2)}) collective-permute-start(f32[152,384]{1,0:T(8,128)S(1)} %dynamic-slice_bitcast_fusion.2), channel_id=1, source_target_pairs={{0,4},{1,5},{2,6},{3,7},{4,0},{5,1},{6,2},{7,3},{8,12},{9,13},{10,... | collective-permute-start | bytes 700424 | tf_op jit(solution)/shard_map/ppermute | solution.py:69
  197.7 18.1 %collective-permute-start.13 = (f32[144,384]{1,0:T(8,128)S(1)}, f32[144,384]{1,0:T(8,128)S(1)}, u32[]{:S(2)}, u32[]{:S(2)}) collective-permute-start(f32[144,384]{1,0:T(8,128)S(1)} %dynamic-slice_bitcast_fusion.5), channel_id=1, source_target_pairs={{0,4},{1,5},{2,6},{3,7},{4,0},{5,1},{6,2},{7,3},{8,12},{9,13},{10,... | collective-permute-start | bytes 663560 | tf_op jit(solution)/shard_map/ppermute | solution.py:69
  200.8 24.0 %collective-permute-start.18 = (f32[144,384]{1,0:T(8,128)S(1)}, f32[144,384]{1,0:T(8,128)S(1)}, u32[]{:S(2)}, u32[]{:S(2)}) collective-permute-start(f32[144,384]{1,0:T(8,128)S(1)} %dynamic-slice_bitcast_fusion.3), channel_id=1, source_target_pairs={{0,4},{1,5},{2,6},{3,7},{4,0},{5,1},{6,2},{7,3},{8,12},{9,13},{10,... | collective-permute-start | bytes 663560 | tf_op jit(solution)/shard_map/ppermute | solution.py:69
  210.9 5.0 %collective-permute-start.21 = (f32[576]{0:T(1024)S(1)}, f32[576]{0:T(1024)S(1)}, u32[]{:S(2)}, u32[]{:S(2)}) collective-permute-start(f32[576]{0:T(1024)S(1)} %slice_add_fusion), channel_id=1, source_target_pairs={{0,32},{16,48},{32,0},{48,16},{64,96},{80,112},{96,64},{112,80},{1... | collective-permute-start | bytes 6920 | tf_op jit(solution)/shard_map/ppermute | solution.py:22
  215.9 8.9 %collective-permute-start.22 = (f32[576]{0:T(1024)S(1)}, f32[576]{0:T(1024)S(1)}, u32[]{:S(2)}, u32[]{:S(2)}) collective-permute-start(f32[576]{0:T(1024)S(1)} %add.244), channel_id=1, source_target_pairs={{0,64},{16,80},{32,96},{48,112},{64,0},{80,16},{96,32},{112,48},{1... | collective-permute-start | bytes 6920 | tf_op jit(solution)/shard_map/ppermute | solution.py:22
  227.9 11.4 %collective-permute-start.24 = (f32[576]{0:T(1024)S(1)}, f32[576]{0:T(1024)S(1)}, u32[]{:S(2)}, u32[]{:S(2)}) collective-permute-start(f32[576]{0:T(1024)S(1)} %add.246), channel_id=1, source_target_pairs={{0,8},{8,0},{1,9},{9,1},{2,10},{10,2},{3,11},{11,3},{4,12},{12,4},... | collective-permute-start | bytes 6920 | tf_op jit(solution)/shard_map/ppermute | solution.py:22
  (17 other events, 188.6 us)
Sparse Core Ops, SparseCore 0:
  108.5 133.2 reduce-scatter.4
  244.3 127.1 reduce-scatter.2

commit v7 on v5

--- a/solution.py
+++ b/solution.py
@@ -24,14 +24,26 @@
     return x
 
 
-def butterfly_softmax_stats(top, logits, axis, n):
+def group_softmax_stats(top, logits, axis, n_hi, n_lo):
     total = jnp.sum(jnp.exp(logits - top[:, None]), axis=1)
-    b = 1
-    while b < n:
-        other = lax.ppermute(jnp.stack([top, total]), axis, [(c, c ^ b) for c in range(n)])
-        other_top, other_total = other[0], other[1]
-        new_top = jnp.maximum(top, other_top)
-        total = total * jnp.exp(top - new_top) + other_total * jnp.exp(other_top - new_top)
+    me = lax.axis_index(axis)
+    lo = me % n_lo
+    packed = jnp.stack([top, total])
+    got = [packed]
+    for k in range(1, n_lo):
+        perm = [(a * n_lo + l, a * n_lo + (l + k) % n_lo) for a in range(n_hi) for l in range(n_lo)]
+        got.append(lax.ppermute(packed, axis, perm))
+    rev = jnp.stack(got[::-1])
+    ordered = lax.dynamic_slice_in_dim(jnp.concatenate([rev, rev], axis=0), (n_lo - 1) - lo, n_lo, axis=0)
+    top = jnp.max(ordered[:, 0, :], axis=0)
+    total = jnp.sum(ordered[:, 1, :] * jnp.exp(ordered[:, 0, :] - top[None, :]), axis=0)
+    b = n_lo
+    while b < n_hi * n_lo:
+        other = lax.ppermute(
+            jnp.stack([top, total]), axis, [(c, c ^ b) for c in range(n_hi * n_lo)]
+        )
+        new_top = jnp.maximum(top, other[0])
+        total = total * jnp.exp(top - new_top) + other[1] * jnp.exp(other[0] - new_top)
         top = new_top
         b *= 2
     return top, total
@@ -85,8 +97,10 @@
     logits = lax.dot_general(
         normed_t, head_weight, (((0,), (0,)), ((), ())), preferred_element_type=jnp.float32
     )
-    row_top, row_total = butterfly_softmax_stats(
-        jnp.max(logits, axis=1), logits, "tensor", n_tensor
+    n_lo = 4 if n_tensor % 4 == 0 else n_tensor
+    n_hi = n_tensor // n_lo
+    row_top, row_total = group_softmax_stats(
+        jnp.max(logits, axis=1), logits, "tensor", n_hi, n_lo
     )
     log_total = row_top + jnp.log(row_total)
     offset = lax.axis_index("tensor") * vocab_rows
@@ -108,8 +122,6 @@
     inner_part = jnp.sum(partial * (norm_gain[:, None] * normalized_t), axis=0)
     gain_part = jnp.sum(partial * normalized_t, axis=1)
 
-    n_lo = 4 if n_tensor % 4 == 0 else n_tensor
-    n_hi = n_tensor // n_lo
     gain_rows = -(-local_cols // tokens)
     gain_chunks = jnp.pad(
         gain_part.reshape(n_tensor, local_cols), ((0, 0), (0, gain_rows * tokens - local_cols))

time: 267 us -> 269 us (level)
  waiting for transfers between devices: 123 us -> 134 us
  starting transfers between devices: 60.6 us -> 50.9 us
  local copies, waits for them, and re-layouts: 19.4 us -> 23.3 us
    ppermute x5, starting transfers between devices: 14.9 us -> 8.61 us  [butterfly_sum(): x = x + lax.ppermute(x, axis, [(c, c ^ b) for c in range(n)])]
    ppermute x4, waiting for transfers between devices: 47.7 us -> 53.6 us  [two_stage_reduce_scatter(): mine = mine + lax.ppermute(other, axis, perm_h)]
    ppermute x4, starting transfers between devices: 9.28 us -> 4.84 us  [two_stage_reduce_scatter(): mine = mine + lax.ppermute(other, axis, perm_h)]
    ppermute x3, waiting for transfers between devices: 16.7 us -> 20.2 us  [two_stage_reduce_scatter(): recv_b = lax.ppermute(send_b, axis, perm_b)]
    unnamed x43 -> x49, local copies, waits for them, and re-layouts: 13.2 us -> 14.4 us
    ppermute x3 -> x4, starting transfers between devices: 16.2 us -> 16.4 us  [the longest x3 14.3 us: group_softmax_stats(): got.append(lax.ppermute(packed, axis, perm))]
  transfers between devices with their start and end apart: 26 -> 27, of which waited for: 18 -> 16; matrix products, arithmetic and copies ran while one was open for 12% -> 12% of each run, Pallas kernels for 0% -> 0%
where the time goes in v7:
time: 269 us; the launch traced here: 268 us
  waiting for transfers between devices  134 us (50%)
  starting transfers between devices  50.9 us (19%)
  local copies, waits for them, and re-layouts  23.3 us (9%)
  other arithmetic  23 us (9%)
  matrix products  22.2 us (8%)
  between operations  14.5 us (5%)
    ppermute x4, waiting for transfers between devices, two_stage_reduce_scatter(): mine = mine + lax.ppermute(other, axis, perm_h)  53.6 us
    ppermute x7, waiting for transfers between devices, shift_gather(): got.append(lax.ppermute(x, axis, [(c, (c + k) % n) for c in range(n)]))  35.9 us
    ppermute x3, waiting for transfers between devices, two_stage_reduce_scatter(): recv_b = lax.ppermute(send_b, axis, perm_b)  20.2 us
    ppermute x3, waiting for transfers between devices, two_stage_reduce_scatter(): recv_f = lax.ppermute(send_f, axis, perm_f)  15.7 us
    unnamed x49, local copies, waits for them, and re-layouts  14.4 us
    ppermute x3, starting transfers between devices, group_softmax_stats(): got.append(lax.ppermute(packed, axis, perm))  14.3 us
    ppermute x7, starting transfers between devices, shift_gather(): got.append(lax.ppermute(x, axis, [(c, (c + k) % n) for c in range(n)]))  11.3 us
    dot_general x1, matrix products, shards(): lax.dot_general(head_weight.reshape(n_tensor, local_cols, vocab_rows), jn...  9.14 us
  transfers between devices with their start and end apart: 27, of which 16 were waited for; matrix products, arithmetic and copies ran while one was open for 12% of the time, Pallas kernels for 0%

profile of v7, /device:TPU:1, one launch (start us, length us, event | category | flops | bytes accessed | tf_op | source)
XLA Modules:
  0.0 267.9 jit_solution(13612299860804582843)
XLA Ops:
  7.2 6.1 %collective-permute-start = (bf16[576,384]{1,0:T(8,128)(2,1)}, bf16[576,384]{1,0:T(8,128)(2,1)S(1)}, u32[]{:S(2)}, u32[]{:S(2)}) collective-permute-start(bf16[576,384]{1,0:T(8,128)(2,1)} %bitcast.106), channel_id=1, source_target_pairs={{0,7},{1,0},{2,1},{3,2},{4,3},{5,4},{6,5},{7,6},{8,15},{9,8},{10,9... | collective-permute-start | bytes 1327112 | tf_op jit(solution)/shard_map/ppermute | solution.py:13
  18.3 10.5 %collective-permute-done = bf16[576,384]{1,0:T(8,128)(2,1)S(1)} collective-permute-done((bf16[576,384]{1,0:T(8,128)(2,1)}, bf16[576,384]{1,0:T(8,128)(2,1)S(1)}, u32[]{:S(2)}, u32[]{:S(2)}) %collective-permute-start) | collective-permute-done | bytes 442400 | tf_op jit(solution)/shard_map/ppermute | solution.py:13
  28.8 15.9 %collective-permute-done.1 = bf16[576,384]{1,0:T(8,128)(2,1)S(1)} collective-permute-done((bf16[576,384]{1,0:T(8,128)(2,1)}, bf16[576,384]{1,0:T(8,128)(2,1)S(1)}, u32[]{:S(2)}, u32[]{:S(2)}) %collective-permute-start.1) | collective-permute-done | bytes 442400 | tf_op jit(solution)/shard_map/ppermute | solution.py:13
  45.1 5.6 %collective-permute-done.2 = bf16[576,384]{1,0:T(8,128)(2,1)S(1)} collective-permute-done((bf16[576,384]{1,0:T(8,128)(2,1)}, bf16[576,384]{1,0:T(8,128)(2,1)S(1)}, u32[]{:S(2)}, u32[]{:S(2)}) %collective-permute-start.2) | collective-permute-done | bytes 442400 | tf_op jit(solution)/shard_map/ppermute | solution.py:13
  50.7 3.9 %collective-permute-done.3 = bf16[576,384]{1,0:T(8,128)(2,1)S(1)} collective-permute-done((bf16[576,384]{1,0:T(8,128)(2,1)}, bf16[576,384]{1,0:T(8,128)(2,1)S(1)}, u32[]{:S(2)}, u32[]{:S(2)}) %collective-permute-start.3) | collective-permute-done | bytes 442400 | tf_op jit(solution)/shard_map/ppermute | solution.py:13
  62.9 3.9 %fusion.18 = (f32[384]{0:T(512)S(1)}, f32[384,1024]{1,0:T(8,128)S(1)}) fusion(bf16[4608,384]{1,0:T(8,128)(2,1)S(1)} %fusion.3, bf16[4608,1024]{1,0:T(8,128)(2,1)S(1)} %bitcast.103), kind=kOutput, calls=%fused_computation.75 | convolution fusion | flops 3624271360 | bytes 14550528 | tf_op jit(solution)/shard_map/dot_general | solution.py:97
  70.5 11.5 %collective-permute-start.8 = (f32[2,384]{1,0:T(2,128)S(1)}, f32[2,384]{1,0:T(2,128)S(1)}, u32[]{:S(2)}, u32[]{:S(2)}) collective-permute-start(f32[2,384]{1,0:T(2,128)S(1)} %pad_maximum_fusion.5), channel_id=1, source_target_pairs={{0,2},{1,3},{2,0},{3,1},{4,6},{5,7},{6,4},{7,5},{8,10},{9,11},{10,... | collective-permute-start | bytes 9224 | tf_op jit(solution)/shard_map/ppermute | solution.py:35
  94.9 9.1 %fusion.19 = f32[4608,1024]{1,0:T(8,128)} fusion(bf16[4608,384]{1,0:T(8,128)(2,1)S(1)} %fusion.3, bf16[384,1024]{1,0:T(8,128)(2,1)S(1)} %subtract_convert_fusion), kind=kOutput, calls=%fused_computation.76 | convolution fusion | flops 3623878656 | bytes 23199744 | tf_op jit(solution)/shard_map/dot_general | solution.py:111
  105.2 9.1 %fusion.1 = (f32[384]{0:T(512)S(1)}, f32[8,576]{1,0:T(8,128)}, f32[8,384,576]{1,2,0:T(8,128)S(1)}) fusion(f32[8,576]{1,0:T(8,128)S(1)} %mul.113, f32[384]{0:T(512)S(1)} %copy-done.11, bf16[16,576,384]{2,1,0:T(8,128)(2,1)} %copy-done.3, s32[]{:T(128)S(6)} %select_n.84, bf16[8,576,1024]{2,1,0:T(8,128)(2,1)} %bitcast.101, bf16[384,1024]{1,0:T(8,128)(2,1)S(1)} %copy-done.7), kind=kOutput, calls=%fused_computation.3 | convolution fusion | flops 3636259840 | bytes 20880388 | tf_op jit(solution)/shard_map/dot_general | solution.py:116
  114.3 2.9 %copy-done = f32[8,384,576]{1,2,0:T(8,128)} copy-done((f32[8,384,576]{1,2,0:T(8,128)}, f32[8,384,576]{1,2,0:T(8,128)S(1)}, u32[]{:S(2)}) %copy-start) | copy-done | bytes 7077912
  129.4 7.3 %collective-permute-done.11 = f32[2,288,384]{2,1,0:T(8,128)} collective-permute-done((f32[2,288,384]{2,1,0:T(8,128)}, f32[2,288,384]{2,1,0:T(8,128)}, u32[]{:S(2)}, u32[]{:S(2)}) %collective-permute-start.11) | collective-permute-done | bytes 884768 | tf_op jit(solution)/shard_map/ppermute | solution.py:69
  138.8 5.8 %collective-permute-done.16 = f32[2,296,384]{2,1,0:T(8,128)} collective-permute-done((f32[2,296,384]{2,1,0:T(8,128)}, f32[2,296,384]{2,1,0:T(8,128)}, u32[]{:S(2)}, u32[]{:S(2)}) %collective-permute-start.16) | collective-permute-done | bytes 909344 | tf_op jit(solution)/shard_map/ppermute | solution.py:70
  147.1 3.4 %collective-permute-start.17 = (f32[2,296,384]{2,1,0:T(8,128)}, f32[2,296,384]{2,1,0:T(8,128)}, u32[]{:S(2)}, u32[]{:S(2)}) collective-permute-start(f32[2,296,384]{2,1,0:T(8,128)} %bitcast_add_fusion), channel_id=1, source_target_pairs={{0,3},{1,0},{2,1},{3,2},{4,7},{5,4},{6,5},{7,6},{8,11},{9,8},{10,9... | collective-permute-start | bytes 2727944 | tf_op jit(solution)/shard_map/ppermute | solution.py:70
  150.6 5.5 %collective-permute-done.12 = f32[2,288,384]{2,1,0:T(8,128)} collective-permute-done((f32[2,288,384]{2,1,0:T(8,128)}, f32[2,288,384]{2,1,0:T(8,128)}, u32[]{:S(2)}, u32[]{:S(2)}) %collective-permute-start.12) | collective-permute-done | bytes 884768 | tf_op jit(solution)/shard_map/ppermute | solution.py:69
  158.2 6.7 %collective-permute-done.17 = f32[2,296,384]{2,1,0:T(8,128)} collective-permute-done((f32[2,296,384]{2,1,0:T(8,128)}, f32[2,296,384]{2,1,0:T(8,128)}, u32[]{:S(2)}, u32[]{:S(2)}) %collective-permute-start.17) | collective-permute-done | bytes 909344 | tf_op jit(solution)/shard_map/ppermute | solution.py:70
  167.4 3.4 %collective-permute-start.18 = (f32[2,296,384]{2,1,0:T(8,128)}, f32[2,296,384]{2,1,0:T(8,128)}, u32[]{:S(2)}, u32[]{:S(2)}) collective-permute-start(f32[2,296,384]{2,1,0:T(8,128)} %bitcast_add_fusion.1), channel_id=1, source_target_pairs={{0,3},{1,0},{2,1},{3,2},{4,7},{5,4},{6,5},{7,6},{8,11},{9,8},{10,9... | collective-permute-start | bytes 2727944 | tf_op jit(solution)/shard_map/ppermute | solution.py:70
  171.6 3.0 %collective-permute-done.13 = f32[2,288,384]{2,1,0:T(8,128)} collective-permute-done((f32[2,288,384]{2,1,0:T(8,128)}, f32[2,288,384]{2,1,0:T(8,128)}, u32[]{:S(2)}, u32[]{:S(2)}) %collective-permute-start.13) | collective-permute-done | bytes 884768 | tf_op jit(solution)/shard_map/ppermute | solution.py:69
  176.5 7.7 %collective-permute-done.18 = f32[2,296,384]{2,1,0:T(8,128)} collective-permute-done((f32[2,296,384]{2,1,0:T(8,128)}, f32[2,296,384]{2,1,0:T(8,128)}, u32[]{:S(2)}, u32[]{:S(2)}) %collective-permute-start.18) | collective-permute-done | bytes 909344 | tf_op jit(solution)/shard_map/ppermute | solution.py:70
  190.3 22.1 %collective-permute-done.20 = f32[152,384]{1,0:T(8,128)S(1)} collective-permute-done((f32[152,384]{1,0:T(8,128)S(1)}, f32[152,384]{1,0:T(8,128)S(1)}, u32[]{:S(2)}, u32[]{:S(2)}) %collective-permute-start.20) | collective-permute-done | bytes 233504 | tf_op jit(solution)/shard_map/ppermute | solution.py:81
  212.5 2.8 %collective-permute-done.21 = f32[576]{0:T(1024)S(1)} collective-permute-done((f32[576]{0:T(1024)S(1)}, f32[576]{0:T(1024)S(1)}, u32[]{:S(2)}, u32[]{:S(2)}) %collective-permute-start.21) | collective-permute-done | bytes 2336 | tf_op jit(solution)/shard_map/ppermute | solution.py:22
  215.4 14.3 %collective-permute-done.14 = f32[144,384]{1,0:T(8,128)S(1)} collective-permute-done((f32[144,384]{1,0:T(8,128)S(1)}, f32[144,384]{1,0:T(8,128)S(1)}, u32[]{:S(2)}, u32[]{:S(2)}) %collective-permute-start.14) | collective-permute-done | bytes 221216 | tf_op jit(solution)/shard_map/ppermute | solution.py:81
  229.8 17.2 %collective-permute-done.19 = f32[144,384]{1,0:T(8,128)S(1)} collective-permute-done((f32[144,384]{1,0:T(8,128)S(1)}, f32[144,384]{1,0:T(8,128)S(1)}, u32[]{:S(2)}, u32[]{:S(2)}) %collective-permute-start.19) | collective-permute-done | bytes 221216 | tf_op jit(solution)/shard_map/ppermute | solution.py:81
  247.2 3.9 %collective-permute-done.24 = f32[576]{0:T(1024)S(1)} collective-permute-done((f32[576]{0:T(1024)S(1)}, f32[576]{0:T(1024)S(1)}, u32[]{:S(2)}, u32[]{:S(2)}) %collective-permute-start.24) | collective-permute-done | bytes 2336 | tf_op jit(solution)/shard_map/ppermute | solution.py:22
  251.0 8.3 %collective-permute-start.25 = (f32[576]{0:T(1024)S(1)}, f32[576]{0:T(1024)S(1)}, u32[]{:S(2)}, u32[]{:S(2)}) collective-permute-start(f32[576]{0:T(1024)S(1)} %add.225), channel_id=1, source_target_pairs={{0,8},{8,0},{1,9},{9,1},{2,10},{10,2},{3,11},{11,3},{4,12},{12,4},... | collective-permute-start | bytes 6920 | tf_op jit(solution)/shard_map/ppermute | solution.py:22
  (143 shorter events, 63.5 us)
Async XLA Ops:
  7.2 253.9 %reduce-scatter.2.cloned.1.call-start = ((), (), s32[]{:S(2)}) async-start(), calls=%async_computation.1 | async-start | bytes 19464192 | tf_op jit(solution)/shard_map/reduce_scatter | solution.py:114
  7.2 21.6 %collective-permute-start = (bf16[576,384]{1,0:T(8,128)(2,1)}, bf16[576,384]{1,0:T(8,128)(2,1)S(1)}, u32[]{:S(2)}, u32[]{:S(2)}) collective-permute-start(bf16[576,384]{1,0:T(8,128)(2,1)} %bitcast.106), channel_id=1, source_target_pairs={{0,7},{1,0},{2,1},{3,2},{4,3},{5,4},{6,5},{7,6},{8,15},{9,8},{10,9... | collective-permute-start | bytes 1327112 | tf_op jit(solution)/shard_map/ppermute | solution.py:13
  13.3 31.4 %collective-permute-start.1 = (bf16[576,384]{1,0:T(8,128)(2,1)}, bf16[576,384]{1,0:T(8,128)(2,1)S(1)}, u32[]{:S(2)}, u32[]{:S(2)}) collective-permute-start(bf16[576,384]{1,0:T(8,128)(2,1)} %bitcast.107), channel_id=1, source_target_pairs={{0,6},{1,7},{2,0},{3,1},{4,2},{5,3},{6,4},{7,5},{8,14},{9,15},{10,... | collective-permute-start | bytes 1327112 | tf_op jit(solution)/shard_map/ppermute | solution.py:13
  13.7 41.2 %collective-permute-start.6 = (bf16[576,384]{1,0:T(8,128)(2,1)}, bf16[576,384]{1,0:T(8,128)(2,1)S(1)}, u32[]{:S(2)}, u32[]{:S(2)}) collective-permute-start(bf16[576,384]{1,0:T(8,128)(2,1)} %bitcast.108), channel_id=1, source_target_pairs={{0,1},{1,2},{2,3},{3,4},{4,5},{5,6},{6,7},{7,0},{8,9},{9,10},{10,1... | collective-permute-start | bytes 1327112 | tf_op jit(solution)/shard_map/ppermute | solution.py:13
  14.4 40.4 %collective-permute-start.5 = (bf16[576,384]{1,0:T(8,128)(2,1)}, bf16[576,384]{1,0:T(8,128)(2,1)S(1)}, u32[]{:S(2)}, u32[]{:S(2)}) collective-permute-start(bf16[576,384]{1,0:T(8,128)(2,1)} %bitcast.109), channel_id=1, source_target_pairs={{0,2},{1,3},{2,4},{3,5},{4,6},{5,7},{6,0},{7,1},{8,10},{9,11},{10,... | collective-permute-start | bytes 1327112 | tf_op jit(solution)/shard_map/ppermute | solution.py:13
  16.3 38.4 %collective-permute-start.4 = (bf16[576,384]{1,0:T(8,128)(2,1)}, bf16[576,384]{1,0:T(8,128)(2,1)S(1)}, u32[]{:S(2)}, u32[]{:S(2)}) collective-permute-start(bf16[576,384]{1,0:T(8,128)(2,1)} %bitcast.110), channel_id=1, source_target_pairs={{0,3},{1,4},{2,5},{3,6},{4,7},{5,0},{6,1},{7,2},{8,11},{9,12},{10,... | collective-permute-start | bytes 1327112 | tf_op jit(solution)/shard_map/ppermute | solution.py:13
  28.8 21.9 %collective-permute-start.2 = (bf16[576,384]{1,0:T(8,128)(2,1)}, bf16[576,384]{1,0:T(8,128)(2,1)S(1)}, u32[]{:S(2)}, u32[]{:S(2)}) collective-permute-start(bf16[576,384]{1,0:T(8,128)(2,1)} %bitcast.111), channel_id=1, source_target_pairs={{0,5},{1,6},{2,7},{3,0},{4,1},{5,2},{6,3},{7,4},{8,13},{9,14},{10,... | collective-permute-start | bytes 1327112 | tf_op jit(solution)/shard_map/ppermute | solution.py:13
  44.8 9.8 %collective-permute-start.3 = (bf16[576,384]{1,0:T(8,128)(2,1)}, bf16[576,384]{1,0:T(8,128)(2,1)S(1)}, u32[]{:S(2)}, u32[]{:S(2)}) collective-permute-start(bf16[576,384]{1,0:T(8,128)(2,1)} %bitcast.112), channel_id=1, source_target_pairs={{0,4},{1,5},{2,6},{3,7},{4,0},{5,1},{6,2},{7,3},{8,12},{9,13},{10,... | collective-permute-start | bytes 1327112 | tf_op jit(solution)/shard_map/ppermute | solution.py:13
  68.4 14.3 %collective-permute-start.9 = (f32[2,384]{1,0:T(2,128)S(1)}, f32[2,384]{1,0:T(2,128)S(1)}, u32[]{:S(2)}, u32[]{:S(2)}) collective-permute-start(f32[2,384]{1,0:T(2,128)S(1)} %pad_maximum_fusion.5), channel_id=1, source_target_pairs={{0,1},{1,2},{2,3},{3,0},{4,5},{5,6},{6,7},{7,4},{8,9},{9,10},{10,1... | collective-permute-start | bytes 9224 | tf_op jit(solution)/shard_map/ppermute | solution.py:35
  70.5 13.5 %collective-permute-start.8 = (f32[2,384]{1,0:T(2,128)S(1)}, f32[2,384]{1,0:T(2,128)S(1)}, u32[]{:S(2)}, u32[]{:S(2)}) collective-permute-start(f32[2,384]{1,0:T(2,128)S(1)} %pad_maximum_fusion.5), channel_id=1, source_target_pairs={{0,2},{1,3},{2,0},{3,1},{4,6},{5,7},{6,4},{7,5},{8,10},{9,11},{10,... | collective-permute-start | bytes 9224 | tf_op jit(solution)/shard_map/ppermute | solution.py:35
  88.1 4.0 %collective-permute-start.10 = (f32[2,384]{1,0:T(2,128)S(1)}, f32[2,384]{1,0:T(2,128)S(1)}, u32[]{:S(2)}, u32[]{:S(2)}) collective-permute-start(f32[2,384]{1,0:T(2,128)S(1)} %pad_maximum_fusion.6), channel_id=1, source_target_pairs={{0,4},{1,5},{2,6},{3,7},{4,0},{5,1},{6,2},{7,3},{8,12},{9,13},{10,... | collective-permute-start | bytes 9224 | tf_op jit(solution)/shard_map/ppermute | solution.py:42
  118.5 18.2 %collective-permute-start.11 = (f32[2,288,384]{2,1,0:T(8,128)}, f32[2,288,384]{2,1,0:T(8,128)}, u32[]{:S(2)}, u32[]{:S(2)}) collective-permute-start(f32[2,288,384]{2,1,0:T(8,128)} %dynamic-slice_bitcast_fusion.1), channel_id=1, source_target_pairs={{0,1},{1,2},{2,3},{3,0},{4,5},{5,6},{6,7},{7,4},{8,9},{9,10},{10,1... | collective-permute-start | bytes 2654216 | tf_op jit(solution)/shard_map/ppermute | solution.py:69
  127.2 17.4 %collective-permute-start.16 = (f32[2,296,384]{2,1,0:T(8,128)}, f32[2,296,384]{2,1,0:T(8,128)}, u32[]{:S(2)}, u32[]{:S(2)}) collective-permute-start(f32[2,296,384]{2,1,0:T(8,128)} %dynamic-slice_bitcast_fusion), channel_id=1, source_target_pairs={{0,3},{1,0},{2,1},{3,2},{4,7},{5,4},{6,5},{7,6},{8,11},{9,8},{10,9... | collective-permute-start | bytes 2727944 | tf_op jit(solution)/shard_map/ppermute | solution.py:70
  138.8 17.2 %collective-permute-start.12 = (f32[2,288,384]{2,1,0:T(8,128)}, f32[2,288,384]{2,1,0:T(8,128)}, u32[]{:S(2)}, u32[]{:S(2)}) collective-permute-start(f32[2,288,384]{2,1,0:T(8,128)} %bitcast_add_fusion.3), channel_id=1, source_target_pairs={{0,1},{1,2},{2,3},{3,0},{4,5},{5,6},{6,7},{7,4},{8,9},{9,10},{10,1... | collective-permute-start | bytes 2654216 | tf_op jit(solution)/shard_map/ppermute | solution.py:69
  147.1 17.8 %collective-permute-start.17 = (f32[2,296,384]{2,1,0:T(8,128)}, f32[2,296,384]{2,1,0:T(8,128)}, u32[]{:S(2)}, u32[]{:S(2)}) collective-permute-start(f32[2,296,384]{2,1,0:T(8,128)} %bitcast_add_fusion), channel_id=1, source_target_pairs={{0,3},{1,0},{2,1},{3,2},{4,7},{5,4},{6,5},{7,6},{8,11},{9,8},{10,9... | collective-permute-start | bytes 2727944 | tf_op jit(solution)/shard_map/ppermute | solution.py:70
  158.2 16.3 %collective-permute-start.13 = (f32[2,288,384]{2,1,0:T(8,128)}, f32[2,288,384]{2,1,0:T(8,128)}, u32[]{:S(2)}, u32[]{:S(2)}) collective-permute-start(f32[2,288,384]{2,1,0:T(8,128)} %bitcast_add_fusion.4), channel_id=1, source_target_pairs={{0,1},{1,2},{2,3},{3,0},{4,5},{5,6},{6,7},{7,4},{8,9},{9,10},{10,1... | collective-permute-start | bytes 2654216 | tf_op jit(solution)/shard_map/ppermute | solution.py:69
  167.4 16.8 %collective-permute-start.18 = (f32[2,296,384]{2,1,0:T(8,128)}, f32[2,296,384]{2,1,0:T(8,128)}, u32[]{:S(2)}, u32[]{:S(2)}) collective-permute-start(f32[2,296,384]{2,1,0:T(8,128)} %bitcast_add_fusion.1), channel_id=1, source_target_pairs={{0,3},{1,0},{2,1},{3,2},{4,7},{5,4},{6,5},{7,6},{8,11},{9,8},{10,9... | collective-permute-start | bytes 2727944 | tf_op jit(solution)/shard_map/ppermute | solution.py:70
  175.9 36.6 %collective-permute-start.15 = (f32[144,384]{1,0:T(8,128)S(1)}, f32[144,384]{1,0:T(8,128)S(1)}, u32[]{:S(2)}, u32[]{:S(2)}) collective-permute-start(f32[144,384]{1,0:T(8,128)S(1)} %dynamic-slice_bitcast_fusion.4), channel_id=1, source_target_pairs={{0,4},{1,5},{2,6},{3,7},{4,0},{5,1},{6,2},{7,3},{8,12},{9,13},{10,... | collective-permute-start | bytes 663560 | tf_op jit(solution)/shard_map/ppermute | solution.py:81
  185.9 26.5 %collective-permute-start.20 = (f32[152,384]{1,0:T(8,128)S(1)}, f32[152,384]{1,0:T(8,128)S(1)}, u32[]{:S(2)}, u32[]{:S(2)}) collective-permute-start(f32[152,384]{1,0:T(8,128)S(1)} %dynamic-slice_bitcast_fusion.2), channel_id=1, source_target_pairs={{0,4},{1,5},{2,6},{3,7},{4,0},{5,1},{6,2},{7,3},{8,12},{9,13},{10,... | collective-permute-start | bytes 700424 | tf_op jit(solution)/shard_map/ppermute | solution.py:81
  187.0 42.6 %collective-permute-start.14 = (f32[144,384]{1,0:T(8,128)S(1)}, f32[144,384]{1,0:T(8,128)S(1)}, u32[]{:S(2)}, u32[]{:S(2)}) collective-permute-start(f32[144,384]{1,0:T(8,128)S(1)} %dynamic-slice_bitcast_fusion.5), channel_id=1, source_target_pairs={{0,4},{1,5},{2,6},{3,7},{4,0},{5,1},{6,2},{7,3},{8,12},{9,13},{10,... | collective-permute-start | bytes 663560 | tf_op jit(solution)/shard_map/ppermute | solution.py:81
  189.1 57.9 %collective-permute-start.19 = (f32[144,384]{1,0:T(8,128)S(1)}, f32[144,384]{1,0:T(8,128)S(1)}, u32[]{:S(2)}, u32[]{:S(2)}) collective-permute-start(f32[144,384]{1,0:T(8,128)S(1)} %dynamic-slice_bitcast_fusion.3), channel_id=1, source_target_pairs={{0,4},{1,5},{2,6},{3,7},{4,0},{5,1},{6,2},{7,3},{8,12},{9,13},{10,... | collective-permute-start | bytes 663560 | tf_op jit(solution)/shard_map/ppermute | solution.py:81
  215.3 14.3 %collective-permute-start.22 = (f32[576]{0:T(1024)S(1)}, f32[576]{0:T(1024)S(1)}, u32[]{:S(2)}, u32[]{:S(2)}) collective-permute-start(f32[576]{0:T(1024)S(1)} %slice_add_fusion), channel_id=1, source_target_pairs={{0,32},{16,48},{32,0},{48,16},{64,96},{80,112},{96,64},{112,80},{1... | collective-permute-start | bytes 6920 | tf_op jit(solution)/shard_map/ppermute | solution.py:22
  229.7 17.3 %collective-permute-start.23 = (f32[576]{0:T(1024)S(1)}, f32[576]{0:T(1024)S(1)}, u32[]{:S(2)}, u32[]{:S(2)}) collective-permute-start(f32[576]{0:T(1024)S(1)} %add.223), channel_id=1, source_target_pairs={{0,64},{16,80},{32,96},{48,112},{64,0},{80,16},{96,32},{112,48},{1... | collective-permute-start | bytes 6920 | tf_op jit(solution)/shard_map/ppermute | solution.py:22
  251.0 9.5 %collective-permute-start.25 = (f32[576]{0:T(1024)S(1)}, f32[576]{0:T(1024)S(1)}, u32[]{:S(2)}, u32[]{:S(2)}) collective-permute-start(f32[576]{0:T(1024)S(1)} %add.225), channel_id=1, source_target_pairs={{0,8},{8,0},{1,9},{9,1},{2,10},{10,2},{3,11},{11,3},{4,12},{12,4},... | collective-permute-start | bytes 6920 | tf_op jit(solution)/shard_map/ppermute | solution.py:22
  (20 other events, 189.8 us)
Sparse Core Ops, SparseCore 0:
  104.2 151.8 reduce-scatter.1

commit v8 on v5

--- a/solution.py
+++ b/solution.py
@@ -14,6 +14,31 @@
     rev = jnp.stack(got[::-1])
     doubled = jnp.concatenate([rev, rev], axis=0)
     return lax.dynamic_slice_in_dim(doubled, (n - 1) - me, n, axis=0)
+
+
+def grid_gather(x, axis, n_hi, n_lo):
+    me = lax.axis_index(axis)
+    h = me // n_lo
+    lo = me % n_lo
+    got = {}
+    offsets = [(a, b) for a in range(n_hi) for b in range(n_lo) if (a, b) != (0, 0)]
+    offsets.sort(key=lambda o: -o[0])
+    for a, b in offsets:
+        perm = [
+            (p * n_lo + q, ((p + a) % n_hi) * n_lo + (q + b) % n_lo)
+            for p in range(n_hi)
+            for q in range(n_lo)
+        ]
+        got[(a, b)] = lax.ppermute(x, axis, perm)
+    got[(0, 0)] = x
+    rev = jnp.stack(
+        [jnp.stack([got[(n_hi - 1 - a, n_lo - 1 - b)] for b in range(n_lo)]) for a in range(n_hi)]
+    )
+    doubled = jnp.concatenate([rev, rev], axis=0)
+    doubled = jnp.concatenate([doubled, doubled], axis=1)
+    ordered = lax.dynamic_slice_in_dim(doubled, (n_hi - 1) - h, n_hi, axis=0)
+    ordered = lax.dynamic_slice_in_dim(ordered, (n_lo - 1) - lo, n_lo, axis=1)
+    return ordered.reshape((n_hi * n_lo,) + x.shape)
 
 
 def butterfly_sum(x, axis, n):
@@ -76,7 +101,9 @@
     width, vocab_rows = head_weight.shape
     n_tensor = width // local_cols
     n_outer = lax.psum(1, "outer")
-    blocks = shift_gather(hidden_input_state.T, "tensor", n_tensor)
+    n_lo = 4 if n_tensor % 4 == 0 else n_tensor
+    n_hi = n_tensor // n_lo
+    blocks = grid_gather(hidden_input_state.T, "tensor", n_hi, n_lo)
     values_t = blocks.reshape(width, tokens).astype(jnp.float32)
     scaled = lax.rsqrt(jnp.mean(values_t * values_t, axis=0) + epsilon)
     scaled_rows = scaled[:, None]
@@ -108,8 +135,6 @@
     inner_part = jnp.sum(partial * (norm_gain[:, None] * normalized_t), axis=0)
     gain_part = jnp.sum(partial * normalized_t, axis=1)
 
-    n_lo = 4 if n_tensor % 4 == 0 else n_tensor
-    n_hi = n_tensor // n_lo
     gain_rows = -(-local_cols // tokens)
     gain_chunks = jnp.pad(
         gain_part.reshape(n_tensor, local_cols), ((0, 0), (0, gain_rows * tokens - local_cols))

time: 267 us -> 264 us (0.989)
  starting transfers between devices: 60.6 us -> 46.9 us
  other arithmetic: 24.2 us -> 35 us
  waiting for transfers between devices: 123 us -> 130 us
  local copies, waits for them, and re-layouts: 19.4 us -> 13.9 us
    ppermute x3, starting transfers between devices: 16.2 us -> 6.78 us  [butterfly_softmax_stats(): lax.ppermute(jnp.stack([top, total]), axis, [(c, c ^ b) for c in range(n)])]
    ppermute x3, waiting for transfers between devices: 16.7 us -> 25.8 us  [two_stage_reduce_scatter(): recv_b = lax.ppermute(send_b, axis, perm_b)]
    ppermute x4, starting transfers between devices: 9.28 us -> 3.58 us  [two_stage_reduce_scatter(): mine = mine + lax.ppermute(other, axis, perm_h)]
    unnamed x43 -> x28, local copies, waits for them, and re-layouts: 13.2 us -> 7.71 us
    ppermute x3, waiting for transfers between devices: 15.2 us -> 11.5 us  [two_stage_reduce_scatter(): recv_f = lax.ppermute(send_f, axis, perm_f)]
    reduce_sum x1, other arithmetic: 0.85 us -> 4.53 us  [shards(): scaled = lax.rsqrt(jnp.mean(values_t * values_t, axis=0) + epsilon)]
    mul x0 -> x1, other arithmetic: none -> 3.61 us  [shards(): normalized_t = values_t * scaled[None, :]]
    ppermute x7, starting transfers between devices: 11.3 us -> 14.9 us  [grid_gather(): got[a, b] = lax.ppermute(x, axis, perm)]
  transfers between devices with their start and end apart: 26 -> 26, of which waited for: 18 -> 17; matrix products, arithmetic and copies ran while one was open for 12% -> 14% of each run, Pallas kernels for 0% -> 0%
where the time goes in v8:
time: 264 us; the launch traced here: 261 us
  waiting for transfers between devices  130 us (49%)
  starting transfers between devices  46.9 us (18%)
  other arithmetic  35 us (13%)
  matrix products  20.7 us (8%)
  between operations  14.5 us (5%)
  local copies, waits for them, and re-layouts  13.9 us (5%)
    ppermute x4, waiting for transfers between devices, two_stage_reduce_scatter(): mine = mine + lax.ppermute(other, axis, perm_h)  49.1 us
    ppermute x7, waiting for transfers between devices, grid_gather(): got[a, b] = lax.ppermute(x, axis, perm)  33 us
    ppermute x3, waiting for transfers between devices, two_stage_reduce_scatter(): recv_b = lax.ppermute(send_b, axis, perm_b)  25.8 us
    ppermute x7, starting transfers between devices, grid_gather(): got[a, b] = lax.ppermute(x, axis, perm)  14.9 us
    ppermute x5, starting transfers between devices, butterfly_sum(): x = x + lax.ppermute(x, axis, [(c, c ^ b) for c in range(n)])  14.4 us
    ppermute x3, waiting for transfers between devices, two_stage_reduce_scatter(): recv_f = lax.ppermute(send_f, axis, perm_f)  11.5 us
    dot_general x1, matrix products, shards(): lax.dot_general(normed_t, dlogits, (((1,), (0,)), ((), ())), preferred_el...  9.07 us
    unnamed x28, local copies, waits for them, and re-layouts  7.71 us
  transfers between devices with their start and end apart: 26, of which 17 were waited for; matrix products, arithmetic and copies ran while one was open for 14% of the time, Pallas kernels for 0%

profile of v8, /device:TPU:1, one launch (start us, length us, event | category | flops | bytes accessed | tf_op | source)
XLA Modules:
  0.0 261.3 jit_solution(4058230470234433499)
XLA Ops:
  13.1 2.7 %collective-permute-start.3 = (bf16[576,384]{1,0:T(8,128)(2,1)}, bf16[576,384]{1,0:T(8,128)(2,1)S(1)}, u32[]{:S(2)}, u32[]{:S(2)}) collective-permute-start(bf16[576,384]{1,0:T(8,128)(2,1)} %bitcast.84), channel_id=1, source_target_pairs={{0,4},{1,5},{2,6},{3,7},{4,0},{5,1},{6,2},{7,3},{8,12},{9,13},{10,... | collective-permute-start | bytes 1327112 | tf_op jit(solution)/shard_map/ppermute | solution.py:32
  16.2 2.7 %collective-permute-done.6 = bf16[576,384]{1,0:T(8,128)(2,1)S(1)} collective-permute-done((bf16[576,384]{1,0:T(8,128)(2,1)}, bf16[576,384]{1,0:T(8,128)(2,1)S(1)}, u32[]{:S(2)}, u32[]{:S(2)}) %collective-permute-start.6) | collective-permute-done | bytes 442400 | tf_op jit(solution)/shard_map/ppermute | solution.py:32
  18.9 5.9 %collective-permute-start.1 = (bf16[576,384]{1,0:T(8,128)(2,1)}, bf16[576,384]{1,0:T(8,128)(2,1)S(1)}, u32[]{:S(2)}, u32[]{:S(2)}) collective-permute-start(bf16[576,384]{1,0:T(8,128)(2,1)} %bitcast.86), channel_id=1, source_target_pairs={{0,6},{1,7},{2,4},{3,5},{4,2},{5,3},{6,0},{7,1},{8,14},{9,15},{10,... | collective-permute-start | bytes 1327112 | tf_op jit(solution)/shard_map/ppermute | solution.py:32
  24.8 21.4 %collective-permute-done.5 = bf16[576,384]{1,0:T(8,128)(2,1)S(1)} collective-permute-done((bf16[576,384]{1,0:T(8,128)(2,1)}, bf16[576,384]{1,0:T(8,128)(2,1)S(1)}, u32[]{:S(2)}, u32[]{:S(2)}) %collective-permute-start.5) | collective-permute-done | bytes 442400 | tf_op jit(solution)/shard_map/ppermute | solution.py:32
  47.6 8.9 %collective-permute-done = bf16[576,384]{1,0:T(8,128)(2,1)S(1)} collective-permute-done((bf16[576,384]{1,0:T(8,128)(2,1)}, bf16[576,384]{1,0:T(8,128)(2,1)S(1)}, u32[]{:S(2)}, u32[]{:S(2)}) %collective-permute-start) | collective-permute-done | bytes 442400 | tf_op jit(solution)/shard_map/ppermute | solution.py:32
  56.8 4.5 %multiply_reduce_fusion = (f32[384]{0:T(512)S(1)}, f32[2,4,576,384]{3,2,1,0:T(8,128)S(1)}) fusion(s32[]{:T(128)S(6)} %select_n.91, s32[]{:T(128)S(6)} %select_n.94, bf16[1,4,576,384]{3,2,1,0:T(8,128)(2,1)S(1)} %maximum_bitcast_fusion.1, bf16[1,4,576,384]{3,2,1,0:T(8,128)(2,1)S(1)} %maximum_bitcast_fusion), kind=kLoop, calls=%fused_computation.16 | loop fusion | flops 17694336 | bytes 10618376 | tf_op jit(solution)/shard_map/reduce_sum | solution.py:108
  64.2 4.0 %fusion.28 = (f32[384]{0:T(512)S(1)}, f32[384,1024]{1,0:T(8,128)S(1)}) fusion(bf16[4608,384]{1,0:T(8,128)(2,1)S(1)} %fusion.3, bf16[4608,1024]{1,0:T(8,128)(2,1)S(1)} %bitcast.80), kind=kOutput, calls=%fused_computation.87 | convolution fusion | flops 3624271360 | bytes 14550528 | tf_op jit(solution)/shard_map/dot_general | solution.py:112
  79.2 4.1 %collective-permute-start.9 = (f32[2,384]{1,0:T(2,128)S(1)}, f32[2,384]{1,0:T(2,128)S(1)}, u32[]{:S(2)}, u32[]{:S(2)}) collective-permute-start(f32[2,384]{1,0:T(2,128)S(1)} %pad_maximum_fusion.7), channel_id=1, source_target_pairs={{0,4},{1,5},{2,6},{3,7},{4,0},{5,1},{6,2},{7,3},{8,12},{9,13},{10,... | collective-permute-start | bytes 9224 | tf_op jit(solution)/shard_map/ppermute | solution.py:56
  87.7 9.1 %fusion.29 = f32[4608,1024]{1,0:T(8,128)} fusion(bf16[4608,384]{1,0:T(8,128)(2,1)S(1)} %fusion.3, bf16[384,1024]{1,0:T(8,128)(2,1)S(1)} %subtract_convert_fusion), kind=kOutput, calls=%fused_computation.88 | convolution fusion | flops 3623878656 | bytes 23199744 | tf_op jit(solution)/shard_map/dot_general | solution.py:124
  98.3 3.6 %bitcast_multiply_fusion = f32[8,576,384]{2,1,0:T(8,128)S(1)} fusion(f32[2,4,576,384]{3,2,1,0:T(8,128)} %copy-done, f32[384]{0:T(512)S(1)} %add_rsqrt_fusion), kind=kLoop, calls=%fused_computation.8 | loop fusion | flops 1769472 | bytes 14157312 | tf_op jit(solution)/shard_map/mul | solution.py:110
  101.9 7.6 %fusion.13 = f32[8,384,576]{1,2,0:T(8,128)S(1)} fusion(bf16[8,576,1024]{2,1,0:T(8,128)(2,1)} %bitcast.78, bf16[384,1024]{1,0:T(8,128)(2,1)S(1)} %copy-done.5), kind=kOutput, calls=%fused_computation.28 | convolution fusion | flops 3623878656 | bytes 17301504 | tf_op jit(solution)/shard_map/dot_general | solution.py:129
  127.0 7.7 %collective-permute-done.15 = f32[2,296,384]{2,1,0:T(8,128)} collective-permute-done((f32[2,296,384]{2,1,0:T(8,128)}, f32[2,296,384]{2,1,0:T(8,128)}, u32[]{:S(2)}, u32[]{:S(2)}) %collective-permute-start.15) | collective-permute-done | bytes 909344 | tf_op jit(solution)/shard_map/ppermute | solution.py:83
  139.7 4.9 %collective-permute-done.11 = f32[2,288,384]{2,1,0:T(8,128)} collective-permute-done((f32[2,288,384]{2,1,0:T(8,128)}, f32[2,288,384]{2,1,0:T(8,128)}, u32[]{:S(2)}, u32[]{:S(2)}) %collective-permute-start.11) | collective-permute-done | bytes 884768 | tf_op jit(solution)/shard_map/ppermute | solution.py:82
  146.8 8.7 %collective-permute-done.16 = f32[2,296,384]{2,1,0:T(8,128)} collective-permute-done((f32[2,296,384]{2,1,0:T(8,128)}, f32[2,296,384]{2,1,0:T(8,128)}, u32[]{:S(2)}, u32[]{:S(2)}) %collective-permute-start.16) | collective-permute-done | bytes 909344 | tf_op jit(solution)/shard_map/ppermute | solution.py:83
  158.0 3.1 %collective-permute-start.17 = (f32[2,296,384]{2,1,0:T(8,128)}, f32[2,296,384]{2,1,0:T(8,128)}, u32[]{:S(2)}, u32[]{:S(2)}) collective-permute-start(f32[2,296,384]{2,1,0:T(8,128)} %bitcast_add_fusion.1), channel_id=1, source_target_pairs={{0,3},{1,0},{2,1},{3,2},{4,7},{5,4},{6,5},{7,6},{8,11},{9,8},{10,9... | collective-permute-start | bytes 2727944 | tf_op jit(solution)/shard_map/ppermute | solution.py:83
  161.8 5.1 %collective-permute-done.12 = f32[2,288,384]{2,1,0:T(8,128)} collective-permute-done((f32[2,288,384]{2,1,0:T(8,128)}, f32[2,288,384]{2,1,0:T(8,128)}, u32[]{:S(2)}, u32[]{:S(2)}) %collective-permute-start.12) | collective-permute-done | bytes 884768 | tf_op jit(solution)/shard_map/ppermute | solution.py:82
  168.4 9.4 %collective-permute-done.17 = f32[2,296,384]{2,1,0:T(8,128)} collective-permute-done((f32[2,296,384]{2,1,0:T(8,128)}, f32[2,296,384]{2,1,0:T(8,128)}, u32[]{:S(2)}, u32[]{:S(2)}) %collective-permute-start.17) | collective-permute-done | bytes 909344 | tf_op jit(solution)/shard_map/ppermute | solution.py:83
  179.9 2.8 %collective-permute-start.13 = (f32[144,384]{1,0:T(8,128)S(1)}, f32[144,384]{1,0:T(8,128)S(1)}, u32[]{:S(2)}, u32[]{:S(2)}) collective-permute-start(f32[144,384]{1,0:T(8,128)S(1)} %dynamic-slice_bitcast_fusion.5), channel_id=1, source_target_pairs={{0,4},{1,5},{2,6},{3,7},{4,0},{5,1},{6,2},{7,3},{8,12},{9,13},{10,... | collective-permute-start | bytes 663560 | tf_op jit(solution)/shard_map/ppermute | solution.py:94
  183.1 17.5 %collective-permute-done.19 = f32[152,384]{1,0:T(8,128)S(1)} collective-permute-done((f32[152,384]{1,0:T(8,128)S(1)}, f32[152,384]{1,0:T(8,128)S(1)}, u32[]{:S(2)}, u32[]{:S(2)}) %collective-permute-start.19) | collective-permute-done | bytes 233504 | tf_op jit(solution)/shard_map/ppermute | solution.py:94
  200.9 2.8 %collective-permute-done.20 = f32[576]{0:T(1024)S(1)} collective-permute-done((f32[576]{0:T(1024)S(1)}, f32[576]{0:T(1024)S(1)}, u32[]{:S(2)}, u32[]{:S(2)}) %collective-permute-start.20) | collective-permute-done | bytes 2336 | tf_op jit(solution)/shard_map/ppermute | solution.py:47
  203.7 14.4 %collective-permute-done.13 = f32[144,384]{1,0:T(8,128)S(1)} collective-permute-done((f32[144,384]{1,0:T(8,128)S(1)}, f32[144,384]{1,0:T(8,128)S(1)}, u32[]{:S(2)}, u32[]{:S(2)}) %collective-permute-start.13) | collective-permute-done | bytes 221216 | tf_op jit(solution)/shard_map/ppermute | solution.py:94
  218.2 17.2 %collective-permute-done.18 = f32[144,384]{1,0:T(8,128)S(1)} collective-permute-done((f32[144,384]{1,0:T(8,128)S(1)}, f32[144,384]{1,0:T(8,128)S(1)}, u32[]{:S(2)}, u32[]{:S(2)}) %collective-permute-start.18) | collective-permute-done | bytes 221216 | tf_op jit(solution)/shard_map/ppermute | solution.py:94
  236.7 3.0 %collective-permute-done.23 = f32[576]{0:T(1024)S(1)} collective-permute-done((f32[576]{0:T(1024)S(1)}, f32[576]{0:T(1024)S(1)}, u32[]{:S(2)}, u32[]{:S(2)}) %collective-permute-start.23) | collective-permute-done | bytes 2336 | tf_op jit(solution)/shard_map/ppermute | solution.py:47
  239.7 13.0 %collective-permute-start.24 = (f32[576]{0:T(1024)S(1)}, f32[576]{0:T(1024)S(1)}, u32[]{:S(2)}, u32[]{:S(2)}) collective-permute-start(f32[576]{0:T(1024)S(1)} %add.254), channel_id=1, source_target_pairs={{0,8},{8,0},{1,9},{9,1},{2,10},{10,2},{3,11},{11,3},{4,12},{12,4},... | collective-permute-start | bytes 6920 | tf_op jit(solution)/shard_map/ppermute | solution.py:47
  (117 shorter events, 62.6 us)
Async XLA Ops:
  7.2 247.3 %reduce-scatter.2.cloned.1.call-start = ((), (), s32[]{:S(2)}) async-start(), calls=%async_computation.1 | async-start | bytes 19464192 | tf_op jit(solution)/shard_map/reduce_scatter | solution.py:127
  7.2 11.7 %collective-permute-start.6 = (bf16[576,384]{1,0:T(8,128)(2,1)}, bf16[576,384]{1,0:T(8,128)(2,1)S(1)}, u32[]{:S(2)}, u32[]{:S(2)}) collective-permute-start(bf16[576,384]{1,0:T(8,128)(2,1)} %bitcast.81), channel_id=1, source_target_pairs={{0,1},{1,2},{2,3},{3,0},{4,5},{5,6},{6,7},{7,4},{8,9},{9,10},{10,1... | collective-permute-start | bytes 1327112 | tf_op jit(solution)/shard_map/ppermute | solution.py:32
  9.4 36.8 %collective-permute-start.5 = (bf16[576,384]{1,0:T(8,128)(2,1)}, bf16[576,384]{1,0:T(8,128)(2,1)S(1)}, u32[]{:S(2)}, u32[]{:S(2)}) collective-permute-start(bf16[576,384]{1,0:T(8,128)(2,1)} %bitcast.82), channel_id=1, source_target_pairs={{0,2},{1,3},{2,0},{3,1},{4,6},{5,7},{6,4},{7,5},{8,10},{9,11},{10,... | collective-permute-start | bytes 1327112 | tf_op jit(solution)/shard_map/ppermute | solution.py:32
  12.0 34.2 %collective-permute-start.4 = (bf16[576,384]{1,0:T(8,128)(2,1)}, bf16[576,384]{1,0:T(8,128)(2,1)S(1)}, u32[]{:S(2)}, u32[]{:S(2)}) collective-permute-start(bf16[576,384]{1,0:T(8,128)(2,1)} %bitcast.83), channel_id=1, source_target_pairs={{0,3},{1,0},{2,1},{3,2},{4,7},{5,4},{6,5},{7,6},{8,11},{9,8},{10,9... | collective-permute-start | bytes 1327112 | tf_op jit(solution)/shard_map/ppermute | solution.py:32
  13.1 34.5 %collective-permute-start.3 = (bf16[576,384]{1,0:T(8,128)(2,1)}, bf16[576,384]{1,0:T(8,128)(2,1)S(1)}, u32[]{:S(2)}, u32[]{:S(2)}) collective-permute-start(bf16[576,384]{1,0:T(8,128)(2,1)} %bitcast.84), channel_id=1, source_target_pairs={{0,4},{1,5},{2,6},{3,7},{4,0},{5,1},{6,2},{7,3},{8,12},{9,13},{10,... | collective-permute-start | bytes 1327112 | tf_op jit(solution)/shard_map/ppermute | solution.py:32
  15.8 31.7 %collective-permute-start.2 = (bf16[576,384]{1,0:T(8,128)(2,1)}, bf16[576,384]{1,0:T(8,128)(2,1)S(1)}, u32[]{:S(2)}, u32[]{:S(2)}) collective-permute-start(bf16[576,384]{1,0:T(8,128)(2,1)} %bitcast.85), channel_id=1, source_target_pairs={{0,5},{1,6},{2,7},{3,4},{4,1},{5,2},{6,3},{7,0},{8,13},{9,14},{10,... | collective-permute-start | bytes 1327112 | tf_op jit(solution)/shard_map/ppermute | solution.py:32
  18.9 28.7 %collective-permute-start.1 = (bf16[576,384]{1,0:T(8,128)(2,1)}, bf16[576,384]{1,0:T(8,128)(2,1)S(1)}, u32[]{:S(2)}, u32[]{:S(2)}) collective-permute-start(bf16[576,384]{1,0:T(8,128)(2,1)} %bitcast.86), channel_id=1, source_target_pairs={{0,6},{1,7},{2,4},{3,5},{4,2},{5,3},{6,0},{7,1},{8,14},{9,15},{10,... | collective-permute-start | bytes 1327112 | tf_op jit(solution)/shard_map/ppermute | solution.py:32
  46.2 10.2 %collective-permute-start = (bf16[576,384]{1,0:T(8,128)(2,1)}, bf16[576,384]{1,0:T(8,128)(2,1)S(1)}, u32[]{:S(2)}, u32[]{:S(2)}) collective-permute-start(bf16[576,384]{1,0:T(8,128)(2,1)} %bitcast.87), channel_id=1, source_target_pairs={{0,7},{1,4},{2,5},{3,6},{4,3},{5,0},{6,1},{7,2},{8,15},{9,12},{10,... | collective-permute-start | bytes 1327112 | tf_op jit(solution)/shard_map/ppermute | solution.py:32
  74.1 4.3 %collective-permute-start.8 = (f32[2,384]{1,0:T(2,128)}, f32[2,384]{1,0:T(2,128)}, u32[]{:S(2)}, u32[]{:S(2)}) collective-permute-start(f32[2,384]{1,0:T(2,128)} %pad_maximum_fusion.6), channel_id=1, source_target_pairs={{0,2},{1,3},{2,0},{3,1},{4,6},{5,7},{6,4},{7,5},{8,10},{9,11},{10,... | collective-permute-start | bytes 9224 | tf_op jit(solution)/shard_map/ppermute | solution.py:56
  79.2 5.1 %collective-permute-start.9 = (f32[2,384]{1,0:T(2,128)S(1)}, f32[2,384]{1,0:T(2,128)S(1)}, u32[]{:S(2)}, u32[]{:S(2)}) collective-permute-start(f32[2,384]{1,0:T(2,128)S(1)} %pad_maximum_fusion.7), channel_id=1, source_target_pairs={{0,4},{1,5},{2,6},{3,7},{4,0},{5,1},{6,2},{7,3},{8,12},{9,13},{10,... | collective-permute-start | bytes 9224 | tf_op jit(solution)/shard_map/ppermute | solution.py:56
  111.0 13.7 %collective-permute-start.10 = (f32[2,288,384]{2,1,0:T(8,128)}, f32[2,288,384]{2,1,0:T(8,128)}, u32[]{:S(2)}, u32[]{:S(2)}) collective-permute-start(f32[2,288,384]{2,1,0:T(8,128)} %dynamic-slice_bitcast_fusion.1), channel_id=1, source_target_pairs={{0,1},{1,2},{2,3},{3,0},{4,5},{5,6},{6,7},{7,4},{8,9},{9,10},{10,1... | collective-permute-start | bytes 2654216 | tf_op jit(solution)/shard_map/ppermute | solution.py:82
  121.8 12.9 %collective-permute-start.15 = (f32[2,296,384]{2,1,0:T(8,128)}, f32[2,296,384]{2,1,0:T(8,128)}, u32[]{:S(2)}, u32[]{:S(2)}) collective-permute-start(f32[2,296,384]{2,1,0:T(8,128)} %dynamic-slice_bitcast_fusion), channel_id=1, source_target_pairs={{0,3},{1,0},{2,1},{3,2},{4,7},{5,4},{6,5},{7,6},{8,11},{9,8},{10,9... | collective-permute-start | bytes 2727944 | tf_op jit(solution)/shard_map/ppermute | solution.py:83
  127.0 17.6 %collective-permute-start.11 = (f32[2,288,384]{2,1,0:T(8,128)}, f32[2,288,384]{2,1,0:T(8,128)}, u32[]{:S(2)}, u32[]{:S(2)}) collective-permute-start(f32[2,288,384]{2,1,0:T(8,128)} %bitcast_add_fusion.3), channel_id=1, source_target_pairs={{0,1},{1,2},{2,3},{3,0},{4,5},{5,6},{6,7},{7,4},{8,9},{9,10},{10,1... | collective-permute-start | bytes 2654216 | tf_op jit(solution)/shard_map/ppermute | solution.py:82
  137.1 18.3 %collective-permute-start.16 = (f32[2,296,384]{2,1,0:T(8,128)}, f32[2,296,384]{2,1,0:T(8,128)}, u32[]{:S(2)}, u32[]{:S(2)}) collective-permute-start(f32[2,296,384]{2,1,0:T(8,128)} %bitcast_add_fusion), channel_id=1, source_target_pairs={{0,3},{1,0},{2,1},{3,2},{4,7},{5,4},{6,5},{7,6},{8,11},{9,8},{10,9... | collective-permute-start | bytes 2727944 | tf_op jit(solution)/shard_map/ppermute | solution.py:83
  146.8 20.2 %collective-permute-start.12 = (f32[2,288,384]{2,1,0:T(8,128)}, f32[2,288,384]{2,1,0:T(8,128)}, u32[]{:S(2)}, u32[]{:S(2)}) collective-permute-start(f32[2,288,384]{2,1,0:T(8,128)} %bitcast_add_fusion.4), channel_id=1, source_target_pairs={{0,1},{1,2},{2,3},{3,0},{4,5},{5,6},{6,7},{7,4},{8,9},{9,10},{10,1... | collective-permute-start | bytes 2654216 | tf_op jit(solution)/shard_map/ppermute | solution.py:82
  158.0 19.9 %collective-permute-start.17 = (f32[2,296,384]{2,1,0:T(8,128)}, f32[2,296,384]{2,1,0:T(8,128)}, u32[]{:S(2)}, u32[]{:S(2)}) collective-permute-start(f32[2,296,384]{2,1,0:T(8,128)} %bitcast_add_fusion.1), channel_id=1, source_target_pairs={{0,3},{1,0},{2,1},{3,2},{4,7},{5,4},{6,5},{7,6},{8,11},{9,8},{10,9... | collective-permute-start | bytes 2727944 | tf_op jit(solution)/shard_map/ppermute | solution.py:83
  168.3 32.5 %collective-permute-start.14 = (f32[144,384]{1,0:T(8,128)S(1)}, f32[144,384]{1,0:T(8,128)S(1)}, u32[]{:S(2)}, u32[]{:S(2)}) collective-permute-start(f32[144,384]{1,0:T(8,128)S(1)} %dynamic-slice_bitcast_fusion.4), channel_id=1, source_target_pairs={{0,4},{1,5},{2,6},{3,7},{4,0},{5,1},{6,2},{7,3},{8,12},{9,13},{10,... | collective-permute-start | bytes 663560 | tf_op jit(solution)/shard_map/ppermute | solution.py:94
  179.5 21.1 %collective-permute-start.19 = (f32[152,384]{1,0:T(8,128)S(1)}, f32[152,384]{1,0:T(8,128)S(1)}, u32[]{:S(2)}, u32[]{:S(2)}) collective-permute-start(f32[152,384]{1,0:T(8,128)S(1)} %dynamic-slice_bitcast_fusion.2), channel_id=1, source_target_pairs={{0,4},{1,5},{2,6},{3,7},{4,0},{5,1},{6,2},{7,3},{8,12},{9,13},{10,... | collective-permute-start | bytes 700424 | tf_op jit(solution)/shard_map/ppermute | solution.py:94
  179.9 38.1 %collective-permute-start.13 = (f32[144,384]{1,0:T(8,128)S(1)}, f32[144,384]{1,0:T(8,128)S(1)}, u32[]{:S(2)}, u32[]{:S(2)}) collective-permute-start(f32[144,384]{1,0:T(8,128)S(1)} %dynamic-slice_bitcast_fusion.5), channel_id=1, source_target_pairs={{0,4},{1,5},{2,6},{3,7},{4,0},{5,1},{6,2},{7,3},{8,12},{9,13},{10,... | collective-permute-start | bytes 663560 | tf_op jit(solution)/shard_map/ppermute | solution.py:94
  182.8 52.6 %collective-permute-start.18 = (f32[144,384]{1,0:T(8,128)S(1)}, f32[144,384]{1,0:T(8,128)S(1)}, u32[]{:S(2)}, u32[]{:S(2)}) collective-permute-start(f32[144,384]{1,0:T(8,128)S(1)} %dynamic-slice_bitcast_fusion.3), channel_id=1, source_target_pairs={{0,4},{1,5},{2,6},{3,7},{4,0},{5,1},{6,2},{7,3},{8,12},{9,13},{10,... | collective-permute-start | bytes 663560 | tf_op jit(solution)/shard_map/ppermute | solution.py:94
  203.7 14.4 %collective-permute-start.21 = (f32[576]{0:T(1024)S(1)}, f32[576]{0:T(1024)S(1)}, u32[]{:S(2)}, u32[]{:S(2)}) collective-permute-start(f32[576]{0:T(1024)S(1)} %slice_add_fusion), channel_id=1, source_target_pairs={{0,32},{16,48},{32,0},{48,16},{64,96},{80,112},{96,64},{112,80},{1... | collective-permute-start | bytes 6920 | tf_op jit(solution)/shard_map/ppermute | solution.py:47
  218.1 17.4 %collective-permute-start.22 = (f32[576]{0:T(1024)S(1)}, f32[576]{0:T(1024)S(1)}, u32[]{:S(2)}, u32[]{:S(2)}) collective-permute-start(f32[576]{0:T(1024)S(1)} %add.252), channel_id=1, source_target_pairs={{0,64},{16,80},{32,96},{48,112},{64,0},{80,16},{96,32},{112,48},{1... | collective-permute-start | bytes 6920 | tf_op jit(solution)/shard_map/ppermute | solution.py:47
  235.5 4.2 %collective-permute-start.23 = (f32[576]{0:T(1024)S(1)}, f32[576]{0:T(1024)S(1)}, u32[]{:S(2)}, u32[]{:S(2)}) collective-permute-start(f32[576]{0:T(1024)S(1)} %add.253), channel_id=1, source_target_pairs={{0,128},{16,144},{32,160},{48,176},{64,192},{80,208},{96,224},{112... | collective-permute-start | bytes 6920 | tf_op jit(solution)/shard_map/ppermute | solution.py:47
  239.7 14.1 %collective-permute-start.24 = (f32[576]{0:T(1024)S(1)}, f32[576]{0:T(1024)S(1)}, u32[]{:S(2)}, u32[]{:S(2)}) collective-permute-start(f32[576]{0:T(1024)S(1)} %add.254), channel_id=1, source_target_pairs={{0,8},{8,0},{1,9},{9,1},{2,10},{10,2},{3,11},{11,3},{4,12},{12,4},... | collective-permute-start | bytes 6920 | tf_op jit(solution)/shard_map/ppermute | solution.py:47
  (16 other events, 119.2 us)
Sparse Core Ops, SparseCore 0:
  97.0 155.2 reduce-scatter.1

commit v9 on v8

--- a/solution.py
+++ b/solution.py
@@ -121,10 +121,18 @@
     onehot = (column_ids == target_ids[:, None]).astype(jnp.float32)
     dlogits = (jnp.exp(logits - log_total[:, None]) - onehot).astype(jnp.bfloat16)
 
-    head_partial = lax.dot_general(
-        normed_t, dlogits, (((1,), (0,)), ((), ())), preferred_element_type=jnp.float32
-    )
-    grad_head = lax.psum_scatter(head_partial, ("outer", "core"), scatter_dimension=0, tiled=True)
+    core = lax.axis_index("core")
+    by_core = normed_t.reshape(n_outer, 2, width // (2 * n_outer), tokens)
+
+    def head_rows(which):
+        rows = lax.dynamic_index_in_dim(by_core, which, 1, keepdims=False).reshape(width // 2, tokens)
+        return lax.dot_general(
+            rows, dlogits, (((1,), (0,)), ((), ())), preferred_element_type=jnp.float32
+        )
+
+    sent = lax.ppermute(head_rows(1 - core), "core", [(0, 1), (1, 0)])
+    kept = head_rows(core) + sent
+    grad_head = lax.psum_scatter(kept, "outer", scatter_dimension=0, tiled=True)
 
     partial = lax.dot_general(
         head_weight.reshape(n_tensor, local_cols, vocab_rows),

time: 264 us -> 265 us (level)
  waiting for transfers between devices: 130 us -> 136 us
  local copies, waits for them, and re-layouts: 13.9 us -> 9.82 us
  starting transfers between devices: 46.9 us -> 50.4 us
    ppermute x4, waiting for transfers between devices: 49.1 us -> 27.1 us  [two_stage_reduce_scatter(): mine = mine + lax.ppermute(other, axis, perm_h)]
    ppermute x0 -> x1, waiting for transfers between devices: none -> 14.3 us  [shards(): sent = lax.ppermute(head_rows(1 - core), 'core', [(0, 1), (1, 0)])]
    ppermute x3, waiting for transfers between devices: 11.5 us -> 23.6 us  [two_stage_reduce_scatter(): recv_f = lax.ppermute(send_f, axis, perm_f)]
    ppermute x0 -> x1, starting transfers between devices: none -> 10.3 us  [shards(): sent = lax.ppermute(head_rows(1 - core), 'core', [(0, 1), (1, 0)])]
    ppermute x5, starting transfers between devices: 14.4 us -> 4.69 us  [butterfly_sum(): x = x + lax.ppermute(x, axis, [(c, c ^ b) for c in range(n)])]
    unnamed x28 -> x20, local copies, waits for them, and re-layouts: 7.71 us -> 3.11 us
    ppermute x5, waiting for transfers between devices: 5.77 us -> 10.3 us  [butterfly_sum(): x = x + lax.ppermute(x, axis, [(c, c ^ b) for c in range(n)])]
    convert_element_type x1 -> x2, other arithmetic: 2 us -> 5.5 us  [shards(): normed_t = (normalized_t * norm_gain[:, None]).astype(jnp.bfloat16)]
  transfers between devices with their start and end apart: 26 -> 27, of which waited for: 17 -> 19; matrix products, arithmetic and copies ran while one was open for 14% -> 15% of each run, Pallas kernels for 0% -> 0%
where the time goes in v9:
time: 265 us; the launch traced here: 264 us
  waiting for transfers between devices  136 us (51%)
  starting transfers between devices  50.4 us (19%)
  other arithmetic  34.4 us (13%)
  matrix products  19.2 us (7%)
  between operations  14.5 us (5%)
  local copies, waits for them, and re-layouts  9.82 us (4%)
    ppermute x7, waiting for transfers between devices, grid_gather(): got[a, b] = lax.ppermute(x, axis, perm)  33 us
    ppermute x4, waiting for transfers between devices, two_stage_reduce_scatter(): mine = mine + lax.ppermute(other, axis, perm_h)  27.1 us
    ppermute x3, waiting for transfers between devices, two_stage_reduce_scatter(): recv_b = lax.ppermute(send_b, axis, perm_b)  25 us
    ppermute x3, waiting for transfers between devices, two_stage_reduce_scatter(): recv_f = lax.ppermute(send_f, axis, perm_f)  23.6 us
    ppermute x7, starting transfers between devices, grid_gather(): got[a, b] = lax.ppermute(x, axis, perm)  14.9 us
    ppermute x1, waiting for transfers between devices, shards(): sent = lax.ppermute(head_rows(1 - core), 'core', [(0, 1), (1, 0)])  14.3 us
    ppermute x5, waiting for transfers between devices, butterfly_sum(): x = x + lax.ppermute(x, axis, [(c, c ^ b) for c in range(n)])  10.3 us
    ppermute x1, starting transfers between devices, shards(): sent = lax.ppermute(head_rows(1 - core), 'core', [(0, 1), (1, 0)])  10.3 us
  transfers between devices with their start and end apart: 27, of which 19 were waited for; matrix products, arithmetic and copies ran while one was open for 15% of the time, Pallas kernels for 0%

profile of v9, /device:TPU:1, one launch (start us, length us, event | category | flops | bytes accessed | tf_op | source)
XLA Modules:
  0.0 264.3 jit_solution(1352005865565176323)
XLA Ops:
  18.9 5.9 %collective-permute-start.1 = (bf16[576,384]{1,0:T(8,128)(2,1)}, bf16[576,384]{1,0:T(8,128)(2,1)S(1)}, u32[]{:S(2)}, u32[]{:S(2)}) collective-permute-start(bf16[576,384]{1,0:T(8,128)(2,1)} %bitcast.94), channel_id=1, source_target_pairs={{0,6},{1,7},{2,4},{3,5},{4,2},{5,3},{6,0},{7,1},{8,14},{9,15},{10,... | collective-permute-start | bytes 1327112 | tf_op jit(solution)/shard_map/ppermute | solution.py:32
  24.8 21.4 %collective-permute-done.5 = bf16[576,384]{1,0:T(8,128)(2,1)S(1)} collective-permute-done((bf16[576,384]{1,0:T(8,128)(2,1)}, bf16[576,384]{1,0:T(8,128)(2,1)S(1)}, u32[]{:S(2)}, u32[]{:S(2)}) %collective-permute-start.5) | collective-permute-done | bytes 442400 | tf_op jit(solution)/shard_map/ppermute | solution.py:32
  47.6 8.9 %collective-permute-done = bf16[576,384]{1,0:T(8,128)(2,1)S(1)} collective-permute-done((bf16[576,384]{1,0:T(8,128)(2,1)}, bf16[576,384]{1,0:T(8,128)(2,1)S(1)}, u32[]{:S(2)}, u32[]{:S(2)}) %collective-permute-start) | collective-permute-done | bytes 442400 | tf_op jit(solution)/shard_map/ppermute | solution.py:32
  56.8 4.5 %multiply_reduce_fusion = (f32[384]{0:T(512)S(1)}, f32[2,4,576,384]{3,2,1,0:T(8,128)S(1)}) fusion(s32[]{:T(128)S(6)} %select_n.98, s32[]{:T(128)S(6)} %select_n.101, bf16[1,4,576,384]{3,2,1,0:T(8,128)(2,1)S(1)} %maximum_bitcast_fusion.1, bf16[1,4,576,384]{3,2,1,0:T(8,128)(2,1)S(1)} %maximum_bitcast_fusion), kind=kLoop, calls=%fused_computation.17 | loop fusion | flops 17694336 | bytes 10618376 | tf_op jit(solution)/shard_map/reduce_sum | solution.py:108
  64.1 3.9 %fusion.28 = (f32[384]{0:T(512)S(1)}, f32[384,1024]{1,0:T(8,128)S(1)}) fusion(bf16[4608,384]{1,0:T(8,128)(2,1)S(1)} %fusion.3, bf16[4608,1024]{1,0:T(8,128)(2,1)S(1)} %bitcast.86), kind=kOutput, calls=%fused_computation.91 | convolution fusion | flops 3624271360 | bytes 14550528 | tf_op jit(solution)/shard_map/dot_general | solution.py:112
  73.4 3.5 %multiply_convert_fusion = bf16[16,2,144,384]{3,2,1,0:T(8,128)(2,1)S(1)} fusion(f32[16,2,144,384]{3,2,1,0:T(8,128)} %bitcast.81, f32[16,2,144]{2,1,0:T(2,128)S(1)} %mul.186, f32[384]{0:T(512)S(1)} %add_rsqrt_fusion), kind=kLoop, calls=%fused_computation.16 | loop fusion | flops 5308416 | bytes 10636800 | tf_op jit(solution)/shard_map/convert_element_type | solution.py:111
  77.0 2.9 %collective-permute-start.9 = (f32[2,384]{1,0:T(2,128)S(1)}, f32[2,384]{1,0:T(2,128)S(1)}, u32[]{:S(2)}, u32[]{:S(2)}) collective-permute-start(f32[2,384]{1,0:T(2,128)S(1)} %pad_maximum_fusion.7), channel_id=1, source_target_pairs={{0,4},{1,5},{2,6},{3,7},{4,0},{5,1},{6,2},{7,3},{8,12},{9,13},{10,... | collective-permute-start | bytes 9224 | tf_op jit(solution)/shard_map/ppermute | solution.py:56
  84.1 10.3 %collective-permute-start.20 = (f32[2304,1024]{1,0:T(8,128)S(1)}, f32[2304,1024]{1,0:T(8,128)S(1)}, u32[]{:S(2)}, u32[]{:S(2)}) collective-permute-start(f32[2304,1024]{1,0:T(8,128)S(1)} %fusion.29), channel_id=1, source_target_pairs={{0,8},{8,0},{1,9},{9,1},{2,10},{10,2},{3,11},{11,3},{4,12},{12,4},... | collective-permute-start | bytes 28311560 | tf_op jit(solution)/shard_map/ppermute | solution.py:133
  94.4 14.3 %collective-permute-done.20 = f32[2304,1024]{1,0:T(8,128)S(1)} collective-permute-done((f32[2304,1024]{1,0:T(8,128)S(1)}, f32[2304,1024]{1,0:T(8,128)S(1)}, u32[]{:S(2)}, u32[]{:S(2)}) %collective-permute-start.20) | collective-permute-done | bytes 9437216 | tf_op jit(solution)/shard_map/ppermute | solution.py:133
  108.7 5.1 %convolution_add_fusion = f32[2304,1024]{1,0:T(8,128)} fusion(f32[2304,1024]{1,0:T(8,128)S(1)} %collective-permute-done.20, bf16[2304,384]{1,0:T(8,128)(2,1)S(1)} %bitcast.87, bf16[384,1024]{1,0:T(8,128)(2,1)S(1)} %subtract_convert_fusion), kind=kOutput, calls=%fused_computation.18 | convolution fusion | flops 1814298624 | bytes 21430272 | tf_op jit(solution)/shard_map/dot_general | solution.py:129
  114.6 3.5 %bitcast_multiply_fusion = f32[8,576,384]{2,1,0:T(8,128)S(1)} fusion(f32[2,4,576,384]{3,2,1,0:T(8,128)} %copy-done, f32[384]{0:T(512)S(1)} %add_rsqrt_fusion), kind=kLoop, calls=%fused_computation.8 | loop fusion | flops 1769472 | bytes 14157312 | tf_op jit(solution)/shard_map/mul | solution.py:110
  118.1 7.6 %fusion.13 = f32[8,384,576]{1,2,0:T(8,128)S(1)} fusion(bf16[8,576,1024]{2,1,0:T(8,128)(2,1)} %bitcast.84, bf16[384,1024]{1,0:T(8,128)(2,1)S(1)} %subtract_convert_fusion), kind=kOutput, calls=%fused_computation.30 | convolution fusion | flops 3623878656 | bytes 17301504 | tf_op jit(solution)/shard_map/dot_general | solution.py:137
  139.8 9.9 %collective-permute-done.10 = f32[2,288,384]{2,1,0:T(8,128)} collective-permute-done((f32[2,288,384]{2,1,0:T(8,128)}, f32[2,288,384]{2,1,0:T(8,128)}, u32[]{:S(2)}, u32[]{:S(2)}) %collective-permute-start.10) | collective-permute-done | bytes 884768 | tf_op jit(solution)/shard_map/ppermute | solution.py:82
  151.9 7.8 %collective-permute-done.15 = f32[2,296,384]{2,1,0:T(8,128)} collective-permute-done((f32[2,296,384]{2,1,0:T(8,128)}, f32[2,296,384]{2,1,0:T(8,128)}, u32[]{:S(2)}, u32[]{:S(2)}) %collective-permute-start.15) | collective-permute-done | bytes 909344 | tf_op jit(solution)/shard_map/ppermute | solution.py:83
  162.2 3.0 %collective-permute-start.16 = (f32[2,296,384]{2,1,0:T(8,128)}, f32[2,296,384]{2,1,0:T(8,128)}, u32[]{:S(2)}, u32[]{:S(2)}) collective-permute-start(f32[2,296,384]{2,1,0:T(8,128)} %bitcast_add_fusion), channel_id=1, source_target_pairs={{0,3},{1,0},{2,1},{3,2},{4,7},{5,4},{6,5},{7,6},{8,11},{9,8},{10,9... | collective-permute-start | bytes 2727944 | tf_op jit(solution)/shard_map/ppermute | solution.py:83
  165.2 8.1 %collective-permute-done.11 = f32[2,288,384]{2,1,0:T(8,128)} collective-permute-done((f32[2,288,384]{2,1,0:T(8,128)}, f32[2,288,384]{2,1,0:T(8,128)}, u32[]{:S(2)}, u32[]{:S(2)}) %collective-permute-start.11) | collective-permute-done | bytes 884768 | tf_op jit(solution)/shard_map/ppermute | solution.py:82
  175.5 8.3 %collective-permute-done.16 = f32[2,296,384]{2,1,0:T(8,128)} collective-permute-done((f32[2,296,384]{2,1,0:T(8,128)}, f32[2,296,384]{2,1,0:T(8,128)}, u32[]{:S(2)}, u32[]{:S(2)}) %collective-permute-start.16) | collective-permute-done | bytes 909344 | tf_op jit(solution)/shard_map/ppermute | solution.py:83
  186.3 3.4 %collective-permute-start.17 = (f32[2,296,384]{2,1,0:T(8,128)}, f32[2,296,384]{2,1,0:T(8,128)}, u32[]{:S(2)}, u32[]{:S(2)}) collective-permute-start(f32[2,296,384]{2,1,0:T(8,128)} %bitcast_add_fusion.1), channel_id=1, source_target_pairs={{0,3},{1,0},{2,1},{3,2},{4,7},{5,4},{6,5},{7,6},{8,11},{9,8},{10,9... | collective-permute-start | bytes 2727944 | tf_op jit(solution)/shard_map/ppermute | solution.py:83
  190.4 5.6 %collective-permute-done.12 = f32[2,288,384]{2,1,0:T(8,128)} collective-permute-done((f32[2,288,384]{2,1,0:T(8,128)}, f32[2,288,384]{2,1,0:T(8,128)}, u32[]{:S(2)}, u32[]{:S(2)}) %collective-permute-start.12) | collective-permute-done | bytes 884768 | tf_op jit(solution)/shard_map/ppermute | solution.py:82
  198.4 8.9 %collective-permute-done.17 = f32[2,296,384]{2,1,0:T(8,128)} collective-permute-done((f32[2,296,384]{2,1,0:T(8,128)}, f32[2,296,384]{2,1,0:T(8,128)}, u32[]{:S(2)}, u32[]{:S(2)}) %collective-permute-start.17) | collective-permute-done | bytes 909344 | tf_op jit(solution)/shard_map/ppermute | solution.py:83
  213.4 22.3 %collective-permute-done.19 = f32[152,384]{1,0:T(8,128)S(1)} collective-permute-done((f32[152,384]{1,0:T(8,128)S(1)}, f32[152,384]{1,0:T(8,128)S(1)}, u32[]{:S(2)}, u32[]{:S(2)}) %collective-permute-start.19) | collective-permute-done | bytes 233504 | tf_op jit(solution)/shard_map/ppermute | solution.py:94
  242.3 2.9 %collective-permute-done.18 = f32[144,384]{1,0:T(8,128)S(1)} collective-permute-done((f32[144,384]{1,0:T(8,128)S(1)}, f32[144,384]{1,0:T(8,128)S(1)}, u32[]{:S(2)}, u32[]{:S(2)}) %collective-permute-start.18) | collective-permute-done | bytes 221216 | tf_op jit(solution)/shard_map/ppermute | solution.py:94
  245.2 3.4 %collective-permute-done.23 = f32[576]{0:T(1024)S(1)} collective-permute-done((f32[576]{0:T(1024)S(1)}, f32[576]{0:T(1024)S(1)}, u32[]{:S(2)}, u32[]{:S(2)}) %collective-permute-start.23) | collective-permute-done | bytes 2336 | tf_op jit(solution)/shard_map/ppermute | solution.py:47
  251.4 4.3 %collective-permute-start.25 = (f32[576]{0:T(1024)S(1)}, f32[576]{0:T(1024)S(1)}, u32[]{:S(2)}, u32[]{:S(2)}) collective-permute-start(f32[576]{0:T(1024)S(1)} %add.268), channel_id=1, source_target_pairs={{0,8},{8,0},{1,9},{9,1},{2,10},{10,2},{3,11},{11,3},{4,12},{12,4},... | collective-permute-start | bytes 6920 | tf_op jit(solution)/shard_map/ppermute | solution.py:47
  (115 shorter events, 70.1 us)
Async XLA Ops:
  7.2 250.2 %reduce-scatter.2.cloned.1.call-start = ((), (), s32[]{:S(2)}) async-start(), calls=%async_computation.1 | async-start | bytes 10027008 | tf_op jit(solution)/shard_map/reduce_scatter | solution.py:135
  7.2 11.7 %collective-permute-start.6 = (bf16[576,384]{1,0:T(8,128)(2,1)}, bf16[576,384]{1,0:T(8,128)(2,1)S(1)}, u32[]{:S(2)}, u32[]{:S(2)}) collective-permute-start(bf16[576,384]{1,0:T(8,128)(2,1)} %bitcast.89), channel_id=1, source_target_pairs={{0,1},{1,2},{2,3},{3,0},{4,5},{5,6},{6,7},{7,4},{8,9},{9,10},{10,1... | collective-permute-start | bytes 1327112 | tf_op jit(solution)/shard_map/ppermute | solution.py:32
  9.4 36.8 %collective-permute-start.5 = (bf16[576,384]{1,0:T(8,128)(2,1)}, bf16[576,384]{1,0:T(8,128)(2,1)S(1)}, u32[]{:S(2)}, u32[]{:S(2)}) collective-permute-start(bf16[576,384]{1,0:T(8,128)(2,1)} %bitcast.90), channel_id=1, source_target_pairs={{0,2},{1,3},{2,0},{3,1},{4,6},{5,7},{6,4},{7,5},{8,10},{9,11},{10,... | collective-permute-start | bytes 1327112 | tf_op jit(solution)/shard_map/ppermute | solution.py:32
  12.0 34.2 %collective-permute-start.4 = (bf16[576,384]{1,0:T(8,128)(2,1)}, bf16[576,384]{1,0:T(8,128)(2,1)S(1)}, u32[]{:S(2)}, u32[]{:S(2)}) collective-permute-start(bf16[576,384]{1,0:T(8,128)(2,1)} %bitcast.91), channel_id=1, source_target_pairs={{0,3},{1,0},{2,1},{3,2},{4,7},{5,4},{6,5},{7,6},{8,11},{9,8},{10,9... | collective-permute-start | bytes 1327112 | tf_op jit(solution)/shard_map/ppermute | solution.py:32
  13.1 34.5 %collective-permute-start.3 = (bf16[576,384]{1,0:T(8,128)(2,1)}, bf16[576,384]{1,0:T(8,128)(2,1)S(1)}, u32[]{:S(2)}, u32[]{:S(2)}) collective-permute-start(bf16[576,384]{1,0:T(8,128)(2,1)} %bitcast.92), channel_id=1, source_target_pairs={{0,4},{1,5},{2,6},{3,7},{4,0},{5,1},{6,2},{7,3},{8,12},{9,13},{10,... | collective-permute-start | bytes 1327112 | tf_op jit(solution)/shard_map/ppermute | solution.py:32
  15.8 31.7 %collective-permute-start.2 = (bf16[576,384]{1,0:T(8,128)(2,1)}, bf16[576,384]{1,0:T(8,128)(2,1)S(1)}, u32[]{:S(2)}, u32[]{:S(2)}) collective-permute-start(bf16[576,384]{1,0:T(8,128)(2,1)} %bitcast.93), channel_id=1, source_target_pairs={{0,5},{1,6},{2,7},{3,4},{4,1},{5,2},{6,3},{7,0},{8,13},{9,14},{10,... | collective-permute-start | bytes 1327112 | tf_op jit(solution)/shard_map/ppermute | solution.py:32
  18.9 28.7 %collective-permute-start.1 = (bf16[576,384]{1,0:T(8,128)(2,1)}, bf16[576,384]{1,0:T(8,128)(2,1)S(1)}, u32[]{:S(2)}, u32[]{:S(2)}) collective-permute-start(bf16[576,384]{1,0:T(8,128)(2,1)} %bitcast.94), channel_id=1, source_target_pairs={{0,6},{1,7},{2,4},{3,5},{4,2},{5,3},{6,0},{7,1},{8,14},{9,15},{10,... | collective-permute-start | bytes 1327112 | tf_op jit(solution)/shard_map/ppermute | solution.py:32
  46.2 10.2 %collective-permute-start = (bf16[576,384]{1,0:T(8,128)(2,1)}, bf16[576,384]{1,0:T(8,128)(2,1)S(1)}, u32[]{:S(2)}, u32[]{:S(2)}) collective-permute-start(bf16[576,384]{1,0:T(8,128)(2,1)} %bitcast.95), channel_id=1, source_target_pairs={{0,7},{1,4},{2,5},{3,6},{4,3},{5,0},{6,1},{7,2},{8,15},{9,12},{10,... | collective-permute-start | bytes 1327112 | tf_op jit(solution)/shard_map/ppermute | solution.py:32
  71.0 5.9 %collective-permute-start.8 = (f32[2,384]{1,0:T(2,128)S(1)}, f32[2,384]{1,0:T(2,128)S(1)}, u32[]{:S(2)}, u32[]{:S(2)}) collective-permute-start(f32[2,384]{1,0:T(2,128)S(1)} %pad_maximum_fusion.6), channel_id=1, source_target_pairs={{0,2},{1,3},{2,0},{3,1},{4,6},{5,7},{6,4},{7,5},{8,10},{9,11},{10,... | collective-permute-start | bytes 9224 | tf_op jit(solution)/shard_map/ppermute | solution.py:56
  77.0 4.0 %collective-permute-start.9 = (f32[2,384]{1,0:T(2,128)S(1)}, f32[2,384]{1,0:T(2,128)S(1)}, u32[]{:S(2)}, u32[]{:S(2)}) collective-permute-start(f32[2,384]{1,0:T(2,128)S(1)} %pad_maximum_fusion.7), channel_id=1, source_target_pairs={{0,4},{1,5},{2,6},{3,7},{4,0},{5,1},{6,2},{7,3},{8,12},{9,13},{10,... | collective-permute-start | bytes 9224 | tf_op jit(solution)/shard_map/ppermute | solution.py:56
  84.1 24.6 %collective-permute-start.20 = (f32[2304,1024]{1,0:T(8,128)S(1)}, f32[2304,1024]{1,0:T(8,128)S(1)}, u32[]{:S(2)}, u32[]{:S(2)}) collective-permute-start(f32[2304,1024]{1,0:T(8,128)S(1)} %fusion.29), channel_id=1, source_target_pairs={{0,8},{8,0},{1,9},{9,1},{2,10},{10,2},{3,11},{11,3},{4,12},{12,4},... | collective-permute-start | bytes 28311560 | tf_op jit(solution)/shard_map/ppermute | solution.py:133
  127.3 22.4 %collective-permute-start.10 = (f32[2,288,384]{2,1,0:T(8,128)}, f32[2,288,384]{2,1,0:T(8,128)}, u32[]{:S(2)}, u32[]{:S(2)}) collective-permute-start(f32[2,288,384]{2,1,0:T(8,128)} %dynamic-slice_bitcast_fusion.1), channel_id=1, source_target_pairs={{0,1},{1,2},{2,3},{3,0},{4,5},{5,6},{6,7},{7,4},{8,9},{9,10},{10,1... | collective-permute-start | bytes 2654216 | tf_op jit(solution)/shard_map/ppermute | solution.py:82
  137.9 21.7 %collective-permute-start.15 = (f32[2,296,384]{2,1,0:T(8,128)}, f32[2,296,384]{2,1,0:T(8,128)}, u32[]{:S(2)}, u32[]{:S(2)}) collective-permute-start(f32[2,296,384]{2,1,0:T(8,128)} %dynamic-slice_bitcast_fusion), channel_id=1, source_target_pairs={{0,3},{1,0},{2,1},{3,2},{4,7},{5,4},{6,5},{7,6},{8,11},{9,8},{10,9... | collective-permute-start | bytes 2727944 | tf_op jit(solution)/shard_map/ppermute | solution.py:83
  151.8 21.5 %collective-permute-start.11 = (f32[2,288,384]{2,1,0:T(8,128)}, f32[2,288,384]{2,1,0:T(8,128)}, u32[]{:S(2)}, u32[]{:S(2)}) collective-permute-start(f32[2,288,384]{2,1,0:T(8,128)} %bitcast_add_fusion.3), channel_id=1, source_target_pairs={{0,1},{1,2},{2,3},{3,0},{4,5},{5,6},{6,7},{7,4},{8,9},{9,10},{10,1... | collective-permute-start | bytes 2654216 | tf_op jit(solution)/shard_map/ppermute | solution.py:82
  162.2 21.6 %collective-permute-start.16 = (f32[2,296,384]{2,1,0:T(8,128)}, f32[2,296,384]{2,1,0:T(8,128)}, u32[]{:S(2)}, u32[]{:S(2)}) collective-permute-start(f32[2,296,384]{2,1,0:T(8,128)} %bitcast_add_fusion), channel_id=1, source_target_pairs={{0,3},{1,0},{2,1},{3,2},{4,7},{5,4},{6,5},{7,6},{8,11},{9,8},{10,9... | collective-permute-start | bytes 2727944 | tf_op jit(solution)/shard_map/ppermute | solution.py:83
  175.5 20.5 %collective-permute-start.12 = (f32[2,288,384]{2,1,0:T(8,128)}, f32[2,288,384]{2,1,0:T(8,128)}, u32[]{:S(2)}, u32[]{:S(2)}) collective-permute-start(f32[2,288,384]{2,1,0:T(8,128)} %bitcast_add_fusion.4), channel_id=1, source_target_pairs={{0,1},{1,2},{2,3},{3,0},{4,5},{5,6},{6,7},{7,4},{8,9},{9,10},{10,1... | collective-permute-start | bytes 2654216 | tf_op jit(solution)/shard_map/ppermute | solution.py:82
  186.3 21.0 %collective-permute-start.17 = (f32[2,296,384]{2,1,0:T(8,128)}, f32[2,296,384]{2,1,0:T(8,128)}, u32[]{:S(2)}, u32[]{:S(2)}) collective-permute-start(f32[2,296,384]{2,1,0:T(8,128)} %bitcast_add_fusion.1), channel_id=1, source_target_pairs={{0,3},{1,0},{2,1},{3,2},{4,7},{5,4},{6,5},{7,6},{8,11},{9,8},{10,9... | collective-permute-start | bytes 2727944 | tf_op jit(solution)/shard_map/ppermute | solution.py:83
  197.4 38.5 %collective-permute-start.14 = (f32[144,384]{1,0:T(8,128)S(1)}, f32[144,384]{1,0:T(8,128)S(1)}, u32[]{:S(2)}, u32[]{:S(2)}) collective-permute-start(f32[144,384]{1,0:T(8,128)S(1)} %dynamic-slice_bitcast_fusion.4), channel_id=1, source_target_pairs={{0,4},{1,5},{2,6},{3,7},{4,0},{5,1},{6,2},{7,3},{8,12},{9,13},{10,... | collective-permute-start | bytes 663560 | tf_op jit(solution)/shard_map/ppermute | solution.py:94
  209.0 26.7 %collective-permute-start.19 = (f32[152,384]{1,0:T(8,128)S(1)}, f32[152,384]{1,0:T(8,128)S(1)}, u32[]{:S(2)}, u32[]{:S(2)}) collective-permute-start(f32[152,384]{1,0:T(8,128)S(1)} %dynamic-slice_bitcast_fusion.2), channel_id=1, source_target_pairs={{0,4},{1,5},{2,6},{3,7},{4,0},{5,1},{6,2},{7,3},{8,12},{9,13},{10,... | collective-permute-start | bytes 700424 | tf_op jit(solution)/shard_map/ppermute | solution.py:94
  210.1 30.3 %collective-permute-start.13 = (f32[144,384]{1,0:T(8,128)S(1)}, f32[144,384]{1,0:T(8,128)S(1)}, u32[]{:S(2)}, u32[]{:S(2)}) collective-permute-start(f32[144,384]{1,0:T(8,128)S(1)} %dynamic-slice_bitcast_fusion.5), channel_id=1, source_target_pairs={{0,4},{1,5},{2,6},{3,7},{4,0},{5,1},{6,2},{7,3},{8,12},{9,13},{10,... | collective-permute-start | bytes 663560 | tf_op jit(solution)/shard_map/ppermute | solution.py:94
  212.2 33.0 %collective-permute-start.18 = (f32[144,384]{1,0:T(8,128)S(1)}, f32[144,384]{1,0:T(8,128)S(1)}, u32[]{:S(2)}, u32[]{:S(2)}) collective-permute-start(f32[144,384]{1,0:T(8,128)S(1)} %dynamic-slice_bitcast_fusion.3), channel_id=1, source_target_pairs={{0,4},{1,5},{2,6},{3,7},{4,0},{5,1},{6,2},{7,3},{8,12},{9,13},{10,... | collective-permute-start | bytes 663560 | tf_op jit(solution)/shard_map/ppermute | solution.py:94
  238.6 3.7 %collective-permute-start.22 = (f32[576]{0:T(1024)S(1)}, f32[576]{0:T(1024)S(1)}, u32[]{:S(2)}, u32[]{:S(2)}) collective-permute-start(f32[576]{0:T(1024)S(1)} %slice_add_fusion), channel_id=1, source_target_pairs={{0,32},{16,48},{32,0},{48,16},{64,96},{80,112},{96,64},{112,80},{1... | collective-permute-start | bytes 6920 | tf_op jit(solution)/shard_map/ppermute | solution.py:47
  242.3 6.4 %collective-permute-start.23 = (f32[576]{0:T(1024)S(1)}, f32[576]{0:T(1024)S(1)}, u32[]{:S(2)}, u32[]{:S(2)}) collective-permute-start(f32[576]{0:T(1024)S(1)} %add.266), channel_id=1, source_target_pairs={{0,64},{16,80},{32,96},{48,112},{64,0},{80,16},{96,32},{112,48},{1... | collective-permute-start | bytes 6920 | tf_op jit(solution)/shard_map/ppermute | solution.py:47
  251.4 5.4 %collective-permute-start.25 = (f32[576]{0:T(1024)S(1)}, f32[576]{0:T(1024)S(1)}, u32[]{:S(2)}, u32[]{:S(2)}) collective-permute-start(f32[576]{0:T(1024)S(1)} %add.268), channel_id=1, source_target_pairs={{0,8},{8,0},{1,9},{9,1},{2,10},{10,2},{3,11},{11,3},{4,12},{12,4},... | collective-permute-start | bytes 6920 | tf_op jit(solution)/shard_map/ppermute | solution.py:47
  (13 other events, 92.1 us)
Sparse Core Ops, SparseCore 0:
  113.9 111.5 reduce-scatter.1

commit v10 on v9

--- a/solution.py
+++ b/solution.py
@@ -124,15 +124,13 @@
     core = lax.axis_index("core")
     by_core = normed_t.reshape(n_outer, 2, width // (2 * n_outer), tokens)
 
-    def head_rows(which):
+    def head_rows(which, by_core):
         rows = lax.dynamic_index_in_dim(by_core, which, 1, keepdims=False).reshape(width // 2, tokens)
         return lax.dot_general(
             rows, dlogits, (((1,), (0,)), ((), ())), preferred_element_type=jnp.float32
         )
 
-    sent = lax.ppermute(head_rows(1 - core), "core", [(0, 1), (1, 0)])
-    kept = head_rows(core) + sent
-    grad_head = lax.psum_scatter(kept, "outer", scatter_dimension=0, tiled=True)
+    sent = lax.ppermute(head_rows(1 - core, by_core), "core", [(0, 1), (1, 0)])
 
     partial = lax.dot_general(
         head_weight.reshape(n_tensor, local_cols, vocab_rows),
@@ -142,6 +140,11 @@
     ).reshape(width, tokens)
     inner_part = jnp.sum(partial * (norm_gain[:, None] * normalized_t), axis=0)
     gain_part = jnp.sum(partial * normalized_t, axis=1)
+    partial, inner_part, gain_part, by_core = lax.optimization_barrier(
+        (partial, inner_part, gain_part, by_core)
+    )
+    kept = head_rows(core, by_core) + sent
+    grad_head = lax.psum_scatter(kept, "outer", scatter_dimension=0, tiled=True)
 
     gain_rows = -(-local_cols // tokens)
     gain_chunks = jnp.pad(

time: 265 us -> 275 us (1.038)
  local copies, waits for them, and re-layouts: 9.82 us -> 18.2 us
  matrix products: 19.2 us -> 24 us
  waiting for transfers between devices: 136 us -> 132 us
    ppermute x1, waiting for transfers between devices: 14.3 us -> 0.01 us  [shards(): sent = lax.ppermute(head_rows(1 - core, by_core), 'core', [(0, 1), (1, 0)])]
    ppermute x4, waiting for transfers between devices: 27.1 us -> 37.4 us  [two_stage_reduce_scatter(): mine = mine + lax.ppermute(other, axis, perm_h)]
    dot_general x2, matrix products: 7.72 us -> 12.5 us  [head_rows(): lax.dot_general(rows, dlogits, (((1,), (0,)), ((), ())), preferred_elemen...]
    ppermute x3, waiting for transfers between devices: 23.6 us -> 27.3 us  [two_stage_reduce_scatter(): recv_f = lax.ppermute(send_f, axis, perm_f)]
    ppermute x3, waiting for transfers between devices: 25 us -> 21.9 us  [two_stage_reduce_scatter(): recv_b = lax.ppermute(send_b, axis, perm_b)]
  transfers between devices with their start and end apart: 27 -> 27, of which waited for: 19 -> 18; matrix products, arithmetic and copies ran while one was open for 15% -> 18% of each run, Pallas kernels for 0% -> 0%
where the time goes in v10:
time: 275 us; the launch traced here: 274 us
  waiting for transfers between devices  132 us (48%)
  starting transfers between devices  49.7 us (18%)
  other arithmetic  35.4 us (13%)
  matrix products  24 us (9%)
  local copies, waits for them, and re-layouts  18.2 us (7%)
  between operations  14.5 us (5%)
    ppermute x4, waiting for transfers between devices, two_stage_reduce_scatter(): mine = mine + lax.ppermute(other, axis, perm_h)  37.4 us
    ppermute x7, waiting for transfers between devices, grid_gather(): got[a, b] = lax.ppermute(x, axis, perm)  33 us
    ppermute x3, waiting for transfers between devices, two_stage_reduce_scatter(): recv_f = lax.ppermute(send_f, axis, perm_f)  27.3 us
    ppermute x3, waiting for transfers between devices, two_stage_reduce_scatter(): recv_b = lax.ppermute(send_b, axis, perm_b)  21.9 us
    ppermute x7, starting transfers between devices, grid_gather(): got[a, b] = lax.ppermute(x, axis, perm)  14.9 us
    dot_general x2, matrix products, head_rows(): lax.dot_general(rows, dlogits, (((1,), (0,)), ((), ())), preferred_elemen...  12.5 us
    ppermute x5, waiting for transfers between devices, butterfly_sum(): x = x + lax.ppermute(x, axis, [(c, c ^ b) for c in range(n)])  10.3 us
    ppermute x1, starting transfers between devices, shards(): sent = lax.ppermute(head_rows(1 - core, by_core), 'core', [(0, 1), (1, 0)])  10.2 us
  transfers between devices with their start and end apart: 27, of which 18 were waited for; matrix products, arithmetic and copies ran while one was open for 18% of the time, Pallas kernels for 0%

profile of v10, /device:TPU:1, one launch (start us, length us, event | category | flops | bytes accessed | tf_op | source)
XLA Modules:
  0.0 273.9 jit_solution(15769817443264779607)
XLA Ops:
  18.9 5.9 %collective-permute-start.1 = (bf16[576,384]{1,0:T(8,128)(2,1)}, bf16[576,384]{1,0:T(8,128)(2,1)S(1)}, u32[]{:S(2)}, u32[]{:S(2)}) collective-permute-start(bf16[576,384]{1,0:T(8,128)(2,1)} %bitcast.95), channel_id=1, source_target_pairs={{0,6},{1,7},{2,4},{3,5},{4,2},{5,3},{6,0},{7,1},{8,14},{9,15},{10,... | collective-permute-start | bytes 1327112 | tf_op jit(solution)/shard_map/ppermute | solution.py:32
  24.8 21.4 %collective-permute-done.5 = bf16[576,384]{1,0:T(8,128)(2,1)S(1)} collective-permute-done((bf16[576,384]{1,0:T(8,128)(2,1)}, bf16[576,384]{1,0:T(8,128)(2,1)S(1)}, u32[]{:S(2)}, u32[]{:S(2)}) %collective-permute-start.5) | collective-permute-done | bytes 442400 | tf_op jit(solution)/shard_map/ppermute | solution.py:32
  47.6 8.9 %collective-permute-done = bf16[576,384]{1,0:T(8,128)(2,1)S(1)} collective-permute-done((bf16[576,384]{1,0:T(8,128)(2,1)}, bf16[576,384]{1,0:T(8,128)(2,1)S(1)}, u32[]{:S(2)}, u32[]{:S(2)}) %collective-permute-start) | collective-permute-done | bytes 442400 | tf_op jit(solution)/shard_map/ppermute | solution.py:32
  56.8 4.5 %multiply_reduce_fusion = (f32[384]{0:T(512)S(1)}, f32[2,4,576,384]{3,2,1,0:T(8,128)S(1)}) fusion(s32[]{:T(128)S(6)} %select_n.98, s32[]{:T(128)S(6)} %select_n.101, bf16[1,4,576,384]{3,2,1,0:T(8,128)(2,1)S(1)} %maximum_bitcast_fusion.1, bf16[1,4,576,384]{3,2,1,0:T(8,128)(2,1)S(1)} %maximum_bitcast_fusion), kind=kLoop, calls=%fused_computation.17 | loop fusion | flops 17694336 | bytes 10618376 | tf_op jit(solution)/shard_map/reduce_sum | solution.py:108
  64.2 3.9 %fusion.28 = (f32[384]{0:T(512)S(1)}, f32[384,1024]{1,0:T(8,128)S(1)}) fusion(bf16[4608,384]{1,0:T(8,128)(2,1)S(1)} %fusion.3, bf16[4608,1024]{1,0:T(8,128)(2,1)S(1)} %bitcast.87), kind=kOutput, calls=%fused_computation.91 | convolution fusion | flops 3624271360 | bytes 14550528 | tf_op jit(solution)/shard_map/dot_general | solution.py:112
  74.6 3.5 %multiply_convert_fusion = bf16[16,2,144,384]{3,2,1,0:T(8,128)(2,1)S(1)} fusion(f32[16,2,144,384]{3,2,1,0:T(8,128)} %bitcast.82, f32[16,2,144]{2,1,0:T(2,128)} %mul.178, f32[384]{0:T(512)S(1)} %add_rsqrt_fusion), kind=kLoop, calls=%fused_computation.16 | loop fusion | flops 5308416 | bytes 10636800 | tf_op jit(solution)/shard_map/convert_element_type | solution.py:111
  78.3 2.9 %collective-permute-start.9 = (f32[2,384]{1,0:T(2,128)S(1)}, f32[2,384]{1,0:T(2,128)S(1)}, u32[]{:S(2)}, u32[]{:S(2)}) collective-permute-start(f32[2,384]{1,0:T(2,128)S(1)} %pad_maximum_fusion.7), channel_id=1, source_target_pairs={{0,4},{1,5},{2,6},{3,7},{4,0},{5,1},{6,2},{7,3},{8,12},{9,13},{10,... | collective-permute-start | bytes 9224 | tf_op jit(solution)/shard_map/ppermute | solution.py:56
  82.8 5.1 %fusion.29 = f32[2304,1024]{1,0:T(8,128)} fusion(bf16[2304,384]{1,0:T(8,128)(2,1)S(1)} %bitcast.89, bf16[384,1024]{1,0:T(8,128)(2,1)S(1)} %subtract_convert_fusion), kind=kOutput, calls=%fused_computation.92 | convolution fusion | flops 1811939328 | bytes 11993088 | tf_op jit(solution)/shard_map/dot_general | solution.py:129
  87.9 10.2 %collective-permute-start.20 = (f32[2304,1024]{1,0:T(8,128)}, f32[2304,1024]{1,0:T(8,128)}, u32[]{:S(2)}, u32[]{:S(2)}) collective-permute-start(f32[2304,1024]{1,0:T(8,128)} %fusion.29), channel_id=1, source_target_pairs={{0,8},{8,0},{1,9},{9,1},{2,10},{10,2},{3,11},{11,3},{4,12},{12,4},... | collective-permute-start | bytes 28311560 | tf_op jit(solution)/shard_map/ppermute | solution.py:133
  99.5 3.6 %bitcast_multiply_fusion = f32[8,576,384]{2,1,0:T(8,128)S(1)} fusion(f32[2,4,576,384]{3,2,1,0:T(8,128)} %copy-done, f32[384]{0:T(512)S(1)} %add_rsqrt_fusion), kind=kLoop, calls=%fused_computation.8 | loop fusion | flops 1769472 | bytes 14157312 | tf_op jit(solution)/shard_map/mul | solution.py:110
  103.1 7.6 %fusion.13 = f32[8,384,576]{1,2,0:T(8,128)S(1)} fusion(bf16[8,576,1024]{2,1,0:T(8,128)(2,1)} %bitcast.85, bf16[384,1024]{1,0:T(8,128)(2,1)S(1)} %copy-done.6), kind=kOutput, calls=%fused_computation.30 | convolution fusion | flops 3623878656 | bytes 17301504 | tf_op jit(solution)/shard_map/dot_general | solution.py:135
  110.8 2.9 %fusion = (f32[8,576]{1,0:T(8,128)}, f32[384]{0:T(512)S(1)}) fusion(f32[8,576,384]{2,1,0:T(8,128)S(1)} %bitcast_multiply_fusion, f32[8,384,576]{1,2,0:T(8,128)S(1)} %fusion.13, f32[8,576]{1,0:T(8,128)S(1)} %copy-done.10), kind=kLoop, calls=%fused_computation.11 | loop fusion | flops 8842368 | bytes 14194176 | tf_op jit(solution)/shard_map/reduce_sum | solution.py:142
  116.2 7.4 %convolution_add_fusion = f32[2304,1024]{1,0:T(8,128)} fusion(f32[2304,1024]{1,0:T(8,128)} %collective-permute-done.20, bf16[2304,384]{1,0:T(8,128)(2,1)S(1)} %bitcast.88, bf16[384,1024]{1,0:T(8,128)(2,1)S(1)} %copy-done.7), kind=kOutput, calls=%fused_computation.18 | convolution fusion | flops 1814298624 | bytes 21430272 | tf_op jit(solution)/shard_map/dot_general | solution.py:129
  139.0 10.8 %collective-permute-done.10 = f32[2,288,384]{2,1,0:T(8,128)} collective-permute-done((f32[2,288,384]{2,1,0:T(8,128)}, f32[2,288,384]{2,1,0:T(8,128)}, u32[]{:S(2)}, u32[]{:S(2)}) %collective-permute-start.10) | collective-permute-done | bytes 884768 | tf_op jit(solution)/shard_map/ppermute | solution.py:82
  151.9 7.3 %collective-permute-done.15 = f32[2,296,384]{2,1,0:T(8,128)} collective-permute-done((f32[2,296,384]{2,1,0:T(8,128)}, f32[2,296,384]{2,1,0:T(8,128)}, u32[]{:S(2)}, u32[]{:S(2)}) %collective-permute-start.15) | collective-permute-done | bytes 909344 | tf_op jit(solution)/shard_map/ppermute | solution.py:83
  164.5 9.4 %collective-permute-done.11 = f32[2,288,384]{2,1,0:T(8,128)} collective-permute-done((f32[2,288,384]{2,1,0:T(8,128)}, f32[2,288,384]{2,1,0:T(8,128)}, u32[]{:S(2)}, u32[]{:S(2)}) %collective-permute-start.11) | collective-permute-done | bytes 884768 | tf_op jit(solution)/shard_map/ppermute | solution.py:82
  176.0 7.1 %collective-permute-done.16 = f32[2,296,384]{2,1,0:T(8,128)} collective-permute-done((f32[2,296,384]{2,1,0:T(8,128)}, f32[2,296,384]{2,1,0:T(8,128)}, u32[]{:S(2)}, u32[]{:S(2)}) %collective-permute-start.16) | collective-permute-done | bytes 909344 | tf_op jit(solution)/shard_map/ppermute | solution.py:83
  185.6 3.4 %collective-permute-start.17 = (f32[2,296,384]{2,1,0:T(8,128)}, f32[2,296,384]{2,1,0:T(8,128)}, u32[]{:S(2)}, u32[]{:S(2)}) collective-permute-start(f32[2,296,384]{2,1,0:T(8,128)} %bitcast_add_fusion.1), channel_id=1, source_target_pairs={{0,3},{1,0},{2,1},{3,2},{4,7},{5,4},{6,5},{7,6},{8,11},{9,8},{10,9... | collective-permute-start | bytes 2727944 | tf_op jit(solution)/shard_map/ppermute | solution.py:83
  189.8 7.2 %collective-permute-done.12 = f32[2,288,384]{2,1,0:T(8,128)} collective-permute-done((f32[2,288,384]{2,1,0:T(8,128)}, f32[2,288,384]{2,1,0:T(8,128)}, u32[]{:S(2)}, u32[]{:S(2)}) %collective-permute-start.12) | collective-permute-done | bytes 884768 | tf_op jit(solution)/shard_map/ppermute | solution.py:82
  199.4 7.4 %collective-permute-done.17 = f32[2,296,384]{2,1,0:T(8,128)} collective-permute-done((f32[2,296,384]{2,1,0:T(8,128)}, f32[2,296,384]{2,1,0:T(8,128)}, u32[]{:S(2)}, u32[]{:S(2)}) %collective-permute-start.17) | collective-permute-done | bytes 909344 | tf_op jit(solution)/shard_map/ppermute | solution.py:83
  212.7 32.6 %collective-permute-done.19 = f32[152,384]{1,0:T(8,128)S(1)} collective-permute-done((f32[152,384]{1,0:T(8,128)S(1)}, f32[152,384]{1,0:T(8,128)S(1)}, u32[]{:S(2)}, u32[]{:S(2)}) %collective-permute-start.19) | collective-permute-done | bytes 233504 | tf_op jit(solution)/shard_map/ppermute | solution.py:94
  251.9 2.9 %collective-permute-done.18 = f32[144,384]{1,0:T(8,128)S(1)} collective-permute-done((f32[144,384]{1,0:T(8,128)S(1)}, f32[144,384]{1,0:T(8,128)S(1)}, u32[]{:S(2)}, u32[]{:S(2)}) %collective-permute-start.18) | collective-permute-done | bytes 221216 | tf_op jit(solution)/shard_map/ppermute | solution.py:94
  254.8 3.4 %collective-permute-done.23 = f32[576]{0:T(1024)S(1)} collective-permute-done((f32[576]{0:T(1024)S(1)}, f32[576]{0:T(1024)S(1)}, u32[]{:S(2)}, u32[]{:S(2)}) %collective-permute-start.23) | collective-permute-done | bytes 2336 | tf_op jit(solution)/shard_map/ppermute | solution.py:47
  261.0 4.3 %collective-permute-start.25 = (f32[576]{0:T(1024)S(1)}, f32[576]{0:T(1024)S(1)}, u32[]{:S(2)}, u32[]{:S(2)}) collective-permute-start(f32[576]{0:T(1024)S(1)} %add.268), channel_id=1, source_target_pairs={{0,8},{8,0},{1,9},{9,1},{2,10},{10,2},{3,11},{11,3},{4,12},{12,4},... | collective-permute-start | bytes 6920 | tf_op jit(solution)/shard_map/ppermute | solution.py:47
  (128 shorter events, 75.7 us)
Async XLA Ops:
  7.2 259.9 %reduce-scatter.2.cloned.1.call-start = ((), (), s32[]{:S(2)}) async-start(), calls=%async_computation.1 | async-start | bytes 10027008 | tf_op jit(solution)/shard_map/reduce_scatter | solution.py:147
  7.2 11.7 %collective-permute-start.6 = (bf16[576,384]{1,0:T(8,128)(2,1)}, bf16[576,384]{1,0:T(8,128)(2,1)S(1)}, u32[]{:S(2)}, u32[]{:S(2)}) collective-permute-start(bf16[576,384]{1,0:T(8,128)(2,1)} %bitcast.90), channel_id=1, source_target_pairs={{0,1},{1,2},{2,3},{3,0},{4,5},{5,6},{6,7},{7,4},{8,9},{9,10},{10,1... | collective-permute-start | bytes 1327112 | tf_op jit(solution)/shard_map/ppermute | solution.py:32
  9.4 36.8 %collective-permute-start.5 = (bf16[576,384]{1,0:T(8,128)(2,1)}, bf16[576,384]{1,0:T(8,128)(2,1)S(1)}, u32[]{:S(2)}, u32[]{:S(2)}) collective-permute-start(bf16[576,384]{1,0:T(8,128)(2,1)} %bitcast.91), channel_id=1, source_target_pairs={{0,2},{1,3},{2,0},{3,1},{4,6},{5,7},{6,4},{7,5},{8,10},{9,11},{10,... | collective-permute-start | bytes 1327112 | tf_op jit(solution)/shard_map/ppermute | solution.py:32
  12.0 34.2 %collective-permute-start.4 = (bf16[576,384]{1,0:T(8,128)(2,1)}, bf16[576,384]{1,0:T(8,128)(2,1)S(1)}, u32[]{:S(2)}, u32[]{:S(2)}) collective-permute-start(bf16[576,384]{1,0:T(8,128)(2,1)} %bitcast.92), channel_id=1, source_target_pairs={{0,3},{1,0},{2,1},{3,2},{4,7},{5,4},{6,5},{7,6},{8,11},{9,8},{10,9... | collective-permute-start | bytes 1327112 | tf_op jit(solution)/shard_map/ppermute | solution.py:32
  13.1 34.5 %collective-permute-start.3 = (bf16[576,384]{1,0:T(8,128)(2,1)}, bf16[576,384]{1,0:T(8,128)(2,1)S(1)}, u32[]{:S(2)}, u32[]{:S(2)}) collective-permute-start(bf16[576,384]{1,0:T(8,128)(2,1)} %bitcast.93), channel_id=1, source_target_pairs={{0,4},{1,5},{2,6},{3,7},{4,0},{5,1},{6,2},{7,3},{8,12},{9,13},{10,... | collective-permute-start | bytes 1327112 | tf_op jit(solution)/shard_map/ppermute | solution.py:32
  15.8 31.7 %collective-permute-start.2 = (bf16[576,384]{1,0:T(8,128)(2,1)}, bf16[576,384]{1,0:T(8,128)(2,1)S(1)}, u32[]{:S(2)}, u32[]{:S(2)}) collective-permute-start(bf16[576,384]{1,0:T(8,128)(2,1)} %bitcast.94), channel_id=1, source_target_pairs={{0,5},{1,6},{2,7},{3,4},{4,1},{5,2},{6,3},{7,0},{8,13},{9,14},{10,... | collective-permute-start | bytes 1327112 | tf_op jit(solution)/shard_map/ppermute | solution.py:32
  18.9 28.7 %collective-permute-start.1 = (bf16[576,384]{1,0:T(8,128)(2,1)}, bf16[576,384]{1,0:T(8,128)(2,1)S(1)}, u32[]{:S(2)}, u32[]{:S(2)}) collective-permute-start(bf16[576,384]{1,0:T(8,128)(2,1)} %bitcast.95), channel_id=1, source_target_pairs={{0,6},{1,7},{2,4},{3,5},{4,2},{5,3},{6,0},{7,1},{8,14},{9,15},{10,... | collective-permute-start | bytes 1327112 | tf_op jit(solution)/shard_map/ppermute | solution.py:32
  46.2 10.2 %collective-permute-start = (bf16[576,384]{1,0:T(8,128)(2,1)}, bf16[576,384]{1,0:T(8,128)(2,1)S(1)}, u32[]{:S(2)}, u32[]{:S(2)}) collective-permute-start(bf16[576,384]{1,0:T(8,128)(2,1)} %bitcast.96), channel_id=1, source_target_pairs={{0,7},{1,4},{2,5},{3,6},{4,3},{5,0},{6,1},{7,2},{8,15},{9,12},{10,... | collective-permute-start | bytes 1327112 | tf_op jit(solution)/shard_map/ppermute | solution.py:32
  72.3 5.9 %collective-permute-start.8 = (f32[2,384]{1,0:T(2,128)S(1)}, f32[2,384]{1,0:T(2,128)S(1)}, u32[]{:S(2)}, u32[]{:S(2)}) collective-permute-start(f32[2,384]{1,0:T(2,128)S(1)} %pad_maximum_fusion.6), channel_id=1, source_target_pairs={{0,2},{1,3},{2,0},{3,1},{4,6},{5,7},{6,4},{7,5},{8,10},{9,11},{10,... | collective-permute-start | bytes 9224 | tf_op jit(solution)/shard_map/ppermute | solution.py:56
  78.3 4.0 %collective-permute-start.9 = (f32[2,384]{1,0:T(2,128)S(1)}, f32[2,384]{1,0:T(2,128)S(1)}, u32[]{:S(2)}, u32[]{:S(2)}) collective-permute-start(f32[2,384]{1,0:T(2,128)S(1)} %pad_maximum_fusion.7), channel_id=1, source_target_pairs={{0,4},{1,5},{2,6},{3,7},{4,0},{5,1},{6,2},{7,3},{8,12},{9,13},{10,... | collective-permute-start | bytes 9224 | tf_op jit(solution)/shard_map/ppermute | solution.py:56
  87.9 27.4 %collective-permute-start.20 = (f32[2304,1024]{1,0:T(8,128)}, f32[2304,1024]{1,0:T(8,128)}, u32[]{:S(2)}, u32[]{:S(2)}) collective-permute-start(f32[2304,1024]{1,0:T(8,128)} %fusion.29), channel_id=1, source_target_pairs={{0,8},{8,0},{1,9},{9,1},{2,10},{10,2},{3,11},{11,3},{4,12},{12,4},... | collective-permute-start | bytes 28311560 | tf_op jit(solution)/shard_map/ppermute | solution.py:133
  127.0 22.8 %collective-permute-start.10 = (f32[2,288,384]{2,1,0:T(8,128)}, f32[2,288,384]{2,1,0:T(8,128)}, u32[]{:S(2)}, u32[]{:S(2)}) collective-permute-start(f32[2,288,384]{2,1,0:T(8,128)} %dynamic-slice_bitcast_fusion.1), channel_id=1, source_target_pairs={{0,1},{1,2},{2,3},{3,0},{4,5},{5,6},{6,7},{7,4},{8,9},{9,10},{10,1... | collective-permute-start | bytes 2654216 | tf_op jit(solution)/shard_map/ppermute | solution.py:82
  137.5 21.8 %collective-permute-start.15 = (f32[2,296,384]{2,1,0:T(8,128)}, f32[2,296,384]{2,1,0:T(8,128)}, u32[]{:S(2)}, u32[]{:S(2)}) collective-permute-start(f32[2,296,384]{2,1,0:T(8,128)} %dynamic-slice_bitcast_fusion), channel_id=1, source_target_pairs={{0,3},{1,0},{2,1},{3,2},{4,7},{5,4},{6,5},{7,6},{8,11},{9,8},{10,9... | collective-permute-start | bytes 2727944 | tf_op jit(solution)/shard_map/ppermute | solution.py:83
  151.9 21.9 %collective-permute-start.11 = (f32[2,288,384]{2,1,0:T(8,128)}, f32[2,288,384]{2,1,0:T(8,128)}, u32[]{:S(2)}, u32[]{:S(2)}) collective-permute-start(f32[2,288,384]{2,1,0:T(8,128)} %bitcast_add_fusion.3), channel_id=1, source_target_pairs={{0,1},{1,2},{2,3},{3,0},{4,5},{5,6},{6,7},{7,4},{8,9},{9,10},{10,1... | collective-permute-start | bytes 2654216 | tf_op jit(solution)/shard_map/ppermute | solution.py:82
  161.7 21.4 %collective-permute-start.16 = (f32[2,296,384]{2,1,0:T(8,128)}, f32[2,296,384]{2,1,0:T(8,128)}, u32[]{:S(2)}, u32[]{:S(2)}) collective-permute-start(f32[2,296,384]{2,1,0:T(8,128)} %bitcast_add_fusion), channel_id=1, source_target_pairs={{0,3},{1,0},{2,1},{3,2},{4,7},{5,4},{6,5},{7,6},{8,11},{9,8},{10,9... | collective-permute-start | bytes 2727944 | tf_op jit(solution)/shard_map/ppermute | solution.py:83
  176.0 21.0 %collective-permute-start.12 = (f32[2,288,384]{2,1,0:T(8,128)}, f32[2,288,384]{2,1,0:T(8,128)}, u32[]{:S(2)}, u32[]{:S(2)}) collective-permute-start(f32[2,288,384]{2,1,0:T(8,128)} %bitcast_add_fusion.4), channel_id=1, source_target_pairs={{0,1},{1,2},{2,3},{3,0},{4,5},{5,6},{6,7},{7,4},{8,9},{9,10},{10,1... | collective-permute-start | bytes 2654216 | tf_op jit(solution)/shard_map/ppermute | solution.py:82
  185.6 21.2 %collective-permute-start.17 = (f32[2,296,384]{2,1,0:T(8,128)}, f32[2,296,384]{2,1,0:T(8,128)}, u32[]{:S(2)}, u32[]{:S(2)}) collective-permute-start(f32[2,296,384]{2,1,0:T(8,128)} %bitcast_add_fusion.1), channel_id=1, source_target_pairs={{0,3},{1,0},{2,1},{3,2},{4,7},{5,4},{6,5},{7,6},{8,11},{9,8},{10,9... | collective-permute-start | bytes 2727944 | tf_op jit(solution)/shard_map/ppermute | solution.py:83
  198.4 47.1 %collective-permute-start.14 = (f32[144,384]{1,0:T(8,128)S(1)}, f32[144,384]{1,0:T(8,128)S(1)}, u32[]{:S(2)}, u32[]{:S(2)}) collective-permute-start(f32[144,384]{1,0:T(8,128)S(1)} %dynamic-slice_bitcast_fusion.4), channel_id=1, source_target_pairs={{0,4},{1,5},{2,6},{3,7},{4,0},{5,1},{6,2},{7,3},{8,12},{9,13},{10,... | collective-permute-start | bytes 663560 | tf_op jit(solution)/shard_map/ppermute | solution.py:94
  208.4 36.9 %collective-permute-start.19 = (f32[152,384]{1,0:T(8,128)S(1)}, f32[152,384]{1,0:T(8,128)S(1)}, u32[]{:S(2)}, u32[]{:S(2)}) collective-permute-start(f32[152,384]{1,0:T(8,128)S(1)} %dynamic-slice_bitcast_fusion.2), channel_id=1, source_target_pairs={{0,4},{1,5},{2,6},{3,7},{4,0},{5,1},{6,2},{7,3},{8,12},{9,13},{10,... | collective-permute-start | bytes 700424 | tf_op jit(solution)/shard_map/ppermute | solution.py:94
  209.5 40.6 %collective-permute-start.13 = (f32[144,384]{1,0:T(8,128)S(1)}, f32[144,384]{1,0:T(8,128)S(1)}, u32[]{:S(2)}, u32[]{:S(2)}) collective-permute-start(f32[144,384]{1,0:T(8,128)S(1)} %dynamic-slice_bitcast_fusion.5), channel_id=1, source_target_pairs={{0,4},{1,5},{2,6},{3,7},{4,0},{5,1},{6,2},{7,3},{8,12},{9,13},{10,... | collective-permute-start | bytes 663560 | tf_op jit(solution)/shard_map/ppermute | solution.py:94
  211.7 43.1 %collective-permute-start.18 = (f32[144,384]{1,0:T(8,128)S(1)}, f32[144,384]{1,0:T(8,128)S(1)}, u32[]{:S(2)}, u32[]{:S(2)}) collective-permute-start(f32[144,384]{1,0:T(8,128)S(1)} %dynamic-slice_bitcast_fusion.3), channel_id=1, source_target_pairs={{0,4},{1,5},{2,6},{3,7},{4,0},{5,1},{6,2},{7,3},{8,12},{9,13},{10,... | collective-permute-start | bytes 663560 | tf_op jit(solution)/shard_map/ppermute | solution.py:94
  248.2 3.7 %collective-permute-start.22 = (f32[576]{0:T(1024)S(1)}, f32[576]{0:T(1024)S(1)}, u32[]{:S(2)}, u32[]{:S(2)}) collective-permute-start(f32[576]{0:T(1024)S(1)} %slice_add_fusion), channel_id=1, source_target_pairs={{0,32},{16,48},{32,0},{48,16},{64,96},{80,112},{96,64},{112,80},{1... | collective-permute-start | bytes 6920 | tf_op jit(solution)/shard_map/ppermute | solution.py:47
  251.9 6.4 %collective-permute-start.23 = (f32[576]{0:T(1024)S(1)}, f32[576]{0:T(1024)S(1)}, u32[]{:S(2)}, u32[]{:S(2)}) collective-permute-start(f32[576]{0:T(1024)S(1)} %add.266), channel_id=1, source_target_pairs={{0,64},{16,80},{32,96},{48,112},{64,0},{80,16},{96,32},{112,48},{1... | collective-permute-start | bytes 6920 | tf_op jit(solution)/shard_map/ppermute | solution.py:47
  261.0 5.4 %collective-permute-start.25 = (f32[576]{0:T(1024)S(1)}, f32[576]{0:T(1024)S(1)}, u32[]{:S(2)}, u32[]{:S(2)}) collective-permute-start(f32[576]{0:T(1024)S(1)} %add.268), channel_id=1, source_target_pairs={{0,8},{8,0},{1,9},{9,1},{2,10},{10,2},{3,11},{11,3},{4,12},{12,4},... | collective-permute-start | bytes 6920 | tf_op jit(solution)/shard_map/ppermute | solution.py:47
  (18 other events, 122.2 us)
Sparse Core Ops, SparseCore 0:
  123.8 111.2 reduce-scatter.1

commit v11 on v9

--- a/solution.py
+++ b/solution.py
@@ -86,8 +86,9 @@
     perm_h = [(a * n_lo + l, (n_hi - 1 - a) * n_lo + l) for a in range(n_hi) for l in range(n_lo)]
     out = []
     for part in (sum_f, sum_b):
-        cut = (part.shape[1] // 2) // 8 * 8
-        for piece in (part[:, :cut], part[:, cut:]):
+        step = (part.shape[1] // 4) // 8 * 8
+        cuts = [0, step, 2 * step, 3 * step, part.shape[1]]
+        for piece in [part[:, cuts[i] : cuts[i + 1]] for i in range(4)]:
             mine = lax.dynamic_index_in_dim(piece, h, 0, keepdims=False)
             if n_hi > 1:
                 other = lax.dynamic_index_in_dim(piece, n_hi - 1 - h, 0, keepdims=False)

time: 265 us -> 274 us (1.034)
  waiting for transfers between devices: 136 us -> 142 us
  starting transfers between devices: 50.4 us -> 54.8 us
    ppermute x4 -> x8, waiting for transfers between devices: 27.1 us -> 34.6 us  [two_stage_reduce_scatter(): mine = mine + lax.ppermute(other, axis, perm_h)]
    ppermute x3, waiting for transfers between devices: 25 us -> 18.6 us  [two_stage_reduce_scatter(): recv_b = lax.ppermute(send_b, axis, perm_b)]
    ppermute x4 -> x8, starting transfers between devices: 5.32 us -> 9.14 us  [two_stage_reduce_scatter(): mine = mine + lax.ppermute(other, axis, perm_h)]
    ppermute x5, waiting for transfers between devices: 10.3 us -> 13.8 us  [butterfly_sum(): x = x + lax.ppermute(x, axis, [(c, c ^ b) for c in range(n)])]
  transfers between devices with their start and end apart: 27 -> 31, of which waited for: 19 -> 24; matrix products, arithmetic and copies ran while one was open for 15% -> 15% of each run, Pallas kernels for 0% -> 0%
where the time goes in v11:
time: 274 us
  waiting for transfers between devices  142 us (52%)
  starting transfers between devices  54.8 us (20%)
  other arithmetic  33.1 us (12%)
  matrix products  19.2 us (7%)
  between operations  14.5 us (5%)
  local copies, waits for them, and re-layouts  9.87 us (4%)
    ppermute x8, waiting for transfers between devices, two_stage_reduce_scatter(): mine = mine + lax.ppermute(other, axis, perm_h)  34.6 us
    ppermute x7, waiting for transfers between devices, grid_gather(): got[a, b] = lax.ppermute(x, axis, perm)  33 us
    ppermute x3, waiting for transfers between devices, two_stage_reduce_scatter(): recv_f = lax.ppermute(send_f, axis, perm_f)  25.2 us
    ppermute x3, waiting for transfers between devices, two_stage_reduce_scatter(): recv_b = lax.ppermute(send_b, axis, perm_b)  18.6 us
    ppermute x7, starting transfers between devices, grid_gather(): got[a, b] = lax.ppermute(x, axis, perm)  14.9 us
    ppermute x1, waiting for transfers between devices, shards(): sent = lax.ppermute(head_rows(1 - core), 'core', [(0, 1), (1, 0)])  14.3 us
    ppermute x5, waiting for transfers between devices, butterfly_sum(): x = x + lax.ppermute(x, axis, [(c, c ^ b) for c in range(n)])  13.8 us
    ppermute x1, starting transfers between devices, shards(): sent = lax.ppermute(head_rows(1 - core), 'core', [(0, 1), (1, 0)])  10.3 us
  transfers between devices with their start and end apart: 31, of which 24 were waited for; matrix products, arithmetic and copies ran while one was open for 15% of the time, Pallas kernels for 0%

profile of v11, /device:TPU:1, one launch (start us, length us, event | category | flops | bytes accessed | tf_op | source)
XLA Modules:
  0.0 273.6 jit_solution(17794691768789931292)
XLA Ops:
  13.1 2.7 %collective-permute-start.3 = (bf16[576,384]{1,0:T(8,128)(2,1)}, bf16[576,384]{1,0:T(8,128)(2,1)S(1)}, u32[]{:S(2)}, u32[]{:S(2)}) collective-permute-start(bf16[576,384]{1,0:T(8,128)(2,1)} %bitcast.123), channel_id=1, source_target_pairs={{0,4},{1,5},{2,6},{3,7},{4,0},{5,1},{6,2},{7,3},{8,12},{9,13},{10,... | collective-permute-start | bytes 1327112 | tf_op jit(solution)/shard_map/ppermute | solution.py:32
  18.9 5.9 %collective-permute-start.1 = (bf16[576,384]{1,0:T(8,128)(2,1)}, bf16[576,384]{1,0:T(8,128)(2,1)S(1)}, u32[]{:S(2)}, u32[]{:S(2)}) collective-permute-start(bf16[576,384]{1,0:T(8,128)(2,1)} %bitcast.125), channel_id=1, source_target_pairs={{0,6},{1,7},{2,4},{3,5},{4,2},{5,3},{6,0},{7,1},{8,14},{9,15},{10,... | collective-permute-start | bytes 1327112 | tf_op jit(solution)/shard_map/ppermute | solution.py:32
  24.8 21.4 %collective-permute-done.5 = bf16[576,384]{1,0:T(8,128)(2,1)S(1)} collective-permute-done((bf16[576,384]{1,0:T(8,128)(2,1)}, bf16[576,384]{1,0:T(8,128)(2,1)S(1)}, u32[]{:S(2)}, u32[]{:S(2)}) %collective-permute-start.5) | collective-permute-done | bytes 442400 | tf_op jit(solution)/shard_map/ppermute | solution.py:32
  47.6 8.9 %collective-permute-done = bf16[576,384]{1,0:T(8,128)(2,1)S(1)} collective-permute-done((bf16[576,384]{1,0:T(8,128)(2,1)}, bf16[576,384]{1,0:T(8,128)(2,1)S(1)}, u32[]{:S(2)}, u32[]{:S(2)}) %collective-permute-start) | collective-permute-done | bytes 442400 | tf_op jit(solution)/shard_map/ppermute | solution.py:32
  56.8 4.5 %multiply_reduce_fusion = (f32[384]{0:T(512)S(1)}, f32[2,4,576,384]{3,2,1,0:T(8,128)S(1)}) fusion(s32[]{:T(128)S(6)} %select_n.106, s32[]{:T(128)S(6)} %select_n.109, bf16[1,4,576,384]{3,2,1,0:T(8,128)(2,1)S(1)} %maximum_bitcast_fusion.1, bf16[1,4,576,384]{3,2,1,0:T(8,128)(2,1)S(1)} %maximum_bitcast_fusion), kind=kLoop, calls=%fused_computation.17 | loop fusion | flops 17694336 | bytes 10618376 | tf_op jit(solution)/shard_map/reduce_sum | solution.py:109
  64.1 3.9 %fusion.35 = (f32[384]{0:T(512)S(1)}, f32[384,1024]{1,0:T(8,128)S(1)}) fusion(bf16[4608,384]{1,0:T(8,128)(2,1)S(1)} %fusion.3, bf16[4608,1024]{1,0:T(8,128)(2,1)S(1)} %bitcast.117), kind=kOutput, calls=%fused_computation.105 | convolution fusion | flops 3624271360 | bytes 14550528 | tf_op jit(solution)/shard_map/dot_general | solution.py:113
  73.4 3.5 %multiply_convert_fusion = bf16[16,2,144,384]{3,2,1,0:T(8,128)(2,1)S(1)} fusion(f32[16,2,144,384]{3,2,1,0:T(8,128)} %bitcast.112, f32[16,2,144]{2,1,0:T(2,128)S(1)} %mul.186, f32[384]{0:T(512)S(1)} %add_rsqrt_fusion), kind=kLoop, calls=%fused_computation.16 | loop fusion | flops 5308416 | bytes 10636800 | tf_op jit(solution)/shard_map/convert_element_type | solution.py:112
  77.0 2.9 %collective-permute-start.9 = (f32[2,384]{1,0:T(2,128)S(1)}, f32[2,384]{1,0:T(2,128)S(1)}, u32[]{:S(2)}, u32[]{:S(2)}) collective-permute-start(f32[2,384]{1,0:T(2,128)S(1)} %pad_maximum_fusion.4), channel_id=1, source_target_pairs={{0,4},{1,5},{2,6},{3,7},{4,0},{5,1},{6,2},{7,3},{8,12},{9,13},{10,... | collective-permute-start | bytes 9224 | tf_op jit(solution)/shard_map/ppermute | solution.py:56
  84.1 10.3 %collective-permute-start.24 = (f32[2304,1024]{1,0:T(8,128)S(1)}, f32[2304,1024]{1,0:T(8,128)S(1)}, u32[]{:S(2)}, u32[]{:S(2)}) collective-permute-start(f32[2304,1024]{1,0:T(8,128)S(1)} %fusion.36), channel_id=1, source_target_pairs={{0,8},{8,0},{1,9},{9,1},{2,10},{10,2},{3,11},{11,3},{4,12},{12,4},... | collective-permute-start | bytes 28311560 | tf_op jit(solution)/shard_map/ppermute | solution.py:134
  94.4 14.3 %collective-permute-done.24 = f32[2304,1024]{1,0:T(8,128)S(1)} collective-permute-done((f32[2304,1024]{1,0:T(8,128)S(1)}, f32[2304,1024]{1,0:T(8,128)S(1)}, u32[]{:S(2)}, u32[]{:S(2)}) %collective-permute-start.24) | collective-permute-done | bytes 9437216 | tf_op jit(solution)/shard_map/ppermute | solution.py:134
  108.7 5.1 %convolution_add_fusion = f32[2304,1024]{1,0:T(8,128)} fusion(f32[2304,1024]{1,0:T(8,128)S(1)} %collective-permute-done.24, bf16[2304,384]{1,0:T(8,128)(2,1)S(1)} %bitcast.118, bf16[384,1024]{1,0:T(8,128)(2,1)S(1)} %subtract_convert_fusion), kind=kOutput, calls=%fused_computation.18 | convolution fusion | flops 1814298624 | bytes 21430272 | tf_op jit(solution)/shard_map/dot_general | solution.py:130
  114.6 3.5 %bitcast_multiply_fusion = f32[8,576,384]{2,1,0:T(8,128)S(1)} fusion(f32[2,4,576,384]{3,2,1,0:T(8,128)} %copy-done, f32[384]{0:T(512)S(1)} %add_rsqrt_fusion), kind=kLoop, calls=%fused_computation.8 | loop fusion | flops 1769472 | bytes 14157312 | tf_op jit(solution)/shard_map/mul | solution.py:111
  118.1 7.6 %fusion.13 = f32[8,384,576]{1,2,0:T(8,128)S(1)} fusion(bf16[8,576,1024]{2,1,0:T(8,128)(2,1)} %bitcast.115, bf16[384,1024]{1,0:T(8,128)(2,1)S(1)} %subtract_convert_fusion), kind=kOutput, calls=%fused_computation.30 | convolution fusion | flops 3623878656 | bytes 17301504 | tf_op jit(solution)/shard_map/dot_general | solution.py:138
  139.8 9.9 %collective-permute-done.10 = f32[2,288,384]{2,1,0:T(8,128)} collective-permute-done((f32[2,288,384]{2,1,0:T(8,128)}, f32[2,288,384]{2,1,0:T(8,128)}, u32[]{:S(2)}, u32[]{:S(2)}) %collective-permute-start.10) | collective-permute-done | bytes 884768 | tf_op jit(solution)/shard_map/ppermute | solution.py:82
  151.9 7.8 %collective-permute-done.17 = f32[2,296,384]{2,1,0:T(8,128)} collective-permute-done((f32[2,296,384]{2,1,0:T(8,128)}, f32[2,296,384]{2,1,0:T(8,128)}, u32[]{:S(2)}, u32[]{:S(2)}) %collective-permute-start.17) | collective-permute-done | bytes 909344 | tf_op jit(solution)/shard_map/ppermute | solution.py:83
  162.2 3.0 %collective-permute-start.18 = (f32[2,296,384]{2,1,0:T(8,128)}, f32[2,296,384]{2,1,0:T(8,128)}, u32[]{:S(2)}, u32[]{:S(2)}) collective-permute-start(f32[2,296,384]{2,1,0:T(8,128)} %bitcast_add_fusion), channel_id=1, source_target_pairs={{0,3},{1,0},{2,1},{3,2},{4,7},{5,4},{6,5},{7,6},{8,11},{9,8},{10,9... | collective-permute-start | bytes 2727944 | tf_op jit(solution)/shard_map/ppermute | solution.py:83
  165.2 8.1 %collective-permute-done.11 = f32[2,288,384]{2,1,0:T(8,128)} collective-permute-done((f32[2,288,384]{2,1,0:T(8,128)}, f32[2,288,384]{2,1,0:T(8,128)}, u32[]{:S(2)}, u32[]{:S(2)}) %collective-permute-start.11) | collective-permute-done | bytes 884768 | tf_op jit(solution)/shard_map/ppermute | solution.py:82
  175.5 8.3 %collective-permute-done.18 = f32[2,296,384]{2,1,0:T(8,128)} collective-permute-done((f32[2,296,384]{2,1,0:T(8,128)}, f32[2,296,384]{2,1,0:T(8,128)}, u32[]{:S(2)}, u32[]{:S(2)}) %collective-permute-start.18) | collective-permute-done | bytes 909344 | tf_op jit(solution)/shard_map/ppermute | solution.py:83
  185.4 3.5 %collective-permute-start.19 = (f32[2,296,384]{2,1,0:T(8,128)S(1)}, f32[2,296,384]{2,1,0:T(8,128)S(1)}, u32[]{:S(2)}, u32[]{:S(2)}) collective-permute-start(f32[2,296,384]{2,1,0:T(8,128)S(1)} %bitcast_add_fusion.1), channel_id=1, source_target_pairs={{0,3},{1,0},{2,1},{3,2},{4,7},{5,4},{6,5},{7,6},{8,11},{9,8},{10,9... | collective-permute-start | bytes 2727944 | tf_op jit(solution)/shard_map/ppermute | solution.py:83
  188.8 7.2 %collective-permute-done.12 = f32[2,288,384]{2,1,0:T(8,128)} collective-permute-done((f32[2,288,384]{2,1,0:T(8,128)}, f32[2,288,384]{2,1,0:T(8,128)}, u32[]{:S(2)}, u32[]{:S(2)}) %collective-permute-start.12) | collective-permute-done | bytes 884768 | tf_op jit(solution)/shard_map/ppermute | solution.py:82
  208.8 19.5 %collective-permute-done.13 = f32[72,384]{1,0:T(8,128)S(1)} collective-permute-done((f32[72,384]{1,0:T(8,128)S(1)}, f32[72,384]{1,0:T(8,128)S(1)}, u32[]{:S(2)}, u32[]{:S(2)}) %collective-permute-start.13) | collective-permute-done | bytes 110624 | tf_op jit(solution)/shard_map/ppermute | solution.py:95
  247.8 3.4 %collective-permute-done.26 = f32[576]{0:T(1024)S(1)} collective-permute-done((f32[576]{0:T(1024)S(1)}, f32[576]{0:T(1024)S(1)}, u32[]{:S(2)}, u32[]{:S(2)}) %collective-permute-start.26) | collective-permute-done | bytes 2336 | tf_op jit(solution)/shard_map/ppermute | solution.py:47
  251.9 5.6 %collective-permute-done.27 = f32[576]{0:T(1024)S(1)} collective-permute-done((f32[576]{0:T(1024)S(1)}, f32[576]{0:T(1024)S(1)}, u32[]{:S(2)}, u32[]{:S(2)}) %collective-permute-start.27) | collective-permute-done | bytes 2336 | tf_op jit(solution)/shard_map/ppermute | solution.py:47
  260.3 4.8 %collective-permute-start.29 = (f32[576]{0:T(1024)S(1)}, f32[576]{0:T(1024)S(1)}, u32[]{:S(2)}, u32[]{:S(2)}) collective-permute-start(f32[576]{0:T(1024)S(1)} %add.292), channel_id=1, source_target_pairs={{0,8},{8,0},{1,9},{9,1},{2,10},{10,2},{3,11},{11,3},{4,12},{12,4},... | collective-permute-start | bytes 6920 | tf_op jit(solution)/shard_map/ppermute | solution.py:47
  (131 shorter events, 83.6 us)
Async XLA Ops:
  7.2 259.6 %reduce-scatter.2.cloned.1.call-start = ((), (), s32[]{:S(2)}) async-start(), calls=%async_computation.1 | async-start | bytes 10027008 | tf_op jit(solution)/shard_map/reduce_scatter | solution.py:136
  7.2 11.7 %collective-permute-start.6 = (bf16[576,384]{1,0:T(8,128)(2,1)}, bf16[576,384]{1,0:T(8,128)(2,1)S(1)}, u32[]{:S(2)}, u32[]{:S(2)}) collective-permute-start(bf16[576,384]{1,0:T(8,128)(2,1)} %bitcast.120), channel_id=1, source_target_pairs={{0,1},{1,2},{2,3},{3,0},{4,5},{5,6},{6,7},{7,4},{8,9},{9,10},{10,1... | collective-permute-start | bytes 1327112 | tf_op jit(solution)/shard_map/ppermute | solution.py:32
  9.4 36.8 %collective-permute-start.5 = (bf16[576,384]{1,0:T(8,128)(2,1)}, bf16[576,384]{1,0:T(8,128)(2,1)S(1)}, u32[]{:S(2)}, u32[]{:S(2)}) collective-permute-start(bf16[576,384]{1,0:T(8,128)(2,1)} %bitcast.121), channel_id=1, source_target_pairs={{0,2},{1,3},{2,0},{3,1},{4,6},{5,7},{6,4},{7,5},{8,10},{9,11},{10,... | collective-permute-start | bytes 1327112 | tf_op jit(solution)/shard_map/ppermute | solution.py:32
  12.0 34.2 %collective-permute-start.4 = (bf16[576,384]{1,0:T(8,128)(2,1)}, bf16[576,384]{1,0:T(8,128)(2,1)S(1)}, u32[]{:S(2)}, u32[]{:S(2)}) collective-permute-start(bf16[576,384]{1,0:T(8,128)(2,1)} %bitcast.122), channel_id=1, source_target_pairs={{0,3},{1,0},{2,1},{3,2},{4,7},{5,4},{6,5},{7,6},{8,11},{9,8},{10,9... | collective-permute-start | bytes 1327112 | tf_op jit(solution)/shard_map/ppermute | solution.py:32
  13.1 34.5 %collective-permute-start.3 = (bf16[576,384]{1,0:T(8,128)(2,1)}, bf16[576,384]{1,0:T(8,128)(2,1)S(1)}, u32[]{:S(2)}, u32[]{:S(2)}) collective-permute-start(bf16[576,384]{1,0:T(8,128)(2,1)} %bitcast.123), channel_id=1, source_target_pairs={{0,4},{1,5},{2,6},{3,7},{4,0},{5,1},{6,2},{7,3},{8,12},{9,13},{10,... | collective-permute-start | bytes 1327112 | tf_op jit(solution)/shard_map/ppermute | solution.py:32
  15.8 31.7 %collective-permute-start.2 = (bf16[576,384]{1,0:T(8,128)(2,1)}, bf16[576,384]{1,0:T(8,128)(2,1)S(1)}, u32[]{:S(2)}, u32[]{:S(2)}) collective-permute-start(bf16[576,384]{1,0:T(8,128)(2,1)} %bitcast.124), channel_id=1, source_target_pairs={{0,5},{1,6},{2,7},{3,4},{4,1},{5,2},{6,3},{7,0},{8,13},{9,14},{10,... | collective-permute-start | bytes 1327112 | tf_op jit(solution)/shard_map/ppermute | solution.py:32
  18.9 28.7 %collective-permute-start.1 = (bf16[576,384]{1,0:T(8,128)(2,1)}, bf16[576,384]{1,0:T(8,128)(2,1)S(1)}, u32[]{:S(2)}, u32[]{:S(2)}) collective-permute-start(bf16[576,384]{1,0:T(8,128)(2,1)} %bitcast.125), channel_id=1, source_target_pairs={{0,6},{1,7},{2,4},{3,5},{4,2},{5,3},{6,0},{7,1},{8,14},{9,15},{10,... | collective-permute-start | bytes 1327112 | tf_op jit(solution)/shard_map/ppermute | solution.py:32
  46.2 10.2 %collective-permute-start = (bf16[576,384]{1,0:T(8,128)(2,1)}, bf16[576,384]{1,0:T(8,128)(2,1)S(1)}, u32[]{:S(2)}, u32[]{:S(2)}) collective-permute-start(bf16[576,384]{1,0:T(8,128)(2,1)} %bitcast.126), channel_id=1, source_target_pairs={{0,7},{1,4},{2,5},{3,6},{4,3},{5,0},{6,1},{7,2},{8,15},{9,12},{10,... | collective-permute-start | bytes 1327112 | tf_op jit(solution)/shard_map/ppermute | solution.py:32
  84.1 24.6 %collective-permute-start.24 = (f32[2304,1024]{1,0:T(8,128)S(1)}, f32[2304,1024]{1,0:T(8,128)S(1)}, u32[]{:S(2)}, u32[]{:S(2)}) collective-permute-start(f32[2304,1024]{1,0:T(8,128)S(1)} %fusion.36), channel_id=1, source_target_pairs={{0,8},{8,0},{1,9},{9,1},{2,10},{10,2},{3,11},{11,3},{4,12},{12,4},... | collective-permute-start | bytes 28311560 | tf_op jit(solution)/shard_map/ppermute | solution.py:134
  127.3 22.4 %collective-permute-start.10 = (f32[2,288,384]{2,1,0:T(8,128)}, f32[2,288,384]{2,1,0:T(8,128)}, u32[]{:S(2)}, u32[]{:S(2)}) collective-permute-start(f32[2,288,384]{2,1,0:T(8,128)} %dynamic-slice_bitcast_fusion.1), channel_id=1, source_target_pairs={{0,1},{1,2},{2,3},{3,0},{4,5},{5,6},{6,7},{7,4},{8,9},{9,10},{10,1... | collective-permute-start | bytes 2654216 | tf_op jit(solution)/shard_map/ppermute | solution.py:82
  138.0 21.7 %collective-permute-start.17 = (f32[2,296,384]{2,1,0:T(8,128)}, f32[2,296,384]{2,1,0:T(8,128)}, u32[]{:S(2)}, u32[]{:S(2)}) collective-permute-start(f32[2,296,384]{2,1,0:T(8,128)} %dynamic-slice_bitcast_fusion), channel_id=1, source_target_pairs={{0,3},{1,0},{2,1},{3,2},{4,7},{5,4},{6,5},{7,6},{8,11},{9,8},{10,9... | collective-permute-start | bytes 2727944 | tf_op jit(solution)/shard_map/ppermute | solution.py:83
  151.9 21.5 %collective-permute-start.11 = (f32[2,288,384]{2,1,0:T(8,128)}, f32[2,288,384]{2,1,0:T(8,128)}, u32[]{:S(2)}, u32[]{:S(2)}) collective-permute-start(f32[2,288,384]{2,1,0:T(8,128)} %bitcast_add_fusion.3), channel_id=1, source_target_pairs={{0,1},{1,2},{2,3},{3,0},{4,5},{5,6},{6,7},{7,4},{8,9},{9,10},{10,1... | collective-permute-start | bytes 2654216 | tf_op jit(solution)/shard_map/ppermute | solution.py:82
  162.2 21.6 %collective-permute-start.18 = (f32[2,296,384]{2,1,0:T(8,128)}, f32[2,296,384]{2,1,0:T(8,128)}, u32[]{:S(2)}, u32[]{:S(2)}) collective-permute-start(f32[2,296,384]{2,1,0:T(8,128)} %bitcast_add_fusion), channel_id=1, source_target_pairs={{0,3},{1,0},{2,1},{3,2},{4,7},{5,4},{6,5},{7,6},{8,11},{9,8},{10,9... | collective-permute-start | bytes 2727944 | tf_op jit(solution)/shard_map/ppermute | solution.py:83
  175.5 20.5 %collective-permute-start.12 = (f32[2,288,384]{2,1,0:T(8,128)}, f32[2,288,384]{2,1,0:T(8,128)}, u32[]{:S(2)}, u32[]{:S(2)}) collective-permute-start(f32[2,288,384]{2,1,0:T(8,128)} %bitcast_add_fusion.4), channel_id=1, source_target_pairs={{0,1},{1,2},{2,3},{3,0},{4,5},{5,6},{6,7},{7,4},{8,9},{9,10},{10,1... | collective-permute-start | bytes 2654216 | tf_op jit(solution)/shard_map/ppermute | solution.py:82
  185.4 20.8 %collective-permute-start.19 = (f32[2,296,384]{2,1,0:T(8,128)S(1)}, f32[2,296,384]{2,1,0:T(8,128)S(1)}, u32[]{:S(2)}, u32[]{:S(2)}) collective-permute-start(f32[2,296,384]{2,1,0:T(8,128)S(1)} %bitcast_add_fusion.1), channel_id=1, source_target_pairs={{0,3},{1,0},{2,1},{3,2},{4,7},{5,4},{6,5},{7,6},{8,11},{9,8},{10,9... | collective-permute-start | bytes 2727944 | tf_op jit(solution)/shard_map/ppermute | solution.py:83
  197.4 30.9 %collective-permute-start.13 = (f32[72,384]{1,0:T(8,128)S(1)}, f32[72,384]{1,0:T(8,128)S(1)}, u32[]{:S(2)}, u32[]{:S(2)}) collective-permute-start(f32[72,384]{1,0:T(8,128)S(1)} %dynamic-slice_bitcast_fusion.9), channel_id=1, source_target_pairs={{0,4},{1,5},{2,6},{3,7},{4,0},{5,1},{6,2},{7,3},{8,12},{9,13},{10,... | collective-permute-start | bytes 331784 | tf_op jit(solution)/shard_map/ppermute | solution.py:95
  198.4 32.3 %collective-permute-start.14 = (f32[72,384]{1,0:T(8,128)S(1)}, f32[72,384]{1,0:T(8,128)S(1)}, u32[]{:S(2)}, u32[]{:S(2)}) collective-permute-start(f32[72,384]{1,0:T(8,128)S(1)} %dynamic-slice_bitcast_fusion.8), channel_id=1, source_target_pairs={{0,4},{1,5},{2,6},{3,7},{4,0},{5,1},{6,2},{7,3},{8,12},{9,13},{10,... | collective-permute-start | bytes 331784 | tf_op jit(solution)/shard_map/ppermute | solution.py:95
  200.6 32.5 %collective-permute-start.15 = (f32[72,384]{1,0:T(8,128)S(1)}, f32[72,384]{1,0:T(8,128)S(1)}, u32[]{:S(2)}, u32[]{:S(2)}) collective-permute-start(f32[72,384]{1,0:T(8,128)S(1)} %dynamic-slice_bitcast_fusion.7), channel_id=1, source_target_pairs={{0,4},{1,5},{2,6},{3,7},{4,0},{5,1},{6,2},{7,3},{8,12},{9,13},{10,... | collective-permute-start | bytes 331784 | tf_op jit(solution)/shard_map/ppermute | solution.py:95
  201.6 33.8 %collective-permute-start.16 = (f32[72,384]{1,0:T(8,128)S(1)}, f32[72,384]{1,0:T(8,128)S(1)}, u32[]{:S(2)}, u32[]{:S(2)}) collective-permute-start(f32[72,384]{1,0:T(8,128)S(1)} %dynamic-slice_bitcast_fusion.6), channel_id=1, source_target_pairs={{0,4},{1,5},{2,6},{3,7},{4,0},{5,1},{6,2},{7,3},{8,12},{9,13},{10,... | collective-permute-start | bytes 331784 | tf_op jit(solution)/shard_map/ppermute | solution.py:95
  207.6 30.2 %collective-permute-start.20 = (f32[72,384]{1,0:T(8,128)S(1)}, f32[72,384]{1,0:T(8,128)S(1)}, u32[]{:S(2)}, u32[]{:S(2)}) collective-permute-start(f32[72,384]{1,0:T(8,128)S(1)} %dynamic-slice_bitcast_fusion.5), channel_id=1, source_target_pairs={{0,4},{1,5},{2,6},{3,7},{4,0},{5,1},{6,2},{7,3},{8,12},{9,13},{10,... | collective-permute-start | bytes 331784 | tf_op jit(solution)/shard_map/ppermute | solution.py:95
  228.3 11.8 %collective-permute-start.21 = (f32[72,384]{1,0:T(8,128)S(1)}, f32[72,384]{1,0:T(8,128)S(1)}, u32[]{:S(2)}, u32[]{:S(2)}) collective-permute-start(f32[72,384]{1,0:T(8,128)S(1)} %dynamic-slice_bitcast_fusion.4), channel_id=1, source_target_pairs={{0,4},{1,5},{2,6},{3,7},{4,0},{5,1},{6,2},{7,3},{8,12},{9,13},{10,... | collective-permute-start | bytes 331784 | tf_op jit(solution)/shard_map/ppermute | solution.py:95
  230.7 11.8 %collective-permute-start.22 = (f32[72,384]{1,0:T(8,128)S(1)}, f32[72,384]{1,0:T(8,128)S(1)}, u32[]{:S(2)}, u32[]{:S(2)}) collective-permute-start(f32[72,384]{1,0:T(8,128)S(1)} %dynamic-slice_bitcast_fusion.3), channel_id=1, source_target_pairs={{0,4},{1,5},{2,6},{3,7},{4,0},{5,1},{6,2},{7,3},{8,12},{9,13},{10,... | collective-permute-start | bytes 331784 | tf_op jit(solution)/shard_map/ppermute | solution.py:95
  233.1 12.1 %collective-permute-start.23 = (f32[80,384]{1,0:T(8,128)S(1)}, f32[80,384]{1,0:T(8,128)S(1)}, u32[]{:S(2)}, u32[]{:S(2)}) collective-permute-start(f32[80,384]{1,0:T(8,128)S(1)} %dynamic-slice_bitcast_fusion.2), channel_id=1, source_target_pairs={{0,4},{1,5},{2,6},{3,7},{4,0},{5,1},{6,2},{7,3},{8,12},{9,13},{10,... | collective-permute-start | bytes 368648 | tf_op jit(solution)/shard_map/ppermute | solution.py:95
  251.2 6.4 %collective-permute-start.27 = (f32[576]{0:T(1024)S(1)}, f32[576]{0:T(1024)S(1)}, u32[]{:S(2)}, u32[]{:S(2)}) collective-permute-start(f32[576]{0:T(1024)S(1)} %add.290), channel_id=1, source_target_pairs={{0,64},{16,80},{32,96},{48,112},{64,0},{80,16},{96,32},{112,48},{1... | collective-permute-start | bytes 6920 | tf_op jit(solution)/shard_map/ppermute | solution.py:47
  (17 other events, 127.7 us)
Sparse Core Ops, SparseCore 0:
  113.9 111.5 reduce-scatter.1

commit v12 on v9

--- a/solution.py
+++ b/solution.py
@@ -49,14 +49,27 @@
     return x
 
 
-def butterfly_softmax_stats(top, logits, axis, n):
+def group_softmax_stats(top, logits, axis, n_hi, n_lo):
     total = jnp.sum(jnp.exp(logits - top[:, None]), axis=1)
-    b = 1
-    while b < n:
-        other = lax.ppermute(jnp.stack([top, total]), axis, [(c, c ^ b) for c in range(n)])
-        other_top, other_total = other[0], other[1]
-        new_top = jnp.maximum(top, other_top)
-        total = total * jnp.exp(top - new_top) + other_total * jnp.exp(other_top - new_top)
+    me = lax.axis_index(axis)
+    lo = me % n_lo
+    packed = jnp.stack([top, total])
+    got = [packed]
+    for k in range(1, n_lo):
+        perm = [(a * n_lo + l, a * n_lo + (l + k) % n_lo) for a in range(n_hi) for l in range(n_lo)]
+        got.append(lax.ppermute(packed, axis, perm))
+    rev = jnp.stack(got[::-1])
+    doubled = jnp.concatenate([rev, rev], axis=0)
+    ordered = lax.dynamic_slice_in_dim(doubled, (n_lo - 1) - lo, n_lo, axis=0)
+    top = jnp.max(ordered[:, 0, :], axis=0)
+    total = jnp.sum(ordered[:, 1, :] * jnp.exp(ordered[:, 0, :] - top[None, :]), axis=0)
+    b = n_lo
+    while b < n_hi * n_lo:
+        other = lax.ppermute(
+            jnp.stack([top, total]), axis, [(c, c ^ b) for c in range(n_hi * n_lo)]
+        )
+        new_top = jnp.maximum(top, other[0])
+        total = total * jnp.exp(top - new_top) + other[1] * jnp.exp(other[0] - new_top)
         top = new_top
         b *= 2
     return top, total
@@ -112,8 +125,8 @@
     logits = lax.dot_general(
         normed_t, head_weight, (((0,), (0,)), ((), ())), preferred_element_type=jnp.float32
     )
-    row_top, row_total = butterfly_softmax_stats(
-        jnp.max(logits, axis=1), logits, "tensor", n_tensor
+    row_top, row_total = group_softmax_stats(
+        jnp.max(logits, axis=1), logits, "tensor", n_hi, n_lo
     )
     log_total = row_top + jnp.log(row_total)
     offset = lax.axis_index("tensor") * vocab_rows

time: 265 us -> 265 us (level)
  local copies, waits for them, and re-layouts: 9.82 us -> 14.3 us
    ppermute x3, waiting for transfers between devices: 23.6 us -> 26.7 us  [two_stage_reduce_scatter(): recv_f = lax.ppermute(send_f, axis, perm_f)]
    convert_element_type x2, other arithmetic: 5.5 us -> 2.85 us  [shards(): normed_t = (normalized_t * norm_gain[:, None]).astype(jnp.bfloat16)]
    ppermute x3 -> x4, starting transfers between devices: 5.81 us -> 6.07 us  [the longest x3 3.87 us: group_softmax_stats(): got.append(lax.ppermute(packed, axis, perm))]
  transfers between devices with their start and end apart: 27 -> 28, of which waited for: 19 -> 19; matrix products, arithmetic and copies ran while one was open for 15% -> 15% of each run, Pallas kernels for 0% -> 0%
where the time goes in v12:
time: 265 us
  waiting for transfers between devices  135 us (51%)
  starting transfers between devices  47.9 us (18%)
  other arithmetic  33.6 us (13%)
  matrix products  19.2 us (7%)
  between operations  14.6 us (6%)
  local copies, waits for them, and re-layouts  14.3 us (5%)
    ppermute x7, waiting for transfers between devices, grid_gather(): got[a, b] = lax.ppermute(x, axis, perm)  31 us
    ppermute x4, waiting for transfers between devices, two_stage_reduce_scatter(): mine = mine + lax.ppermute(other, axis, perm_h)  27.6 us
    ppermute x3, waiting for transfers between devices, two_stage_reduce_scatter(): recv_f = lax.ppermute(send_f, axis, perm_f)  26.7 us
    ppermute x3, waiting for transfers between devices, two_stage_reduce_scatter(): recv_b = lax.ppermute(send_b, axis, perm_b)  22.4 us
    ppermute x7, starting transfers between devices, grid_gather(): got[a, b] = lax.ppermute(x, axis, perm)  14.9 us
    ppermute x1, waiting for transfers between devices, shards(): sent = lax.ppermute(head_rows(1 - core), 'core', [(0, 1), (1, 0)])  14.3 us
    ppermute x1, starting transfers between devices, shards(): sent = lax.ppermute(head_rows(1 - core), 'core', [(0, 1), (1, 0)])  10.9 us
    ppermute x5, waiting for transfers between devices, butterfly_sum(): x = x + lax.ppermute(x, axis, [(c, c ^ b) for c in range(n)])  10.3 us
  transfers between devices with their start and end apart: 28, of which 19 were waited for; matrix products, arithmetic and copies ran while one was open for 15% of the time, Pallas kernels for 0%

profile of v12, /device:TPU:1, one launch (start us, length us, event | category | flops | bytes accessed | tf_op | source)
XLA Modules:
  0.0 264.6 jit_solution(8630435640672671595)
XLA Ops:
  13.1 2.7 %collective-permute-start.3 = (bf16[576,384]{1,0:T(8,128)(2,1)}, bf16[576,384]{1,0:T(8,128)(2,1)S(1)}, u32[]{:S(2)}, u32[]{:S(2)}) collective-permute-start(bf16[576,384]{1,0:T(8,128)(2,1)} %bitcast.107), channel_id=1, source_target_pairs={{0,4},{1,5},{2,6},{3,7},{4,0},{5,1},{6,2},{7,3},{8,12},{9,13},{10,... | collective-permute-start | bytes 1327112 | tf_op jit(solution)/shard_map/ppermute | solution.py:32
  16.2 2.7 %collective-permute-done.6 = bf16[576,384]{1,0:T(8,128)(2,1)S(1)} collective-permute-done((bf16[576,384]{1,0:T(8,128)(2,1)}, bf16[576,384]{1,0:T(8,128)(2,1)S(1)}, u32[]{:S(2)}, u32[]{:S(2)}) %collective-permute-start.6) | collective-permute-done | bytes 442400 | tf_op jit(solution)/shard_map/ppermute | solution.py:32
  18.9 5.9 %collective-permute-start.1 = (bf16[576,384]{1,0:T(8,128)(2,1)}, bf16[576,384]{1,0:T(8,128)(2,1)S(1)}, u32[]{:S(2)}, u32[]{:S(2)}) collective-permute-start(bf16[576,384]{1,0:T(8,128)(2,1)} %bitcast.109), channel_id=1, source_target_pairs={{0,6},{1,7},{2,4},{3,5},{4,2},{5,3},{6,0},{7,1},{8,14},{9,15},{10,... | collective-permute-start | bytes 1327112 | tf_op jit(solution)/shard_map/ppermute | solution.py:32
  24.8 21.4 %collective-permute-done.5 = bf16[576,384]{1,0:T(8,128)(2,1)S(1)} collective-permute-done((bf16[576,384]{1,0:T(8,128)(2,1)}, bf16[576,384]{1,0:T(8,128)(2,1)S(1)}, u32[]{:S(2)}, u32[]{:S(2)}) %collective-permute-start.5) | collective-permute-done | bytes 442400 | tf_op jit(solution)/shard_map/ppermute | solution.py:32
  49.6 6.9 %collective-permute-done = bf16[576,384]{1,0:T(8,128)(2,1)S(1)} collective-permute-done((bf16[576,384]{1,0:T(8,128)(2,1)}, bf16[576,384]{1,0:T(8,128)(2,1)S(1)}, u32[]{:S(2)}, u32[]{:S(2)}) %collective-permute-start) | collective-permute-done | bytes 442400 | tf_op jit(solution)/shard_map/ppermute | solution.py:32
  56.8 4.5 %multiply_reduce_fusion = (f32[384]{0:T(512)S(1)}, f32[2,4,576,384]{3,2,1,0:T(8,128)S(1)}) fusion(s32[]{:T(128)S(6)} %select_n.101, s32[]{:T(128)S(6)} %select_n.104, bf16[1,4,576,384]{3,2,1,0:T(8,128)(2,1)S(1)} %maximum_bitcast_fusion.1, bf16[1,4,576,384]{3,2,1,0:T(8,128)(2,1)S(1)} %maximum_bitcast_fusion), kind=kLoop, calls=%fused_computation.17 | loop fusion | flops 17694336 | bytes 10618376 | tf_op jit(solution)/shard_map/reduce_sum | solution.py:121
  63.4 3.9 %fusion.29 = (f32[384]{0:T(512)S(1)}, f32[384,1024]{1,0:T(8,128)S(1)}) fusion(bf16[4608,384]{1,0:T(8,128)(2,1)S(1)} %fusion.3, bf16[4608,1024]{1,0:T(8,128)(2,1)S(1)} %bitcast.101), kind=kOutput, calls=%fused_computation.84 | convolution fusion | flops 3624271360 | bytes 14550528 | tf_op jit(solution)/shard_map/dot_general | solution.py:125
  68.3 3.0 %collective-permute-start.8 = (f32[2,384]{1,0:T(2,128)S(1)}, f32[2,384]{1,0:T(2,128)S(1)}, u32[]{:S(2)}, u32[]{:S(2)}) collective-permute-start(f32[2,384]{1,0:T(2,128)S(1)} %pad_maximum_fusion.5), channel_id=1, source_target_pairs={{0,2},{1,3},{2,0},{3,1},{4,6},{5,7},{6,4},{7,5},{8,10},{9,11},{10,... | collective-permute-start | bytes 9224 | tf_op jit(solution)/shard_map/ppermute | solution.py:60
  84.5 10.9 %collective-permute-start.21 = (f32[2304,1024]{1,0:T(8,128)S(1)}, f32[2304,1024]{1,0:T(8,128)S(1)}, u32[]{:S(2)}, u32[]{:S(2)}) collective-permute-start(f32[2304,1024]{1,0:T(8,128)S(1)} %fusion.30), channel_id=1, source_target_pairs={{0,8},{8,0},{1,9},{9,1},{2,10},{10,2},{3,11},{11,3},{4,12},{12,4},... | collective-permute-start | bytes 28311560 | tf_op jit(solution)/shard_map/ppermute | solution.py:146
  95.4 14.3 %collective-permute-done.21 = f32[2304,1024]{1,0:T(8,128)S(1)} collective-permute-done((f32[2304,1024]{1,0:T(8,128)S(1)}, f32[2304,1024]{1,0:T(8,128)S(1)}, u32[]{:S(2)}, u32[]{:S(2)}) %collective-permute-start.21) | collective-permute-done | bytes 9437216 | tf_op jit(solution)/shard_map/ppermute | solution.py:146
  109.6 5.1 %convolution_add_fusion = f32[2304,1024]{1,0:T(8,128)} fusion(f32[2304,1024]{1,0:T(8,128)S(1)} %collective-permute-done.21, bf16[2304,384]{1,0:T(8,128)(2,1)S(1)} %bitcast.102, bf16[384,1024]{1,0:T(8,128)(2,1)S(1)} %subtract_convert_fusion), kind=kOutput, calls=%fused_computation.18 | convolution fusion | flops 1814298624 | bytes 21430272 | tf_op jit(solution)/shard_map/dot_general | solution.py:142
  116.2 3.5 %bitcast_multiply_fusion = f32[8,576,384]{2,1,0:T(8,128)S(1)} fusion(f32[2,4,576,384]{3,2,1,0:T(8,128)} %copy-done, f32[384]{0:T(512)S(1)} %add_rsqrt_fusion), kind=kLoop, calls=%fused_computation.8 | loop fusion | flops 1769472 | bytes 14157312 | tf_op jit(solution)/shard_map/mul | solution.py:123
  119.8 7.6 %fusion.13 = f32[8,384,576]{1,2,0:T(8,128)S(1)} fusion(bf16[8,576,1024]{2,1,0:T(8,128)(2,1)} %bitcast.99, bf16[384,1024]{1,0:T(8,128)(2,1)S(1)} %subtract_convert_fusion), kind=kOutput, calls=%fused_computation.30 | convolution fusion | flops 3623878656 | bytes 17301504 | tf_op jit(solution)/shard_map/dot_general | solution.py:150
  140.7 10.6 %collective-permute-done.11 = f32[2,288,384]{2,1,0:T(8,128)} collective-permute-done((f32[2,288,384]{2,1,0:T(8,128)}, f32[2,288,384]{2,1,0:T(8,128)}, u32[]{:S(2)}, u32[]{:S(2)}) %collective-permute-start.11) | collective-permute-done | bytes 884768 | tf_op jit(solution)/shard_map/ppermute | solution.py:95
  153.5 7.8 %collective-permute-done.16 = f32[2,296,384]{2,1,0:T(8,128)} collective-permute-done((f32[2,296,384]{2,1,0:T(8,128)}, f32[2,296,384]{2,1,0:T(8,128)}, u32[]{:S(2)}, u32[]{:S(2)}) %collective-permute-start.16) | collective-permute-done | bytes 909344 | tf_op jit(solution)/shard_map/ppermute | solution.py:96
  165.8 9.1 %collective-permute-done.12 = f32[2,288,384]{2,1,0:T(8,128)} collective-permute-done((f32[2,288,384]{2,1,0:T(8,128)}, f32[2,288,384]{2,1,0:T(8,128)}, u32[]{:S(2)}, u32[]{:S(2)}) %collective-permute-start.12) | collective-permute-done | bytes 884768 | tf_op jit(solution)/shard_map/ppermute | solution.py:95
  177.2 7.4 %collective-permute-done.17 = f32[2,296,384]{2,1,0:T(8,128)} collective-permute-done((f32[2,296,384]{2,1,0:T(8,128)}, f32[2,296,384]{2,1,0:T(8,128)}, u32[]{:S(2)}, u32[]{:S(2)}) %collective-permute-start.17) | collective-permute-done | bytes 909344 | tf_op jit(solution)/shard_map/ppermute | solution.py:96
  187.1 3.0 %collective-permute-start.18 = (f32[2,296,384]{2,1,0:T(8,128)}, f32[2,296,384]{2,1,0:T(8,128)}, u32[]{:S(2)}, u32[]{:S(2)}) collective-permute-start(f32[2,296,384]{2,1,0:T(8,128)} %bitcast_add_fusion.1), channel_id=1, source_target_pairs={{0,3},{1,0},{2,1},{3,2},{4,7},{5,4},{6,5},{7,6},{8,11},{9,8},{10,9... | collective-permute-start | bytes 2727944 | tf_op jit(solution)/shard_map/ppermute | solution.py:96
  190.8 7.0 %collective-permute-done.13 = f32[2,288,384]{2,1,0:T(8,128)} collective-permute-done((f32[2,288,384]{2,1,0:T(8,128)}, f32[2,288,384]{2,1,0:T(8,128)}, u32[]{:S(2)}, u32[]{:S(2)}) %collective-permute-start.13) | collective-permute-done | bytes 884768 | tf_op jit(solution)/shard_map/ppermute | solution.py:95
  200.1 7.3 %collective-permute-done.18 = f32[2,296,384]{2,1,0:T(8,128)} collective-permute-done((f32[2,296,384]{2,1,0:T(8,128)}, f32[2,296,384]{2,1,0:T(8,128)}, u32[]{:S(2)}, u32[]{:S(2)}) %collective-permute-start.18) | collective-permute-done | bytes 909344 | tf_op jit(solution)/shard_map/ppermute | solution.py:96
  213.2 22.8 %collective-permute-done.20 = f32[152,384]{1,0:T(8,128)S(1)} collective-permute-done((f32[152,384]{1,0:T(8,128)S(1)}, f32[152,384]{1,0:T(8,128)S(1)}, u32[]{:S(2)}, u32[]{:S(2)}) %collective-permute-start.20) | collective-permute-done | bytes 233504 | tf_op jit(solution)/shard_map/ppermute | solution.py:107
  242.6 2.9 %collective-permute-done.19 = f32[144,384]{1,0:T(8,128)S(1)} collective-permute-done((f32[144,384]{1,0:T(8,128)S(1)}, f32[144,384]{1,0:T(8,128)S(1)}, u32[]{:S(2)}, u32[]{:S(2)}) %collective-permute-start.19) | collective-permute-done | bytes 221216 | tf_op jit(solution)/shard_map/ppermute | solution.py:107
  245.5 3.4 %collective-permute-done.24 = f32[576]{0:T(1024)S(1)} collective-permute-done((f32[576]{0:T(1024)S(1)}, f32[576]{0:T(1024)S(1)}, u32[]{:S(2)}, u32[]{:S(2)}) %collective-permute-start.24) | collective-permute-done | bytes 2336 | tf_op jit(solution)/shard_map/ppermute | solution.py:47
  251.7 4.3 %collective-permute-start.26 = (f32[576]{0:T(1024)S(1)}, f32[576]{0:T(1024)S(1)}, u32[]{:S(2)}, u32[]{:S(2)}) collective-permute-start(f32[576]{0:T(1024)S(1)} %add.245), channel_id=1, source_target_pairs={{0,8},{8,0},{1,9},{9,1},{2,10},{10,2},{3,11},{11,3},{4,12},{12,4},... | collective-permute-start | bytes 6920 | tf_op jit(solution)/shard_map/ppermute | solution.py:47
  (133 shorter events, 72.1 us)
Async XLA Ops:
  7.2 250.6 %reduce-scatter.2.cloned.1.call-start = ((), (), s32[]{:S(2)}) async-start(), calls=%async_computation.1 | async-start | bytes 10027008 | tf_op jit(solution)/shard_map/reduce_scatter | solution.py:148
  7.2 11.7 %collective-permute-start.6 = (bf16[576,384]{1,0:T(8,128)(2,1)}, bf16[576,384]{1,0:T(8,128)(2,1)S(1)}, u32[]{:S(2)}, u32[]{:S(2)}) collective-permute-start(bf16[576,384]{1,0:T(8,128)(2,1)} %bitcast.104), channel_id=1, source_target_pairs={{0,1},{1,2},{2,3},{3,0},{4,5},{5,6},{6,7},{7,4},{8,9},{9,10},{10,1... | collective-permute-start | bytes 1327112 | tf_op jit(solution)/shard_map/ppermute | solution.py:32
  9.4 36.8 %collective-permute-start.5 = (bf16[576,384]{1,0:T(8,128)(2,1)}, bf16[576,384]{1,0:T(8,128)(2,1)S(1)}, u32[]{:S(2)}, u32[]{:S(2)}) collective-permute-start(bf16[576,384]{1,0:T(8,128)(2,1)} %bitcast.105), channel_id=1, source_target_pairs={{0,2},{1,3},{2,0},{3,1},{4,6},{5,7},{6,4},{7,5},{8,10},{9,11},{10,... | collective-permute-start | bytes 1327112 | tf_op jit(solution)/shard_map/ppermute | solution.py:32
  12.0 36.3 %collective-permute-start.4 = (bf16[576,384]{1,0:T(8,128)(2,1)}, bf16[576,384]{1,0:T(8,128)(2,1)S(1)}, u32[]{:S(2)}, u32[]{:S(2)}) collective-permute-start(bf16[576,384]{1,0:T(8,128)(2,1)} %bitcast.106), channel_id=1, source_target_pairs={{0,3},{1,0},{2,1},{3,2},{4,7},{5,4},{6,5},{7,6},{8,11},{9,8},{10,9... | collective-permute-start | bytes 1327112 | tf_op jit(solution)/shard_map/ppermute | solution.py:32
  13.1 36.5 %collective-permute-start.3 = (bf16[576,384]{1,0:T(8,128)(2,1)}, bf16[576,384]{1,0:T(8,128)(2,1)S(1)}, u32[]{:S(2)}, u32[]{:S(2)}) collective-permute-start(bf16[576,384]{1,0:T(8,128)(2,1)} %bitcast.107), channel_id=1, source_target_pairs={{0,4},{1,5},{2,6},{3,7},{4,0},{5,1},{6,2},{7,3},{8,12},{9,13},{10,... | collective-permute-start | bytes 1327112 | tf_op jit(solution)/shard_map/ppermute | solution.py:32
  15.8 33.7 %collective-permute-start.2 = (bf16[576,384]{1,0:T(8,128)(2,1)}, bf16[576,384]{1,0:T(8,128)(2,1)S(1)}, u32[]{:S(2)}, u32[]{:S(2)}) collective-permute-start(bf16[576,384]{1,0:T(8,128)(2,1)} %bitcast.108), channel_id=1, source_target_pairs={{0,5},{1,6},{2,7},{3,4},{4,1},{5,2},{6,3},{7,0},{8,13},{9,14},{10,... | collective-permute-start | bytes 1327112 | tf_op jit(solution)/shard_map/ppermute | solution.py:32
  18.9 30.7 %collective-permute-start.1 = (bf16[576,384]{1,0:T(8,128)(2,1)}, bf16[576,384]{1,0:T(8,128)(2,1)S(1)}, u32[]{:S(2)}, u32[]{:S(2)}) collective-permute-start(bf16[576,384]{1,0:T(8,128)(2,1)} %bitcast.109), channel_id=1, source_target_pairs={{0,6},{1,7},{2,4},{3,5},{4,2},{5,3},{6,0},{7,1},{8,14},{9,15},{10,... | collective-permute-start | bytes 1327112 | tf_op jit(solution)/shard_map/ppermute | solution.py:32
  46.2 10.2 %collective-permute-start = (bf16[576,384]{1,0:T(8,128)(2,1)}, bf16[576,384]{1,0:T(8,128)(2,1)S(1)}, u32[]{:S(2)}, u32[]{:S(2)}) collective-permute-start(bf16[576,384]{1,0:T(8,128)(2,1)} %bitcast.110), channel_id=1, source_target_pairs={{0,7},{1,4},{2,5},{3,6},{4,3},{5,0},{6,1},{7,2},{8,15},{9,12},{10,... | collective-permute-start | bytes 1327112 | tf_op jit(solution)/shard_map/ppermute | solution.py:32
  67.7 4.8 %collective-permute-start.9 = (f32[2,384]{1,0:T(2,128)S(1)}, f32[2,384]{1,0:T(2,128)S(1)}, u32[]{:S(2)}, u32[]{:S(2)}) collective-permute-start(f32[2,384]{1,0:T(2,128)S(1)} %pad_maximum_fusion.5), channel_id=1, source_target_pairs={{0,1},{1,2},{2,3},{3,0},{4,5},{5,6},{6,7},{7,4},{8,9},{9,10},{10,1... | collective-permute-start | bytes 9224 | tf_op jit(solution)/shard_map/ppermute | solution.py:60
  68.3 4.2 %collective-permute-start.8 = (f32[2,384]{1,0:T(2,128)S(1)}, f32[2,384]{1,0:T(2,128)S(1)}, u32[]{:S(2)}, u32[]{:S(2)}) collective-permute-start(f32[2,384]{1,0:T(2,128)S(1)} %pad_maximum_fusion.5), channel_id=1, source_target_pairs={{0,2},{1,3},{2,0},{3,1},{4,6},{5,7},{6,4},{7,5},{8,10},{9,11},{10,... | collective-permute-start | bytes 9224 | tf_op jit(solution)/shard_map/ppermute | solution.py:60
  77.3 4.0 %collective-permute-start.10 = (f32[2,384]{1,0:T(2,128)S(1)}, f32[2,384]{1,0:T(2,128)S(1)}, u32[]{:S(2)}, u32[]{:S(2)}) collective-permute-start(f32[2,384]{1,0:T(2,128)S(1)} %pad_maximum_fusion.6), channel_id=1, source_target_pairs={{0,4},{1,5},{2,6},{3,7},{4,0},{5,1},{6,2},{7,3},{8,12},{9,13},{10,... | collective-permute-start | bytes 9224 | tf_op jit(solution)/shard_map/ppermute | solution.py:68
  84.5 25.1 %collective-permute-start.21 = (f32[2304,1024]{1,0:T(8,128)S(1)}, f32[2304,1024]{1,0:T(8,128)S(1)}, u32[]{:S(2)}, u32[]{:S(2)}) collective-permute-start(f32[2304,1024]{1,0:T(8,128)S(1)} %fusion.30), channel_id=1, source_target_pairs={{0,8},{8,0},{1,9},{9,1},{2,10},{10,2},{3,11},{11,3},{4,12},{12,4},... | collective-permute-start | bytes 28311560 | tf_op jit(solution)/shard_map/ppermute | solution.py:146
  128.9 22.4 %collective-permute-start.11 = (f32[2,288,384]{2,1,0:T(8,128)}, f32[2,288,384]{2,1,0:T(8,128)}, u32[]{:S(2)}, u32[]{:S(2)}) collective-permute-start(f32[2,288,384]{2,1,0:T(8,128)} %dynamic-slice_bitcast_fusion.1), channel_id=1, source_target_pairs={{0,1},{1,2},{2,3},{3,0},{4,5},{5,6},{6,7},{7,4},{8,9},{9,10},{10,1... | collective-permute-start | bytes 2654216 | tf_op jit(solution)/shard_map/ppermute | solution.py:95
  139.6 21.7 %collective-permute-start.16 = (f32[2,296,384]{2,1,0:T(8,128)}, f32[2,296,384]{2,1,0:T(8,128)}, u32[]{:S(2)}, u32[]{:S(2)}) collective-permute-start(f32[2,296,384]{2,1,0:T(8,128)} %dynamic-slice_bitcast_fusion), channel_id=1, source_target_pairs={{0,3},{1,0},{2,1},{3,2},{4,7},{5,4},{6,5},{7,6},{8,11},{9,8},{10,9... | collective-permute-start | bytes 2727944 | tf_op jit(solution)/shard_map/ppermute | solution.py:96
  153.5 21.5 %collective-permute-start.12 = (f32[2,288,384]{2,1,0:T(8,128)}, f32[2,288,384]{2,1,0:T(8,128)}, u32[]{:S(2)}, u32[]{:S(2)}) collective-permute-start(f32[2,288,384]{2,1,0:T(8,128)} %bitcast_add_fusion.3), channel_id=1, source_target_pairs={{0,1},{1,2},{2,3},{3,0},{4,5},{5,6},{6,7},{7,4},{8,9},{9,10},{10,1... | collective-permute-start | bytes 2654216 | tf_op jit(solution)/shard_map/ppermute | solution.py:95
  163.8 20.8 %collective-permute-start.17 = (f32[2,296,384]{2,1,0:T(8,128)}, f32[2,296,384]{2,1,0:T(8,128)}, u32[]{:S(2)}, u32[]{:S(2)}) collective-permute-start(f32[2,296,384]{2,1,0:T(8,128)} %bitcast_add_fusion), channel_id=1, source_target_pairs={{0,3},{1,0},{2,1},{3,2},{4,7},{5,4},{6,5},{7,6},{8,11},{9,8},{10,9... | collective-permute-start | bytes 2727944 | tf_op jit(solution)/shard_map/ppermute | solution.py:96
  177.2 20.6 %collective-permute-start.13 = (f32[2,288,384]{2,1,0:T(8,128)}, f32[2,288,384]{2,1,0:T(8,128)}, u32[]{:S(2)}, u32[]{:S(2)}) collective-permute-start(f32[2,288,384]{2,1,0:T(8,128)} %bitcast_add_fusion.4), channel_id=1, source_target_pairs={{0,1},{1,2},{2,3},{3,0},{4,5},{5,6},{6,7},{7,4},{8,9},{9,10},{10,1... | collective-permute-start | bytes 2654216 | tf_op jit(solution)/shard_map/ppermute | solution.py:95
  187.1 20.3 %collective-permute-start.18 = (f32[2,296,384]{2,1,0:T(8,128)}, f32[2,296,384]{2,1,0:T(8,128)}, u32[]{:S(2)}, u32[]{:S(2)}) collective-permute-start(f32[2,296,384]{2,1,0:T(8,128)} %bitcast_add_fusion.1), channel_id=1, source_target_pairs={{0,3},{1,0},{2,1},{3,2},{4,7},{5,4},{6,5},{7,6},{8,11},{9,8},{10,9... | collective-permute-start | bytes 2727944 | tf_op jit(solution)/shard_map/ppermute | solution.py:96
  199.1 37.1 %collective-permute-start.15 = (f32[144,384]{1,0:T(8,128)S(1)}, f32[144,384]{1,0:T(8,128)S(1)}, u32[]{:S(2)}, u32[]{:S(2)}) collective-permute-start(f32[144,384]{1,0:T(8,128)S(1)} %dynamic-slice_bitcast_fusion.4), channel_id=1, source_target_pairs={{0,4},{1,5},{2,6},{3,7},{4,0},{5,1},{6,2},{7,3},{8,12},{9,13},{10,... | collective-permute-start | bytes 663560 | tf_op jit(solution)/shard_map/ppermute | solution.py:107
  209.0 27.0 %collective-permute-start.20 = (f32[152,384]{1,0:T(8,128)S(1)}, f32[152,384]{1,0:T(8,128)S(1)}, u32[]{:S(2)}, u32[]{:S(2)}) collective-permute-start(f32[152,384]{1,0:T(8,128)S(1)} %dynamic-slice_bitcast_fusion.2), channel_id=1, source_target_pairs={{0,4},{1,5},{2,6},{3,7},{4,0},{5,1},{6,2},{7,3},{8,12},{9,13},{10,... | collective-permute-start | bytes 700424 | tf_op jit(solution)/shard_map/ppermute | solution.py:107
  210.0 30.7 %collective-permute-start.14 = (f32[144,384]{1,0:T(8,128)S(1)}, f32[144,384]{1,0:T(8,128)S(1)}, u32[]{:S(2)}, u32[]{:S(2)}) collective-permute-start(f32[144,384]{1,0:T(8,128)S(1)} %dynamic-slice_bitcast_fusion.5), channel_id=1, source_target_pairs={{0,4},{1,5},{2,6},{3,7},{4,0},{5,1},{6,2},{7,3},{8,12},{9,13},{10,... | collective-permute-start | bytes 663560 | tf_op jit(solution)/shard_map/ppermute | solution.py:107
  212.2 33.3 %collective-permute-start.19 = (f32[144,384]{1,0:T(8,128)S(1)}, f32[144,384]{1,0:T(8,128)S(1)}, u32[]{:S(2)}, u32[]{:S(2)}) collective-permute-start(f32[144,384]{1,0:T(8,128)S(1)} %dynamic-slice_bitcast_fusion.3), channel_id=1, source_target_pairs={{0,4},{1,5},{2,6},{3,7},{4,0},{5,1},{6,2},{7,3},{8,12},{9,13},{10,... | collective-permute-start | bytes 663560 | tf_op jit(solution)/shard_map/ppermute | solution.py:107
  242.6 6.4 %collective-permute-start.24 = (f32[576]{0:T(1024)S(1)}, f32[576]{0:T(1024)S(1)}, u32[]{:S(2)}, u32[]{:S(2)}) collective-permute-start(f32[576]{0:T(1024)S(1)} %add.243), channel_id=1, source_target_pairs={{0,64},{16,80},{32,96},{48,112},{64,0},{80,16},{96,32},{112,48},{1... | collective-permute-start | bytes 6920 | tf_op jit(solution)/shard_map/ppermute | solution.py:47
  251.7 5.4 %collective-permute-start.26 = (f32[576]{0:T(1024)S(1)}, f32[576]{0:T(1024)S(1)}, u32[]{:S(2)}, u32[]{:S(2)}) collective-permute-start(f32[576]{0:T(1024)S(1)} %add.245), channel_id=1, source_target_pairs={{0,8},{8,0},{1,9},{9,1},{2,10},{10,2},{3,11},{11,3},{4,12},{12,4},... | collective-permute-start | bytes 6920 | tf_op jit(solution)/shard_map/ppermute | solution.py:47
  (19 other events, 123.5 us)
Sparse Core Ops, SparseCore 0:
  114.9 110.9 reduce-scatter.1

commit v13 on v9

--- a/solution.py
+++ b/solution.py
@@ -86,8 +86,7 @@
     perm_h = [(a * n_lo + l, (n_hi - 1 - a) * n_lo + l) for a in range(n_hi) for l in range(n_lo)]
     out = []
     for part in (sum_f, sum_b):
-        cut = (part.shape[1] // 2) // 8 * 8
-        for piece in (part[:, :cut], part[:, cut:]):
+        for piece in (part,):
             mine = lax.dynamic_index_in_dim(piece, h, 0, keepdims=False)
             if n_hi > 1:
                 other = lax.dynamic_index_in_dim(piece, n_hi - 1 - h, 0, keepdims=False)

time: 265 us -> 266 us (level)
  starting transfers between devices: 50.4 us -> 46.8 us
    ppermute x3, waiting for transfers between devices: 25 us -> 48.5 us  [two_stage_reduce_scatter(): recv_b = lax.ppermute(send_b, axis, perm_b)]
    ppermute x3, waiting for transfers between devices: 23.6 us -> 0.43 us  [two_stage_reduce_scatter(): recv_f = lax.ppermute(send_f, axis, perm_f)]
    ppermute x4 -> x2, waiting for transfers between devices: 27.1 us -> 27.3 us  [two_stage_reduce_scatter(): mine = mine + lax.ppermute(other, axis, perm_h)]
  transfers between devices with their start and end apart: 27 -> 25, of which waited for: 19 -> 16; matrix products, arithmetic and copies ran while one was open for 15% -> 16% of each run, Pallas kernels for 0% -> 0%
where the time goes in v13:
time: 266 us; the launch traced here: 265 us
  waiting for transfers between devices  138 us (52%)
  starting transfers between devices  46.8 us (18%)
  other arithmetic  36.3 us (14%)
  matrix products  19.2 us (7%)
  between operations  14.4 us (5%)
  local copies, waits for them, and re-layouts  11 us (4%)
    ppermute x3, waiting for transfers between devices, two_stage_reduce_scatter(): recv_b = lax.ppermute(send_b, axis, perm_b)  48.5 us
    ppermute x7, waiting for transfers between devices, grid_gather(): got[a, b] = lax.ppermute(x, axis, perm)  33 us
    ppermute x2, waiting for transfers between devices, two_stage_reduce_scatter(): mine = mine + lax.ppermute(other, axis, perm_h)  27.3 us
    ppermute x7, starting transfers between devices, grid_gather(): got[a, b] = lax.ppermute(x, axis, perm)  14.9 us
    ppermute x1, waiting for transfers between devices, shards(): sent = lax.ppermute(head_rows(1 - core), 'core', [(0, 1), (1, 0)])  14.3 us
    ppermute x5, waiting for transfers between devices, butterfly_sum(): x = x + lax.ppermute(x, axis, [(c, c ^ b) for c in range(n)])  11.6 us
    ppermute x1, starting transfers between devices, shards(): sent = lax.ppermute(head_rows(1 - core), 'core', [(0, 1), (1, 0)])  10.3 us
    ppermute x3, starting transfers between devices, two_stage_reduce_scatter(): recv_b = lax.ppermute(send_b, axis, perm_b)  8.33 us
  transfers between devices with their start and end apart: 25, of which 16 were waited for; matrix products, arithmetic and copies ran while one was open for 16% of the time, Pallas kernels for 0%

profile of v13, /device:TPU:1, one launch (start us, length us, event | category | flops | bytes accessed | tf_op | source)
XLA Modules:
  0.0 265.4 jit_solution(12082172822982457341)
XLA Ops:
  13.1 2.7 %collective-permute-start.3 = (bf16[576,384]{1,0:T(8,128)(2,1)}, bf16[576,384]{1,0:T(8,128)(2,1)S(1)}, u32[]{:S(2)}, u32[]{:S(2)}) collective-permute-start(bf16[576,384]{1,0:T(8,128)(2,1)} %bitcast.84), channel_id=1, source_target_pairs={{0,4},{1,5},{2,6},{3,7},{4,0},{5,1},{6,2},{7,3},{8,12},{9,13},{10,... | collective-permute-start | bytes 1327112 | tf_op jit(solution)/shard_map/ppermute | solution.py:32
  16.2 2.7 %collective-permute-done.6 = bf16[576,384]{1,0:T(8,128)(2,1)S(1)} collective-permute-done((bf16[576,384]{1,0:T(8,128)(2,1)}, bf16[576,384]{1,0:T(8,128)(2,1)S(1)}, u32[]{:S(2)}, u32[]{:S(2)}) %collective-permute-start.6) | collective-permute-done | bytes 442400 | tf_op jit(solution)/shard_map/ppermute | solution.py:32
  18.9 5.9 %collective-permute-start.1 = (bf16[576,384]{1,0:T(8,128)(2,1)}, bf16[576,384]{1,0:T(8,128)(2,1)S(1)}, u32[]{:S(2)}, u32[]{:S(2)}) collective-permute-start(bf16[576,384]{1,0:T(8,128)(2,1)} %bitcast.86), channel_id=1, source_target_pairs={{0,6},{1,7},{2,4},{3,5},{4,2},{5,3},{6,0},{7,1},{8,14},{9,15},{10,... | collective-permute-start | bytes 1327112 | tf_op jit(solution)/shard_map/ppermute | solution.py:32
  24.8 21.4 %collective-permute-done.5 = bf16[576,384]{1,0:T(8,128)(2,1)S(1)} collective-permute-done((bf16[576,384]{1,0:T(8,128)(2,1)}, bf16[576,384]{1,0:T(8,128)(2,1)S(1)}, u32[]{:S(2)}, u32[]{:S(2)}) %collective-permute-start.5) | collective-permute-done | bytes 442400 | tf_op jit(solution)/shard_map/ppermute | solution.py:32
  47.6 8.9 %collective-permute-done = bf16[576,384]{1,0:T(8,128)(2,1)S(1)} collective-permute-done((bf16[576,384]{1,0:T(8,128)(2,1)}, bf16[576,384]{1,0:T(8,128)(2,1)S(1)}, u32[]{:S(2)}, u32[]{:S(2)}) %collective-permute-start) | collective-permute-done | bytes 442400 | tf_op jit(solution)/shard_map/ppermute | solution.py:32
  56.8 4.5 %multiply_reduce_fusion = (f32[384]{0:T(512)S(1)}, f32[2,4,576,384]{3,2,1,0:T(8,128)S(1)}) fusion(s32[]{:T(128)S(6)} %select_n.94, s32[]{:T(128)S(6)} %select_n.97, bf16[1,4,576,384]{3,2,1,0:T(8,128)(2,1)S(1)} %maximum_bitcast_fusion.1, bf16[1,4,576,384]{3,2,1,0:T(8,128)(2,1)S(1)} %maximum_bitcast_fusion), kind=kLoop, calls=%fused_computation.17 | loop fusion | flops 17694336 | bytes 10618376 | tf_op jit(solution)/shard_map/reduce_sum | solution.py:107
  64.1 3.9 %fusion.27 = (f32[384]{0:T(512)S(1)}, f32[384,1024]{1,0:T(8,128)S(1)}) fusion(bf16[4608,384]{1,0:T(8,128)(2,1)S(1)} %fusion.3, bf16[4608,1024]{1,0:T(8,128)(2,1)S(1)} %bitcast.78), kind=kOutput, calls=%fused_computation.84 | convolution fusion | flops 3624271360 | bytes 14550528 | tf_op jit(solution)/shard_map/dot_general | solution.py:111
  73.4 3.5 %multiply_convert_fusion = bf16[16,2,144,384]{3,2,1,0:T(8,128)(2,1)S(1)} fusion(f32[16,2,144,384]{3,2,1,0:T(8,128)} %bitcast.73, f32[16,2,144]{2,1,0:T(2,128)S(1)} %mul.186, f32[384]{0:T(512)S(1)} %add_rsqrt_fusion), kind=kLoop, calls=%fused_computation.16 | loop fusion | flops 5308416 | bytes 10636800 | tf_op jit(solution)/shard_map/convert_element_type | solution.py:110
  77.0 2.9 %collective-permute-start.9 = (f32[2,384]{1,0:T(2,128)S(1)}, f32[2,384]{1,0:T(2,128)S(1)}, u32[]{:S(2)}, u32[]{:S(2)}) collective-permute-start(f32[2,384]{1,0:T(2,128)S(1)} %pad_maximum_fusion.5), channel_id=1, source_target_pairs={{0,4},{1,5},{2,6},{3,7},{4,0},{5,1},{6,2},{7,3},{8,12},{9,13},{10,... | collective-permute-start | bytes 9224 | tf_op jit(solution)/shard_map/ppermute | solution.py:56
  84.1 10.3 %collective-permute-start.18 = (f32[2304,1024]{1,0:T(8,128)S(1)}, f32[2304,1024]{1,0:T(8,128)S(1)}, u32[]{:S(2)}, u32[]{:S(2)}) collective-permute-start(f32[2304,1024]{1,0:T(8,128)S(1)} %fusion.28), channel_id=1, source_target_pairs={{0,8},{8,0},{1,9},{9,1},{2,10},{10,2},{3,11},{11,3},{4,12},{12,4},... | collective-permute-start | bytes 28311560 | tf_op jit(solution)/shard_map/ppermute | solution.py:132
  94.4 14.3 %collective-permute-done.18 = f32[2304,1024]{1,0:T(8,128)S(1)} collective-permute-done((f32[2304,1024]{1,0:T(8,128)S(1)}, f32[2304,1024]{1,0:T(8,128)S(1)}, u32[]{:S(2)}, u32[]{:S(2)}) %collective-permute-start.18) | collective-permute-done | bytes 9437216 | tf_op jit(solution)/shard_map/ppermute | solution.py:132
  108.7 5.1 %convolution_add_fusion = f32[2304,1024]{1,0:T(8,128)} fusion(f32[2304,1024]{1,0:T(8,128)S(1)} %collective-permute-done.18, bf16[2304,384]{1,0:T(8,128)(2,1)S(1)} %bitcast.79, bf16[384,1024]{1,0:T(8,128)(2,1)S(1)} %subtract_convert_fusion), kind=kOutput, calls=%fused_computation.18 | convolution fusion | flops 1814298624 | bytes 21430272 | tf_op jit(solution)/shard_map/dot_general | solution.py:128
  114.0 3.5 %bitcast_multiply_fusion = f32[8,576,384]{2,1,0:T(8,128)S(1)} fusion(f32[2,4,576,384]{3,2,1,0:T(8,128)} %copy-done, f32[384]{0:T(512)S(1)} %add_rsqrt_fusion), kind=kLoop, calls=%fused_computation.8 | loop fusion | flops 1769472 | bytes 14157312 | tf_op jit(solution)/shard_map/mul | solution.py:109
  117.5 7.6 %fusion.13 = f32[8,384,576]{1,2,0:T(8,128)S(1)} fusion(bf16[8,576,1024]{2,1,0:T(8,128)(2,1)} %bitcast.76, bf16[384,1024]{1,0:T(8,128)(2,1)S(1)} %subtract_convert_fusion), kind=kOutput, calls=%fused_computation.30 | convolution fusion | flops 3623878656 | bytes 17301504 | tf_op jit(solution)/shard_map/dot_general | solution.py:136
  138.2 16.6 %collective-permute-done.14 = f32[2,296,384]{2,1,0:T(8,128)} collective-permute-done((f32[2,296,384]{2,1,0:T(8,128)}, f32[2,296,384]{2,1,0:T(8,128)}, u32[]{:S(2)}, u32[]{:S(2)}) %collective-permute-start.14) | collective-permute-done | bytes 909344 | tf_op jit(solution)/shard_map/ppermute | solution.py:83
  157.3 3.1 %collective-permute-start.15 = (f32[2,296,384]{2,1,0:T(8,128)}, f32[2,296,384]{2,1,0:T(8,128)}, u32[]{:S(2)}, u32[]{:S(2)}) collective-permute-start(f32[2,296,384]{2,1,0:T(8,128)} %bitcast_add_fusion), channel_id=1, source_target_pairs={{0,3},{1,0},{2,1},{3,2},{4,7},{5,4},{6,5},{7,6},{8,11},{9,8},{10,9... | collective-permute-start | bytes 2727944 | tf_op jit(solution)/shard_map/ppermute | solution.py:83
  162.6 16.4 %collective-permute-done.15 = f32[2,296,384]{2,1,0:T(8,128)} collective-permute-done((f32[2,296,384]{2,1,0:T(8,128)}, f32[2,296,384]{2,1,0:T(8,128)}, u32[]{:S(2)}, u32[]{:S(2)}) %collective-permute-start.15) | collective-permute-done | bytes 909344 | tf_op jit(solution)/shard_map/ppermute | solution.py:83
  181.5 3.4 %collective-permute-start.16 = (f32[2,296,384]{2,1,0:T(8,128)}, f32[2,296,384]{2,1,0:T(8,128)}, u32[]{:S(2)}, u32[]{:S(2)}) collective-permute-start(f32[2,296,384]{2,1,0:T(8,128)} %bitcast_add_fusion.1), channel_id=1, source_target_pairs={{0,3},{1,0},{2,1},{3,2},{4,7},{5,4},{6,5},{7,6},{8,11},{9,8},{10,9... | collective-permute-start | bytes 2727944 | tf_op jit(solution)/shard_map/ppermute | solution.py:83
  187.0 15.5 %collective-permute-done.16 = f32[2,296,384]{2,1,0:T(8,128)} collective-permute-done((f32[2,296,384]{2,1,0:T(8,128)}, f32[2,296,384]{2,1,0:T(8,128)}, u32[]{:S(2)}, u32[]{:S(2)}) %collective-permute-start.16) | collective-permute-done | bytes 909344 | tf_op jit(solution)/shard_map/ppermute | solution.py:83
  210.3 25.5 %collective-permute-done.17 = f32[296,384]{1,0:T(8,128)} collective-permute-done((f32[296,384]{1,0:T(8,128)}, f32[296,384]{1,0:T(8,128)}, u32[]{:S(2)}, u32[]{:S(2)}) %collective-permute-start.17) | collective-permute-done | bytes 454688 | tf_op jit(solution)/shard_map/ppermute | solution.py:93
  237.0 2.7 %collective-permute-done.19 = f32[576]{0:T(1024)S(1)} collective-permute-done((f32[576]{0:T(1024)S(1)}, f32[576]{0:T(1024)S(1)}, u32[]{:S(2)}, u32[]{:S(2)}) %collective-permute-start.19) | collective-permute-done | bytes 2336 | tf_op jit(solution)/shard_map/ppermute | solution.py:47
  240.5 2.9 %collective-permute-done.20 = f32[576]{0:T(1024)S(1)} collective-permute-done((f32[576]{0:T(1024)S(1)}, f32[576]{0:T(1024)S(1)}, u32[]{:S(2)}, u32[]{:S(2)}) %collective-permute-start.20) | collective-permute-done | bytes 2336 | tf_op jit(solution)/shard_map/ppermute | solution.py:47
  246.3 3.5 %collective-permute-done.21 = f32[576]{0:T(1024)S(1)} collective-permute-done((f32[576]{0:T(1024)S(1)}, f32[576]{0:T(1024)S(1)}, u32[]{:S(2)}, u32[]{:S(2)}) %collective-permute-start.21) | collective-permute-done | bytes 2336 | tf_op jit(solution)/shard_map/ppermute | solution.py:47
  252.6 4.3 %collective-permute-start.23 = (f32[576]{0:T(1024)S(1)}, f32[576]{0:T(1024)S(1)}, u32[]{:S(2)}, u32[]{:S(2)}) collective-permute-start(f32[576]{0:T(1024)S(1)} %add.256), channel_id=1, source_target_pairs={{0,8},{8,0},{1,9},{9,1},{2,10},{10,2},{3,11},{11,3},{4,12},{12,4},... | collective-permute-start | bytes 6920 | tf_op jit(solution)/shard_map/ppermute | solution.py:47
  (108 shorter events, 59.9 us)
Async XLA Ops:
  7.2 251.4 %reduce-scatter.2.cloned.1.call-start = ((), (), s32[]{:S(2)}) async-start(), calls=%async_computation.1 | async-start | bytes 10027008 | tf_op jit(solution)/shard_map/reduce_scatter | solution.py:134
  7.2 11.7 %collective-permute-start.6 = (bf16[576,384]{1,0:T(8,128)(2,1)}, bf16[576,384]{1,0:T(8,128)(2,1)S(1)}, u32[]{:S(2)}, u32[]{:S(2)}) collective-permute-start(bf16[576,384]{1,0:T(8,128)(2,1)} %bitcast.81), channel_id=1, source_target_pairs={{0,1},{1,2},{2,3},{3,0},{4,5},{5,6},{6,7},{7,4},{8,9},{9,10},{10,1... | collective-permute-start | bytes 1327112 | tf_op jit(solution)/shard_map/ppermute | solution.py:32
  9.4 36.8 %collective-permute-start.5 = (bf16[576,384]{1,0:T(8,128)(2,1)}, bf16[576,384]{1,0:T(8,128)(2,1)S(1)}, u32[]{:S(2)}, u32[]{:S(2)}) collective-permute-start(bf16[576,384]{1,0:T(8,128)(2,1)} %bitcast.82), channel_id=1, source_target_pairs={{0,2},{1,3},{2,0},{3,1},{4,6},{5,7},{6,4},{7,5},{8,10},{9,11},{10,... | collective-permute-start | bytes 1327112 | tf_op jit(solution)/shard_map/ppermute | solution.py:32
  12.0 34.2 %collective-permute-start.4 = (bf16[576,384]{1,0:T(8,128)(2,1)}, bf16[576,384]{1,0:T(8,128)(2,1)S(1)}, u32[]{:S(2)}, u32[]{:S(2)}) collective-permute-start(bf16[576,384]{1,0:T(8,128)(2,1)} %bitcast.83), channel_id=1, source_target_pairs={{0,3},{1,0},{2,1},{3,2},{4,7},{5,4},{6,5},{7,6},{8,11},{9,8},{10,9... | collective-permute-start | bytes 1327112 | tf_op jit(solution)/shard_map/ppermute | solution.py:32
  13.1 34.5 %collective-permute-start.3 = (bf16[576,384]{1,0:T(8,128)(2,1)}, bf16[576,384]{1,0:T(8,128)(2,1)S(1)}, u32[]{:S(2)}, u32[]{:S(2)}) collective-permute-start(bf16[576,384]{1,0:T(8,128)(2,1)} %bitcast.84), channel_id=1, source_target_pairs={{0,4},{1,5},{2,6},{3,7},{4,0},{5,1},{6,2},{7,3},{8,12},{9,13},{10,... | collective-permute-start | bytes 1327112 | tf_op jit(solution)/shard_map/ppermute | solution.py:32
  15.8 31.7 %collective-permute-start.2 = (bf16[576,384]{1,0:T(8,128)(2,1)}, bf16[576,384]{1,0:T(8,128)(2,1)S(1)}, u32[]{:S(2)}, u32[]{:S(2)}) collective-permute-start(bf16[576,384]{1,0:T(8,128)(2,1)} %bitcast.85), channel_id=1, source_target_pairs={{0,5},{1,6},{2,7},{3,4},{4,1},{5,2},{6,3},{7,0},{8,13},{9,14},{10,... | collective-permute-start | bytes 1327112 | tf_op jit(solution)/shard_map/ppermute | solution.py:32
  18.9 28.7 %collective-permute-start.1 = (bf16[576,384]{1,0:T(8,128)(2,1)}, bf16[576,384]{1,0:T(8,128)(2,1)S(1)}, u32[]{:S(2)}, u32[]{:S(2)}) collective-permute-start(bf16[576,384]{1,0:T(8,128)(2,1)} %bitcast.86), channel_id=1, source_target_pairs={{0,6},{1,7},{2,4},{3,5},{4,2},{5,3},{6,0},{7,1},{8,14},{9,15},{10,... | collective-permute-start | bytes 1327112 | tf_op jit(solution)/shard_map/ppermute | solution.py:32
  46.2 10.2 %collective-permute-start = (bf16[576,384]{1,0:T(8,128)(2,1)}, bf16[576,384]{1,0:T(8,128)(2,1)S(1)}, u32[]{:S(2)}, u32[]{:S(2)}) collective-permute-start(bf16[576,384]{1,0:T(8,128)(2,1)} %bitcast.87), channel_id=1, source_target_pairs={{0,7},{1,4},{2,5},{3,6},{4,3},{5,0},{6,1},{7,2},{8,15},{9,12},{10,... | collective-permute-start | bytes 1327112 | tf_op jit(solution)/shard_map/ppermute | solution.py:32
  71.0 5.9 %collective-permute-start.8 = (f32[2,384]{1,0:T(2,128)S(1)}, f32[2,384]{1,0:T(2,128)S(1)}, u32[]{:S(2)}, u32[]{:S(2)}) collective-permute-start(f32[2,384]{1,0:T(2,128)S(1)} %pad_maximum_fusion.4), channel_id=1, source_target_pairs={{0,2},{1,3},{2,0},{3,1},{4,6},{5,7},{6,4},{7,5},{8,10},{9,11},{10,... | collective-permute-start | bytes 9224 | tf_op jit(solution)/shard_map/ppermute | solution.py:56
  77.0 4.0 %collective-permute-start.9 = (f32[2,384]{1,0:T(2,128)S(1)}, f32[2,384]{1,0:T(2,128)S(1)}, u32[]{:S(2)}, u32[]{:S(2)}) collective-permute-start(f32[2,384]{1,0:T(2,128)S(1)} %pad_maximum_fusion.5), channel_id=1, source_target_pairs={{0,4},{1,5},{2,6},{3,7},{4,0},{5,1},{6,2},{7,3},{8,12},{9,13},{10,... | collective-permute-start | bytes 9224 | tf_op jit(solution)/shard_map/ppermute | solution.py:56
  84.1 24.6 %collective-permute-start.18 = (f32[2304,1024]{1,0:T(8,128)S(1)}, f32[2304,1024]{1,0:T(8,128)S(1)}, u32[]{:S(2)}, u32[]{:S(2)}) collective-permute-start(f32[2304,1024]{1,0:T(8,128)S(1)} %fusion.28), channel_id=1, source_target_pairs={{0,8},{8,0},{1,9},{9,1},{2,10},{10,2},{3,11},{11,3},{4,12},{12,4},... | collective-permute-start | bytes 28311560 | tf_op jit(solution)/shard_map/ppermute | solution.py:132
  133.1 21.7 %collective-permute-start.14 = (f32[2,296,384]{2,1,0:T(8,128)}, f32[2,296,384]{2,1,0:T(8,128)}, u32[]{:S(2)}, u32[]{:S(2)}) collective-permute-start(f32[2,296,384]{2,1,0:T(8,128)} %dynamic-slice_bitcast_fusion), channel_id=1, source_target_pairs={{0,3},{1,0},{2,1},{3,2},{4,7},{5,4},{6,5},{7,6},{8,11},{9,8},{10,9... | collective-permute-start | bytes 2727944 | tf_op jit(solution)/shard_map/ppermute | solution.py:83
  138.2 22.1 %collective-permute-start.10 = (f32[2,288,384]{2,1,0:T(8,128)}, f32[2,288,384]{2,1,0:T(8,128)}, u32[]{:S(2)}, u32[]{:S(2)}) collective-permute-start(f32[2,288,384]{2,1,0:T(8,128)} %dynamic-slice_bitcast_fusion.1), channel_id=1, source_target_pairs={{0,1},{1,2},{2,3},{3,0},{4,5},{5,6},{6,7},{7,4},{8,9},{9,10},{10,1... | collective-permute-start | bytes 2654216 | tf_op jit(solution)/shard_map/ppermute | solution.py:82
  157.3 21.7 %collective-permute-start.15 = (f32[2,296,384]{2,1,0:T(8,128)}, f32[2,296,384]{2,1,0:T(8,128)}, u32[]{:S(2)}, u32[]{:S(2)}) collective-permute-start(f32[2,296,384]{2,1,0:T(8,128)} %bitcast_add_fusion), channel_id=1, source_target_pairs={{0,3},{1,0},{2,1},{3,2},{4,7},{5,4},{6,5},{7,6},{8,11},{9,8},{10,9... | collective-permute-start | bytes 2727944 | tf_op jit(solution)/shard_map/ppermute | solution.py:83
  162.6 22.3 %collective-permute-start.11 = (f32[2,288,384]{2,1,0:T(8,128)}, f32[2,288,384]{2,1,0:T(8,128)}, u32[]{:S(2)}, u32[]{:S(2)}) collective-permute-start(f32[2,288,384]{2,1,0:T(8,128)} %bitcast_add_fusion.3), channel_id=1, source_target_pairs={{0,1},{1,2},{2,3},{3,0},{4,5},{5,6},{6,7},{7,4},{8,9},{9,10},{10,1... | collective-permute-start | bytes 2654216 | tf_op jit(solution)/shard_map/ppermute | solution.py:82
  181.5 21.0 %collective-permute-start.16 = (f32[2,296,384]{2,1,0:T(8,128)}, f32[2,296,384]{2,1,0:T(8,128)}, u32[]{:S(2)}, u32[]{:S(2)}) collective-permute-start(f32[2,296,384]{2,1,0:T(8,128)} %bitcast_add_fusion.1), channel_id=1, source_target_pairs={{0,3},{1,0},{2,1},{3,2},{4,7},{5,4},{6,5},{7,6},{8,11},{9,8},{10,9... | collective-permute-start | bytes 2727944 | tf_op jit(solution)/shard_map/ppermute | solution.py:83
  187.0 20.3 %collective-permute-start.12 = (f32[2,288,384]{2,1,0:T(8,128)}, f32[2,288,384]{2,1,0:T(8,128)}, u32[]{:S(2)}, u32[]{:S(2)}) collective-permute-start(f32[2,288,384]{2,1,0:T(8,128)} %bitcast_add_fusion.4), channel_id=1, source_target_pairs={{0,1},{1,2},{2,3},{3,0},{4,5},{5,6},{6,7},{7,4},{8,9},{9,10},{10,1... | collective-permute-start | bytes 2654216 | tf_op jit(solution)/shard_map/ppermute | solution.py:82
  205.8 30.0 %collective-permute-start.17 = (f32[296,384]{1,0:T(8,128)}, f32[296,384]{1,0:T(8,128)}, u32[]{:S(2)}, u32[]{:S(2)}) collective-permute-start(f32[296,384]{1,0:T(8,128)} %dynamic-slice_bitcast_fusion.2), channel_id=1, source_target_pairs={{0,4},{1,5},{2,6},{3,7},{4,0},{5,1},{6,2},{7,3},{8,12},{9,13},{10,... | collective-permute-start | bytes 1363976 | tf_op jit(solution)/shard_map/ppermute | solution.py:93
  208.6 36.6 %collective-permute-start.13 = (f32[288,384]{1,0:T(8,128)S(1)}, f32[288,384]{1,0:T(8,128)S(1)}, u32[]{:S(2)}, u32[]{:S(2)}) collective-permute-start(f32[288,384]{1,0:T(8,128)S(1)} %dynamic-slice_bitcast_fusion.3), channel_id=1, source_target_pairs={{0,4},{1,5},{2,6},{3,7},{4,0},{5,1},{6,2},{7,3},{8,12},{9,13},{10,... | collective-permute-start | bytes 1327112 | tf_op jit(solution)/shard_map/ppermute | solution.py:93
  236.9 2.8 %collective-permute-start.19 = (f32[576]{0:T(1024)S(1)}, f32[576]{0:T(1024)S(1)}, u32[]{:S(2)}, u32[]{:S(2)}) collective-permute-start(f32[576]{0:T(1024)S(1)} %bitcast.96), channel_id=1, source_target_pairs={{0,16},{16,0},{32,48},{48,32},{64,80},{80,64},{96,112},{112,96},{1... | collective-permute-start | bytes 6920 | tf_op jit(solution)/shard_map/ppermute | solution.py:47
  239.8 3.7 %collective-permute-start.20 = (f32[576]{0:T(1024)S(1)}, f32[576]{0:T(1024)S(1)}, u32[]{:S(2)}, u32[]{:S(2)}) collective-permute-start(f32[576]{0:T(1024)S(1)} %slice_add_fusion), channel_id=1, source_target_pairs={{0,32},{16,48},{32,0},{48,16},{64,96},{80,112},{96,64},{112,80},{1... | collective-permute-start | bytes 6920 | tf_op jit(solution)/shard_map/ppermute | solution.py:47
  243.4 6.4 %collective-permute-start.21 = (f32[576]{0:T(1024)S(1)}, f32[576]{0:T(1024)S(1)}, u32[]{:S(2)}, u32[]{:S(2)}) collective-permute-start(f32[576]{0:T(1024)S(1)} %add.254), channel_id=1, source_target_pairs={{0,64},{16,80},{32,96},{48,112},{64,0},{80,16},{96,32},{112,48},{1... | collective-permute-start | bytes 6920 | tf_op jit(solution)/shard_map/ppermute | solution.py:47
  249.8 2.8 %collective-permute-start.22 = (f32[576]{0:T(1024)S(1)}, f32[576]{0:T(1024)S(1)}, u32[]{:S(2)}, u32[]{:S(2)}) collective-permute-start(f32[576]{0:T(1024)S(1)} %add.255), channel_id=1, source_target_pairs={{0,128},{16,144},{32,160},{48,176},{64,192},{80,208},{96,224},{112... | collective-permute-start | bytes 6920 | tf_op jit(solution)/shard_map/ppermute | solution.py:47
  252.6 5.4 %collective-permute-start.23 = (f32[576]{0:T(1024)S(1)}, f32[576]{0:T(1024)S(1)}, u32[]{:S(2)}, u32[]{:S(2)}) collective-permute-start(f32[576]{0:T(1024)S(1)} %add.256), channel_id=1, source_target_pairs={{0,8},{8,0},{1,9},{9,1},{2,10},{10,2},{3,11},{11,3},{4,12},{12,4},... | collective-permute-start | bytes 6920 | tf_op jit(solution)/shard_map/ppermute | solution.py:47
  (13 other events, 142.7 us)
Sparse Core Ops, SparseCore 0:
  113.9 111.5 reduce-scatter.1
